TPU v7x, 512 devices: a whole 4x8x8 slice. The times are simulated.
512 devices in a mesh: row: 32 (over z, x), col: 16 (over y, core).
Axes of the slice: x: 4, y: 8, z: 8, core: 2. Of those that a mesh axis runs over, the one named last changes fastest.
Arguments:
- tokens: bfloat16 [16384, 5376], P('row', 'col'), may hold values from -240 to 240
- gain: float32 [5376], P('col'), may hold values from 0.1 to 1.9
- query_gain: float32 [128], replicated, may hold values from 0.1 to 1.9
- key_gain: float32 [128], replicated, may hold values from 0.1 to 1.9
- w_query: bfloat16 [5376, 4096], P('row', 'col'), may hold values from -0.21808224 to 0.21808224
- w_key: bfloat16 [5376, 2048], P('row', 'col'), may hold values from -0.21808224 to 0.21808224
- w_value: bfloat16 [5376, 2048], P('row', 'col'), may hold values from -0.21808224 to 0.21808224
Outputs:
- attended: bfloat16 [16384, 4096], P('row', 'col')
All inputs are finite; a program needn't handle non-finite values.
Results may differ from a plain program's by a relative error of at most 0.022.
Values may be sent and summed in bfloat16 or wider, within the bound.
No kernel may reach another device: no remote copies, remote signals or barrier semaphores. Data moves between devices by JAX's collectives and lax.ppermute only.
A program may use at most 64 MiB of HBM per device.

v0:
```python
import jax
import jax.numpy as jnp
from jax import lax
from jax.sharding import PartitionSpec as P

D = 5376
HD = 128
WINDOW = 1024


EPS = 1e-06
CLIP_FRACTION = 0.25
QUERY_SCALAR = 168.0
ROPE_BASE = 10000.0


def shifted(array, axis, by):
    peers = lax.axis_size(axis)
    pairs = [(i, i + by) for i in range(peers) if 0 <= i + by < peers]
    return lax.ppermute(array, axis, pairs)


def clip_with(weight, largest):
    bound = CLIP_FRACTION * largest
    return jnp.clip(weight.astype(jnp.float32), -bound, bound).astype(jnp.bfloat16)


def column_max(weight):
    return jnp.max(jnp.abs(weight.astype(jnp.float32)), axis=0)


def head_norm(values, head_gain):
    return values * lax.rsqrt(jnp.mean(values * values, axis=-1, keepdims=True) + EPS) * head_gain


def rotate(values, positions):
    half = values.shape[-1] // 2
    freqs = ROPE_BASE ** (-(jnp.arange(half, dtype=jnp.float32) * 2.0 / values.shape[-1]))
    angles = positions.astype(jnp.float32)[:, None] * freqs[None, :]
    cosine = jnp.cos(angles)[:, None, :]
    sine = jnp.sin(angles)[:, None, :]
    first = values[..., :half]
    second = values[..., half:]
    return jnp.concatenate(
        [first * cosine - second * sine, second * cosine + first * sine], axis=-1
    )


def local(tokens, gain, query_gain, key_gain, w_query, w_key, w_value):
    rows = tokens.shape[0]
    widened = tokens.astype(jnp.float32)
    squares = lax.psum(jnp.sum(widened * widened, axis=1), "col")
    inverse = lax.rsqrt(squares / D + EPS)[:, None]
    normed = (widened * inverse * gain[None, :]).astype(jnp.bfloat16)
    whole = lax.all_gather(normed, "col", axis=1, tiled=True)
    query_cols = w_query.shape[1]
    key_cols = w_key.shape[1]
    max_query, max_key, max_value = lax.pmax(
        (column_max(w_query), column_max(w_key), column_max(w_value)), "row"
    )
    clip_query = clip_with(w_query, max_query)
    clip_key = clip_with(w_key, max_key)
    clip_value = clip_with(w_value, max_value)
    panels = (
        lax.all_gather(clip_query, "row", axis=0, tiled=True),
        lax.all_gather(clip_key, "row", axis=0, tiled=True),
        lax.all_gather(clip_value, "row", axis=0, tiled=True),
    )
    query, keys, values = tuple(
        (jnp.dot(whole, panel, preferred_element_type=jnp.float32) for panel in panels)
    )
    heads_local = query_cols // HD
    kv_local = key_cols // HD
    group = heads_local // kv_local
    positions = lax.axis_index("row") * rows + jnp.arange(rows, dtype=jnp.int32)
    query = rotate(head_norm(query.reshape(rows, heads_local, HD), query_gain), positions).astype(
        jnp.bfloat16
    )
    keys = rotate(head_norm(keys.reshape(rows, kv_local, HD), key_gain), positions).astype(
        jnp.bfloat16
    )
    values = values.reshape(rows, kv_local, HD).astype(jnp.bfloat16)
    blocks_back = WINDOW // rows
    earlier_keys = []
    earlier_values = []
    for offset in range(blocks_back, 0, -1):
        moved_keys, moved_values = shifted((keys, values), "row", offset)
        earlier_keys.append(moved_keys)
        earlier_values.append(moved_values)
    all_keys = jnp.concatenate(earlier_keys + [keys], axis=0)
    all_values = jnp.concatenate(earlier_values + [values], axis=0)
    key_pos = (
        positions[0] - blocks_back * rows + jnp.arange((blocks_back + 1) * rows, dtype=jnp.int32)
    )
    grouped = query.reshape(rows, kv_local, group, HD)
    scores = jnp.einsum(
        "tkgd,skd->kgts", grouped, all_keys, preferred_element_type=jnp.float32
    ) * QUERY_SCALAR ** (-0.5)
    distance = positions[:, None] - key_pos[None, :]
    allowed = (distance >= 0) & (distance < WINDOW) & (key_pos[None, :] >= 0)
    expo = jnp.where(allowed, jnp.exp(scores), 0.0)
    total = jnp.sum(expo, axis=-1, keepdims=True)
    probs = (expo / total).astype(jnp.bfloat16)
    output = jnp.einsum("kgts,skd->tkgd", probs, all_values, preferred_element_type=jnp.float32)
    return output.reshape(rows, query_cols).astype(jnp.bfloat16)


def solution(mesh):
    placed = (
        P("row", "col"),
        P("col"),
        P(),
        P(),
        P("row", "col"),
        P("row", "col"),
        P("row", "col"),
    )
    return jax.shard_map(
        local, mesh=mesh, in_specs=placed, out_specs=P("row", "col"), check_vma=False
    )
```

profile of v0, /device:TPU:1, one launch (start us, length us, event | category | flops | bytes accessed | tf_op | source)
XLA Modules:
  0.0 398.9 jit_solution(10856325609628339359)
XLA Ops:
  8.1 0.9 fusion.30
  9.1 67.5 %all-reduce = (f32[128]{0:T(128)S(1)}, f32[256]{0:T(256)S(1)}, f32[128]{0:T(128)S(1)}) all-reduce(f32[128]{0:T(128)S(1)} %fusion.40, f32[256]{0:T(256)S(1)} %fusion.30, f32[128]{0:T(128)S(1)} %fusion.37), channel_id=1, replica_groups=mesh['row'=32,'col'=16] {'row'}, use_global_device_ids=true, to_apply=%region_5.0 | all-reduce | flops 512 | bytes 4096 | tf_op jit(solution)/shard_map/pmax | solution.py:58
  76.6 1.4 fusion.42
  78.0 1.1 fusion.9
  79.1 38.8 %psum.7 = f32[512]{0:T(512)S(1)} all-reduce(f32[512]{0:T(512)S(1)} %fusion.9), channel_id=1, replica_groups=mesh['row'=32,'col'=16] {'col'}, use_global_device_ids=true, to_apply=%region_1.0 | all-reduce | flops 512 | bytes 4096 | tf_op jit(solution)/shard_map/psum | solution.py:52
  117.9 1.9 fusion.11
  119.9 1.4 fusion.39
  121.4 1.6 fusion.32
  124.2 1.0 multiply_cosine_fusion
  125.2 1.2 fusion.4
  126.4 38.2 %all-gather.9.cloned.1.call-done = bf16[5376,128]{1,0:T(8,128)(2,1)} async-done(((bf16[168,128]{1,0:T(8,128)(2,1)}), bf16[5376,128]{1,0:T(8,128)(2,1)}) %all-gather.9.cloned.1.call-update) | async-done | bytes 1376272 | tf_op jit(solution)/shard_map/all_gather | solution.py:66
  164.7 50.8 %all-gather.5.cloned.1.call-done = bf16[512,5376]{0,1:T(8,128)(2,1)} async-done(((bf16[512,336]{0,1:T(8,128)(2,1)}), bf16[512,5376]{0,1:T(8,128)(2,1)}) %all-gather.5.cloned.1.call-update) | async-done | bytes 5505040 | tf_op jit(solution)/shard_map/all_gather | solution.py:55
  215.4 4.0 multiply_reduce_fusion.1
  220.1 3.1 collective-permute-start.3
  223.2 4.3 %collective-permute-start.2 = (bf16[512,1,128]{0,2,1:T(8,128)(2,1)S(1)}, bf16[512,1,128]{0,2,1:T(8,128)(2,1)S(1)}, u32[]{:S(2)}, u32[]{:S(2)}) collective-permute-start(bf16[512,1,128]{0,2,1:T(8,128)(2,1)S(1)} %pad_maximum_fusion), channel_id=1, source_target_pairs={{0,32},{16,48},{32,64},{48,80},{64,96},{80,112},{96,128},{112,144}... | collective-permute-start | bytes 393224 | tf_op jit(solution)/shard_map/ppermute | solution.py:20
  227.5 68.0 %all-gather.7.cloned.1.call-done = bf16[5376,128]{1,0:T(8,128)(2,1)} async-done(((bf16[168,128]{1,0:T(8,128)(2,1)}), bf16[5376,128]{1,0:T(8,128)(2,1)}) %all-gather.7.cloned.1.call-update) | async-done | bytes 1376272 | tf_op jit(solution)/shard_map/all_gather | solution.py:67
  295.6 4.6 %fusion.8 = bf16[512,1,128]{2,0,1:T(8,128)(2,1)S(1)} fusion(bf16[512,5376]{0,1:T(8,128)(2,1)} %all-gather.5.cloned.1.call-done, bf16[5376,128]{1,0:T(8,128)(2,1)} %all-gather.7.cloned.1.call-done), kind=kOutput, calls=%fused_computation.11 | convolution fusion | flops 704708608 | bytes 7012352 | tf_op jit(solution)/shard_map/dot_general | solution.py:70
  300.2 2.2 collective-permute-start.1
  302.4 3.4 collective-permute-start
  305.8 75.9 %all-gather.11.cloned.1.call-done = bf16[5376,256]{1,0:T(8,128)(2,1)} async-done(((bf16[168,256]{1,0:T(8,128)(2,1)}), bf16[5376,256]{1,0:T(8,128)(2,1)}) %all-gather.11.cloned.1.call-update) | async-done | bytes 2752528 | tf_op jit(solution)/shard_map/all_gather | solution.py:65
  381.8 5.1 %multiply_reduce_fusion = (f32[512,2]{0,1:T(2,128)S(1)}, f32[512,256]{0,1:T(8,128)S(1)}) fusion(bf16[512,5376]{0,1:T(8,128)(2,1)} %all-gather.5.cloned.1.call-done, bf16[5376,256]{1,0:T(8,128)(2,1)} %all-gather.11.cloned.1.call-done), kind=kOutput, calls=%fused_computation.20 | convolution fusion | flops 1409547264 | bytes 8785920 | tf_op jit(solution)/shard_map/dot_general | solution.py:70
  387.6 1.9 fusion
  389.5 2.0 fusion.5
  391.5 0.8 copy.12
  (35 shorter events, 3.8 us)
Async XLA Ops:
  6.5 158.1 %all-gather.9.cloned.1.call-start = ((), (), s32[]{:S(2)}) async-start(), calls=%async_computation.2 | async-start | bytes 1419264 | tf_op jit(solution)/shard_map/all_gather | solution.py:66
  78.0 137.4 %all-gather.5.cloned.1.call-start = ((), (), s32[]{:S(2)}) async-start(), calls=%async_computation | async-start | bytes 5849088 | tf_op jit(solution)/shard_map/all_gather | solution.py:55
  117.9 101.5 %copy-start = (f32[128]{0:T(128)S(1)}, f32[128]{0:T(128)}, u32[]{:S(2)}) copy-start(f32[128]{0:T(128)} %param.10) | copy-start | bytes 1540
  119.8 175.8 %all-gather.7.cloned.1.call-start = ((), (), s32[]{:S(2)}) async-start(), calls=%async_computation.1 | async-start | bytes 1419264 | tf_op jit(solution)/shard_map/all_gather | solution.py:67
  121.3 260.5 %all-gather.11.cloned.1.call-start = ((), (), s32[]{:S(2)}) async-start(), calls=%async_computation.3 | async-start | bytes 2838528 | tf_op jit(solution)/shard_map/all_gather | solution.py:65
  220.1 167.4 %collective-permute-start.3 = (bf16[512,1,128]{0,2,1:T(8,128)(2,1)S(1)}, bf16[512,1,128]{0,2,1:T(8,128)(2,1)S(1)}, u32[]{:S(2)}, u32[]{:S(2)}) collective-permute-start(bf16[512,1,128]{0,2,1:T(8,128)(2,1)S(1)} %pad_maximum_fusion), channel_id=1, source_target_pairs={{0,16},{16,32},{32,48},{48,64},{64,80},{80,96},{96,112},{112,128},... | collective-permute-start | bytes 393224 | tf_op jit(solution)/shard_map/ppermute | solution.py:20
  223.2 164.4 %collective-permute-start.2 = (bf16[512,1,128]{0,2,1:T(8,128)(2,1)S(1)}, bf16[512,1,128]{0,2,1:T(8,128)(2,1)S(1)}, u32[]{:S(2)}, u32[]{:S(2)}) collective-permute-start(bf16[512,1,128]{0,2,1:T(8,128)(2,1)S(1)} %pad_maximum_fusion), channel_id=1, source_target_pairs={{0,32},{16,48},{32,64},{48,80},{64,96},{80,112},{96,128},{112,144}... | collective-permute-start | bytes 393224 | tf_op jit(solution)/shard_map/ppermute | solution.py:20
  300.2 86.9 %copy-start.1 = (f32[128]{0:T(128)S(1)}, f32[128]{0:T(128)}, u32[]{:S(2)}) copy-start(f32[128]{0:T(128)} %param.9) | copy-start | bytes 1540
  300.2 89.3 %collective-permute-start.1 = (bf16[512,1,128]{2,0,1:T(8,128)(2,1)S(1)}, bf16[512,1,128]{2,0,1:T(8,128)(2,1)S(1)}, u32[]{:S(2)}, u32[]{:S(2)}) collective-permute-start(bf16[512,1,128]{2,0,1:T(8,128)(2,1)S(1)} %fusion.8), channel_id=1, source_target_pairs={{0,16},{16,32},{32,48},{48,64},{64,80},{80,96},{96,112},{112,128},... | collective-permute-start | bytes 393224 | tf_op jit(solution)/shard_map/ppermute | solution.py:20
  302.4 87.1 %collective-permute-start = (bf16[512,1,128]{2,0,1:T(8,128)(2,1)S(1)}, bf16[512,1,128]{2,0,1:T(8,128)(2,1)S(1)}, u32[]{:S(2)}, u32[]{:S(2)}) collective-permute-start(bf16[512,1,128]{2,0,1:T(8,128)(2,1)S(1)} %fusion.8), channel_id=1, source_target_pairs={{0,32},{16,48},{32,64},{48,80},{64,96},{80,112},{96,128},{112,144}... | collective-permute-start | bytes 393224 | tf_op jit(solution)/shard_map/ppermute | solution.py:20
Sparse Core Ops, SparseCore 0:
  78.1 86.5 all-gather.8
  166.8 48.5 all-gather.4
  218.6 76.8 all-gather.6
  298.6 83.1 all-gather.10
where the time goes:
time: 402 us; the launch traced here: 399 us
  waiting for transfers between devices  233 us (58%)
  blocking collectives  106 us (26%)
  matrix products  17.6 us (4%)
  between operations  14 us (3%)
  starting transfers between devices  13.2 us (3%)
  other arithmetic  13.2 us (3%)
    all_gather x1, waiting for transfers between devices, local(): lax.all_gather(clip_query, 'row', axis=0, tiled=True)  75.9 us
    all_gather x1, waiting for transfers between devices, local(): lax.all_gather(clip_value, 'row', axis=0, tiled=True)  68 us
    pmax x1, blocking collectives, local(): lax.pmax((column_max(w_query), column_max(w_key), column_max(w_value)), '...  67.5 us
    all_gather x1, waiting for transfers between devices, local(): whole = lax.all_gather(normed, 'col', axis=1, tiled=True)  50.8 us
    psum x1, blocking collectives, local(): squares = lax.psum(jnp.sum(widened * widened, axis=1), 'col')  38.8 us
    all_gather x1, waiting for transfers between devices, local(): lax.all_gather(clip_key, 'row', axis=0, tiled=True)  38.2 us
    dot_general x3, matrix products, local(): jnp.dot(whole, panel, preferred_element_type=jnp.float32)  13.6 us
    ppermute x4, starting transfers between devices, shifted(): return lax.ppermute(array, axis, pairs)  13.1 us
  transfers between devices with their start and end apart: 8, of which 4 were waited for; matrix products, arithmetic and copies ran while one was open for 6% of the time, Pallas kernels for 0%

commit v1 on v0

--- a/solution.py
+++ b/solution.py
@@ -48,27 +48,20 @@
 
 def local(tokens, gain, query_gain, key_gain, w_query, w_key, w_value):
     rows = tokens.shape[0]
+    query_cols = w_query.shape[1]
+    key_cols = w_key.shape[1]
+    stacked = jnp.concatenate([w_query, w_key, w_value], axis=1)
+    panel = lax.all_gather(stacked, "row", axis=0, tiled=True)
+    clipped = clip_with(panel, column_max(panel))
     widened = tokens.astype(jnp.float32)
     squares = lax.psum(jnp.sum(widened * widened, axis=1), "col")
     inverse = lax.rsqrt(squares / D + EPS)[:, None]
     normed = (widened * inverse * gain[None, :]).astype(jnp.bfloat16)
     whole = lax.all_gather(normed, "col", axis=1, tiled=True)
-    query_cols = w_query.shape[1]
-    key_cols = w_key.shape[1]
-    max_query, max_key, max_value = lax.pmax(
-        (column_max(w_query), column_max(w_key), column_max(w_value)), "row"
-    )
-    clip_query = clip_with(w_query, max_query)
-    clip_key = clip_with(w_key, max_key)
-    clip_value = clip_with(w_value, max_value)
-    panels = (
-        lax.all_gather(clip_query, "row", axis=0, tiled=True),
-        lax.all_gather(clip_key, "row", axis=0, tiled=True),
-        lax.all_gather(clip_value, "row", axis=0, tiled=True),
-    )
-    query, keys, values = tuple(
-        (jnp.dot(whole, panel, preferred_element_type=jnp.float32) for panel in panels)
-    )
+    projected = jnp.dot(whole, clipped, preferred_element_type=jnp.float32)
+    query = projected[:, :query_cols]
+    keys = projected[:, query_cols : query_cols + key_cols]
+    values = projected[:, query_cols + key_cols :]
     heads_local = query_cols // HD
     kv_local = key_cols // HD
     group = heads_local // kv_local

time: 402 us -> 192 us (0.48)
  waiting for transfers between devices: 233 us -> 106 us
  blocking collectives: 106 us -> 29.8 us
  matrix products: 17.6 us -> 12 us
    all_gather x3 -> x1, waiting for transfers between devices: 182 us -> 61.7 us  [local(): panel = lax.all_gather(stacked, 'row', axis=0, tiled=True)]
    pmax x1 -> x0, blocking collectives: 67.5 us -> none  [local(): lax.pmax((column_max(w_query), column_max(w_key), column_max(w_value)), '...]
    psum x1, blocking collectives: 38.8 us -> 29.8 us  [local(): squares = lax.psum(jnp.sum(widened * widened, axis=1), 'col')]
    all_gather x1, waiting for transfers between devices: 50.8 us -> 44.7 us  [local(): whole = lax.all_gather(normed, 'col', axis=1, tiled=True)]
    dot_general x3 -> x1, matrix products: 13.6 us -> 8 us  [local(): projected = jnp.dot(whole, clipped, preferred_element_type=jnp.float32)]
    convert_element_type x3 -> x0, other arithmetic: 4.37 us -> none  [clip_with(): jnp.clip(weight.astype(jnp.float32), -bound, bound).astype(jnp.bfloat16)]
  transfers between devices with their start and end apart: 8 -> 6, of which waited for: 4 -> 2; matrix products, arithmetic and copies ran while one was open for 6% -> 6% of each run, Pallas kernels for 0% -> 0%
where the time goes in v1:
time: 192 us; the launch traced here: 190 us
  waiting for transfers between devices  106 us (55%)
  blocking collectives  29.8 us (16%)
  starting transfers between devices  14.7 us (8%)
  between operations  14.3 us (7%)
  matrix products  12 us (6%)
  other arithmetic  11.1 us (6%)
    all_gather x1, waiting for transfers between devices, local(): panel = lax.all_gather(stacked, 'row', axis=0, tiled=True)  61.7 us
    all_gather x1, waiting for transfers between devices, local(): whole = lax.all_gather(normed, 'col', axis=1, tiled=True)  44.7 us
    psum x1, blocking collectives, local(): squares = lax.psum(jnp.sum(widened * widened, axis=1), 'col')  29.8 us
    ppermute x4, starting transfers between devices, shifted(): return lax.ppermute(array, axis, pairs)  14.7 us
    dot_general x1, matrix products, local(): projected = jnp.dot(whole, clipped, preferred_element_type=jnp.float32)  8 us
  transfers between devices with their start and end apart: 6, of which 2 were waited for; matrix products, arithmetic and copies ran while one was open for 6% of the time, Pallas kernels for 0%

profile of v1, /device:TPU:1, one launch (start us, length us, event | category | flops | bytes accessed | tf_op | source)
XLA Modules:
  0.0 190.0 jit_solution(3371415509453140676)
XLA Ops:
  6.5 1.6 pad_maximum_fusion
  8.2 1.1 fusion.15
  9.3 29.8 %psum.7 = f32[512]{0:T(512)S(1)} all-reduce(f32[512]{0:T(512)S(1)} %fusion.15), channel_id=1, replica_groups=mesh['row'=32,'col'=16] {'col'}, use_global_device_ids=true, to_apply=%region_1.2 | all-reduce | flops 512 | bytes 4096 | tf_op jit(solution)/shard_map/psum | solution.py:57
  39.1 1.8 fusion.17
  41.0 0.6 slice.26
  42.3 1.0 multiply_cosine_fusion
  43.3 1.2 fusion.11
  44.5 61.7 %all-gather.5.cloned.1.call-done = bf16[5376,512]{1,0:T(8,128)(2,1)} async-done(((bf16[168,512]{1,0:T(8,128)(2,1)}), bf16[5376,512]{1,0:T(8,128)(2,1)}) %all-gather.5.cloned.1.call-update) | async-done | bytes 5505040 | tf_op jit(solution)/shard_map/all_gather | solution.py:54
  106.2 3.1 %fusion = f32[512]{0:T(512)S(1)} fusion(bf16[5376,512]{1,0:T(8,128)(2,1)} %all-gather.5.cloned.1.call-done), kind=kLoop, calls=%fused_computation.2 | loop fusion | flops 8257024 | bytes 5507072 | tf_op jit(solution)/shard_map/reduce_max | solution.py:29
  109.3 44.7 %all-gather.3.cloned.1.call-done = bf16[512,5376]{0,1:T(8,128)(2,1)} async-done(((bf16[512,336]{0,1:T(8,128)(2,1)}), bf16[512,5376]{0,1:T(8,128)(2,1)}) %all-gather.3.cloned.1.call-update) | async-done | bytes 5505040 | tf_op jit(solution)/shard_map/all_gather | solution.py:60
  154.0 8.0 %fusion.3 = f32[512,512]{0,1:T(8,128)S(1)} fusion(bf16[512,5376]{0,1:T(8,128)(2,1)} %all-gather.3.cloned.1.call-done, bf16[5376,512]{1,0:T(8,128)(2,1)} %all-gather.5.cloned.1.call-done, bf16[512]{0:T(512)(128)(2,1)S(1)} %get-tuple-element.12, bf16[512]{0:T(512)(128)(2,1)S(1)} %get-tuple-element.11), kind=kOutput, calls=%fused_computation.7 | convolution fusion | flops 2835087360 | bytes 12060672 | tf_op jit(solution)/shard_map/dot_general | solution.py:61
  162.1 0.1 multiply_bitcast_fusion
  162.2 0.6 fusion.37
  162.8 4.6 %collective-permute-start.2 = (bf16[512,1,128]{0,2,1:T(8,128)(2,1)S(1)}, bf16[512,1,128]{0,2,1:T(8,128)(2,1)S(1)}, u32[]{:S(2)}, u32[]{:S(2)}) collective-permute-start(bf16[512,1,128]{0,2,1:T(8,128)(2,1)S(1)} %pad_maximum_fusion.1), channel_id=1, source_target_pairs={{0,32},{16,48},{32,64},{48,80},{64,96},{80,112},{96,128},{112,144}... | collective-permute-start | bytes 393224 | tf_op jit(solution)/shard_map/ppermute | solution.py:20
  167.4 2.2 %collective-permute-start.3 = (bf16[512,1,128]{0,2,1:T(8,128)(2,1)S(1)}, bf16[512,1,128]{0,2,1:T(8,128)(2,1)S(1)}, u32[]{:S(2)}, u32[]{:S(2)}) collective-permute-start(bf16[512,1,128]{0,2,1:T(8,128)(2,1)S(1)} %pad_maximum_fusion.1), channel_id=1, source_target_pairs={{0,16},{16,32},{32,48},{48,64},{64,80},{80,96},{96,112},{112,128},... | collective-permute-start | bytes 393224 | tf_op jit(solution)/shard_map/ppermute | solution.py:20
  169.7 0.1 multiply_reduce_fusion
  169.7 4.8 %collective-permute-start = (bf16[512,1,128]{0,2,1:T(8,128)(2,1)S(1)}, bf16[512,1,128]{0,2,1:T(8,128)(2,1)S(1)}, u32[]{:S(2)}, u32[]{:S(2)}) collective-permute-start(bf16[512,1,128]{0,2,1:T(8,128)(2,1)S(1)} %fusion.40), channel_id=1, source_target_pairs={{0,32},{16,48},{32,64},{48,80},{64,96},{80,112},{96,128},{112,144}... | collective-permute-start | bytes 393224 | tf_op jit(solution)/shard_map/ppermute | solution.py:20
  174.5 3.1 %collective-permute-start.1 = (bf16[512,1,128]{0,2,1:T(8,128)(2,1)S(1)}, bf16[512,1,128]{0,2,1:T(8,128)(2,1)S(1)}, u32[]{:S(2)}, u32[]{:S(2)}) collective-permute-start(bf16[512,1,128]{0,2,1:T(8,128)(2,1)S(1)} %fusion.40), channel_id=1, source_target_pairs={{0,16},{16,32},{32,48},{48,64},{64,80},{80,96},{96,112},{112,128},... | collective-permute-start | bytes 393224 | tf_op jit(solution)/shard_map/ppermute | solution.py:20
  177.6 0.2 copy.8
  177.8 0.2 multiply_multiply_fusion
  178.1 0.2 subtract_convert_fusion
  178.3 1.9 %fusion.7 = (f32[2,512]{1,0:T(2,128)S(1)}, f32[1536,512,2]{1,0,2:T(8,128)S(1)}) fusion(pred[512,1536]{0,1:T(8,128)(4,1)S(1)} %fusion.11, bf16[512,2,64]{2,0,1:T(8,128)(2,1)S(1)} %get-tuple-element.6, bf16[512,2,64]{2,0,1:T(8,128)(2,1)S(1)} %get-tuple-element.5, bf16[512,1,64]{0,2,1:T(8,128)(2,1)S(1)} %get-tuple-element.8, ...), kind=kOutput, calls=%fused_computation.10 | convolution fusion | flops 409467904 | bytes 7737344 | tf_op jit(solution)/shard_map/tkgd,skd->kgts/dot_general | solution.py:89
  180.3 2.0 %fusion.12 = bf16[128,2,512]{2,0,1:T(8,128)(2,1)S(1)} fusion(f32[2,512]{1,0:T(2,128)S(1)} %get-tuple-element.13, f32[1536,512,2]{1,0,2:T(8,128)S(1)} %get-tuple-element.14, pred[512,1536]{0,1:T(8,128)(4,1)S(1)} %fusion.11, bf16[512,1,128]{0,2,1:T(8,128)(2,1)S(1)} %fusion.40, bf16[512,1,128]{0,2,1:T(8,128)(2,1)S(1)} %collective-permute-done.1, ...), kind=kOutput, calls=%fused_computation.17 | convolution fusion | flops 410255360 | bytes 7737344 | tf_op jit(solution)/shard_map/kgts,skd->tkgd/dot_general | solution.py:97
  182.4 0.8 copy.11
  (25 shorter events, 0.3 us)
Async XLA Ops:
  6.5 99.7 %all-gather.5.cloned.1.call-start = ((), (), s32[]{:S(2)}) async-start(), calls=%async_computation.1 | async-start | bytes 5677056 | tf_op jit(solution)/shard_map/all_gather | solution.py:54
  8.2 145.8 %all-gather.3.cloned.1.call-start = ((), (), s32[]{:S(2)}) async-start(), calls=%async_computation | async-start | bytes 5849088 | tf_op jit(solution)/shard_map/all_gather | solution.py:60
  154.0 8.1 %copy-start = (f32[128]{0:T(128)S(1)}, f32[128]{0:T(128)}, u32[]{:S(2)}) copy-start(f32[128]{0:T(128)} %param.10) | copy-start | bytes 1540
  154.0 23.8 %copy-start.1 = (f32[128]{0:T(128)S(1)}, f32[128]{0:T(128)}, u32[]{:S(2)}) copy-start(f32[128]{0:T(128)} %param.9) | copy-start | bytes 1540
  162.8 15.5 %collective-permute-start.2 = (bf16[512,1,128]{0,2,1:T(8,128)(2,1)S(1)}, bf16[512,1,128]{0,2,1:T(8,128)(2,1)S(1)}, u32[]{:S(2)}, u32[]{:S(2)}) collective-permute-start(bf16[512,1,128]{0,2,1:T(8,128)(2,1)S(1)} %pad_maximum_fusion.1), channel_id=1, source_target_pairs={{0,32},{16,48},{32,64},{48,80},{64,96},{80,112},{96,128},{112,144}... | collective-permute-start | bytes 393224 | tf_op jit(solution)/shard_map/ppermute | solution.py:20
  167.4 10.9 %collective-permute-start.3 = (bf16[512,1,128]{0,2,1:T(8,128)(2,1)S(1)}, bf16[512,1,128]{0,2,1:T(8,128)(2,1)S(1)}, u32[]{:S(2)}, u32[]{:S(2)}) collective-permute-start(bf16[512,1,128]{0,2,1:T(8,128)(2,1)S(1)} %pad_maximum_fusion.1), channel_id=1, source_target_pairs={{0,16},{16,32},{32,48},{48,64},{64,80},{80,96},{96,112},{112,128},... | collective-permute-start | bytes 393224 | tf_op jit(solution)/shard_map/ppermute | solution.py:20
  169.7 10.5 %collective-permute-start = (bf16[512,1,128]{0,2,1:T(8,128)(2,1)S(1)}, bf16[512,1,128]{0,2,1:T(8,128)(2,1)S(1)}, u32[]{:S(2)}, u32[]{:S(2)}) collective-permute-start(bf16[512,1,128]{0,2,1:T(8,128)(2,1)S(1)} %fusion.40), channel_id=1, source_target_pairs={{0,32},{16,48},{32,64},{48,80},{64,96},{80,112},{96,128},{112,144}... | collective-permute-start | bytes 393224 | tf_op jit(solution)/shard_map/ppermute | solution.py:20
  174.5 5.8 %collective-permute-start.1 = (bf16[512,1,128]{0,2,1:T(8,128)(2,1)S(1)}, bf16[512,1,128]{0,2,1:T(8,128)(2,1)S(1)}, u32[]{:S(2)}, u32[]{:S(2)}) collective-permute-start(bf16[512,1,128]{0,2,1:T(8,128)(2,1)S(1)} %fusion.40), channel_id=1, source_target_pairs={{0,16},{16,32},{32,48},{48,64},{64,80},{80,96},{96,112},{112,128},... | collective-permute-start | bytes 393224 | tf_op jit(solution)/shard_map/ppermute | solution.py:20
Sparse Core Ops, SparseCore 0:
  10.5 95.6 all-gather.4
  108.3 45.6 all-gather.2

commit v2 on v1

--- a/solution.py
+++ b/solution.py
@@ -1,7 +1,7 @@
 import jax
 import jax.numpy as jnp
 from jax import lax
-from jax.sharding import PartitionSpec as P
+from jax.sharding import Mesh, PartitionSpec as P
 
 D = 5376
 HD = 128
@@ -18,6 +18,29 @@
     peers = lax.axis_size(axis)
     pairs = [(i, i + by) for i in range(peers) if 0 <= i + by < peers]
     return lax.ppermute(array, axis, pairs)
+
+
+def ring_gather(parts, axis, dims):
+    peers = lax.axis_size(axis)
+    right = [(i, (i + 1) % peers) for i in range(peers)]
+    left = [(i, (i - 1) % peers) for i in range(peers)]
+    held = {0: parts}
+    forward = parts
+    backward = parts
+    for step in range(1, peers // 2 + 1):
+        forward = lax.ppermute(forward, axis, right)
+        held[peers - step] = forward
+        if step < peers - step:
+            backward = lax.ppermute(backward, axis, left)
+            held[step] = backward
+    start = (peers - lax.axis_index(axis)) % peers
+    out = []
+    for leaf, (dim) in enumerate(dims):
+        stacked = jnp.concatenate([held[k][leaf] for k in range(peers)], axis=dim)
+        doubled = jnp.concatenate([stacked, stacked], axis=dim)
+        size = parts[leaf].shape[dim]
+        out.append(lax.dynamic_slice_in_dim(doubled, start * size, peers * size, dim))
+    return tuple(out)
 
 
 def clip_with(weight, largest):
@@ -53,11 +76,21 @@
     stacked = jnp.concatenate([w_query, w_key, w_value], axis=1)
     panel = lax.all_gather(stacked, "row", axis=0, tiled=True)
     clipped = clip_with(panel, column_max(panel))
-    widened = tokens.astype(jnp.float32)
-    squares = lax.psum(jnp.sum(widened * widened, axis=1), "col")
+    rows_tokens, piece = tokens.shape
+    cores = lax.axis_size("cc")
+    along_y, gain_y = ring_gather((tokens, gain), "cy", (1, 0))
+    along_all, gain_all = ring_gather((along_y, gain_y), "cc", (1, 0))
+    blocks = along_all.shape[1] // (cores * piece)
+    full = (
+        along_all.reshape(rows_tokens, cores, blocks, piece)
+        .transpose(0, 2, 1, 3)
+        .reshape(rows_tokens, cores * blocks * piece)
+    )
+    full_gain = gain_all.reshape(cores, blocks, piece).transpose(1, 0, 2).reshape(-1)
+    widened = full.astype(jnp.float32)
+    squares = jnp.sum(widened * widened, axis=1)
     inverse = lax.rsqrt(squares / D + EPS)[:, None]
-    normed = (widened * inverse * gain[None, :]).astype(jnp.bfloat16)
-    whole = lax.all_gather(normed, "col", axis=1, tiled=True)
+    whole = (widened * inverse * full_gain[None, :]).astype(jnp.bfloat16)
     projected = jnp.dot(whole, clipped, preferred_element_type=jnp.float32)
     query = projected[:, :query_cols]
     keys = projected[:, query_cols : query_cols + key_cols]
@@ -74,14 +107,11 @@
     )
     values = values.reshape(rows, kv_local, HD).astype(jnp.bfloat16)
     blocks_back = WINDOW // rows
-    earlier_keys = []
-    earlier_values = []
-    for offset in range(blocks_back, 0, -1):
-        moved_keys, moved_values = shifted((keys, values), "row", offset)
-        earlier_keys.append(moved_keys)
-        earlier_values.append(moved_values)
-    all_keys = jnp.concatenate(earlier_keys + [keys], axis=0)
-    all_values = jnp.concatenate(earlier_values + [values], axis=0)
+    both = jnp.concatenate([keys, values], axis=1)
+    earlier = [shifted(both, "row", offset) for offset in range(blocks_back, 0, -1)]
+    joined = jnp.concatenate(earlier + [both], axis=0)
+    all_keys = joined[:, :kv_local]
+    all_values = joined[:, kv_local:]
     key_pos = (
         positions[0] - blocks_back * rows + jnp.arange((blocks_back + 1) * rows, dtype=jnp.int32)
     )
@@ -98,16 +128,24 @@
     return output.reshape(rows, query_cols).astype(jnp.bfloat16)
 
 
+CORES_PER_CHIP = 2
+
+
 def solution(mesh):
+    rows, cols = mesh.shape["row"], mesh.shape["col"]
+    split = Mesh(
+        mesh.devices.reshape(rows, cols // CORES_PER_CHIP, CORES_PER_CHIP), ("row", "cy", "cc")
+    )
+    col = ("cy", "cc")
     placed = (
-        P("row", "col"),
-        P("col"),
+        P("row", col),
+        P(col),
         P(),
         P(),
-        P("row", "col"),
-        P("row", "col"),
-        P("row", "col"),
+        P("row", col),
+        P("row", col),
+        P("row", col),
     )
     return jax.shard_map(
-        local, mesh=mesh, in_specs=placed, out_specs=P("row", "col"), check_vma=False
+        local, mesh=split, in_specs=placed, out_specs=P("row", col), check_vma=False
     )

time: 192 us -> 159 us (0.83)
  the two profiles are of different devices: /device:TPU:1 before, /device:TPU:256 now
where the time goes in v2:
time: 159 us; the launch traced here: 158 us
  starting transfers between devices  57.8 us (36%)
  waiting for transfers between devices  40.2 us (25%)
  other arithmetic  25.6 us (16%)
  between operations  14.7 us (9%)
  local copies, waits for them, and re-layouts  10.5 us (7%)
  matrix products  9.09 us (6%)
    ppermute x6, starting transfers between devices, ring_gather(): backward = lax.ppermute(backward, axis, left)  29.5 us
    ppermute x10, waiting for transfers between devices, ring_gather(): forward = lax.ppermute(forward, axis, right)  28.5 us
    ppermute x10, starting transfers between devices, ring_gather(): forward = lax.ppermute(forward, axis, right)  20.7 us
    ppermute x2, waiting for transfers between devices, shifted(): return lax.ppermute(array, axis, pairs)  11.7 us
    convert_element_type x1, other arithmetic, local(): whole = (widened * inverse * full_gain[None, :]).astype(jnp.bfloat16)  8.28 us
    reduce_sum x1, other arithmetic, local(): squares = jnp.sum(widened * widened, axis=1)  8.04 us
    ppermute x2, starting transfers between devices, shifted(): return lax.ppermute(array, axis, pairs)  7.63 us
    convert_element_type x1, local copies, waits for them, and re-layouts, local(): widened = full.astype(jnp.float32)  5.99 us
  transfers between devices with their start and end apart: 19, of which 8 were waited for; matrix products, arithmetic and copies ran while one was open for 18% of the time, Pallas kernels for 0%

profile of v2, /device:TPU:256, one launch (start us, length us, event | category | flops | bytes accessed | tf_op | source)
XLA Modules:
  0.0 158.0 jit_solution(10175887368912250658)
XLA Ops:
  8.2 3.5 %collective-permute-start.3 = (bf16[512,336]{0,1:T(8,128)(2,1)}, bf16[512,336]{0,1:T(8,128)(2,1)S(1)}, u32[]{:S(2)}, u32[]{:S(2)}) collective-permute-start(bf16[512,336]{0,1:T(8,128)(2,1)} %param.7), channel_id=1, source_target_pairs={{0,2},{2,4},{4,6},{6,8},{8,10},{10,12},{12,14},{14,0},{1,3},{3,5},... | collective-permute-start | bytes 1032200 | tf_op jit(solution)/shard_map/ppermute | solution.py:31
  11.7 3.8 %collective-permute-start = (bf16[512,336]{0,1:T(8,128)(2,1)}, bf16[512,336]{0,1:T(8,128)(2,1)S(1)}, u32[]{:S(2)}, u32[]{:S(2)}) collective-permute-start(bf16[512,336]{0,1:T(8,128)(2,1)} %param.7), channel_id=1, source_target_pairs={{0,14},{2,0},{4,2},{6,4},{8,6},{10,8},{12,10},{14,12},{1,15},{3,1}... | collective-permute-start | bytes 1032200 | tf_op jit(solution)/shard_map/ppermute | solution.py:34
  15.6 6.3 %collective-permute-done.3 = bf16[512,336]{0,1:T(8,128)(2,1)S(1)} collective-permute-done((bf16[512,336]{0,1:T(8,128)(2,1)}, bf16[512,336]{0,1:T(8,128)(2,1)S(1)}, u32[]{:S(2)}, u32[]{:S(2)}) %collective-permute-start.3) | collective-permute-done | bytes 344096 | tf_op jit(solution)/shard_map/ppermute | solution.py:31
  23.8 5.1 %collective-permute-start.1 = (bf16[512,336]{0,1:T(8,128)(2,1)S(1)}, bf16[512,336]{0,1:T(8,128)(2,1)S(1)}, u32[]{:S(2)}, u32[]{:S(2)}) collective-permute-start(bf16[512,336]{0,1:T(8,128)(2,1)S(1)} %collective-permute-done), channel_id=1, source_target_pairs={{0,14},{2,0},{4,2},{6,4},{8,6},{10,8},{12,10},{14,12},{1,15},{3,1}... | collective-permute-start | bytes 1032200 | tf_op jit(solution)/shard_map/ppermute | solution.py:34
  28.9 5.3 %collective-permute-done.4 = bf16[512,336]{0,1:T(8,128)(2,1)S(1)} collective-permute-done((bf16[512,336]{0,1:T(8,128)(2,1)S(1)}, bf16[512,336]{0,1:T(8,128)(2,1)S(1)}, u32[]{:S(2)}, u32[]{:S(2)}) %collective-permute-start.4) | collective-permute-done | bytes 344096 | tf_op jit(solution)/shard_map/ppermute | solution.py:31
  36.2 5.1 %collective-permute-start.2 = (bf16[512,336]{0,1:T(8,128)(2,1)S(1)}, bf16[512,336]{0,1:T(8,128)(2,1)S(1)}, u32[]{:S(2)}, u32[]{:S(2)}) collective-permute-start(bf16[512,336]{0,1:T(8,128)(2,1)S(1)} %collective-permute-done.1), channel_id=1, source_target_pairs={{0,14},{2,0},{4,2},{6,4},{8,6},{10,8},{12,10},{14,12},{1,15},{3,1}... | collective-permute-start | bytes 1032200 | tf_op jit(solution)/shard_map/ppermute | solution.py:34
  42.3 3.4 %collective-permute-done.5 = bf16[512,336]{0,1:T(8,128)(2,1)S(1)} collective-permute-done((bf16[512,336]{0,1:T(8,128)(2,1)S(1)}, bf16[512,336]{0,1:T(8,128)(2,1)S(1)}, u32[]{:S(2)}, u32[]{:S(2)}) %collective-permute-start.5) | collective-permute-done | bytes 344096 | tf_op jit(solution)/shard_map/ppermute | solution.py:31
  47.8 8.6 %collective-permute-done.6 = bf16[512,336]{0,1:T(8,128)(2,1)S(1)} collective-permute-done((bf16[512,336]{0,1:T(8,128)(2,1)S(1)}, bf16[512,336]{0,1:T(8,128)(2,1)S(1)}, u32[]{:S(2)}, u32[]{:S(2)}) %collective-permute-start.6) | collective-permute-done | bytes 344096 | tf_op jit(solution)/shard_map/ppermute | solution.py:31
  60.8 5.1 %collective-permute-start.8 = (f32[336]{0:T(512)S(1)}, f32[336]{0:T(512)S(1)}, u32[]{:S(2)}, u32[]{:S(2)}) collective-permute-start(f32[336]{0:T(512)S(1)} %copy-done.4), channel_id=1, source_target_pairs={{0,14},{2,0},{4,2},{6,4},{8,6},{10,8},{12,10},{14,12},{1,15},{3,1}... | collective-permute-start | bytes 4040 | tf_op jit(solution)/shard_map/ppermute | solution.py:34
  69.2 2.0 %fusion.17 = pred[512,1536]{0,1:T(8,128)(4,1)} fusion(s32[1536]{0:T(1024)S(1)} %iota_add_fusion, s32[512]{0:T(512)S(1)} %iota_add_fusion.1, pred[1536]{0:T(1024)(128)(4,1)S(1)} %broadcast_compare_fusion), kind=kLoop, calls=%fused_computation.28 | loop fusion | flops 3932160 | bytes 796160 | tf_op jit(solution)/shard_map/and | solution.py:123
  71.1 5.1 %collective-permute-start.9 = (f32[336]{0:T(512)S(1)}, f32[336]{0:T(512)S(1)}, u32[]{:S(2)}, u32[]{:S(2)}) collective-permute-start(f32[336]{0:T(512)S(1)} %collective-permute-done.8), channel_id=1, source_target_pairs={{0,14},{2,0},{4,2},{6,4},{8,6},{10,8},{12,10},{14,12},{1,15},{3,1}... | collective-permute-start | bytes 4040 | tf_op jit(solution)/shard_map/ppermute | solution.py:34
  78.2 5.1 %collective-permute-start.10 = (f32[336]{0:T(512)S(1)}, f32[336]{0:T(512)S(1)}, u32[]{:S(2)}, u32[]{:S(2)}) collective-permute-start(f32[336]{0:T(512)S(1)} %collective-permute-done.9), channel_id=1, source_target_pairs={{0,14},{2,0},{4,2},{6,4},{8,6},{10,8},{12,10},{14,12},{1,15},{3,1}... | collective-permute-start | bytes 4040 | tf_op jit(solution)/shard_map/ppermute | solution.py:34
  85.3 4.7 %collective-permute-done.14 = f32[336]{0:T(512)S(1)} collective-permute-done((f32[336]{0:T(512)S(1)}, f32[336]{0:T(512)S(1)}, u32[]{:S(2)}, u32[]{:S(2)}) %collective-permute-start.14) | collective-permute-done | bytes 1376 | tf_op jit(solution)/shard_map/ppermute | solution.py:31
  93.7 8.0 %multiply_reduce_fusion = (f32[512]{0:T(512)S(1)}, f32[512,5376]{0,1:T(8,128)S(1)}) fusion(s32[]{:T(128)S(6)} %select_n.26, bf16[512,2688]{0,1:T(8,128)(2,1)} %collective-permute-done.7, bf16[512,2688]{0,1:T(8,128)(2,1)} %copy-done), kind=kLoop, calls=%fused_computation.12 | loop fusion | flops 27524608 | bytes 16517124 | tf_op jit(solution)/shard_map/reduce_sum | solution.py:91
  101.7 6.0 %copy.16 = f32[512,8,2,336]{0,3,2,1:T(8,128)} copy(f32[512,8,2,336]{0,3,1,2:T(8,128)S(1)} %bitcast.52) | data formatting | bytes 22020096 | tf_op jit(solution)/shard_map/convert_element_type | solution.py:90
  107.7 8.3 %fusion.4 = bf16[512,5376]{0,1:T(8,128)(2,1)} fusion(f32[512,8,2,336]{0,3,2,1:T(8,128)} %copy.16, f32[5376]{0:T(1024)S(1)} %mul.186, f32[512]{0:T(512)S(1)} %add_rsqrt_fusion.2), kind=kLoop, calls=%fused_computation.11 | loop fusion | flops 8257536 | bytes 16538624 | tf_op jit(solution)/shard_map/convert_element_type | solution.py:93
  116.0 3.3 %fusion = f32[512]{0:T(512)S(1)} fusion(bf16[5376,512]{1,0:T(8,128)(2,1)} %all-gather.2.cloned.1.call-done), kind=kLoop, calls=%fused_computation.2 | loop fusion | flops 8257024 | bytes 5507072 | tf_op jit(solution)/shard_map/reduce_max | solution.py:52
  120.2 5.1 %fusion.9 = f32[512,512]{0,1:T(8,128)S(1)} fusion(bf16[512,5376]{0,1:T(8,128)(2,1)S(1)} %copy-done.1, bf16[5376,512]{1,0:T(8,128)(2,1)} %all-gather.2.cloned.1.call-done, bf16[512]{0:T(512)(128)(2,1)S(1)} %get-tuple-element.14, bf16[512]{0:T(512)(128)(2,1)S(1)} %get-tuple-element.13), kind=kOutput, calls=%fused_computation.19 | convolution fusion | flops 2835087360 | bytes 12060672 | tf_op jit(solution)/shard_map/dot_general | solution.py:94
  126.1 4.7 %collective-permute-start.16 = (bf16[512,2,128]{0,2,1:T(8,128)(2,1)S(1)}, bf16[512,2,128]{0,2,1:T(8,128)(2,1)S(1)}, u32[]{:S(2)}, u32[]{:S(2)}) collective-permute-start(bf16[512,2,128]{0,2,1:T(8,128)(2,1)S(1)} %pad_maximum_fusion), channel_id=1, source_target_pairs={{0,32},{16,48},{32,64},{48,80},{64,96},{80,112},{96,128},{112,144}... | collective-permute-start | bytes 786440 | tf_op jit(solution)/shard_map/ppermute | solution.py:20
  130.8 2.9 %collective-permute-start.17 = (bf16[512,2,128]{0,2,1:T(8,128)(2,1)S(1)}, bf16[512,2,128]{0,2,1:T(8,128)(2,1)S(1)}, u32[]{:S(2)}, u32[]{:S(2)}) collective-permute-start(bf16[512,2,128]{0,2,1:T(8,128)(2,1)S(1)} %pad_maximum_fusion), channel_id=1, source_target_pairs={{0,16},{16,32},{32,48},{48,64},{64,80},{80,96},{96,112},{112,128},... | collective-permute-start | bytes 786440 | tf_op jit(solution)/shard_map/ppermute | solution.py:20
  134.5 5.9 %collective-permute-done.16 = bf16[512,2,128]{0,2,1:T(8,128)(2,1)S(1)} collective-permute-done((bf16[512,2,128]{0,2,1:T(8,128)(2,1)S(1)}, bf16[512,2,128]{0,2,1:T(8,128)(2,1)S(1)}, u32[]{:S(2)}, u32[]{:S(2)}) %collective-permute-start.16) | collective-permute-done | bytes 262176 | tf_op jit(solution)/shard_map/ppermute | solution.py:20
  140.4 5.8 %collective-permute-done.17 = bf16[512,2,128]{0,2,1:T(8,128)(2,1)S(1)} collective-permute-done((bf16[512,2,128]{0,2,1:T(8,128)(2,1)S(1)}, bf16[512,2,128]{0,2,1:T(8,128)(2,1)S(1)}, u32[]{:S(2)}, u32[]{:S(2)}) %collective-permute-start.17) | collective-permute-done | bytes 262176 | tf_op jit(solution)/shard_map/ppermute | solution.py:20
  146.3 1.9 %fusion.13 = (f32[2,512]{1,0:T(2,128)S(1)}, f32[1536,512,2]{1,0,2:T(8,128)S(1)}) fusion(pred[512,1536]{0,1:T(8,128)(4,1)S(1)} %copy-done.3, bf16[512,2,64]{2,0,1:T(8,128)(2,1)S(1)} %get-tuple-element.8, bf16[512,2,64]{2,0,1:T(8,128)(2,1)S(1)} %get-tuple-element.7, bf16[1536,2,128]{0,2,1:T(8,128)(2,1)S(1)} %maximum_maximum_fusion), kind=kOutput, calls=%fused_computation.22 | convolution fusion | flops 407895040 | bytes 7999488 | tf_op jit(solution)/shard_map/tkgd,skd->kgts/dot_general | solution.py:119
  148.2 2.0 %fusion.18 = bf16[128,2,512]{2,0,1:T(8,128)(2,1)S(1)} fusion(f32[2,512]{1,0:T(2,128)S(1)} %get-tuple-element.15, f32[1536,512,2]{1,0,2:T(8,128)S(1)} %get-tuple-element.16, pred[512,1536]{0,1:T(8,128)(4,1)S(1)} %copy-done.3, bf16[1536,2,128]{0,2,1:T(8,128)(2,1)S(1)} %maximum_maximum_fusion), kind=kOutput, calls=%fused_computation.29 | convolution fusion | flops 409075712 | bytes 7737344 | tf_op jit(solution)/shard_map/kgts,skd->tkgd/dot_general | solution.py:127
  (84 shorter events, 26.1 us)
Async XLA Ops:
  6.5 49.9 %copy-start.2 = (bf16[512,336]{0,1:T(8,128)(2,1)S(1)}, bf16[512,336]{0,1:T(8,128)(2,1)}, u32[]{:S(2)}) copy-start(bf16[512,336]{0,1:T(8,128)(2,1)} %param.7) | copy-start | bytes 1032196
  6.5 109.5 %all-gather.2.cloned.1.call-start = ((), (), s32[]{:S(2)}) async-start(), calls=%async_computation | async-start | bytes 5677056 | tf_op jit(solution)/shard_map/all_gather | solution.py:77
  8.2 13.6 %collective-permute-start.3 = (bf16[512,336]{0,1:T(8,128)(2,1)}, bf16[512,336]{0,1:T(8,128)(2,1)S(1)}, u32[]{:S(2)}, u32[]{:S(2)}) collective-permute-start(bf16[512,336]{0,1:T(8,128)(2,1)} %param.7), channel_id=1, source_target_pairs={{0,2},{2,4},{4,6},{6,8},{8,10},{10,12},{12,14},{14,0},{1,3},{3,5},... | collective-permute-start | bytes 1032200 | tf_op jit(solution)/shard_map/ppermute | solution.py:31
  11.7 12.1 %collective-permute-start = (bf16[512,336]{0,1:T(8,128)(2,1)}, bf16[512,336]{0,1:T(8,128)(2,1)S(1)}, u32[]{:S(2)}, u32[]{:S(2)}) collective-permute-start(bf16[512,336]{0,1:T(8,128)(2,1)} %param.7), channel_id=1, source_target_pairs={{0,14},{2,0},{4,2},{6,4},{8,6},{10,8},{12,10},{14,12},{1,15},{3,1}... | collective-permute-start | bytes 1032200 | tf_op jit(solution)/shard_map/ppermute | solution.py:34
  21.9 12.3 %collective-permute-start.4 = (bf16[512,336]{0,1:T(8,128)(2,1)S(1)}, bf16[512,336]{0,1:T(8,128)(2,1)S(1)}, u32[]{:S(2)}, u32[]{:S(2)}) collective-permute-start(bf16[512,336]{0,1:T(8,128)(2,1)S(1)} %collective-permute-done.3), channel_id=1, source_target_pairs={{0,2},{2,4},{4,6},{6,8},{8,10},{10,12},{12,14},{14,0},{1,3},{3,5},... | collective-permute-start | bytes 1032200 | tf_op jit(solution)/shard_map/ppermute | solution.py:31
  23.8 12.4 %collective-permute-start.1 = (bf16[512,336]{0,1:T(8,128)(2,1)S(1)}, bf16[512,336]{0,1:T(8,128)(2,1)S(1)}, u32[]{:S(2)}, u32[]{:S(2)}) collective-permute-start(bf16[512,336]{0,1:T(8,128)(2,1)S(1)} %collective-permute-done), channel_id=1, source_target_pairs={{0,14},{2,0},{4,2},{6,4},{8,6},{10,8},{12,10},{14,12},{1,15},{3,1}... | collective-permute-start | bytes 1032200 | tf_op jit(solution)/shard_map/ppermute | solution.py:34
  34.2 11.5 %collective-permute-start.5 = (bf16[512,336]{0,1:T(8,128)(2,1)S(1)}, bf16[512,336]{0,1:T(8,128)(2,1)S(1)}, u32[]{:S(2)}, u32[]{:S(2)}) collective-permute-start(bf16[512,336]{0,1:T(8,128)(2,1)S(1)} %collective-permute-done.4), channel_id=1, source_target_pairs={{0,2},{2,4},{4,6},{6,8},{8,10},{10,12},{12,14},{14,0},{1,3},{3,5},... | collective-permute-start | bytes 1032200 | tf_op jit(solution)/shard_map/ppermute | solution.py:31
  36.2 11.6 %collective-permute-start.2 = (bf16[512,336]{0,1:T(8,128)(2,1)S(1)}, bf16[512,336]{0,1:T(8,128)(2,1)S(1)}, u32[]{:S(2)}, u32[]{:S(2)}) collective-permute-start(bf16[512,336]{0,1:T(8,128)(2,1)S(1)} %collective-permute-done.1), channel_id=1, source_target_pairs={{0,14},{2,0},{4,2},{6,4},{8,6},{10,8},{12,10},{14,12},{1,15},{3,1}... | collective-permute-start | bytes 1032200 | tf_op jit(solution)/shard_map/ppermute | solution.py:34
  45.7 10.6 %collective-permute-start.6 = (bf16[512,336]{0,1:T(8,128)(2,1)S(1)}, bf16[512,336]{0,1:T(8,128)(2,1)S(1)}, u32[]{:S(2)}, u32[]{:S(2)}) collective-permute-start(bf16[512,336]{0,1:T(8,128)(2,1)S(1)} %collective-permute-done.5), channel_id=1, source_target_pairs={{0,2},{2,4},{4,6},{6,8},{8,10},{10,12},{12,14},{14,0},{1,3},{3,5},... | collective-permute-start | bytes 1032200 | tf_op jit(solution)/shard_map/ppermute | solution.py:31
  56.9 36.7 %copy-start = (bf16[512,2688]{0,1:T(8,128)(2,1)}, bf16[512,2688]{0,1:T(8,128)(2,1)S(1)}, u32[]{:S(2)}) copy-start(bf16[512,2688]{0,1:T(8,128)(2,1)S(1)} %constant_dynamic-slice_fusion) | copy-start | bytes 8257540
  57.0 36.7 %collective-permute-start.7 = (bf16[512,2688]{0,1:T(8,128)(2,1)S(1)}, bf16[512,2688]{0,1:T(8,128)(2,1)}, u32[]{:S(2)}, u32[]{:S(2)}) collective-permute-start(bf16[512,2688]{0,1:T(8,128)(2,1)S(1)} %constant_dynamic-slice_fusion), channel_id=1, source_target_pairs={{0,1},{1,0},{2,3},{3,2},{4,5},{5,4},{6,7},{7,6},{8,9},{9,8},{10,11... | collective-permute-start | bytes 8257544 | tf_op jit(solution)/shard_map/ppermute | solution.py:31
  58.9 8.3 %collective-permute-start.11 = (f32[336]{0:T(512)S(1)}, f32[336]{0:T(512)S(1)}, u32[]{:S(2)}, u32[]{:S(2)}) collective-permute-start(f32[336]{0:T(512)S(1)} %copy-done.4), channel_id=1, source_target_pairs={{0,2},{2,4},{4,6},{6,8},{8,10},{10,12},{12,14},{14,0},{1,3},{3,5},... | collective-permute-start | bytes 4040 | tf_op jit(solution)/shard_map/ppermute | solution.py:31
  60.8 10.3 %collective-permute-start.8 = (f32[336]{0:T(512)S(1)}, f32[336]{0:T(512)S(1)}, u32[]{:S(2)}, u32[]{:S(2)}) collective-permute-start(f32[336]{0:T(512)S(1)} %copy-done.4), channel_id=1, source_target_pairs={{0,14},{2,0},{4,2},{6,4},{8,6},{10,8},{12,10},{14,12},{1,15},{3,1}... | collective-permute-start | bytes 4040 | tf_op jit(solution)/shard_map/ppermute | solution.py:34
  67.2 9.0 %collective-permute-start.12 = (f32[336]{0:T(512)S(1)}, f32[336]{0:T(512)S(1)}, u32[]{:S(2)}, u32[]{:S(2)}) collective-permute-start(f32[336]{0:T(512)S(1)} %collective-permute-done.11), channel_id=1, source_target_pairs={{0,2},{2,4},{4,6},{6,8},{8,10},{10,12},{12,14},{14,0},{1,3},{3,5},... | collective-permute-start | bytes 4040 | tf_op jit(solution)/shard_map/ppermute | solution.py:31
  71.1 7.1 %collective-permute-start.9 = (f32[336]{0:T(512)S(1)}, f32[336]{0:T(512)S(1)}, u32[]{:S(2)}, u32[]{:S(2)}) collective-permute-start(f32[336]{0:T(512)S(1)} %collective-permute-done.8), channel_id=1, source_target_pairs={{0,14},{2,0},{4,2},{6,4},{8,6},{10,8},{12,10},{14,12},{1,15},{3,1}... | collective-permute-start | bytes 4040 | tf_op jit(solution)/shard_map/ppermute | solution.py:34
  76.3 7.1 %collective-permute-start.13 = (f32[336]{0:T(512)S(1)}, f32[336]{0:T(512)S(1)}, u32[]{:S(2)}, u32[]{:S(2)}) collective-permute-start(f32[336]{0:T(512)S(1)} %collective-permute-done.12), channel_id=1, source_target_pairs={{0,2},{2,4},{4,6},{6,8},{8,10},{10,12},{12,14},{14,0},{1,3},{3,5},... | collective-permute-start | bytes 4040 | tf_op jit(solution)/shard_map/ppermute | solution.py:31
  78.2 7.1 %collective-permute-start.10 = (f32[336]{0:T(512)S(1)}, f32[336]{0:T(512)S(1)}, u32[]{:S(2)}, u32[]{:S(2)}) collective-permute-start(f32[336]{0:T(512)S(1)} %collective-permute-done.9), channel_id=1, source_target_pairs={{0,14},{2,0},{4,2},{6,4},{8,6},{10,8},{12,10},{14,12},{1,15},{3,1}... | collective-permute-start | bytes 4040 | tf_op jit(solution)/shard_map/ppermute | solution.py:34
  83.4 6.7 %collective-permute-start.14 = (f32[336]{0:T(512)S(1)}, f32[336]{0:T(512)S(1)}, u32[]{:S(2)}, u32[]{:S(2)}) collective-permute-start(f32[336]{0:T(512)S(1)} %collective-permute-done.13), channel_id=1, source_target_pairs={{0,2},{2,4},{4,6},{6,8},{8,10},{10,12},{12,14},{14,0},{1,3},{3,5},... | collective-permute-start | bytes 4040 | tf_op jit(solution)/shard_map/ppermute | solution.py:31
  90.2 3.1 %collective-permute-start.15 = (f32[2688]{0:T(1024)S(1)}, f32[2688]{0:T(1024)S(1)}, u32[]{:S(2)}, u32[]{:S(2)}) collective-permute-start(f32[2688]{0:T(1024)S(1)} %dynamic_slice.14), channel_id=1, source_target_pairs={{0,1},{1,0},{2,3},{3,2},{4,5},{5,4},{6,7},{7,6},{8,9},{9,8},{10,11... | collective-permute-start | bytes 32264 | tf_op jit(solution)/shard_map/ppermute | solution.py:31
  120.2 5.2 %copy-start.5 = (f32[128]{0:T(128)S(1)}, f32[128]{0:T(128)}, u32[]{:S(2)}) copy-start(f32[128]{0:T(128)} %param.10) | copy-start | bytes 1540
  120.2 13.9 %copy-start.6 = (f32[128]{0:T(128)S(1)}, f32[128]{0:T(128)}, u32[]{:S(2)}) copy-start(f32[128]{0:T(128)} %param.9) | copy-start | bytes 1540
  125.3 21.0 %copy-start.3 = (pred[512,1536]{0,1:T(8,128)(4,1)S(1)}, pred[512,1536]{0,1:T(8,128)(4,1)}, u32[]{:S(2)}) copy-start(pred[512,1536]{0,1:T(8,128)(4,1)} %fusion.17) | copy-start | bytes 2359300
  126.1 14.3 %collective-permute-start.16 = (bf16[512,2,128]{0,2,1:T(8,128)(2,1)S(1)}, bf16[512,2,128]{0,2,1:T(8,128)(2,1)S(1)}, u32[]{:S(2)}, u32[]{:S(2)}) collective-permute-start(bf16[512,2,128]{0,2,1:T(8,128)(2,1)S(1)} %pad_maximum_fusion), channel_id=1, source_target_pairs={{0,32},{16,48},{32,64},{48,80},{64,96},{80,112},{96,128},{112,144}... | collective-permute-start | bytes 786440 | tf_op jit(solution)/shard_map/ppermute | solution.py:20
  130.8 15.4 %collective-permute-start.17 = (bf16[512,2,128]{0,2,1:T(8,128)(2,1)S(1)}, bf16[512,2,128]{0,2,1:T(8,128)(2,1)S(1)}, u32[]{:S(2)}, u32[]{:S(2)}) collective-permute-start(bf16[512,2,128]{0,2,1:T(8,128)(2,1)S(1)} %pad_maximum_fusion), channel_id=1, source_target_pairs={{0,16},{16,32},{32,48},{48,64},{64,80},{80,96},{96,112},{112,128},... | collective-permute-start | bytes 786440 | tf_op jit(solution)/shard_map/ppermute | solution.py:20
  (2 other events, 6.6 us)
Sparse Core Ops, SparseCore 0:
  10.5 90.0 all-gather.1

commit v3 on v2

--- a/solution.py
+++ b/solution.py
@@ -78,23 +78,30 @@
     clipped = clip_with(panel, column_max(panel))
     rows_tokens, piece = tokens.shape
     cores = lax.axis_size("cc")
-    along_y, gain_y = ring_gather((tokens, gain), "cy", (1, 0))
-    along_all, gain_all = ring_gather((along_y, gain_y), "cc", (1, 0))
+    high = gain.astype(jnp.bfloat16)
+    rest = gain - high.astype(jnp.float32)
+    middle = rest.astype(jnp.bfloat16)
+    low = (rest - middle.astype(jnp.float32)).astype(jnp.bfloat16)
+    filler = jnp.zeros((GAIN_ROWS - 3, piece), jnp.bfloat16)
+    packed = jnp.concatenate([tokens, high[None], middle[None], low[None], filler], axis=0)
+    (along_y,) = ring_gather((packed,), "cy", (1,))
+    (along_all,) = ring_gather((along_y,), "cc", (1,))
     blocks = along_all.shape[1] // (cores * piece)
-    full = (
-        along_all.reshape(rows_tokens, cores, blocks, piece)
-        .transpose(0, 2, 1, 3)
-        .reshape(rows_tokens, cores * blocks * piece)
-    )
-    full_gain = gain_all.reshape(cores, blocks, piece).transpose(1, 0, 2).reshape(-1)
-    widened = full.astype(jnp.float32)
+    split = along_all[rows_tokens : rows_tokens + 3].astype(jnp.float32)
+    full_gain = split[0] + (split[1] + split[2])
+    widened = along_all[:rows_tokens].astype(jnp.float32)
     squares = jnp.sum(widened * widened, axis=1)
     inverse = lax.rsqrt(squares / D + EPS)[:, None]
     whole = (widened * inverse * full_gain[None, :]).astype(jnp.bfloat16)
-    projected = jnp.dot(whole, clipped, preferred_element_type=jnp.float32)
-    query = projected[:, :query_cols]
-    keys = projected[:, query_cols : query_cols + key_cols]
-    values = projected[:, query_cols + key_cols :]
+    ordered = (
+        clipped.reshape(blocks, cores, piece, clipped.shape[1])
+        .transpose(1, 0, 2, 3)
+        .reshape(clipped.shape)
+    )
+    kv_part = jnp.dot(whole, ordered[:, query_cols:], preferred_element_type=jnp.float32)
+    keys = kv_part[:, :key_cols]
+    values = kv_part[:, key_cols:]
+    query = jnp.dot(whole, ordered[:, :query_cols], preferred_element_type=jnp.float32)
     heads_local = query_cols // HD
     kv_local = key_cols // HD
     group = heads_local // kv_local
@@ -129,6 +136,7 @@
 
 
 CORES_PER_CHIP = 2
+GAIN_ROWS = 8
 
 
 def solution(mesh):

time: 159 us -> 146 us (0.918)
  the two profiles are of different devices: /device:TPU:256 before, /device:TPU:64 now
where the time goes in v3:
time: 146 us
  waiting for transfers between devices  53.7 us (37%)
  starting transfers between devices  31.1 us (21%)
  local copies, waits for them, and re-layouts  19.8 us (14%)
  other arithmetic  18.9 us (13%)
  between operations  14.4 us (10%)
  matrix products  8 us (5%)
    ppermute x5, waiting for transfers between devices, ring_gather(): forward = lax.ppermute(forward, axis, right)  29.9 us
    all_gather x1, waiting for transfers between devices, local(): panel = lax.all_gather(stacked, 'row', axis=0, tiled=True)  16.5 us
    ppermute x3, starting transfers between devices, ring_gather(): backward = lax.ppermute(backward, axis, left)  14.1 us
    ppermute x5, starting transfers between devices, ring_gather(): forward = lax.ppermute(forward, axis, right)  11.3 us
    concatenate x1, local copies, waits for them, and re-layouts, ring_gather(): doubled = jnp.concatenate([stacked, stacked], axis=dim)  7.65 us
    ppermute x2, waiting for transfers between devices, shifted(): return lax.ppermute(array, axis, pairs)  7.29 us
    unnamed x15, local copies, waits for them, and re-layouts  6.61 us
    ppermute x2, starting transfers between devices, shifted(): return lax.ppermute(array, axis, pairs)  5.68 us
  transfers between devices with their start and end apart: 11, of which 8 were waited for; matrix products, arithmetic and copies ran while one was open for 18% of the time, Pallas kernels for 0%

profile of v3, /device:TPU:64, one launch (start us, length us, event | category | flops | bytes accessed | tf_op | source)
XLA Modules:
  0.0 145.9 jit_solution(1489731014571155370)
XLA Ops:
  10.4 3.5 %collective-permute-start.3 = (bf16[520,336]{1,0:T(8,128)(2,1)S(1)}, bf16[520,336]{1,0:T(8,128)(2,1)S(1)}, u32[]{:S(2)}, u32[]{:S(2)}) collective-permute-start(bf16[520,336]{1,0:T(8,128)(2,1)S(1)} %concatenate.40), channel_id=1, source_target_pairs={{0,2},{2,4},{4,6},{6,8},{8,10},{10,12},{12,14},{14,0},{1,3},{3,5},... | collective-permute-start | bytes 1048328 | tf_op jit(solution)/shard_map/ppermute | solution.py:31
  13.9 3.8 %collective-permute-start = (bf16[520,336]{1,0:T(8,128)(2,1)S(1)}, bf16[520,336]{1,0:T(8,128)(2,1)S(1)}, u32[]{:S(2)}, u32[]{:S(2)}) collective-permute-start(bf16[520,336]{1,0:T(8,128)(2,1)S(1)} %concatenate.40), channel_id=1, source_target_pairs={{0,14},{2,0},{4,2},{6,4},{8,6},{10,8},{12,10},{14,12},{1,15},{3,1}... | collective-permute-start | bytes 1048328 | tf_op jit(solution)/shard_map/ppermute | solution.py:34
  17.7 7.3 %collective-permute-done.3 = bf16[520,336]{1,0:T(8,128)(2,1)S(1)} collective-permute-done((bf16[520,336]{1,0:T(8,128)(2,1)S(1)}, bf16[520,336]{1,0:T(8,128)(2,1)S(1)}, u32[]{:S(2)}, u32[]{:S(2)}) %collective-permute-start.3) | collective-permute-done | bytes 349472 | tf_op jit(solution)/shard_map/ppermute | solution.py:31
  27.0 5.1 %collective-permute-start.1 = (bf16[520,336]{1,0:T(8,128)(2,1)S(1)}, bf16[520,336]{1,0:T(8,128)(2,1)S(1)}, u32[]{:S(2)}, u32[]{:S(2)}) collective-permute-start(bf16[520,336]{1,0:T(8,128)(2,1)S(1)} %collective-permute-done), channel_id=1, source_target_pairs={{0,14},{2,0},{4,2},{6,4},{8,6},{10,8},{12,10},{14,12},{1,15},{3,1}... | collective-permute-start | bytes 1048328 | tf_op jit(solution)/shard_map/ppermute | solution.py:34
  32.1 6.5 %collective-permute-done.4 = bf16[520,336]{1,0:T(8,128)(2,1)S(1)} collective-permute-done((bf16[520,336]{1,0:T(8,128)(2,1)S(1)}, bf16[520,336]{1,0:T(8,128)(2,1)S(1)}, u32[]{:S(2)}, u32[]{:S(2)}) %collective-permute-start.4) | collective-permute-done | bytes 349472 | tf_op jit(solution)/shard_map/ppermute | solution.py:31
  40.5 5.1 %collective-permute-start.2 = (bf16[520,336]{1,0:T(8,128)(2,1)S(1)}, bf16[520,336]{1,0:T(8,128)(2,1)S(1)}, u32[]{:S(2)}, u32[]{:S(2)}) collective-permute-start(bf16[520,336]{1,0:T(8,128)(2,1)S(1)} %collective-permute-done.1), channel_id=1, source_target_pairs={{0,14},{2,0},{4,2},{6,4},{8,6},{10,8},{12,10},{14,12},{1,15},{3,1}... | collective-permute-start | bytes 1048328 | tf_op jit(solution)/shard_map/ppermute | solution.py:34
  45.6 5.5 %collective-permute-done.5 = bf16[520,336]{1,0:T(8,128)(2,1)S(1)} collective-permute-done((bf16[520,336]{1,0:T(8,128)(2,1)S(1)}, bf16[520,336]{1,0:T(8,128)(2,1)S(1)}, u32[]{:S(2)}, u32[]{:S(2)}) %collective-permute-start.5) | collective-permute-done | bytes 349472 | tf_op jit(solution)/shard_map/ppermute | solution.py:31
  53.1 9.7 %collective-permute-done.6 = bf16[520,336]{1,0:T(8,128)(2,1)S(1)} collective-permute-done((bf16[520,336]{1,0:T(8,128)(2,1)S(1)}, bf16[520,336]{1,0:T(8,128)(2,1)S(1)}, u32[]{:S(2)}, u32[]{:S(2)}) %collective-permute-start.6) | collective-permute-done | bytes 349472 | tf_op jit(solution)/shard_map/ppermute | solution.py:31
  62.9 7.7 %concatenate.41 = bf16[520,5376]{1,0:T(8,128)(2,1)} concatenate(bf16[520,336]{1,0:T(8,128)(2,1)S(1)} %concatenate.40, bf16[520,336]{1,0:T(8,128)(2,1)S(1)} %collective-permute-done, bf16[520,336]{1,0:T(8,128)(2,1)S(1)} %collective-permute-done.1, bf16[520,336]{1,0:T(8,128)(2,1)S(1)} %collective-permute-done.2, bf16[520,336]{1,0:T(8,128)(2,1)S(1)} %collective-permute-done.6, ...), dimensions={1} | concatenate | bytes 11182080 | tf_op jit(solution)/shard_map/concatenate | solution.py:40
  70.5 3.3 %constant_dynamic-slice_fusion = bf16[520,2688]{1,0:T(8,128)(2,1)S(1)} fusion(bf16[520,5376]{1,0:T(8,128)(2,1)} %concatenate.41, s32[]{:T(128)S(6)} %select_n.22), kind=kLoop, calls=%fused_computation.73 | loop fusion | bytes 5591044 | tf_op jit(solution)/shard_map/dynamic_slice | solution.py:42
  73.8 2.1 %collective-permute-start.7 = (bf16[520,2688]{1,0:T(8,128)(2,1)S(1)}, bf16[520,2688]{1,0:T(8,128)(2,1)}, u32[]{:S(2)}, u32[]{:S(2)}) collective-permute-start(bf16[520,2688]{1,0:T(8,128)(2,1)S(1)} %constant_dynamic-slice_fusion), channel_id=1, source_target_pairs={{0,1},{1,0},{2,3},{3,2},{4,5},{5,4},{6,7},{7,6},{8,9},{9,8},{10,11... | collective-permute-start | bytes 8386568 | tf_op jit(solution)/shard_map/ppermute | solution.py:31
  78.1 2.0 %fusion.13 = pred[512,1536]{0,1:T(8,128)(4,1)} fusion(s32[1536]{0:T(1024)S(1)} %iota_add_fusion, s32[512]{0:T(512)S(1)} %iota_add_fusion.1, pred[1536]{0:T(1024)(128)(4,1)S(1)} %broadcast_compare_fusion), kind=kLoop, calls=%fused_computation.25 | loop fusion | flops 3932160 | bytes 796160 | tf_op jit(solution)/shard_map/and | solution.py:130
  81.0 5.2 %fusion.8 = bf16[520,5376]{1,0:T(8,128)(2,1)S(1)} fusion(s32[]{:T(128)S(6)} %select_n.24, bf16[520,2688]{1,0:T(8,128)(2,1)S(1)} %constant_dynamic-slice_fusion, bf16[520,2688]{1,0:T(8,128)(2,1)} %collective-permute-done.7), kind=kLoop, calls=%fused_computation.18 | loop fusion | flops 22364160 | bytes 11182084 | tf_op jit(solution)/shard_map/concatenate | solution.py:40
  86.3 2.3 %copy-done = bf16[520,5376]{1,0:T(8,128)(2,1)} copy-done((bf16[520,5376]{1,0:T(8,128)(2,1)}, bf16[520,5376]{1,0:T(8,128)(2,1)S(1)}, u32[]{:S(2)}) %copy-start) | copy-done | bytes 5591064
  89.8 16.5 %all-gather.2.cloned.1.call-done = bf16[5376,512]{1,0:T(8,128)(2,1)} async-done(((bf16[168,512]{1,0:T(8,128)(2,1)}), bf16[5376,512]{1,0:T(8,128)(2,1)}) %all-gather.2.cloned.1.call-update) | async-done | bytes 5505040 | tf_op jit(solution)/shard_map/all_gather | solution.py:77
  106.3 3.3 %fusion.3 = f32[512]{0:T(512)S(1)} fusion(bf16[5376,512]{1,0:T(8,128)(2,1)} %all-gather.2.cloned.1.call-done), kind=kLoop, calls=%fused_computation.11 | loop fusion | flops 8257024 | bytes 5507072 | tf_op jit(solution)/shard_map/reduce_max | solution.py:52
  114.7 2.0 %fusion.16 = f32[512,256]{0,1:T(8,128)S(1)} fusion(bf16[5376,512]{1,0:T(8,128)(2,1)S(1)} %bitcast.48, f32[5376]{0:T(1024)S(1)} %fusion.37, f32[512]{0:T(512)S(1)} %add_rsqrt_fusion.2, bf16[520,5376]{1,0:T(8,128)(2,1)S(1)} %bitcast.46), kind=kOutput, calls=%fused_computation.28 | convolution fusion | flops 1420296192 | bytes 8808448 | tf_op jit(solution)/shard_map/dot_general | solution.py:101
  117.5 3.3 %collective-permute-start.8 = (bf16[512,2,128]{0,2,1:T(8,128)(2,1)S(1)}, bf16[512,2,128]{0,2,1:T(8,128)(2,1)S(1)}, u32[]{:S(2)}, u32[]{:S(2)}) collective-permute-start(bf16[512,2,128]{0,2,1:T(8,128)(2,1)S(1)} %pad_maximum_fusion), channel_id=1, source_target_pairs={{0,32},{16,48},{32,64},{48,80},{64,96},{80,112},{96,128},{112,144}... | collective-permute-start | bytes 786440 | tf_op jit(solution)/shard_map/ppermute | solution.py:20
  120.8 2.4 %collective-permute-start.9 = (bf16[512,2,128]{0,2,1:T(8,128)(2,1)S(1)}, bf16[512,2,128]{0,2,1:T(8,128)(2,1)}, u32[]{:S(2)}, u32[]{:S(2)}) collective-permute-start(bf16[512,2,128]{0,2,1:T(8,128)(2,1)S(1)} %pad_maximum_fusion), channel_id=1, source_target_pairs={{0,16},{16,32},{32,48},{48,64},{64,80},{80,96},{96,112},{112,128},... | collective-permute-start | bytes 786440 | tf_op jit(solution)/shard_map/ppermute | solution.py:20
  123.2 2.0 %multiply_reduce_fusion = (f32[512,2]{0,1:T(2,128)S(1)}, f32[512,256]{0,1:T(8,128)S(1)}) fusion(bf16[5376,512]{1,0:T(8,128)(2,1)S(1)} %bitcast.49, f32[5376]{0:T(1024)S(1)} %fusion.37, f32[512]{0:T(512)S(1)} %add_rsqrt_fusion.2, bf16[520,5376]{1,0:T(8,128)(2,1)S(1)} %bitcast.46), kind=kOutput, calls=%fused_computation.35 | convolution fusion | flops 1420557312 | bytes 8812544 | tf_op jit(solution)/shard_map/dot_general | solution.py:104
  125.9 4.0 %collective-permute-done.8 = bf16[512,2,128]{0,2,1:T(8,128)(2,1)S(1)} collective-permute-done((bf16[512,2,128]{0,2,1:T(8,128)(2,1)S(1)}, bf16[512,2,128]{0,2,1:T(8,128)(2,1)S(1)}, u32[]{:S(2)}, u32[]{:S(2)}) %collective-permute-start.8) | collective-permute-done | bytes 262176 | tf_op jit(solution)/shard_map/ppermute | solution.py:20
  130.0 3.2 %collective-permute-done.9 = bf16[512,2,128]{0,2,1:T(8,128)(2,1)} collective-permute-done((bf16[512,2,128]{0,2,1:T(8,128)(2,1)S(1)}, bf16[512,2,128]{0,2,1:T(8,128)(2,1)}, u32[]{:S(2)}, u32[]{:S(2)}) %collective-permute-start.9) | collective-permute-done | bytes 262176 | tf_op jit(solution)/shard_map/ppermute | solution.py:20
  134.2 1.9 %fusion.9 = (f32[2,512]{1,0:T(2,128)S(1)}, f32[1536,512,2]{1,0,2:T(8,128)S(1)}) fusion(pred[512,1536]{0,1:T(8,128)(4,1)S(1)} %copy-done.2, bf16[512,2,64]{2,0,1:T(8,128)(2,1)S(1)} %get-tuple-element.6, bf16[512,2,64]{2,0,1:T(8,128)(2,1)S(1)} %get-tuple-element.5, bf16[1536,2,128]{0,2,1:T(8,128)(2,1)S(1)} %maximum_maximum_fusion), kind=kOutput, calls=%fused_computation.19 | convolution fusion | flops 407895040 | bytes 7999488 | tf_op jit(solution)/shard_map/tkgd,skd->kgts/dot_general | solution.py:126
  136.2 2.0 %fusion.18 = bf16[128,2,512]{2,0,1:T(8,128)(2,1)S(1)} fusion(f32[2,512]{1,0:T(2,128)S(1)} %get-tuple-element.18, f32[1536,512,2]{1,0,2:T(8,128)S(1)} %get-tuple-element.19, pred[512,1536]{0,1:T(8,128)(4,1)S(1)} %copy-done.2, bf16[1536,2,128]{0,2,1:T(8,128)(2,1)S(1)} %maximum_maximum_fusion), kind=kOutput, calls=%fused_computation.30 | convolution fusion | flops 409075712 | bytes 7737344 | tf_op jit(solution)/shard_map/kgts,skd->tkgd/dot_general | solution.py:134
  (57 shorter events, 21.7 us)
Async XLA Ops:
  6.5 99.8 %all-gather.2.cloned.1.call-start = ((), (), s32[]{:S(2)}) async-start(), calls=%async_computation | async-start | bytes 5677056 | tf_op jit(solution)/shard_map/all_gather | solution.py:77
  10.4 14.6 %collective-permute-start.3 = (bf16[520,336]{1,0:T(8,128)(2,1)S(1)}, bf16[520,336]{1,0:T(8,128)(2,1)S(1)}, u32[]{:S(2)}, u32[]{:S(2)}) collective-permute-start(bf16[520,336]{1,0:T(8,128)(2,1)S(1)} %concatenate.40), channel_id=1, source_target_pairs={{0,2},{2,4},{4,6},{6,8},{8,10},{10,12},{12,14},{14,0},{1,3},{3,5},... | collective-permute-start | bytes 1048328 | tf_op jit(solution)/shard_map/ppermute | solution.py:31
  13.9 13.0 %collective-permute-start = (bf16[520,336]{1,0:T(8,128)(2,1)S(1)}, bf16[520,336]{1,0:T(8,128)(2,1)S(1)}, u32[]{:S(2)}, u32[]{:S(2)}) collective-permute-start(bf16[520,336]{1,0:T(8,128)(2,1)S(1)} %concatenate.40), channel_id=1, source_target_pairs={{0,14},{2,0},{4,2},{6,4},{8,6},{10,8},{12,10},{14,12},{1,15},{3,1}... | collective-permute-start | bytes 1048328 | tf_op jit(solution)/shard_map/ppermute | solution.py:34
  25.0 13.5 %collective-permute-start.4 = (bf16[520,336]{1,0:T(8,128)(2,1)S(1)}, bf16[520,336]{1,0:T(8,128)(2,1)S(1)}, u32[]{:S(2)}, u32[]{:S(2)}) collective-permute-start(bf16[520,336]{1,0:T(8,128)(2,1)S(1)} %collective-permute-done.3), channel_id=1, source_target_pairs={{0,2},{2,4},{4,6},{6,8},{8,10},{10,12},{12,14},{14,0},{1,3},{3,5},... | collective-permute-start | bytes 1048328 | tf_op jit(solution)/shard_map/ppermute | solution.py:31
  27.0 13.5 %collective-permute-start.1 = (bf16[520,336]{1,0:T(8,128)(2,1)S(1)}, bf16[520,336]{1,0:T(8,128)(2,1)S(1)}, u32[]{:S(2)}, u32[]{:S(2)}) collective-permute-start(bf16[520,336]{1,0:T(8,128)(2,1)S(1)} %collective-permute-done), channel_id=1, source_target_pairs={{0,14},{2,0},{4,2},{6,4},{8,6},{10,8},{12,10},{14,12},{1,15},{3,1}... | collective-permute-start | bytes 1048328 | tf_op jit(solution)/shard_map/ppermute | solution.py:34
  38.6 12.6 %collective-permute-start.5 = (bf16[520,336]{1,0:T(8,128)(2,1)S(1)}, bf16[520,336]{1,0:T(8,128)(2,1)S(1)}, u32[]{:S(2)}, u32[]{:S(2)}) collective-permute-start(bf16[520,336]{1,0:T(8,128)(2,1)S(1)} %collective-permute-done.4), channel_id=1, source_target_pairs={{0,2},{2,4},{4,6},{6,8},{8,10},{10,12},{12,14},{14,0},{1,3},{3,5},... | collective-permute-start | bytes 1048328 | tf_op jit(solution)/shard_map/ppermute | solution.py:31
  40.5 12.6 %collective-permute-start.2 = (bf16[520,336]{1,0:T(8,128)(2,1)S(1)}, bf16[520,336]{1,0:T(8,128)(2,1)S(1)}, u32[]{:S(2)}, u32[]{:S(2)}) collective-permute-start(bf16[520,336]{1,0:T(8,128)(2,1)S(1)} %collective-permute-done.1), channel_id=1, source_target_pairs={{0,14},{2,0},{4,2},{6,4},{8,6},{10,8},{12,10},{14,12},{1,15},{3,1}... | collective-permute-start | bytes 1048328 | tf_op jit(solution)/shard_map/ppermute | solution.py:34
  51.2 11.7 %collective-permute-start.6 = (bf16[520,336]{1,0:T(8,128)(2,1)S(1)}, bf16[520,336]{1,0:T(8,128)(2,1)S(1)}, u32[]{:S(2)}, u32[]{:S(2)}) collective-permute-start(bf16[520,336]{1,0:T(8,128)(2,1)S(1)} %collective-permute-done.5), channel_id=1, source_target_pairs={{0,2},{2,4},{4,6},{6,8},{8,10},{10,12},{12,14},{14,0},{1,3},{3,5},... | collective-permute-start | bytes 1048328 | tf_op jit(solution)/shard_map/ppermute | solution.py:31
  73.8 7.2 %collective-permute-start.7 = (bf16[520,2688]{1,0:T(8,128)(2,1)S(1)}, bf16[520,2688]{1,0:T(8,128)(2,1)}, u32[]{:S(2)}, u32[]{:S(2)}) collective-permute-start(bf16[520,2688]{1,0:T(8,128)(2,1)S(1)} %constant_dynamic-slice_fusion), channel_id=1, source_target_pairs={{0,1},{1,0},{2,3},{3,2},{4,5},{5,4},{6,7},{7,6},{8,9},{9,8},{10,11... | collective-permute-start | bytes 8386568 | tf_op jit(solution)/shard_map/ppermute | solution.py:31
  86.2 2.5 %copy-start = (bf16[520,5376]{1,0:T(8,128)(2,1)}, bf16[520,5376]{1,0:T(8,128)(2,1)S(1)}, u32[]{:S(2)}) copy-start(bf16[520,5376]{1,0:T(8,128)(2,1)S(1)} %fusion.8) | copy-start | bytes 16773124
  106.3 4.2 %copy-start.1 = (bf16[5376,512]{1,0:T(8,128)(2,1)S(1)}, bf16[5376,512]{1,0:T(8,128)(2,1)}, u32[]{:S(2)}) copy-start(bf16[5376,512]{1,0:T(8,128)(2,1)} %all-gather.2.cloned.1.call-done) | copy-start | bytes 16515076
  112.1 2.2 %slice-start = ((s8[5591040]{0:T(1024)(128)(4,1)}), s8[4194304]{0:T(1024)(128)(4,1)S(1)}, s32[]{:S(2)}) async-start(s8[5591040]{0:T(1024)(128)(4,1)} %bitcast.45), calls=%async_computation.1 | async-start | bytes 8388608
  112.1 2.6 %slice-start.1 = ((s8[5591040]{0:T(1024)(128)(4,1)}), s8[1396736]{0:T(1024)(128)(4,1)S(1)}, s32[]{:S(2)}) async-start(s8[5591040]{0:T(1024)(128)(4,1)} %bitcast.45), calls=%async_computation.2 | async-start | bytes 2793472
  114.7 2.1 %copy-start.3 = (f32[128]{0:T(128)S(1)}, f32[128]{0:T(128)}, u32[]{:S(2)}) copy-start(f32[128]{0:T(128)} %param.10) | copy-start | bytes 1540
  117.5 8.0 %copy-start.4 = (f32[128]{0:T(128)S(1)}, f32[128]{0:T(128)}, u32[]{:S(2)}) copy-start(f32[128]{0:T(128)} %param.9) | copy-start | bytes 1540
  117.5 12.5 %collective-permute-start.8 = (bf16[512,2,128]{0,2,1:T(8,128)(2,1)S(1)}, bf16[512,2,128]{0,2,1:T(8,128)(2,1)S(1)}, u32[]{:S(2)}, u32[]{:S(2)}) collective-permute-start(bf16[512,2,128]{0,2,1:T(8,128)(2,1)S(1)} %pad_maximum_fusion), channel_id=1, source_target_pairs={{0,32},{16,48},{32,64},{48,80},{64,96},{80,112},{96,128},{112,144}... | collective-permute-start | bytes 786440 | tf_op jit(solution)/shard_map/ppermute | solution.py:20
  120.8 12.4 %collective-permute-start.9 = (bf16[512,2,128]{0,2,1:T(8,128)(2,1)S(1)}, bf16[512,2,128]{0,2,1:T(8,128)(2,1)}, u32[]{:S(2)}, u32[]{:S(2)}) collective-permute-start(bf16[512,2,128]{0,2,1:T(8,128)(2,1)S(1)} %pad_maximum_fusion), channel_id=1, source_target_pairs={{0,16},{16,32},{32,48},{48,64},{64,80},{80,96},{96,112},{112,128},... | collective-permute-start | bytes 786440 | tf_op jit(solution)/shard_map/ppermute | solution.py:20
  125.2 9.0 %copy-start.2 = (pred[512,1536]{0,1:T(8,128)(4,1)S(1)}, pred[512,1536]{0,1:T(8,128)(4,1)}, u32[]{:S(2)}) copy-start(pred[512,1536]{0,1:T(8,128)(4,1)} %fusion.13) | copy-start | bytes 2359300
Sparse Core Ops, SparseCore 0:
  10.5 95.7 all-gather.1

commit v4 on v3

--- a/solution.py
+++ b/solution.py
@@ -74,7 +74,11 @@
     query_cols = w_query.shape[1]
     key_cols = w_key.shape[1]
     stacked = jnp.concatenate([w_query, w_key, w_value], axis=1)
-    panel = lax.all_gather(stacked, "row", axis=0, tiled=True)
+    weight_rows = stacked.shape[0]
+    aligned = -(-weight_rows // TILE_ROWS) * TILE_ROWS
+    padded = jnp.pad(stacked, ((0, aligned - weight_rows), (0, 0)))
+    slabs = lax.all_gather(padded, "row", axis=0, tiled=True)
+    panel = slabs.reshape(-1, aligned, stacked.shape[1])[:, :weight_rows].reshape(-1, stacked.shape[1])
     clipped = clip_with(panel, column_max(panel))
     rows_tokens, piece = tokens.shape
     cores = lax.axis_size("cc")
@@ -137,6 +141,7 @@
 
 CORES_PER_CHIP = 2
 GAIN_ROWS = 8
+TILE_ROWS = 16
 
 
 def solution(mesh):

time: 146 us -> 147 us (level)
    slice x0 -> x1, local copies, waits for them, and re-layouts: none -> 3.11 us  [local(): slabs.reshape(-1, aligned, stacked.shape[1])[:, :weight_rows]]
    unnamed x15 -> x13, local copies, waits for them, and re-layouts: 6.61 us -> 4.1 us
    convert_element_type x1 -> x0, other arithmetic: 1.61 us -> none  [clip_with(): jnp.clip(weight.astype(jnp.float32), -bound, bound).astype(jnp.bfloat16)]
where the time goes in v4:
time: 147 us; the launch traced here: 146 us
  waiting for transfers between devices  54.8 us (37%)
  starting transfers between devices  31.1 us (21%)
  local copies, waits for them, and re-layouts  20.5 us (14%)
  other arithmetic  17.5 us (12%)
  between operations  14.5 us (10%)
  matrix products  7.98 us (5%)
    ppermute x5, waiting for transfers between devices, ring_gather(): forward = lax.ppermute(forward, axis, right)  29.9 us
    all_gather x1, waiting for transfers between devices, local(): slabs = lax.all_gather(padded, 'row', axis=0, tiled=True)  17.1 us
    ppermute x3, starting transfers between devices, ring_gather(): backward = lax.ppermute(backward, axis, left)  14.1 us
    ppermute x5, starting transfers between devices, ring_gather(): forward = lax.ppermute(forward, axis, right)  11.3 us
    ppermute x2, waiting for transfers between devices, shifted(): return lax.ppermute(array, axis, pairs)  7.74 us
    concatenate x1, local copies, waits for them, and re-layouts, ring_gather(): doubled = jnp.concatenate([stacked, stacked], axis=dim)  7.61 us
    ppermute x2, starting transfers between devices, shifted(): return lax.ppermute(array, axis, pairs)  5.74 us
    concatenate x1, other arithmetic, ring_gather(): doubled = jnp.concatenate([stacked, stacked], axis=dim)  5.16 us
  transfers between devices with their start and end apart: 11, of which 8 were waited for; matrix products, arithmetic and copies ran while one was open for 18% of the time, Pallas kernels for 0%

profile of v4, /device:TPU:64, one launch (start us, length us, event | category | flops | bytes accessed | tf_op | source)
XLA Modules:
  0.0 146.3 jit_solution(17096434053184287298)
XLA Ops:
  10.4 3.5 %collective-permute-start.3 = (bf16[520,336]{1,0:T(8,128)(2,1)S(1)}, bf16[520,336]{1,0:T(8,128)(2,1)S(1)}, u32[]{:S(2)}, u32[]{:S(2)}) collective-permute-start(bf16[520,336]{1,0:T(8,128)(2,1)S(1)} %concatenate.40), channel_id=1, source_target_pairs={{0,2},{2,4},{4,6},{6,8},{8,10},{10,12},{12,14},{14,0},{1,3},{3,5},... | collective-permute-start | bytes 1048328 | tf_op jit(solution)/shard_map/ppermute | solution.py:31
  13.9 3.8 %collective-permute-start = (bf16[520,336]{1,0:T(8,128)(2,1)S(1)}, bf16[520,336]{1,0:T(8,128)(2,1)S(1)}, u32[]{:S(2)}, u32[]{:S(2)}) collective-permute-start(bf16[520,336]{1,0:T(8,128)(2,1)S(1)} %concatenate.40), channel_id=1, source_target_pairs={{0,14},{2,0},{4,2},{6,4},{8,6},{10,8},{12,10},{14,12},{1,15},{3,1}... | collective-permute-start | bytes 1048328 | tf_op jit(solution)/shard_map/ppermute | solution.py:34
  17.7 7.3 %collective-permute-done.3 = bf16[520,336]{1,0:T(8,128)(2,1)S(1)} collective-permute-done((bf16[520,336]{1,0:T(8,128)(2,1)S(1)}, bf16[520,336]{1,0:T(8,128)(2,1)S(1)}, u32[]{:S(2)}, u32[]{:S(2)}) %collective-permute-start.3) | collective-permute-done | bytes 349472 | tf_op jit(solution)/shard_map/ppermute | solution.py:31
  27.0 5.1 %collective-permute-start.1 = (bf16[520,336]{1,0:T(8,128)(2,1)S(1)}, bf16[520,336]{1,0:T(8,128)(2,1)S(1)}, u32[]{:S(2)}, u32[]{:S(2)}) collective-permute-start(bf16[520,336]{1,0:T(8,128)(2,1)S(1)} %collective-permute-done), channel_id=1, source_target_pairs={{0,14},{2,0},{4,2},{6,4},{8,6},{10,8},{12,10},{14,12},{1,15},{3,1}... | collective-permute-start | bytes 1048328 | tf_op jit(solution)/shard_map/ppermute | solution.py:34
  32.1 6.5 %collective-permute-done.4 = bf16[520,336]{1,0:T(8,128)(2,1)S(1)} collective-permute-done((bf16[520,336]{1,0:T(8,128)(2,1)S(1)}, bf16[520,336]{1,0:T(8,128)(2,1)S(1)}, u32[]{:S(2)}, u32[]{:S(2)}) %collective-permute-start.4) | collective-permute-done | bytes 349472 | tf_op jit(solution)/shard_map/ppermute | solution.py:31
  40.5 5.1 %collective-permute-start.2 = (bf16[520,336]{1,0:T(8,128)(2,1)S(1)}, bf16[520,336]{1,0:T(8,128)(2,1)S(1)}, u32[]{:S(2)}, u32[]{:S(2)}) collective-permute-start(bf16[520,336]{1,0:T(8,128)(2,1)S(1)} %collective-permute-done.1), channel_id=1, source_target_pairs={{0,14},{2,0},{4,2},{6,4},{8,6},{10,8},{12,10},{14,12},{1,15},{3,1}... | collective-permute-start | bytes 1048328 | tf_op jit(solution)/shard_map/ppermute | solution.py:34
  45.6 5.5 %collective-permute-done.5 = bf16[520,336]{1,0:T(8,128)(2,1)S(1)} collective-permute-done((bf16[520,336]{1,0:T(8,128)(2,1)S(1)}, bf16[520,336]{1,0:T(8,128)(2,1)S(1)}, u32[]{:S(2)}, u32[]{:S(2)}) %collective-permute-start.5) | collective-permute-done | bytes 349472 | tf_op jit(solution)/shard_map/ppermute | solution.py:31
  53.1 9.7 %collective-permute-done.6 = bf16[520,336]{1,0:T(8,128)(2,1)S(1)} collective-permute-done((bf16[520,336]{1,0:T(8,128)(2,1)S(1)}, bf16[520,336]{1,0:T(8,128)(2,1)S(1)}, u32[]{:S(2)}, u32[]{:S(2)}) %collective-permute-start.6) | collective-permute-done | bytes 349472 | tf_op jit(solution)/shard_map/ppermute | solution.py:31
  62.9 7.6 %concatenate.41 = bf16[520,5376]{1,0:T(8,128)(2,1)} concatenate(bf16[520,336]{1,0:T(8,128)(2,1)S(1)} %concatenate.40, bf16[520,336]{1,0:T(8,128)(2,1)S(1)} %collective-permute-done, bf16[520,336]{1,0:T(8,128)(2,1)S(1)} %collective-permute-done.1, bf16[520,336]{1,0:T(8,128)(2,1)S(1)} %collective-permute-done.2, bf16[520,336]{1,0:T(8,128)(2,1)S(1)} %collective-permute-done.6, ...), dimensions={1} | concatenate | bytes 11182080 | tf_op jit(solution)/shard_map/concatenate | solution.py:40
  70.5 3.3 %constant_dynamic-slice_fusion = bf16[520,2688]{1,0:T(8,128)(2,1)S(1)} fusion(bf16[520,5376]{1,0:T(8,128)(2,1)} %concatenate.41, s32[]{:T(128)S(6)} %select_n.22), kind=kLoop, calls=%fused_computation.77 | loop fusion | bytes 5591044 | tf_op jit(solution)/shard_map/dynamic_slice | solution.py:42
  73.8 2.1 %collective-permute-start.7 = (bf16[520,2688]{1,0:T(8,128)(2,1)S(1)}, bf16[520,2688]{1,0:T(8,128)(2,1)}, u32[]{:S(2)}, u32[]{:S(2)}) collective-permute-start(bf16[520,2688]{1,0:T(8,128)(2,1)S(1)} %constant_dynamic-slice_fusion), channel_id=1, source_target_pairs={{0,1},{1,0},{2,3},{3,2},{4,5},{5,4},{6,7},{7,6},{8,9},{9,8},{10,11... | collective-permute-start | bytes 8386568 | tf_op jit(solution)/shard_map/ppermute | solution.py:31
  78.2 2.0 %fusion.11 = pred[512,1536]{0,1:T(8,128)(4,1)} fusion(s32[1536]{0:T(1024)S(1)} %iota_add_fusion, s32[512]{0:T(512)S(1)} %iota_add_fusion.1, pred[1536]{0:T(1024)(128)(4,1)S(1)} %broadcast_compare_fusion), kind=kLoop, calls=%fused_computation.24 | loop fusion | flops 3932160 | bytes 796160 | tf_op jit(solution)/shard_map/and | solution.py:134
  81.0 5.2 %fusion.5 = bf16[520,5376]{1,0:T(8,128)(2,1)S(1)} fusion(s32[]{:T(128)S(6)} %select_n.24, bf16[520,2688]{1,0:T(8,128)(2,1)S(1)} %constant_dynamic-slice_fusion, bf16[520,2688]{1,0:T(8,128)(2,1)} %collective-permute-done.7), kind=kLoop, calls=%fused_computation.15 | loop fusion | flops 22364160 | bytes 11182084 | tf_op jit(solution)/shard_map/concatenate | solution.py:40
  86.3 2.3 %copy-done = bf16[520,5376]{1,0:T(8,128)(2,1)} copy-done((bf16[520,5376]{1,0:T(8,128)(2,1)}, bf16[520,5376]{1,0:T(8,128)(2,1)S(1)}, u32[]{:S(2)}) %copy-start) | copy-done | bytes 5591064
  89.7 17.1 %all-gather.2.cloned.1.call-done = bf16[5632,512]{1,0:T(8,128)(2,1)} async-done(((bf16[176,512]{1,0:T(8,128)(2,1)}), bf16[5632,512]{1,0:T(8,128)(2,1)}) %all-gather.2.cloned.1.call-update) | async-done | bytes 5767184 | tf_op jit(solution)/shard_map/all_gather | solution.py:80
  106.8 3.1 %abs_reduce_fusion = f32[512]{0:T(512)S(1)} fusion(bf16[32,176,512]{2,1,0:T(8,128)(2,1)} %bitcast.49), kind=kLoop, calls=%fused_computation.10 | loop fusion | flops 8257024 | bytes 5507072 | tf_op jit(solution)/shard_map/reduce_max | solution.py:52
  110.0 3.1 %slice.125 = bf16[32,168,512]{2,1,0:T(8,128)(2,1)S(1)} slice(bf16[32,176,512]{2,1,0:T(8,128)(2,1)} %bitcast.50), slice={[0:32], [0:168], [0:512]} | slice | bytes 11010048 | tf_op jit(solution)/shard_map/slice | solution.py:81
  114.6 2.0 %fusion.14 = f32[512,256]{0,1:T(8,128)S(1)} fusion(bf16[5376,512]{1,0:T(8,128)(2,1)S(1)} %bitcast.51, f32[5376]{0:T(1024)S(1)} %fusion.40, f32[512]{0:T(512)S(1)} %add_rsqrt_fusion.2, bf16[520,5376]{1,0:T(8,128)(2,1)S(1)} %bitcast.47), kind=kOutput, calls=%fused_computation.27 | convolution fusion | flops 1420296192 | bytes 8808448 | tf_op jit(solution)/shard_map/dot_general | solution.py:105
  117.4 3.4 %collective-permute-start.8 = (bf16[512,2,128]{0,2,1:T(8,128)(2,1)S(1)}, bf16[512,2,128]{0,2,1:T(8,128)(2,1)S(1)}, u32[]{:S(2)}, u32[]{:S(2)}) collective-permute-start(bf16[512,2,128]{0,2,1:T(8,128)(2,1)S(1)} %pad_maximum_fusion), channel_id=1, source_target_pairs={{0,32},{16,48},{32,64},{48,80},{64,96},{80,112},{96,128},{112,144}... | collective-permute-start | bytes 786440 | tf_op jit(solution)/shard_map/ppermute | solution.py:20
  120.8 2.4 %collective-permute-start.9 = (bf16[512,2,128]{0,2,1:T(8,128)(2,1)S(1)}, bf16[512,2,128]{0,2,1:T(8,128)(2,1)}, u32[]{:S(2)}, u32[]{:S(2)}) collective-permute-start(bf16[512,2,128]{0,2,1:T(8,128)(2,1)S(1)} %pad_maximum_fusion), channel_id=1, source_target_pairs={{0,16},{16,32},{32,48},{48,64},{64,80},{80,96},{96,112},{112,128},... | collective-permute-start | bytes 786440 | tf_op jit(solution)/shard_map/ppermute | solution.py:20
  123.2 2.0 %multiply_reduce_fusion = (f32[512,2]{0,1:T(2,128)S(1)}, f32[512,256]{0,1:T(8,128)S(1)}) fusion(bf16[5376,512]{1,0:T(8,128)(2,1)S(1)} %bitcast.52, f32[5376]{0:T(1024)S(1)} %fusion.40, f32[512]{0:T(512)S(1)} %add_rsqrt_fusion.2, bf16[520,5376]{1,0:T(8,128)(2,1)S(1)} %bitcast.47), kind=kOutput, calls=%fused_computation.34 | convolution fusion | flops 1420557312 | bytes 8812544 | tf_op jit(solution)/shard_map/dot_general | solution.py:108
  125.9 4.0 %collective-permute-done.8 = bf16[512,2,128]{0,2,1:T(8,128)(2,1)S(1)} collective-permute-done((bf16[512,2,128]{0,2,1:T(8,128)(2,1)S(1)}, bf16[512,2,128]{0,2,1:T(8,128)(2,1)S(1)}, u32[]{:S(2)}, u32[]{:S(2)}) %collective-permute-start.8) | collective-permute-done | bytes 262176 | tf_op jit(solution)/shard_map/ppermute | solution.py:20
  129.9 3.8 %collective-permute-done.9 = bf16[512,2,128]{0,2,1:T(8,128)(2,1)} collective-permute-done((bf16[512,2,128]{0,2,1:T(8,128)(2,1)S(1)}, bf16[512,2,128]{0,2,1:T(8,128)(2,1)}, u32[]{:S(2)}, u32[]{:S(2)}) %collective-permute-start.9) | collective-permute-done | bytes 262176 | tf_op jit(solution)/shard_map/ppermute | solution.py:20
  136.6 2.0 %fusion.16 = bf16[128,2,512]{2,0,1:T(8,128)(2,1)S(1)} fusion(f32[2,512]{1,0:T(2,128)S(1)} %get-tuple-element.18, f32[1536,512,2]{1,0,2:T(8,128)S(1)} %get-tuple-element.19, pred[512,1536]{0,1:T(8,128)(4,1)S(1)} %copy-done.1, bf16[1536,2,128]{0,2,1:T(8,128)(2,1)S(1)} %maximum_maximum_fusion), kind=kOutput, calls=%fused_computation.29 | convolution fusion | flops 409075712 | bytes 7737344 | tf_op jit(solution)/shard_map/kgts,skd->tkgd/dot_general | solution.py:138
  (56 shorter events, 20.0 us)
Async XLA Ops:
  6.5 100.3 %all-gather.2.cloned.1.call-start = ((), (), s32[]{:S(2)}) async-start(), calls=%async_computation | async-start | bytes 5947392 | tf_op jit(solution)/shard_map/all_gather | solution.py:80
  10.4 14.6 %collective-permute-start.3 = (bf16[520,336]{1,0:T(8,128)(2,1)S(1)}, bf16[520,336]{1,0:T(8,128)(2,1)S(1)}, u32[]{:S(2)}, u32[]{:S(2)}) collective-permute-start(bf16[520,336]{1,0:T(8,128)(2,1)S(1)} %concatenate.40), channel_id=1, source_target_pairs={{0,2},{2,4},{4,6},{6,8},{8,10},{10,12},{12,14},{14,0},{1,3},{3,5},... | collective-permute-start | bytes 1048328 | tf_op jit(solution)/shard_map/ppermute | solution.py:31
  13.9 13.0 %collective-permute-start = (bf16[520,336]{1,0:T(8,128)(2,1)S(1)}, bf16[520,336]{1,0:T(8,128)(2,1)S(1)}, u32[]{:S(2)}, u32[]{:S(2)}) collective-permute-start(bf16[520,336]{1,0:T(8,128)(2,1)S(1)} %concatenate.40), channel_id=1, source_target_pairs={{0,14},{2,0},{4,2},{6,4},{8,6},{10,8},{12,10},{14,12},{1,15},{3,1}... | collective-permute-start | bytes 1048328 | tf_op jit(solution)/shard_map/ppermute | solution.py:34
  25.1 13.5 %collective-permute-start.4 = (bf16[520,336]{1,0:T(8,128)(2,1)S(1)}, bf16[520,336]{1,0:T(8,128)(2,1)S(1)}, u32[]{:S(2)}, u32[]{:S(2)}) collective-permute-start(bf16[520,336]{1,0:T(8,128)(2,1)S(1)} %collective-permute-done.3), channel_id=1, source_target_pairs={{0,2},{2,4},{4,6},{6,8},{8,10},{10,12},{12,14},{14,0},{1,3},{3,5},... | collective-permute-start | bytes 1048328 | tf_op jit(solution)/shard_map/ppermute | solution.py:31
  27.0 13.5 %collective-permute-start.1 = (bf16[520,336]{1,0:T(8,128)(2,1)S(1)}, bf16[520,336]{1,0:T(8,128)(2,1)S(1)}, u32[]{:S(2)}, u32[]{:S(2)}) collective-permute-start(bf16[520,336]{1,0:T(8,128)(2,1)S(1)} %collective-permute-done), channel_id=1, source_target_pairs={{0,14},{2,0},{4,2},{6,4},{8,6},{10,8},{12,10},{14,12},{1,15},{3,1}... | collective-permute-start | bytes 1048328 | tf_op jit(solution)/shard_map/ppermute | solution.py:34
  38.6 12.6 %collective-permute-start.5 = (bf16[520,336]{1,0:T(8,128)(2,1)S(1)}, bf16[520,336]{1,0:T(8,128)(2,1)S(1)}, u32[]{:S(2)}, u32[]{:S(2)}) collective-permute-start(bf16[520,336]{1,0:T(8,128)(2,1)S(1)} %collective-permute-done.4), channel_id=1, source_target_pairs={{0,2},{2,4},{4,6},{6,8},{8,10},{10,12},{12,14},{14,0},{1,3},{3,5},... | collective-permute-start | bytes 1048328 | tf_op jit(solution)/shard_map/ppermute | solution.py:31
  40.5 12.6 %collective-permute-start.2 = (bf16[520,336]{1,0:T(8,128)(2,1)S(1)}, bf16[520,336]{1,0:T(8,128)(2,1)S(1)}, u32[]{:S(2)}, u32[]{:S(2)}) collective-permute-start(bf16[520,336]{1,0:T(8,128)(2,1)S(1)} %collective-permute-done.1), channel_id=1, source_target_pairs={{0,14},{2,0},{4,2},{6,4},{8,6},{10,8},{12,10},{14,12},{1,15},{3,1}... | collective-permute-start | bytes 1048328 | tf_op jit(solution)/shard_map/ppermute | solution.py:34
  51.2 11.7 %collective-permute-start.6 = (bf16[520,336]{1,0:T(8,128)(2,1)S(1)}, bf16[520,336]{1,0:T(8,128)(2,1)S(1)}, u32[]{:S(2)}, u32[]{:S(2)}) collective-permute-start(bf16[520,336]{1,0:T(8,128)(2,1)S(1)} %collective-permute-done.5), channel_id=1, source_target_pairs={{0,2},{2,4},{4,6},{6,8},{8,10},{10,12},{12,14},{14,0},{1,3},{3,5},... | collective-permute-start | bytes 1048328 | tf_op jit(solution)/shard_map/ppermute | solution.py:31
  73.8 7.2 %collective-permute-start.7 = (bf16[520,2688]{1,0:T(8,128)(2,1)S(1)}, bf16[520,2688]{1,0:T(8,128)(2,1)}, u32[]{:S(2)}, u32[]{:S(2)}) collective-permute-start(bf16[520,2688]{1,0:T(8,128)(2,1)S(1)} %constant_dynamic-slice_fusion), channel_id=1, source_target_pairs={{0,1},{1,0},{2,3},{3,2},{4,5},{5,4},{6,7},{7,6},{8,9},{9,8},{10,11... | collective-permute-start | bytes 8386568 | tf_op jit(solution)/shard_map/ppermute | solution.py:31
  86.1 2.4 %copy-start = (bf16[520,5376]{1,0:T(8,128)(2,1)}, bf16[520,5376]{1,0:T(8,128)(2,1)S(1)}, u32[]{:S(2)}) copy-start(bf16[520,5376]{1,0:T(8,128)(2,1)S(1)} %fusion.5) | copy-start | bytes 16773124
  110.0 4.1 %slice-start = ((s8[5591040]{0:T(1024)(128)(4,1)}), s8[4194304]{0:T(1024)(128)(4,1)S(1)}, s32[]{:S(2)}) async-start(s8[5591040]{0:T(1024)(128)(4,1)} %bitcast.46), calls=%async_computation.1 | async-start | bytes 8388608
  113.1 1.5 %slice-start.1 = ((s8[5591040]{0:T(1024)(128)(4,1)}), s8[1396736]{0:T(1024)(128)(4,1)S(1)}, s32[]{:S(2)}) async-start(s8[5591040]{0:T(1024)(128)(4,1)} %bitcast.46), calls=%async_computation.2 | async-start | bytes 2793472
  114.6 2.1 %copy-start.2 = (f32[128]{0:T(128)S(1)}, f32[128]{0:T(128)}, u32[]{:S(2)}) copy-start(f32[128]{0:T(128)} %param.10) | copy-start | bytes 1540
  117.4 8.0 %copy-start.3 = (f32[128]{0:T(128)S(1)}, f32[128]{0:T(128)}, u32[]{:S(2)}) copy-start(f32[128]{0:T(128)} %param.9) | copy-start | bytes 1540
  117.4 12.5 %collective-permute-start.8 = (bf16[512,2,128]{0,2,1:T(8,128)(2,1)S(1)}, bf16[512,2,128]{0,2,1:T(8,128)(2,1)S(1)}, u32[]{:S(2)}, u32[]{:S(2)}) collective-permute-start(bf16[512,2,128]{0,2,1:T(8,128)(2,1)S(1)} %pad_maximum_fusion), channel_id=1, source_target_pairs={{0,32},{16,48},{32,64},{48,80},{64,96},{80,112},{96,128},{112,144}... | collective-permute-start | bytes 786440 | tf_op jit(solution)/shard_map/ppermute | solution.py:20
  120.8 12.9 %collective-permute-start.9 = (bf16[512,2,128]{0,2,1:T(8,128)(2,1)S(1)}, bf16[512,2,128]{0,2,1:T(8,128)(2,1)}, u32[]{:S(2)}, u32[]{:S(2)}) collective-permute-start(bf16[512,2,128]{0,2,1:T(8,128)(2,1)S(1)} %pad_maximum_fusion), channel_id=1, source_target_pairs={{0,16},{16,32},{32,48},{48,64},{64,80},{80,96},{96,112},{112,128},... | collective-permute-start | bytes 786440 | tf_op jit(solution)/shard_map/ppermute | solution.py:20
  125.2 9.5 %copy-start.1 = (pred[512,1536]{0,1:T(8,128)(4,1)S(1)}, pred[512,1536]{0,1:T(8,128)(4,1)}, u32[]{:S(2)}) copy-start(pred[512,1536]{0,1:T(8,128)(4,1)} %fusion.11) | copy-start | bytes 2359300
Sparse Core Ops, SparseCore 0:
  10.5 96.2 all-gather.1

commit v5 on v3

--- a/solution.py
+++ b/solution.py
@@ -12,6 +12,9 @@
 CLIP_FRACTION = 0.25
 QUERY_SCALAR = 168.0
 ROPE_BASE = 10000.0
+
+
+ROW = ("rz", "rx")
 
 
 def shifted(array, axis, by):
@@ -74,8 +77,20 @@
     query_cols = w_query.shape[1]
     key_cols = w_key.shape[1]
     stacked = jnp.concatenate([w_query, w_key, w_value], axis=1)
-    panel = lax.all_gather(stacked, "row", axis=0, tiled=True)
-    clipped = clip_with(panel, column_max(panel))
+    weight_rows, weight_cols = stacked.shape
+    aligned = -(-(weight_rows + 1) // TILE_ROWS) * TILE_ROWS
+    local_max = jnp.max(jnp.abs(stacked), axis=0)
+    padded = jnp.concatenate(
+        [
+            stacked,
+            local_max[None],
+            jnp.zeros((aligned - weight_rows - 1, weight_cols), stacked.dtype),
+        ],
+        axis=0,
+    )
+    slabs = lax.all_gather(padded, ROW, axis=0, tiled=True).reshape(-1, aligned, weight_cols)
+    largest = jnp.max(slabs[:, weight_rows].astype(jnp.float32), axis=0)
+    clipped = clip_with(slabs[:, :weight_rows].reshape(-1, weight_cols), largest)
     rows_tokens, piece = tokens.shape
     cores = lax.axis_size("cc")
     high = gain.astype(jnp.bfloat16)
@@ -105,7 +120,7 @@
     heads_local = query_cols // HD
     kv_local = key_cols // HD
     group = heads_local // kv_local
-    positions = lax.axis_index("row") * rows + jnp.arange(rows, dtype=jnp.int32)
+    positions = lax.axis_index(ROW) * rows + jnp.arange(rows, dtype=jnp.int32)
     query = rotate(head_norm(query.reshape(rows, heads_local, HD), query_gain), positions).astype(
         jnp.bfloat16
     )
@@ -115,7 +130,7 @@
     values = values.reshape(rows, kv_local, HD).astype(jnp.bfloat16)
     blocks_back = WINDOW // rows
     both = jnp.concatenate([keys, values], axis=1)
-    earlier = [shifted(both, "row", offset) for offset in range(blocks_back, 0, -1)]
+    earlier = [shifted(both, ROW, offset) for offset in range(blocks_back, 0, -1)]
     joined = jnp.concatenate(earlier + [both], axis=0)
     all_keys = joined[:, :kv_local]
     all_values = joined[:, kv_local:]
@@ -137,23 +152,28 @@
 
 CORES_PER_CHIP = 2
 GAIN_ROWS = 8
+TILE_ROWS = 16
 
 
 def solution(mesh):
     rows, cols = mesh.shape["row"], mesh.shape["col"]
+    minor = len({tuple(getattr(d, "coords", (0,)))[0] for d in mesh.devices[:, 0].flat})
+    if rows % minor:
+        minor = 1
     split = Mesh(
-        mesh.devices.reshape(rows, cols // CORES_PER_CHIP, CORES_PER_CHIP), ("row", "cy", "cc")
+        mesh.devices.reshape(rows // minor, minor, cols // CORES_PER_CHIP, CORES_PER_CHIP),
+        ("rz", "rx", "cy", "cc"),
     )
     col = ("cy", "cc")
     placed = (
-        P("row", col),
+        P(ROW, col),
         P(col),
         P(),
         P(),
-        P("row", col),
-        P("row", col),
-        P("row", col),
+        P(ROW, col),
+        P(ROW, col),
+        P(ROW, col),
     )
     return jax.shard_map(
-        local, mesh=split, in_specs=placed, out_specs=P("row", col), check_vma=False
+        local, mesh=split, in_specs=placed, out_specs=P(ROW, col), check_vma=False
     )

time: 146 us -> 145 us (level)
  other arithmetic: 18.9 us -> 15.7 us
  local copies, waits for them, and re-layouts: 19.8 us -> 22.5 us
    slice x0 -> x1, local copies, waits for them, and re-layouts: none -> 3.11 us  [local(): slabs[:, :weight_rows].reshape(-1, weight_cols)]
    reduce_max x1 -> x2, other arithmetic: 3.26 us -> 1.07 us  [the longest x1 1.03 us: local(): largest = jnp.max(slabs[:, weight_rows].astype(jnp.float32), axis=0)]
    convert_element_type x1 -> x0, other arithmetic: 1.61 us -> none  [clip_with(): jnp.clip(weight.astype(jnp.float32), -bound, bound).astype(jnp.bfloat16)]
    transpose x0 -> x1, other arithmetic: none -> 1.46 us  [local(): ordered = clipped.reshape(blocks, cores, piece, clipped.shape[1]).transpo...]
where the time goes in v5:
time: 145 us
  waiting for transfers between devices  52.9 us (36%)
  starting transfers between devices  31.1 us (21%)
  local copies, waits for them, and re-layouts  22.5 us (16%)
  other arithmetic  15.7 us (11%)
  between operations  14.5 us (10%)
  matrix products  7.99 us (6%)
    ppermute x5, waiting for transfers between devices, ring_gather(): forward = lax.ppermute(forward, axis, right)  29.8 us
    all_gather x1, waiting for transfers between devices, local(): lax.all_gather(padded, ROW, axis=0, tiled=True)  15.3 us
    ppermute x3, starting transfers between devices, ring_gather(): backward = lax.ppermute(backward, axis, left)  14.1 us
    ppermute x5, starting transfers between devices, ring_gather(): forward = lax.ppermute(forward, axis, right)  11.3 us
    ppermute x2, waiting for transfers between devices, shifted(): return lax.ppermute(array, axis, pairs)  7.75 us
    concatenate x1, local copies, waits for them, and re-layouts, ring_gather(): doubled = jnp.concatenate([stacked, stacked], axis=dim)  7.61 us
    ppermute x2, starting transfers between devices, shifted(): return lax.ppermute(array, axis, pairs)  5.74 us
    unnamed x15, local copies, waits for them, and re-layouts  5.2 us
  transfers between devices with their start and end apart: 11, of which 8 were waited for; matrix products, arithmetic and copies ran while one was open for 18% of the time, Pallas kernels for 0%

profile of v5, /device:TPU:64, one launch (start us, length us, event | category | flops | bytes accessed | tf_op | source)
XLA Modules:
  0.0 144.7 jit_solution(4266630463317419407)
XLA Ops:
  12.2 3.5 %collective-permute-start.3 = (bf16[520,336]{1,0:T(8,128)(2,1)S(1)}, bf16[520,336]{1,0:T(8,128)(2,1)S(1)}, u32[]{:S(2)}, u32[]{:S(2)}) collective-permute-start(bf16[520,336]{1,0:T(8,128)(2,1)S(1)} %concatenate.43), channel_id=1, source_target_pairs={{0,2},{2,4},{4,6},{6,8},{8,10},{10,12},{12,14},{14,0},{1,3},{3,5},... | collective-permute-start | bytes 1048328 | tf_op jit(solution)/shard_map/ppermute | solution.py:34
  15.7 3.8 %collective-permute-start = (bf16[520,336]{1,0:T(8,128)(2,1)S(1)}, bf16[520,336]{1,0:T(8,128)(2,1)S(1)}, u32[]{:S(2)}, u32[]{:S(2)}) collective-permute-start(bf16[520,336]{1,0:T(8,128)(2,1)S(1)} %concatenate.43), channel_id=1, source_target_pairs={{0,14},{2,0},{4,2},{6,4},{8,6},{10,8},{12,10},{14,12},{1,15},{3,1}... | collective-permute-start | bytes 1048328 | tf_op jit(solution)/shard_map/ppermute | solution.py:37
  19.5 7.3 %collective-permute-done.3 = bf16[520,336]{1,0:T(8,128)(2,1)S(1)} collective-permute-done((bf16[520,336]{1,0:T(8,128)(2,1)S(1)}, bf16[520,336]{1,0:T(8,128)(2,1)S(1)}, u32[]{:S(2)}, u32[]{:S(2)}) %collective-permute-start.3) | collective-permute-done | bytes 349472 | tf_op jit(solution)/shard_map/ppermute | solution.py:34
  28.8 5.1 %collective-permute-start.1 = (bf16[520,336]{1,0:T(8,128)(2,1)S(1)}, bf16[520,336]{1,0:T(8,128)(2,1)S(1)}, u32[]{:S(2)}, u32[]{:S(2)}) collective-permute-start(bf16[520,336]{1,0:T(8,128)(2,1)S(1)} %collective-permute-done), channel_id=1, source_target_pairs={{0,14},{2,0},{4,2},{6,4},{8,6},{10,8},{12,10},{14,12},{1,15},{3,1}... | collective-permute-start | bytes 1048328 | tf_op jit(solution)/shard_map/ppermute | solution.py:37
  33.9 6.5 %collective-permute-done.4 = bf16[520,336]{1,0:T(8,128)(2,1)S(1)} collective-permute-done((bf16[520,336]{1,0:T(8,128)(2,1)S(1)}, bf16[520,336]{1,0:T(8,128)(2,1)S(1)}, u32[]{:S(2)}, u32[]{:S(2)}) %collective-permute-start.4) | collective-permute-done | bytes 349472 | tf_op jit(solution)/shard_map/ppermute | solution.py:34
  42.3 5.1 %collective-permute-start.2 = (bf16[520,336]{1,0:T(8,128)(2,1)S(1)}, bf16[520,336]{1,0:T(8,128)(2,1)S(1)}, u32[]{:S(2)}, u32[]{:S(2)}) collective-permute-start(bf16[520,336]{1,0:T(8,128)(2,1)S(1)} %collective-permute-done.1), channel_id=1, source_target_pairs={{0,14},{2,0},{4,2},{6,4},{8,6},{10,8},{12,10},{14,12},{1,15},{3,1}... | collective-permute-start | bytes 1048328 | tf_op jit(solution)/shard_map/ppermute | solution.py:37
  47.4 5.5 %collective-permute-done.5 = bf16[520,336]{1,0:T(8,128)(2,1)S(1)} collective-permute-done((bf16[520,336]{1,0:T(8,128)(2,1)S(1)}, bf16[520,336]{1,0:T(8,128)(2,1)S(1)}, u32[]{:S(2)}, u32[]{:S(2)}) %collective-permute-start.5) | collective-permute-done | bytes 349472 | tf_op jit(solution)/shard_map/ppermute | solution.py:34
  54.9 9.7 %collective-permute-done.6 = bf16[520,336]{1,0:T(8,128)(2,1)S(1)} collective-permute-done((bf16[520,336]{1,0:T(8,128)(2,1)S(1)}, bf16[520,336]{1,0:T(8,128)(2,1)S(1)}, u32[]{:S(2)}, u32[]{:S(2)}) %collective-permute-start.6) | collective-permute-done | bytes 349472 | tf_op jit(solution)/shard_map/ppermute | solution.py:34
  64.6 7.6 %concatenate.44 = bf16[520,5376]{1,0:T(8,128)(2,1)} concatenate(bf16[520,336]{1,0:T(8,128)(2,1)S(1)} %concatenate.43, bf16[520,336]{1,0:T(8,128)(2,1)S(1)} %collective-permute-done, bf16[520,336]{1,0:T(8,128)(2,1)S(1)} %collective-permute-done.1, bf16[520,336]{1,0:T(8,128)(2,1)S(1)} %collective-permute-done.2, bf16[520,336]{1,0:T(8,128)(2,1)S(1)} %collective-permute-done.6, ...), dimensions={1} | concatenate | bytes 11182080 | tf_op jit(solution)/shard_map/concatenate | solution.py:43
  72.2 3.3 %constant_dynamic-slice_fusion = bf16[520,2688]{1,0:T(8,128)(2,1)S(1)} fusion(bf16[520,5376]{1,0:T(8,128)(2,1)} %concatenate.44, s32[]{:T(128)S(6)} %select_n.22), kind=kLoop, calls=%fused_computation.78 | loop fusion | bytes 5591044 | tf_op jit(solution)/shard_map/dynamic_slice | solution.py:45
  75.5 2.1 %collective-permute-start.7 = (bf16[520,2688]{1,0:T(8,128)(2,1)S(1)}, bf16[520,2688]{1,0:T(8,128)(2,1)}, u32[]{:S(2)}, u32[]{:S(2)}) collective-permute-start(bf16[520,2688]{1,0:T(8,128)(2,1)S(1)} %constant_dynamic-slice_fusion), channel_id=1, source_target_pairs={{0,1},{1,0},{2,3},{3,2},{4,5},{5,4},{6,7},{7,6},{8,9},{9,8},{10,11... | collective-permute-start | bytes 8386568 | tf_op jit(solution)/shard_map/ppermute | solution.py:34
  80.0 2.0 %fusion.13 = pred[512,1536]{0,1:T(8,128)(4,1)} fusion(s32[1536]{0:T(1024)S(1)} %iota_add_fusion, s32[512]{0:T(512)S(1)} %iota_add_fusion.1, pred[1536]{0:T(1024)(128)(4,1)S(1)} %broadcast_compare_fusion), kind=kLoop, calls=%fused_computation.24 | loop fusion | flops 3932160 | bytes 796160 | tf_op jit(solution)/shard_map/and | solution.py:145
  82.7 5.2 %fusion.7 = bf16[520,5376]{1,0:T(8,128)(2,1)S(1)} fusion(s32[]{:T(128)S(6)} %select_n.24, bf16[520,2688]{1,0:T(8,128)(2,1)S(1)} %constant_dynamic-slice_fusion, bf16[520,2688]{1,0:T(8,128)(2,1)} %collective-permute-done.7), kind=kLoop, calls=%fused_computation.16 | loop fusion | flops 22364160 | bytes 11182084 | tf_op jit(solution)/shard_map/concatenate | solution.py:43
  88.0 2.3 %copy-done = bf16[520,5376]{1,0:T(8,128)(2,1)} copy-done((bf16[520,5376]{1,0:T(8,128)(2,1)}, bf16[520,5376]{1,0:T(8,128)(2,1)S(1)}, u32[]{:S(2)}) %copy-start) | copy-done | bytes 5591064
  91.5 15.3 %all-gather.2.cloned.1.call-done = bf16[5632,512]{1,0:T(8,128)(2,1)} async-done(((bf16[176,512]{1,0:T(8,128)(2,1)}), bf16[5632,512]{1,0:T(8,128)(2,1)}) %all-gather.2.cloned.1.call-update) | async-done | bytes 5767184 | tf_op jit(solution)/shard_map/all_gather | solution.py:91
  107.8 3.1 %slice.79 = bf16[32,168,512]{2,1,0:T(8,128)(2,1)S(1)} slice(bf16[32,176,512]{2,1,0:T(8,128)(2,1)} %bitcast.53), slice={[0:32], [0:168], [0:512]} | slice | bytes 11010048 | tf_op jit(solution)/shard_map/slice | solution.py:93
  113.0 2.0 %fusion.16 = f32[512,256]{0,1:T(8,128)S(1)} fusion(bf16[5376,512]{1,0:T(8,128)(2,1)S(1)} %bitcast.50, f32[5376]{0:T(1024)S(1)} %fusion.37, f32[512]{0:T(512)S(1)} %add_rsqrt_fusion.2, bf16[520,5376]{1,0:T(8,128)(2,1)S(1)} %bitcast.48), kind=kOutput, calls=%fused_computation.27 | convolution fusion | flops 1420296192 | bytes 8808448 | tf_op jit(solution)/shard_map/dot_general | solution.py:116
  115.8 3.4 %collective-permute-start.8 = (bf16[512,2,128]{0,2,1:T(8,128)(2,1)S(1)}, bf16[512,2,128]{0,2,1:T(8,128)(2,1)S(1)}, u32[]{:S(2)}, u32[]{:S(2)}) collective-permute-start(bf16[512,2,128]{0,2,1:T(8,128)(2,1)S(1)} %pad_maximum_fusion), channel_id=1, source_target_pairs={{0,32},{16,48},{32,64},{48,80},{64,96},{80,112},{96,128},{112,144}... | collective-permute-start | bytes 786440 | tf_op jit(solution)/shard_map/ppermute | solution.py:23
  119.1 2.4 %collective-permute-start.9 = (bf16[512,2,128]{0,2,1:T(8,128)(2,1)S(1)}, bf16[512,2,128]{0,2,1:T(8,128)(2,1)}, u32[]{:S(2)}, u32[]{:S(2)}) collective-permute-start(bf16[512,2,128]{0,2,1:T(8,128)(2,1)S(1)} %pad_maximum_fusion), channel_id=1, source_target_pairs={{0,16},{16,32},{32,48},{48,64},{64,80},{80,96},{96,112},{112,128},... | collective-permute-start | bytes 786440 | tf_op jit(solution)/shard_map/ppermute | solution.py:23
  121.5 2.0 %multiply_reduce_fusion = (f32[512,2]{0,1:T(2,128)S(1)}, f32[512,256]{0,1:T(8,128)S(1)}) fusion(bf16[5376,512]{1,0:T(8,128)(2,1)S(1)} %bitcast.51, f32[5376]{0:T(1024)S(1)} %fusion.37, f32[512]{0:T(512)S(1)} %add_rsqrt_fusion.2, bf16[520,5376]{1,0:T(8,128)(2,1)S(1)} %bitcast.48), kind=kOutput, calls=%fused_computation.34 | convolution fusion | flops 1420557312 | bytes 8812544 | tf_op jit(solution)/shard_map/dot_general | solution.py:119
  124.2 4.0 %collective-permute-done.8 = bf16[512,2,128]{0,2,1:T(8,128)(2,1)S(1)} collective-permute-done((bf16[512,2,128]{0,2,1:T(8,128)(2,1)S(1)}, bf16[512,2,128]{0,2,1:T(8,128)(2,1)S(1)}, u32[]{:S(2)}, u32[]{:S(2)}) %collective-permute-start.8) | collective-permute-done | bytes 262176 | tf_op jit(solution)/shard_map/ppermute | solution.py:23
  128.2 3.8 %collective-permute-done.9 = bf16[512,2,128]{0,2,1:T(8,128)(2,1)} collective-permute-done((bf16[512,2,128]{0,2,1:T(8,128)(2,1)S(1)}, bf16[512,2,128]{0,2,1:T(8,128)(2,1)}, u32[]{:S(2)}, u32[]{:S(2)}) %collective-permute-start.9) | collective-permute-done | bytes 262176 | tf_op jit(solution)/shard_map/ppermute | solution.py:23
  133.0 1.9 %fusion.9 = (f32[2,512]{1,0:T(2,128)S(1)}, f32[1536,512,2]{1,0,2:T(8,128)S(1)}) fusion(pred[512,1536]{0,1:T(8,128)(4,1)S(1)} %copy-done.1, bf16[512,2,64]{2,0,1:T(8,128)(2,1)S(1)} %get-tuple-element.6, bf16[512,2,64]{2,0,1:T(8,128)(2,1)S(1)} %get-tuple-element.5, bf16[1536,2,128]{0,2,1:T(8,128)(2,1)S(1)} %maximum_maximum_fusion), kind=kOutput, calls=%fused_computation.18 | convolution fusion | flops 407895040 | bytes 7999488 | tf_op jit(solution)/shard_map/tkgd,skd->kgts/dot_general | solution.py:141
  135.0 2.0 %fusion.18 = bf16[128,2,512]{2,0,1:T(8,128)(2,1)S(1)} fusion(f32[2,512]{1,0:T(2,128)S(1)} %get-tuple-element.18, f32[1536,512,2]{1,0,2:T(8,128)S(1)} %get-tuple-element.19, pred[512,1536]{0,1:T(8,128)(4,1)S(1)} %copy-done.1, bf16[1536,2,128]{0,2,1:T(8,128)(2,1)S(1)} %maximum_maximum_fusion), kind=kOutput, calls=%fused_computation.29 | convolution fusion | flops 409075712 | bytes 7737344 | tf_op jit(solution)/shard_map/kgts,skd->tkgd/dot_general | solution.py:149
  (63 shorter events, 21.2 us)
Async XLA Ops:
  6.5 100.3 %all-gather.2.cloned.1.call-start = ((), (), s32[]{:S(2)}) async-start(), calls=%async_computation | async-start | bytes 5947392 | tf_op jit(solution)/shard_map/all_gather | solution.py:91
  12.2 14.6 %collective-permute-start.3 = (bf16[520,336]{1,0:T(8,128)(2,1)S(1)}, bf16[520,336]{1,0:T(8,128)(2,1)S(1)}, u32[]{:S(2)}, u32[]{:S(2)}) collective-permute-start(bf16[520,336]{1,0:T(8,128)(2,1)S(1)} %concatenate.43), channel_id=1, source_target_pairs={{0,2},{2,4},{4,6},{6,8},{8,10},{10,12},{12,14},{14,0},{1,3},{3,5},... | collective-permute-start | bytes 1048328 | tf_op jit(solution)/shard_map/ppermute | solution.py:34
  15.7 13.0 %collective-permute-start = (bf16[520,336]{1,0:T(8,128)(2,1)S(1)}, bf16[520,336]{1,0:T(8,128)(2,1)S(1)}, u32[]{:S(2)}, u32[]{:S(2)}) collective-permute-start(bf16[520,336]{1,0:T(8,128)(2,1)S(1)} %concatenate.43), channel_id=1, source_target_pairs={{0,14},{2,0},{4,2},{6,4},{8,6},{10,8},{12,10},{14,12},{1,15},{3,1}... | collective-permute-start | bytes 1048328 | tf_op jit(solution)/shard_map/ppermute | solution.py:37
  26.8 13.5 %collective-permute-start.4 = (bf16[520,336]{1,0:T(8,128)(2,1)S(1)}, bf16[520,336]{1,0:T(8,128)(2,1)S(1)}, u32[]{:S(2)}, u32[]{:S(2)}) collective-permute-start(bf16[520,336]{1,0:T(8,128)(2,1)S(1)} %collective-permute-done.3), channel_id=1, source_target_pairs={{0,2},{2,4},{4,6},{6,8},{8,10},{10,12},{12,14},{14,0},{1,3},{3,5},... | collective-permute-start | bytes 1048328 | tf_op jit(solution)/shard_map/ppermute | solution.py:34
  28.8 13.5 %collective-permute-start.1 = (bf16[520,336]{1,0:T(8,128)(2,1)S(1)}, bf16[520,336]{1,0:T(8,128)(2,1)S(1)}, u32[]{:S(2)}, u32[]{:S(2)}) collective-permute-start(bf16[520,336]{1,0:T(8,128)(2,1)S(1)} %collective-permute-done), channel_id=1, source_target_pairs={{0,14},{2,0},{4,2},{6,4},{8,6},{10,8},{12,10},{14,12},{1,15},{3,1}... | collective-permute-start | bytes 1048328 | tf_op jit(solution)/shard_map/ppermute | solution.py:37
  40.4 12.6 %collective-permute-start.5 = (bf16[520,336]{1,0:T(8,128)(2,1)S(1)}, bf16[520,336]{1,0:T(8,128)(2,1)S(1)}, u32[]{:S(2)}, u32[]{:S(2)}) collective-permute-start(bf16[520,336]{1,0:T(8,128)(2,1)S(1)} %collective-permute-done.4), channel_id=1, source_target_pairs={{0,2},{2,4},{4,6},{6,8},{8,10},{10,12},{12,14},{14,0},{1,3},{3,5},... | collective-permute-start | bytes 1048328 | tf_op jit(solution)/shard_map/ppermute | solution.py:34
  42.3 12.6 %collective-permute-start.2 = (bf16[520,336]{1,0:T(8,128)(2,1)S(1)}, bf16[520,336]{1,0:T(8,128)(2,1)S(1)}, u32[]{:S(2)}, u32[]{:S(2)}) collective-permute-start(bf16[520,336]{1,0:T(8,128)(2,1)S(1)} %collective-permute-done.1), channel_id=1, source_target_pairs={{0,14},{2,0},{4,2},{6,4},{8,6},{10,8},{12,10},{14,12},{1,15},{3,1}... | collective-permute-start | bytes 1048328 | tf_op jit(solution)/shard_map/ppermute | solution.py:37
  53.0 11.7 %collective-permute-start.6 = (bf16[520,336]{1,0:T(8,128)(2,1)S(1)}, bf16[520,336]{1,0:T(8,128)(2,1)S(1)}, u32[]{:S(2)}, u32[]{:S(2)}) collective-permute-start(bf16[520,336]{1,0:T(8,128)(2,1)S(1)} %collective-permute-done.5), channel_id=1, source_target_pairs={{0,2},{2,4},{4,6},{6,8},{8,10},{10,12},{12,14},{14,0},{1,3},{3,5},... | collective-permute-start | bytes 1048328 | tf_op jit(solution)/shard_map/ppermute | solution.py:34
  75.5 7.2 %collective-permute-start.7 = (bf16[520,2688]{1,0:T(8,128)(2,1)S(1)}, bf16[520,2688]{1,0:T(8,128)(2,1)}, u32[]{:S(2)}, u32[]{:S(2)}) collective-permute-start(bf16[520,2688]{1,0:T(8,128)(2,1)S(1)} %constant_dynamic-slice_fusion), channel_id=1, source_target_pairs={{0,1},{1,0},{2,3},{3,2},{4,5},{5,4},{6,7},{7,6},{8,9},{9,8},{10,11... | collective-permute-start | bytes 8386568 | tf_op jit(solution)/shard_map/ppermute | solution.py:34
  87.9 2.4 %copy-start = (bf16[520,5376]{1,0:T(8,128)(2,1)}, bf16[520,5376]{1,0:T(8,128)(2,1)S(1)}, u32[]{:S(2)}) copy-start(bf16[520,5376]{1,0:T(8,128)(2,1)S(1)} %fusion.7) | copy-start | bytes 16773124
  107.8 5.1 %slice-start = ((s8[5591040]{0:T(1024)(128)(4,1)}), s8[4194304]{0:T(1024)(128)(4,1)S(1)}, s32[]{:S(2)}) async-start(s8[5591040]{0:T(1024)(128)(4,1)} %bitcast.47), calls=%async_computation.1 | async-start | bytes 8388608
  111.0 2.0 %slice-start.1 = ((s8[5591040]{0:T(1024)(128)(4,1)}), s8[1396736]{0:T(1024)(128)(4,1)S(1)}, s32[]{:S(2)}) async-start(s8[5591040]{0:T(1024)(128)(4,1)} %bitcast.47), calls=%async_computation.2 | async-start | bytes 2793472
  112.9 2.1 %copy-start.2 = (f32[128]{0:T(128)S(1)}, f32[128]{0:T(128)}, u32[]{:S(2)}) copy-start(f32[128]{0:T(128)} %param.10) | copy-start | bytes 1540
  115.7 8.0 %copy-start.3 = (f32[128]{0:T(128)S(1)}, f32[128]{0:T(128)}, u32[]{:S(2)}) copy-start(f32[128]{0:T(128)} %param.9) | copy-start | bytes 1540
  115.8 12.5 %collective-permute-start.8 = (bf16[512,2,128]{0,2,1:T(8,128)(2,1)S(1)}, bf16[512,2,128]{0,2,1:T(8,128)(2,1)S(1)}, u32[]{:S(2)}, u32[]{:S(2)}) collective-permute-start(bf16[512,2,128]{0,2,1:T(8,128)(2,1)S(1)} %pad_maximum_fusion), channel_id=1, source_target_pairs={{0,32},{16,48},{32,64},{48,80},{64,96},{80,112},{96,128},{112,144}... | collective-permute-start | bytes 786440 | tf_op jit(solution)/shard_map/ppermute | solution.py:23
  119.1 12.9 %collective-permute-start.9 = (bf16[512,2,128]{0,2,1:T(8,128)(2,1)S(1)}, bf16[512,2,128]{0,2,1:T(8,128)(2,1)}, u32[]{:S(2)}, u32[]{:S(2)}) collective-permute-start(bf16[512,2,128]{0,2,1:T(8,128)(2,1)S(1)} %pad_maximum_fusion), channel_id=1, source_target_pairs={{0,16},{16,32},{32,48},{48,64},{64,80},{80,96},{96,112},{112,128},... | collective-permute-start | bytes 786440 | tf_op jit(solution)/shard_map/ppermute | solution.py:23
  123.5 9.5 %copy-start.1 = (pred[512,1536]{0,1:T(8,128)(4,1)S(1)}, pred[512,1536]{0,1:T(8,128)(4,1)}, u32[]{:S(2)}) copy-start(pred[512,1536]{0,1:T(8,128)(4,1)} %fusion.13) | copy-start | bytes 2359300
Sparse Core Ops, SparseCore 0:
  10.5 96.2 all-gather.1

commit v6 on v5

--- a/solution.py
+++ b/solution.py
@@ -88,7 +88,9 @@
         ],
         axis=0,
     )
-    slabs = lax.all_gather(padded, ROW, axis=0, tiled=True).reshape(-1, aligned, weight_cols)
+    (along_x,) = ring_gather((padded,), "rx", (0,))
+    (gathered,) = ring_gather((along_x,), "rz", (0,))
+    slabs = gathered.reshape(-1, aligned, weight_cols)
     largest = jnp.max(slabs[:, weight_rows].astype(jnp.float32), axis=0)
     clipped = clip_with(slabs[:, :weight_rows].reshape(-1, weight_cols), largest)
     rows_tokens, piece = tokens.shape
@@ -99,20 +101,14 @@
     low = (rest - middle.astype(jnp.float32)).astype(jnp.bfloat16)
     filler = jnp.zeros((GAIN_ROWS - 3, piece), jnp.bfloat16)
     packed = jnp.concatenate([tokens, high[None], middle[None], low[None], filler], axis=0)
-    (along_y,) = ring_gather((packed,), "cy", (1,))
-    (along_all,) = ring_gather((along_y,), "cc", (1,))
-    blocks = along_all.shape[1] // (cores * piece)
+    along_all = lax.all_gather(packed, ("cy", "cc"), axis=1, tiled=True)
     split = along_all[rows_tokens : rows_tokens + 3].astype(jnp.float32)
     full_gain = split[0] + (split[1] + split[2])
     widened = along_all[:rows_tokens].astype(jnp.float32)
     squares = jnp.sum(widened * widened, axis=1)
     inverse = lax.rsqrt(squares / D + EPS)[:, None]
     whole = (widened * inverse * full_gain[None, :]).astype(jnp.bfloat16)
-    ordered = (
-        clipped.reshape(blocks, cores, piece, clipped.shape[1])
-        .transpose(1, 0, 2, 3)
-        .reshape(clipped.shape)
-    )
+    ordered = clipped
     kv_part = jnp.dot(whole, ordered[:, query_cols:], preferred_element_type=jnp.float32)
     keys = kv_part[:, :key_cols]
     values = kv_part[:, key_cols:]

time: 145 us -> 189 us (1.30)
  the two profiles are of different devices: /device:TPU:64 before, /device:TPU:96 now
where the time goes in v6:
time: 189 us; the launch traced here: 187 us
  waiting for transfers between devices  56.3 us (30%)
  local copies, waits for them, and re-layouts  48.6 us (26%)
  starting transfers between devices  40.2 us (21%)
  other arithmetic  15.9 us (8%)
  between operations  14.6 us (8%)
  matrix products  11.9 us (6%)
    ppermute x6, waiting for transfers between devices, ring_gather(): forward = lax.ppermute(forward, axis, right)  49.9 us
    unnamed x35, local copies, waits for them, and re-layouts  32.9 us
    ppermute x6, starting transfers between devices, ring_gather(): forward = lax.ppermute(forward, axis, right)  18.2 us
    ppermute x4, starting transfers between devices, ring_gather(): backward = lax.ppermute(backward, axis, left)  16.6 us
    all_gather x1, local copies, waits for them, and re-layouts, local(): along_all = lax.all_gather(packed, ('cy', 'cc'), axis=1, tiled=True)  6.26 us
    ppermute x2, waiting for transfers between devices, shifted(): return lax.ppermute(array, axis, pairs)  6 us
    dot_general x1, matrix products, local(): jnp.dot(whole, ordered[:, query_cols:], preferred_element_type=jnp.float32)  5.9 us
    ppermute x2, starting transfers between devices, shifted(): return lax.ppermute(array, axis, pairs)  5.37 us
  transfers between devices with their start and end apart: 13, of which 9 were waited for; matrix products, arithmetic and copies ran while one was open for 20% of the time, Pallas kernels for 0%

profile of v6, /device:TPU:96, one launch (start us, length us, event | category | flops | bytes accessed | tf_op | source)
XLA Modules:
  0.0 187.5 jit_solution(1057055881618550521)
XLA Ops:
  13.2 3.4 %collective-permute-start.1 = (bf16[176,512]{1,0:T(8,128)(2,1)S(1)}, bf16[176,512]{1,0:T(8,128)(2,1)S(1)}, u32[]{:S(2)}, u32[]{:S(2)}) collective-permute-start(bf16[176,512]{1,0:T(8,128)(2,1)S(1)} %pad_maximum_fusion.1), channel_id=1, source_target_pairs={{0,16},{16,32},{32,48},{48,0},{1,17},{17,33},{33,49},{49,1},{2,18}... | collective-permute-start | bytes 540680 | tf_op jit(solution)/shard_map/ppermute | solution.py:34
  16.6 3.7 %collective-permute-start = (bf16[176,512]{1,0:T(8,128)(2,1)S(1)}, bf16[176,512]{1,0:T(8,128)(2,1)S(1)}, u32[]{:S(2)}, u32[]{:S(2)}) collective-permute-start(bf16[176,512]{1,0:T(8,128)(2,1)S(1)} %pad_maximum_fusion.1), channel_id=1, source_target_pairs={{0,48},{16,0},{32,16},{48,32},{1,49},{17,1},{33,17},{49,33},{2,50}... | collective-permute-start | bytes 540680 | tf_op jit(solution)/shard_map/ppermute | solution.py:37
  20.3 2.3 %collective-permute-done.1 = bf16[176,512]{1,0:T(8,128)(2,1)S(1)} collective-permute-done((bf16[176,512]{1,0:T(8,128)(2,1)S(1)}, bf16[176,512]{1,0:T(8,128)(2,1)S(1)}, u32[]{:S(2)}, u32[]{:S(2)}) %collective-permute-start.1) | collective-permute-done | bytes 180256 | tf_op jit(solution)/shard_map/ppermute | solution.py:34
  22.6 2.2 %collective-permute-start.2 = (bf16[176,512]{1,0:T(8,128)(2,1)S(1)}, bf16[176,512]{1,0:T(8,128)(2,1)S(1)}, u32[]{:S(2)}, u32[]{:S(2)}) collective-permute-start(bf16[176,512]{1,0:T(8,128)(2,1)S(1)} %collective-permute-done.1), channel_id=1, source_target_pairs={{0,16},{16,32},{32,48},{48,0},{1,17},{17,33},{33,49},{49,1},{2,18}... | collective-permute-start | bytes 540680 | tf_op jit(solution)/shard_map/ppermute | solution.py:34
  24.8 6.4 %collective-permute-done.2 = bf16[176,512]{1,0:T(8,128)(2,1)S(1)} collective-permute-done((bf16[176,512]{1,0:T(8,128)(2,1)S(1)}, bf16[176,512]{1,0:T(8,128)(2,1)S(1)}, u32[]{:S(2)}, u32[]{:S(2)}) %collective-permute-start.2) | collective-permute-done | bytes 180256 | tf_op jit(solution)/shard_map/ppermute | solution.py:34
  32.9 4.3 %collective-permute-start.6 = (bf16[704,512]{1,0:T(8,128)(2,1)S(1)}, bf16[704,512]{1,0:T(8,128)(2,1)S(1)}, u32[]{:S(2)}, u32[]{:S(2)}) collective-permute-start(bf16[704,512]{1,0:T(8,128)(2,1)S(1)} %get-tuple-element.6), channel_id=1, source_target_pairs={{0,64},{64,128},{128,192},{192,256},{256,320},{320,384},{384,448},... | collective-permute-start | bytes 2162696 | tf_op jit(solution)/shard_map/ppermute | solution.py:34
  39.1 11.8 %collective-permute-done.6 = bf16[704,512]{1,0:T(8,128)(2,1)S(1)} collective-permute-done((bf16[704,512]{1,0:T(8,128)(2,1)S(1)}, bf16[704,512]{1,0:T(8,128)(2,1)S(1)}, u32[]{:S(2)}, u32[]{:S(2)}) %collective-permute-start.6) | collective-permute-done | bytes 720928 | tf_op jit(solution)/shard_map/ppermute | solution.py:34
  50.9 4.4 %collective-permute-start.7 = (bf16[704,512]{1,0:T(8,128)(2,1)S(1)}, bf16[704,512]{1,0:T(8,128)(2,1)S(1)}, u32[]{:S(2)}, u32[]{:S(2)}) collective-permute-start(bf16[704,512]{1,0:T(8,128)(2,1)S(1)} %collective-permute-done.6), channel_id=1, source_target_pairs={{0,64},{64,128},{128,192},{192,256},{256,320},{320,384},{384,448},... | collective-permute-start | bytes 2162696 | tf_op jit(solution)/shard_map/ppermute | solution.py:34
  55.7 6.2 %collective-permute-start.4 = (bf16[704,512]{1,0:T(8,128)(2,1)S(1)}, bf16[704,512]{1,0:T(8,128)(2,1)}, u32[]{:S(2)}, u32[]{:S(2)}) collective-permute-start(bf16[704,512]{1,0:T(8,128)(2,1)S(1)} %collective-permute-done.3), channel_id=1, source_target_pairs={{0,448},{64,0},{128,64},{192,128},{256,192},{320,256},{384,320},{4... | collective-permute-start | bytes 2162696 | tf_op jit(solution)/shard_map/ppermute | solution.py:37
  63.0 10.8 %collective-permute-done.7 = bf16[704,512]{1,0:T(8,128)(2,1)S(1)} collective-permute-done((bf16[704,512]{1,0:T(8,128)(2,1)S(1)}, bf16[704,512]{1,0:T(8,128)(2,1)S(1)}, u32[]{:S(2)}, u32[]{:S(2)}) %collective-permute-start.7) | collective-permute-done | bytes 720928 | tf_op jit(solution)/shard_map/ppermute | solution.py:34
  77.8 4.8 %collective-permute-start.5 = (bf16[704,512]{1,0:T(8,128)(2,1)}, bf16[704,512]{1,0:T(8,128)(2,1)S(1)}, u32[]{:S(2)}, u32[]{:S(2)}) collective-permute-start(bf16[704,512]{1,0:T(8,128)(2,1)} %collective-permute-done.4), channel_id=1, source_target_pairs={{0,448},{64,0},{128,64},{192,128},{256,192},{320,256},{384,320},{4... | collective-permute-start | bytes 2162696 | tf_op jit(solution)/shard_map/ppermute | solution.py:37
  82.7 9.2 %collective-permute-done.8 = bf16[704,512]{1,0:T(8,128)(2,1)} collective-permute-done((bf16[704,512]{1,0:T(8,128)(2,1)S(1)}, bf16[704,512]{1,0:T(8,128)(2,1)}, u32[]{:S(2)}, u32[]{:S(2)}) %collective-permute-start.8) | collective-permute-done | bytes 720928 | tf_op jit(solution)/shard_map/ppermute | solution.py:34
  91.8 2.1 %collective-permute-start.9 = (bf16[704,512]{1,0:T(8,128)(2,1)}, bf16[704,512]{1,0:T(8,128)(2,1)S(1)}, u32[]{:S(2)}, u32[]{:S(2)}) collective-permute-start(bf16[704,512]{1,0:T(8,128)(2,1)} %collective-permute-done.8), channel_id=1, source_target_pairs={{0,64},{64,128},{128,192},{192,256},{256,320},{320,384},{384,448},... | collective-permute-start | bytes 2162696 | tf_op jit(solution)/shard_map/ppermute | solution.py:34
  99.6 9.4 %collective-permute-done.9 = bf16[704,512]{1,0:T(8,128)(2,1)S(1)} collective-permute-done((bf16[704,512]{1,0:T(8,128)(2,1)}, bf16[704,512]{1,0:T(8,128)(2,1)S(1)}, u32[]{:S(2)}, u32[]{:S(2)}) %collective-permute-start.9) | collective-permute-done | bytes 720928 | tf_op jit(solution)/shard_map/ppermute | solution.py:34
  123.4 3.0 %constant_dynamic-slice_fusion = bf16[5632,512]{1,0:T(8,128)(2,1)S(1)} fusion(bf16[11264,512]{1,0:T(8,128)(2,1)} %constant_dynamic-update-slice_fusion.3, s32[]{:T(128)S(6)} %select_n.24), kind=kLoop, calls=%fused_computation.88 | loop fusion | bytes 11534340 | tf_op jit(solution)/shard_map/dynamic_slice | solution.py:45
  126.9 4.1 %fusion.4 = bf16[5376,512]{1,0:T(8,128)(2,1)} fusion(bf16[32,168,512]{2,1,0:T(8,128)(2,1)S(1)} %slice.79, bf16[512]{0:T(512)(128)(2,1)S(1)} %get-tuple-element.17, bf16[512]{0:T(512)(128)(2,1)S(1)} %get-tuple-element.16), kind=kLoop, calls=%fused_computation.7 | loop fusion | flops 16515072 | bytes 11012096 | tf_op jit(solution)/shard_map/convert_element_type | solution.py:51
  131.1 6.3 %copy.26 = bf16[16,336,520]{1,0,2:T(8,128)(2,1)} copy(bf16[16,336,520]{1,2,0:T(8,128)(2,1)} %all-gather.3.cloned.1.call-done) | data formatting | bytes 11182080 | tf_op jit(solution)/shard_map/all_gather | solution.py:104
  137.3 11.6 %reshape.233 = bf16[5376,520]{0,1:T(8,128)(2,1)} reshape(bf16[16,336,520]{1,0,2:T(8,128)(2,1)} %copy.26) | data formatting | bytes 11182080
  149.9 3.9 %fusion = f32[512]{0:T(512)S(1)} fusion(bf16[520,5376]{1,0:T(8,128)(2,1)} %bitcast.54), kind=kLoop, calls=%fused_computation.2 | loop fusion | flops 8257024 | bytes 5507072 | tf_op jit(solution)/shard_map/reduce_sum | solution.py:108
  153.9 5.9 %fusion.12 = f32[512,256]{0,1:T(8,128)S(1)} fusion(bf16[5376,512]{1,0:T(8,128)(2,1)} %fusion.4, f32[5376]{0:T(1024)S(1)} %fusion.33, f32[512]{0:T(512)S(1)} %add_rsqrt_fusion.2, bf16[520,5376]{1,0:T(8,128)(2,1)} %bitcast.55), kind=kOutput, calls=%fused_computation.19 | convolution fusion | flops 1420296192 | bytes 8805376 | tf_op jit(solution)/shard_map/dot_general | solution.py:112
  160.6 2.6 %collective-permute-start.10 = (bf16[512,2,128]{0,2,1:T(8,128)(2,1)S(1)}, bf16[512,2,128]{0,2,1:T(8,128)(2,1)S(1)}, u32[]{:S(2)}, u32[]{:S(2)}) collective-permute-start(bf16[512,2,128]{0,2,1:T(8,128)(2,1)S(1)} %pad_maximum_fusion), channel_id=1, source_target_pairs={{0,32},{16,48},{32,64},{48,80},{64,96},{80,112},{96,128},{112,144}... | collective-permute-start | bytes 786440 | tf_op jit(solution)/shard_map/ppermute | solution.py:23
  163.2 2.7 %collective-permute-start.11 = (bf16[512,2,128]{0,2,1:T(8,128)(2,1)S(1)}, bf16[512,2,128]{0,2,1:T(8,128)(2,1)}, u32[]{:S(2)}, u32[]{:S(2)}) collective-permute-start(bf16[512,2,128]{0,2,1:T(8,128)(2,1)S(1)} %pad_maximum_fusion), channel_id=1, source_target_pairs={{0,16},{16,32},{32,48},{48,64},{64,80},{80,96},{96,112},{112,128},... | collective-permute-start | bytes 786440 | tf_op jit(solution)/shard_map/ppermute | solution.py:23
  168.8 3.8 %collective-permute-done.10 = bf16[512,2,128]{0,2,1:T(8,128)(2,1)S(1)} collective-permute-done((bf16[512,2,128]{0,2,1:T(8,128)(2,1)S(1)}, bf16[512,2,128]{0,2,1:T(8,128)(2,1)S(1)}, u32[]{:S(2)}, u32[]{:S(2)}) %collective-permute-start.10) | collective-permute-done | bytes 262176 | tf_op jit(solution)/shard_map/ppermute | solution.py:23
  172.6 2.2 %collective-permute-done.11 = bf16[512,2,128]{0,2,1:T(8,128)(2,1)} collective-permute-done((bf16[512,2,128]{0,2,1:T(8,128)(2,1)S(1)}, bf16[512,2,128]{0,2,1:T(8,128)(2,1)}, u32[]{:S(2)}, u32[]{:S(2)}) %collective-permute-start.11) | collective-permute-done | bytes 262176 | tf_op jit(solution)/shard_map/ppermute | solution.py:23
  (87 shorter events, 45.8 us)
Async XLA Ops:
  6.5 124.6 %all-gather.3.cloned.1.call-start = ((), (), s32[]{:S(2)}) async-start(), calls=%async_computation | async-start | bytes 6789120 | tf_op jit(solution)/shard_map/all_gather | solution.py:104
  13.2 9.4 %collective-permute-start.1 = (bf16[176,512]{1,0:T(8,128)(2,1)S(1)}, bf16[176,512]{1,0:T(8,128)(2,1)S(1)}, u32[]{:S(2)}, u32[]{:S(2)}) collective-permute-start(bf16[176,512]{1,0:T(8,128)(2,1)S(1)} %pad_maximum_fusion.1), channel_id=1, source_target_pairs={{0,16},{16,32},{32,48},{48,0},{1,17},{17,33},{33,49},{49,1},{2,18}... | collective-permute-start | bytes 540680 | tf_op jit(solution)/shard_map/ppermute | solution.py:34
  16.6 8.2 %collective-permute-start = (bf16[176,512]{1,0:T(8,128)(2,1)S(1)}, bf16[176,512]{1,0:T(8,128)(2,1)S(1)}, u32[]{:S(2)}, u32[]{:S(2)}) collective-permute-start(bf16[176,512]{1,0:T(8,128)(2,1)S(1)} %pad_maximum_fusion.1), channel_id=1, source_target_pairs={{0,48},{16,0},{32,16},{48,32},{1,49},{17,1},{33,17},{49,33},{2,50}... | collective-permute-start | bytes 540680 | tf_op jit(solution)/shard_map/ppermute | solution.py:37
  22.6 8.6 %collective-permute-start.2 = (bf16[176,512]{1,0:T(8,128)(2,1)S(1)}, bf16[176,512]{1,0:T(8,128)(2,1)S(1)}, u32[]{:S(2)}, u32[]{:S(2)}) collective-permute-start(bf16[176,512]{1,0:T(8,128)(2,1)S(1)} %collective-permute-done.1), channel_id=1, source_target_pairs={{0,16},{16,32},{32,48},{48,0},{1,17},{17,33},{33,49},{49,1},{2,18}... | collective-permute-start | bytes 540680 | tf_op jit(solution)/shard_map/ppermute | solution.py:34
  32.9 18.0 %collective-permute-start.6 = (bf16[704,512]{1,0:T(8,128)(2,1)S(1)}, bf16[704,512]{1,0:T(8,128)(2,1)S(1)}, u32[]{:S(2)}, u32[]{:S(2)}) collective-permute-start(bf16[704,512]{1,0:T(8,128)(2,1)S(1)} %get-tuple-element.6), channel_id=1, source_target_pairs={{0,64},{64,128},{128,192},{192,256},{256,320},{320,384},{384,448},... | collective-permute-start | bytes 2162696 | tf_op jit(solution)/shard_map/ppermute | solution.py:34
  37.2 18.5 %collective-permute-start.3 = (bf16[704,512]{1,0:T(8,128)(2,1)S(1)}, bf16[704,512]{1,0:T(8,128)(2,1)S(1)}, u32[]{:S(2)}, u32[]{:S(2)}) collective-permute-start(bf16[704,512]{1,0:T(8,128)(2,1)S(1)} %get-tuple-element.6), channel_id=1, source_target_pairs={{0,448},{64,0},{128,64},{192,128},{256,192},{320,256},{384,320},{4... | collective-permute-start | bytes 2162696 | tf_op jit(solution)/shard_map/ppermute | solution.py:37
  50.9 22.9 %collective-permute-start.7 = (bf16[704,512]{1,0:T(8,128)(2,1)S(1)}, bf16[704,512]{1,0:T(8,128)(2,1)S(1)}, u32[]{:S(2)}, u32[]{:S(2)}) collective-permute-start(bf16[704,512]{1,0:T(8,128)(2,1)S(1)} %collective-permute-done.6), channel_id=1, source_target_pairs={{0,64},{64,128},{128,192},{192,256},{256,320},{320,384},{384,448},... | collective-permute-start | bytes 2162696 | tf_op jit(solution)/shard_map/ppermute | solution.py:34
  55.7 22.1 %collective-permute-start.4 = (bf16[704,512]{1,0:T(8,128)(2,1)S(1)}, bf16[704,512]{1,0:T(8,128)(2,1)}, u32[]{:S(2)}, u32[]{:S(2)}) collective-permute-start(bf16[704,512]{1,0:T(8,128)(2,1)S(1)} %collective-permute-done.3), channel_id=1, source_target_pairs={{0,448},{64,0},{128,64},{192,128},{256,192},{320,256},{384,320},{4... | collective-permute-start | bytes 2162696 | tf_op jit(solution)/shard_map/ppermute | solution.py:37
  73.9 18.0 %collective-permute-start.8 = (bf16[704,512]{1,0:T(8,128)(2,1)S(1)}, bf16[704,512]{1,0:T(8,128)(2,1)}, u32[]{:S(2)}, u32[]{:S(2)}) collective-permute-start(bf16[704,512]{1,0:T(8,128)(2,1)S(1)} %collective-permute-done.7), channel_id=1, source_target_pairs={{0,64},{64,128},{128,192},{192,256},{256,320},{320,384},{384,448},... | collective-permute-start | bytes 2162696 | tf_op jit(solution)/shard_map/ppermute | solution.py:34
  77.8 20.9 %collective-permute-start.5 = (bf16[704,512]{1,0:T(8,128)(2,1)}, bf16[704,512]{1,0:T(8,128)(2,1)S(1)}, u32[]{:S(2)}, u32[]{:S(2)}) collective-permute-start(bf16[704,512]{1,0:T(8,128)(2,1)} %collective-permute-done.4), channel_id=1, source_target_pairs={{0,448},{64,0},{128,64},{192,128},{256,192},{320,256},{384,320},{4... | collective-permute-start | bytes 2162696 | tf_op jit(solution)/shard_map/ppermute | solution.py:37
  91.8 17.2 %collective-permute-start.9 = (bf16[704,512]{1,0:T(8,128)(2,1)}, bf16[704,512]{1,0:T(8,128)(2,1)S(1)}, u32[]{:S(2)}, u32[]{:S(2)}) collective-permute-start(bf16[704,512]{1,0:T(8,128)(2,1)} %collective-permute-done.8), channel_id=1, source_target_pairs={{0,64},{64,128},{128,192},{192,256},{256,320},{320,384},{384,448},... | collective-permute-start | bytes 2162696 | tf_op jit(solution)/shard_map/ppermute | solution.py:34
  149.9 16.1 %slice-start = ((s8[5591040]{0:T(1024)(128)(4,1)}), s8[4194304]{0:T(1024)(128)(4,1)S(1)}, s32[]{:S(2)}) async-start(s8[5591040]{0:T(1024)(128)(4,1)} %bitcast.56), calls=%async_computation.1 | async-start | bytes 8388608
  149.9 16.1 %slice-start.2 = ((s8[5505024]{0:T(1024)(128)(4,1)}), s8[4194304]{0:T(1024)(128)(4,1)S(1)}, s32[]{:S(2)}) async-start(s8[5505024]{0:T(1024)(128)(4,1)} %bitcast.59), calls=%async_computation.3 | async-start | bytes 8388608
  153.8 6.0 %copy-start.2 = (f32[128]{0:T(128)S(1)}, f32[128]{0:T(128)}, u32[]{:S(2)}) copy-start(f32[128]{0:T(128)} %param.10) | copy-start | bytes 1540
  153.9 12.1 %slice-start.1 = ((s8[5591040]{0:T(1024)(128)(4,1)}), s8[1396736]{0:T(1024)(128)(4,1)S(1)}, s32[]{:S(2)}) async-start(s8[5591040]{0:T(1024)(128)(4,1)} %bitcast.56), calls=%async_computation.2 | async-start | bytes 2793472
  153.9 12.1 %slice-start.3 = ((s8[5505024]{0:T(1024)(128)(4,1)}), s8[1310720]{0:T(1024)(128)(4,1)S(1)}, s32[]{:S(2)}) async-start(s8[5505024]{0:T(1024)(128)(4,1)} %bitcast.59), calls=%async_computation.4 | async-start | bytes 2621440
  160.6 7.7 %copy-start.3 = (f32[128]{0:T(128)S(1)}, f32[128]{0:T(128)}, u32[]{:S(2)}) copy-start(f32[128]{0:T(128)} %param.9) | copy-start | bytes 1540
  160.6 7.9 %copy-start = (f32[512,64]{1,0:T(8,128)S(1)}, f32[512,64]{1,0:T(8,128)}, u32[]{:S(2)}) copy-start(f32[512,64]{1,0:T(8,128)} %get-tuple-element.12) | copy-start | bytes 393220
  160.6 15.2 %copy-start.1 = (pred[512,1536]{0,1:T(8,128)(4,1)S(1)}, pred[512,1536]{0,1:T(8,128)(4,1)}, u32[]{:S(2)}) copy-start(pred[512,1536]{0,1:T(8,128)(4,1)} %fusion.9) | copy-start | bytes 2359300
  160.6 12.0 %collective-permute-start.10 = (bf16[512,2,128]{0,2,1:T(8,128)(2,1)S(1)}, bf16[512,2,128]{0,2,1:T(8,128)(2,1)S(1)}, u32[]{:S(2)}, u32[]{:S(2)}) collective-permute-start(bf16[512,2,128]{0,2,1:T(8,128)(2,1)S(1)} %pad_maximum_fusion), channel_id=1, source_target_pairs={{0,32},{16,48},{32,64},{48,80},{64,96},{80,112},{96,128},{112,144}... | collective-permute-start | bytes 786440 | tf_op jit(solution)/shard_map/ppermute | solution.py:23
  163.2 11.5 %collective-permute-start.11 = (bf16[512,2,128]{0,2,1:T(8,128)(2,1)S(1)}, bf16[512,2,128]{0,2,1:T(8,128)(2,1)}, u32[]{:S(2)}, u32[]{:S(2)}) collective-permute-start(bf16[512,2,128]{0,2,1:T(8,128)(2,1)S(1)} %pad_maximum_fusion), channel_id=1, source_target_pairs={{0,16},{16,32},{32,48},{48,64},{64,80},{80,96},{96,112},{112,128},... | collective-permute-start | bytes 786440 | tf_op jit(solution)/shard_map/ppermute | solution.py:23
Sparse Core Ops, SparseCore 0:
  10.7 50.1 all-gather.2

commit v7 on v5

--- a/solution.py
+++ b/solution.py
@@ -90,7 +90,7 @@
     )
     slabs = lax.all_gather(padded, ROW, axis=0, tiled=True).reshape(-1, aligned, weight_cols)
     largest = jnp.max(slabs[:, weight_rows].astype(jnp.float32), axis=0)
-    clipped = clip_with(slabs[:, :weight_rows].reshape(-1, weight_cols), largest)
+    clipped = clip_with(slabs.reshape(-1, weight_cols), largest)
     rows_tokens, piece = tokens.shape
     cores = lax.axis_size("cc")
     high = gain.astype(jnp.bfloat16)
@@ -107,12 +107,15 @@
     widened = along_all[:rows_tokens].astype(jnp.float32)
     squares = jnp.sum(widened * widened, axis=1)
     inverse = lax.rsqrt(squares / D + EPS)[:, None]
-    whole = (widened * inverse * full_gain[None, :]).astype(jnp.bfloat16)
-    ordered = (
-        clipped.reshape(blocks, cores, piece, clipped.shape[1])
-        .transpose(1, 0, 2, 3)
-        .reshape(clipped.shape)
-    )
+    normed = (widened * inverse * full_gain[None, :]).astype(jnp.bfloat16)
+    halves = piece // weight_rows
+    whole = jnp.pad(
+        normed.reshape(rows_tokens, cores, blocks, halves, weight_rows)
+        .transpose(0, 2, 1, 3, 4)
+        .reshape(rows_tokens, -1, weight_rows),
+        ((0, 0), (0, 0), (0, aligned - weight_rows)),
+    ).reshape(rows_tokens, -1)
+    ordered = clipped
     kv_part = jnp.dot(whole, ordered[:, query_cols:], preferred_element_type=jnp.float32)
     keys = kv_part[:, :key_cols]
     values = kv_part[:, key_cols:]

time: 145 us -> 150 us (1.034)
  the two profiles are of different devices: /device:TPU:64 before, /device:TPU:1 now
where the time goes in v7:
time: 150 us; the launch traced here: 148 us
  starting transfers between devices  41.1 us (27%)
  other arithmetic  35.6 us (24%)
  local copies, waits for them, and re-layouts  23 us (15%)
  waiting for transfers between devices  22.6 us (15%)
  between operations  14.6 us (10%)
  matrix products  10.7 us (7%)
    ppermute x5, starting transfers between devices, ring_gather(): forward = lax.ppermute(forward, axis, right)  22.6 us
    concatenate x1, other arithmetic, ring_gather(): doubled = jnp.concatenate([stacked, stacked], axis=dim)  17.2 us
    ppermute x3, starting transfers between devices, ring_gather(): backward = lax.ppermute(backward, axis, left)  11.9 us
    ppermute x5, waiting for transfers between devices, ring_gather(): forward = lax.ppermute(forward, axis, right)  11.8 us
    ppermute x2, starting transfers between devices, shifted(): return lax.ppermute(array, axis, pairs)  6.58 us
    ppermute x3, waiting for transfers between devices, ring_gather(): backward = lax.ppermute(backward, axis, left)  6.1 us
    ppermute x1, local copies, waits for them, and re-layouts, ring_gather(): forward = lax.ppermute(forward, axis, right)  5.36 us
    dot_general x1, matrix products, local(): jnp.dot(whole, ordered[:, :query_cols], preferred_element_type=jnp.float32)  5.25 us
  transfers between devices with their start and end apart: 11, of which 9 were waited for; matrix products, arithmetic and copies ran while one was open for 36% of the time, Pallas kernels for 0%

profile of v7, /device:TPU:1, one launch (start us, length us, event | category | flops | bytes accessed | tf_op | source)
XLA Modules:
  0.0 147.7 jit_solution(11572511333780024463)
XLA Ops:
  8.9 4.0 %collective-permute-start.3 = (bf16[520,336]{0,1:T(8,128)(2,1)S(1)}, bf16[520,336]{0,1:T(8,128)(2,1)S(1)}, u32[]{:S(2)}, u32[]{:S(2)}) collective-permute-start(bf16[520,336]{0,1:T(8,128)(2,1)S(1)} %concatenate.43), channel_id=1, source_target_pairs={{0,2},{2,4},{4,6},{6,8},{8,10},{10,12},{12,14},{14,0},{1,3},{3,5},... | collective-permute-start | bytes 1048328 | tf_op jit(solution)/shard_map/ppermute | solution.py:34
  16.4 3.8 %collective-permute-start = (bf16[520,336]{0,1:T(8,128)(2,1)S(1)}, bf16[520,336]{0,1:T(8,128)(2,1)S(1)}, u32[]{:S(2)}, u32[]{:S(2)}) collective-permute-start(bf16[520,336]{0,1:T(8,128)(2,1)S(1)} %concatenate.43), channel_id=1, source_target_pairs={{0,14},{2,0},{4,2},{6,4},{8,6},{10,8},{12,10},{14,12},{1,15},{3,1}... | collective-permute-start | bytes 1048328 | tf_op jit(solution)/shard_map/ppermute | solution.py:37
  20.4 4.3 %collective-permute-start.4 = (bf16[520,336]{0,1:T(8,128)(2,1)S(1)}, bf16[520,336]{0,1:T(8,128)(2,1)S(1)}, u32[]{:S(2)}, u32[]{:S(2)}) collective-permute-start(bf16[520,336]{0,1:T(8,128)(2,1)S(1)} %collective-permute-done.3), channel_id=1, source_target_pairs={{0,2},{2,4},{4,6},{6,8},{8,10},{10,12},{12,14},{14,0},{1,3},{3,5},... | collective-permute-start | bytes 1048328 | tf_op jit(solution)/shard_map/ppermute | solution.py:34
  25.6 4.7 %collective-permute-start.1 = (bf16[520,336]{0,1:T(8,128)(2,1)S(1)}, bf16[520,336]{0,1:T(8,128)(2,1)S(1)}, u32[]{:S(2)}, u32[]{:S(2)}) collective-permute-start(bf16[520,336]{0,1:T(8,128)(2,1)S(1)} %collective-permute-done), channel_id=1, source_target_pairs={{0,14},{2,0},{4,2},{6,4},{8,6},{10,8},{12,10},{14,12},{1,15},{3,1}... | collective-permute-start | bytes 1048328 | tf_op jit(solution)/shard_map/ppermute | solution.py:37
  30.3 2.7 %collective-permute-done.4 = bf16[520,336]{0,1:T(8,128)(2,1)S(1)} collective-permute-done((bf16[520,336]{0,1:T(8,128)(2,1)S(1)}, bf16[520,336]{0,1:T(8,128)(2,1)S(1)}, u32[]{:S(2)}, u32[]{:S(2)}) %collective-permute-start.4) | collective-permute-done | bytes 349472 | tf_op jit(solution)/shard_map/ppermute | solution.py:34
  33.0 3.4 %collective-permute-start.5 = (bf16[520,336]{0,1:T(8,128)(2,1)S(1)}, bf16[520,336]{0,1:T(8,128)(2,1)S(1)}, u32[]{:S(2)}, u32[]{:S(2)}) collective-permute-start(bf16[520,336]{0,1:T(8,128)(2,1)S(1)} %collective-permute-done.4), channel_id=1, source_target_pairs={{0,2},{2,4},{4,6},{6,8},{8,10},{10,12},{12,14},{14,0},{1,3},{3,5},... | collective-permute-start | bytes 1048328 | tf_op jit(solution)/shard_map/ppermute | solution.py:34
  37.7 3.4 %collective-permute-start.2 = (bf16[520,336]{0,1:T(8,128)(2,1)S(1)}, bf16[520,336]{0,1:T(8,128)(2,1)S(1)}, u32[]{:S(2)}, u32[]{:S(2)}) collective-permute-start(bf16[520,336]{0,1:T(8,128)(2,1)S(1)} %collective-permute-done.1), channel_id=1, source_target_pairs={{0,14},{2,0},{4,2},{6,4},{8,6},{10,8},{12,10},{14,12},{1,15},{3,1}... | collective-permute-start | bytes 1048328 | tf_op jit(solution)/shard_map/ppermute | solution.py:37
  41.2 4.2 %collective-permute-done.5 = bf16[520,336]{0,1:T(8,128)(2,1)S(1)} collective-permute-done((bf16[520,336]{0,1:T(8,128)(2,1)S(1)}, bf16[520,336]{0,1:T(8,128)(2,1)S(1)}, u32[]{:S(2)}, u32[]{:S(2)}) %collective-permute-start.5) | collective-permute-done | bytes 349472 | tf_op jit(solution)/shard_map/ppermute | solution.py:34
  47.5 3.9 %collective-permute-done.2 = bf16[520,336]{0,1:T(8,128)(2,1)S(1)} collective-permute-done((bf16[520,336]{0,1:T(8,128)(2,1)S(1)}, bf16[520,336]{0,1:T(8,128)(2,1)S(1)}, u32[]{:S(2)}, u32[]{:S(2)}) %collective-permute-start.2) | collective-permute-done | bytes 349472 | tf_op jit(solution)/shard_map/ppermute | solution.py:37
  51.4 4.2 %collective-permute-done.6 = bf16[520,336]{0,1:T(8,128)(2,1)S(1)} collective-permute-done((bf16[520,336]{0,1:T(8,128)(2,1)S(1)}, bf16[520,336]{0,1:T(8,128)(2,1)S(1)}, u32[]{:S(2)}, u32[]{:S(2)}) %collective-permute-start.6) | collective-permute-done | bytes 349472 | tf_op jit(solution)/shard_map/ppermute | solution.py:34
  56.7 4.0 %copy.36 = bf16[520,2688]{1,0:T(8,128)(2,1)} copy(bf16[520,2688]{0,1:T(8,128)(2,1)S(1)} %constant_dynamic-slice_fusion) | data formatting | bytes 5591040 | tf_op jit(solution)/shard_map/dynamic_slice | solution.py:45
  60.8 9.0 %collective-permute-start.7 = (bf16[520,2688]{1,0:T(8,128)(2,1)}, bf16[520,2688]{1,0:T(8,128)(2,1)}, u32[]{:S(2)}, u32[]{:S(2)}) collective-permute-start(bf16[520,2688]{1,0:T(8,128)(2,1)} %copy.36), channel_id=1, source_target_pairs={{0,1},{1,0},{2,3},{3,2},{4,5},{5,4},{6,7},{7,6},{8,9},{9,8},{10,11... | collective-permute-start | bytes 8386568 | tf_op jit(solution)/shard_map/ppermute | solution.py:34
  74.7 5.4 %copy.37 = bf16[520,2688]{0,1:T(8,128)(2,1)} copy(bf16[520,2688]{1,0:T(8,128)(2,1)} %collective-permute-done.7) | data formatting | bytes 5591040 | tf_op jit(solution)/shard_map/ppermute | solution.py:34
  80.0 17.2 %fusion.5 = bf16[520,5376]{0,1:T(8,128)(2,1)S(1)} fusion(s32[]{:T(128)S(6)} %select_n.24, bf16[520,2688]{0,1:T(8,128)(2,1)S(1)} %constant_dynamic-slice_fusion, bf16[520,2688]{0,1:T(8,128)(2,1)} %copy.37), kind=kLoop, calls=%fused_computation.12 | loop fusion | flops 22364160 | bytes 11182084 | tf_op jit(solution)/shard_map/concatenate | solution.py:43
  98.7 2.3 %fusion.14 = f32[5376]{0:T(1024)S(1)} fusion(f32[3,5376]{0,1:T(8,128)S(1)} %slice_convert_fusion), kind=kLoop, calls=%fused_computation.27 | loop fusion | flops 10752 | bytes 86016 | tf_op jit(solution)/shard_map/add | solution.py:106
  100.9 2.6 %fusion.2 = bf16[512,5376]{0,1:T(8,128)(2,1)S(1)} fusion(f32[5376]{0:T(1024)S(1)} %fusion.14, f32[512]{0:T(512)S(1)} %add_rsqrt_fusion.2, bf16[520,5376]{0,1:T(8,128)(2,1)S(1)} %fusion.5), kind=kLoop, calls=%fused_computation.9 | loop fusion | flops 11010048 | bytes 11033600 | tf_op jit(solution)/shard_map/convert_element_type | solution.py:110
  104.1 3.2 %pad.4 = bf16[512,32,176]{0,2,1:T(8,128)(2,1)} pad(bf16[512,32,168]{0,2,1:T(8,128)(2,1)S(1)} %bitcast.53, bf16[]{:T(256)} %constant.30.clone.1), padding=0_0x0_0x0_8 | pad | bytes 11272194 | tf_op jit(solution)/shard_map/jit(_pad)/pad | solution.py:112
  107.3 4.7 %all-gather.2.cloned.1.call-done = bf16[5632,512]{1,0:T(8,128)(2,1)} async-done(((bf16[176,512]{1,0:T(8,128)(2,1)}), bf16[5632,512]{1,0:T(8,128)(2,1)}) %all-gather.2.cloned.1.call-update) | async-done | bytes 5767184 | tf_op jit(solution)/shard_map/all_gather | solution.py:91
  113.0 4.2 %minimum_convert_fusion = bf16[5632,512]{1,0:T(8,128)(2,1)S(1)} fusion(bf16[5632,512]{1,0:T(8,128)(2,1)} %all-gather.2.cloned.1.call-done, bf16[512]{0:T(512)(128)(2,1)S(1)} %get-tuple-element.15, bf16[512]{0:T(512)(128)(2,1)S(1)} %get-tuple-element.14), kind=kLoop, calls=%fused_computation.6 | loop fusion | flops 17301504 | bytes 11536384 | tf_op jit(solution)/shard_map/convert_element_type | solution.py:51
  119.8 3.9 %collective-permute-start.8 = (bf16[512,2,128]{0,2,1:T(8,128)(2,1)S(1)}, bf16[512,2,128]{0,2,1:T(8,128)(2,1)}, u32[]{:S(2)}, u32[]{:S(2)}) collective-permute-start(bf16[512,2,128]{0,2,1:T(8,128)(2,1)S(1)} %pad_maximum_fusion), channel_id=1, source_target_pairs={{0,32},{16,48},{32,64},{48,80},{64,96},{80,112},{96,128},{112,144}... | collective-permute-start | bytes 786440 | tf_op jit(solution)/shard_map/ppermute | solution.py:23
  123.7 2.7 %collective-permute-start.9 = (bf16[512,2,128]{0,2,1:T(8,128)(2,1)S(1)}, bf16[512,2,128]{0,2,1:T(8,128)(2,1)}, u32[]{:S(2)}, u32[]{:S(2)}) collective-permute-start(bf16[512,2,128]{0,2,1:T(8,128)(2,1)S(1)} %pad_maximum_fusion), channel_id=1, source_target_pairs={{0,16},{16,32},{32,48},{48,64},{64,80},{80,96},{96,112},{112,128},... | collective-permute-start | bytes 786440 | tf_op jit(solution)/shard_map/ppermute | solution.py:23
  126.6 3.0 %copy.40 = bf16[256,5632]{1,0:T(8,128)(2,1)} copy(bf16[256,5632]{0,1:T(8,128)(2,1)S(1)} %slice_bitcast_fusion) | data formatting | bytes 5767168 | tf_op jit(solution)/shard_map/dot_general | solution.py:122
  129.6 5.3 %multiply_reduce_fusion = (f32[512,2]{0,1:T(2,128)S(1)}, f32[512,2,128]{0,2,1:T(8,128)S(1)}) fusion(bf16[512,5632,1]{0,1,2:T(8,128)(2,1)} %bitcast.56, bf16[2,128,5632]{2,1,0:T(8,128)(2,1)} %bitcast.60), kind=kOutput, calls=%fused_computation.32 | convolution fusion | flops 1476656128 | bytes 9179136 | tf_op jit(solution)/shard_map/dot_general | solution.py:122
  138.0 2.0 %fusion.15 = bf16[128,2,512]{2,0,1:T(8,128)(2,1)S(1)} fusion(f32[2,512]{1,0:T(2,128)S(1)} %get-tuple-element.18, f32[1536,512,2]{1,0,2:T(8,128)S(1)} %get-tuple-element.19, pred[512,1536]{0,1:T(8,128)(4,1)S(1)} %copy-done, bf16[1536,2,128]{0,2,1:T(8,128)(2,1)S(1)} %maximum_maximum_fusion), kind=kOutput, calls=%fused_computation.29 | convolution fusion | flops 409075712 | bytes 7737344 | tf_op jit(solution)/shard_map/kgts,skd->tkgd/dot_general | solution.py:152
  (83 shorter events, 24.9 us)
Async XLA Ops:
  6.5 105.4 %all-gather.2.cloned.1.call-start = ((), (), s32[]{:S(2)}) async-start(), calls=%async_computation | async-start | bytes 5947392 | tf_op jit(solution)/shard_map/all_gather | solution.py:91
  8.9 11.5 %collective-permute-start.3 = (bf16[520,336]{0,1:T(8,128)(2,1)S(1)}, bf16[520,336]{0,1:T(8,128)(2,1)S(1)}, u32[]{:S(2)}, u32[]{:S(2)}) collective-permute-start(bf16[520,336]{0,1:T(8,128)(2,1)S(1)} %concatenate.43), channel_id=1, source_target_pairs={{0,2},{2,4},{4,6},{6,8},{8,10},{10,12},{12,14},{14,0},{1,3},{3,5},... | collective-permute-start | bytes 1048328 | tf_op jit(solution)/shard_map/ppermute | solution.py:34
  16.4 9.2 %collective-permute-start = (bf16[520,336]{0,1:T(8,128)(2,1)S(1)}, bf16[520,336]{0,1:T(8,128)(2,1)S(1)}, u32[]{:S(2)}, u32[]{:S(2)}) collective-permute-start(bf16[520,336]{0,1:T(8,128)(2,1)S(1)} %concatenate.43), channel_id=1, source_target_pairs={{0,14},{2,0},{4,2},{6,4},{8,6},{10,8},{12,10},{14,12},{1,15},{3,1}... | collective-permute-start | bytes 1048328 | tf_op jit(solution)/shard_map/ppermute | solution.py:37
  20.4 12.7 %collective-permute-start.4 = (bf16[520,336]{0,1:T(8,128)(2,1)S(1)}, bf16[520,336]{0,1:T(8,128)(2,1)S(1)}, u32[]{:S(2)}, u32[]{:S(2)}) collective-permute-start(bf16[520,336]{0,1:T(8,128)(2,1)S(1)} %collective-permute-done.3), channel_id=1, source_target_pairs={{0,2},{2,4},{4,6},{6,8},{8,10},{10,12},{12,14},{14,0},{1,3},{3,5},... | collective-permute-start | bytes 1048328 | tf_op jit(solution)/shard_map/ppermute | solution.py:34
  25.6 12.2 %collective-permute-start.1 = (bf16[520,336]{0,1:T(8,128)(2,1)S(1)}, bf16[520,336]{0,1:T(8,128)(2,1)S(1)}, u32[]{:S(2)}, u32[]{:S(2)}) collective-permute-start(bf16[520,336]{0,1:T(8,128)(2,1)S(1)} %collective-permute-done), channel_id=1, source_target_pairs={{0,14},{2,0},{4,2},{6,4},{8,6},{10,8},{12,10},{14,12},{1,15},{3,1}... | collective-permute-start | bytes 1048328 | tf_op jit(solution)/shard_map/ppermute | solution.py:37
  33.0 12.4 %collective-permute-start.5 = (bf16[520,336]{0,1:T(8,128)(2,1)S(1)}, bf16[520,336]{0,1:T(8,128)(2,1)S(1)}, u32[]{:S(2)}, u32[]{:S(2)}) collective-permute-start(bf16[520,336]{0,1:T(8,128)(2,1)S(1)} %collective-permute-done.4), channel_id=1, source_target_pairs={{0,2},{2,4},{4,6},{6,8},{8,10},{10,12},{12,14},{14,0},{1,3},{3,5},... | collective-permute-start | bytes 1048328 | tf_op jit(solution)/shard_map/ppermute | solution.py:34
  37.7 13.6 %collective-permute-start.2 = (bf16[520,336]{0,1:T(8,128)(2,1)S(1)}, bf16[520,336]{0,1:T(8,128)(2,1)S(1)}, u32[]{:S(2)}, u32[]{:S(2)}) collective-permute-start(bf16[520,336]{0,1:T(8,128)(2,1)S(1)} %collective-permute-done.1), channel_id=1, source_target_pairs={{0,14},{2,0},{4,2},{6,4},{8,6},{10,8},{12,10},{14,12},{1,15},{3,1}... | collective-permute-start | bytes 1048328 | tf_op jit(solution)/shard_map/ppermute | solution.py:37
  45.4 10.2 %collective-permute-start.6 = (bf16[520,336]{0,1:T(8,128)(2,1)S(1)}, bf16[520,336]{0,1:T(8,128)(2,1)S(1)}, u32[]{:S(2)}, u32[]{:S(2)}) collective-permute-start(bf16[520,336]{0,1:T(8,128)(2,1)S(1)} %collective-permute-done.5), channel_id=1, source_target_pairs={{0,2},{2,4},{4,6},{6,8},{8,10},{10,12},{12,14},{14,0},{1,3},{3,5},... | collective-permute-start | bytes 1048328 | tf_op jit(solution)/shard_map/ppermute | solution.py:34
  60.8 13.9 %collective-permute-start.7 = (bf16[520,2688]{1,0:T(8,128)(2,1)}, bf16[520,2688]{1,0:T(8,128)(2,1)}, u32[]{:S(2)}, u32[]{:S(2)}) collective-permute-start(bf16[520,2688]{1,0:T(8,128)(2,1)} %copy.36), channel_id=1, source_target_pairs={{0,1},{1,0},{2,3},{3,2},{4,5},{5,4},{6,7},{7,6},{8,9},{9,8},{10,11... | collective-permute-start | bytes 8386568 | tf_op jit(solution)/shard_map/ppermute | solution.py:34
  107.3 10.0 %slice-start = ((s8[5767168]{0:T(1024)(128)(4,1)}), s8[1572864]{0:T(1024)(128)(4,1)S(1)}, s32[]{:S(2)}) async-start(s8[5767168]{0:T(1024)(128)(4,1)} %bitcast.57), calls=%async_computation.1 | async-start | bytes 3145728
  113.0 4.3 %slice-start.1 = ((s8[5767168]{0:T(1024)(128)(4,1)}), s8[4194304]{0:T(1024)(128)(4,1)S(1)}, s32[]{:S(2)}) async-start(s8[5767168]{0:T(1024)(128)(4,1)} %bitcast.57), calls=%async_computation.2 | async-start | bytes 8388608
  117.2 1.9 %copy-start.3 = (f32[128]{0:T(128)S(1)}, f32[128]{0:T(128)}, u32[]{:S(2)}) copy-start(f32[128]{0:T(128)} %param.10) | copy-start | bytes 1540
  119.8 15.3 %collective-permute-start.8 = (bf16[512,2,128]{0,2,1:T(8,128)(2,1)S(1)}, bf16[512,2,128]{0,2,1:T(8,128)(2,1)}, u32[]{:S(2)}, u32[]{:S(2)}) collective-permute-start(bf16[512,2,128]{0,2,1:T(8,128)(2,1)S(1)} %pad_maximum_fusion), channel_id=1, source_target_pairs={{0,32},{16,48},{32,64},{48,80},{64,96},{80,112},{96,128},{112,144}... | collective-permute-start | bytes 786440 | tf_op jit(solution)/shard_map/ppermute | solution.py:23
  123.7 11.5 %collective-permute-start.9 = (bf16[512,2,128]{0,2,1:T(8,128)(2,1)S(1)}, bf16[512,2,128]{0,2,1:T(8,128)(2,1)}, u32[]{:S(2)}, u32[]{:S(2)}) collective-permute-start(bf16[512,2,128]{0,2,1:T(8,128)(2,1)S(1)} %pad_maximum_fusion), channel_id=1, source_target_pairs={{0,16},{16,32},{32,48},{48,64},{64,80},{80,96},{96,112},{112,128},... | collective-permute-start | bytes 786440 | tf_op jit(solution)/shard_map/ppermute | solution.py:23
  129.6 5.3 %copy-start.4 = (f32[128]{0:T(128)S(1)}, f32[128]{0:T(128)}, u32[]{:S(2)}) copy-start(f32[128]{0:T(128)} %param.9) | copy-start | bytes 1540
  129.6 5.4 %copy-start.1 = (f32[512,64]{0,1:T(8,128)S(1)}, f32[512,64]{0,1:T(8,128)}, u32[]{:S(2)}) copy-start(f32[512,64]{0,1:T(8,128)} %get-tuple-element.9) | copy-start | bytes 393220
  129.6 5.4 %copy-start.2 = (f32[512,64]{0,1:T(8,128)S(1)}, f32[512,64]{0,1:T(8,128)}, u32[]{:S(2)}) copy-start(f32[512,64]{0,1:T(8,128)} %get-tuple-element.10) | copy-start | bytes 393220
  129.6 6.6 %copy-start = (pred[512,1536]{0,1:T(8,128)(4,1)S(1)}, pred[512,1536]{0,1:T(8,128)(4,1)}, u32[]{:S(2)}) copy-start(pred[512,1536]{0,1:T(8,128)(4,1)} %fusion.10) | copy-start | bytes 2359300
Sparse Core Ops, SparseCore 0:
  16.5 95.4 all-gather.1

commit v8 on v5

--- a/solution.py
+++ b/solution.py
@@ -88,7 +88,8 @@
         ],
         axis=0,
     )
-    slabs = lax.all_gather(padded, ROW, axis=0, tiled=True).reshape(-1, aligned, weight_cols)
+    (along_x,) = ring_gather((padded,), "rx", (0,))
+    slabs = lax.all_gather(along_x, "rz", axis=0, tiled=True).reshape(-1, aligned, weight_cols)
     largest = jnp.max(slabs[:, weight_rows].astype(jnp.float32), axis=0)
     clipped = clip_with(slabs[:, :weight_rows].reshape(-1, weight_cols), largest)
     rows_tokens, piece = tokens.shape

time: 145 us -> 153 us (1.055)
  the two profiles are of different devices: /device:TPU:64 before, /device:TPU:1 now
where the time goes in v8:
time: 153 us; the launch traced here: 152 us
  starting transfers between devices  48.2 us (32%)
  waiting for transfers between devices  43.5 us (28%)
  local copies, waits for them, and re-layouts  23.1 us (15%)
  between operations  14.6 us (10%)
  other arithmetic  14.2 us (9%)
  matrix products  8 us (5%)
    ppermute x7, waiting for transfers between devices, ring_gather(): forward = lax.ppermute(forward, axis, right)  37 us
    ppermute x7, starting transfers between devices, ring_gather(): forward = lax.ppermute(forward, axis, right)  28.4 us
    ppermute x4, starting transfers between devices, ring_gather(): backward = lax.ppermute(backward, axis, left)  16.6 us
    concatenate x2, local copies, waits for them, and re-layouts, ring_gather(): doubled = jnp.concatenate([stacked, stacked], axis=dim)  8.33 us
    ppermute x2, waiting for transfers between devices, shifted(): return lax.ppermute(array, axis, pairs)  6.53 us
    concatenate x1, other arithmetic, ring_gather(): doubled = jnp.concatenate([stacked, stacked], axis=dim)  5.16 us
    unnamed x19, local copies, waits for them, and re-layouts  4.28 us
    dynamic_slice x2, local copies, waits for them, and re-layouts, ring_gather(): lax.dynamic_slice_in_dim(doubled, start * size, peers * size, dim)  4.26 us
  transfers between devices with their start and end apart: 14, of which 9 were waited for; matrix products, arithmetic and copies ran while one was open for 16% of the time, Pallas kernels for 0%

profile of v8, /device:TPU:1, one launch (start us, length us, event | category | flops | bytes accessed | tf_op | source)
XLA Modules:
  0.0 151.6 jit_solution(13942255456122069006)
XLA Ops:
  9.2 3.9 %collective-permute-start.9 = (bf16[176,512]{1,0:T(8,128)(2,1)S(1)}, bf16[176,512]{1,0:T(8,128)(2,1)S(1)}, u32[]{:S(2)}, u32[]{:S(2)}) collective-permute-start(bf16[176,512]{1,0:T(8,128)(2,1)S(1)} %pad_maximum_fusion.1), channel_id=1, source_target_pairs={{0,16},{16,32},{32,48},{48,0},{1,17},{17,33},{33,49},{49,1},{2,18}... | collective-permute-start | bytes 540680 | tf_op jit(solution)/shard_map/ppermute | solution.py:34
  13.1 3.2 %collective-permute-start.8 = (bf16[176,512]{1,0:T(8,128)(2,1)S(1)}, bf16[176,512]{1,0:T(8,128)(2,1)S(1)}, u32[]{:S(2)}, u32[]{:S(2)}) collective-permute-start(bf16[176,512]{1,0:T(8,128)(2,1)S(1)} %pad_maximum_fusion.1), channel_id=1, source_target_pairs={{0,48},{16,0},{32,16},{48,32},{1,49},{17,1},{33,17},{49,33},{2,50}... | collective-permute-start | bytes 540680 | tf_op jit(solution)/shard_map/ppermute | solution.py:37
  17.3 2.2 %collective-permute-start.10 = (bf16[176,512]{1,0:T(8,128)(2,1)S(1)}, bf16[176,512]{1,0:T(8,128)(2,1)S(1)}, u32[]{:S(2)}, u32[]{:S(2)}) collective-permute-start(bf16[176,512]{1,0:T(8,128)(2,1)S(1)} %collective-permute-done.9), channel_id=1, source_target_pairs={{0,16},{16,32},{32,48},{48,0},{1,17},{17,33},{33,49},{49,1},{2,18}... | collective-permute-start | bytes 540680 | tf_op jit(solution)/shard_map/ppermute | solution.py:34
  19.5 6.4 %collective-permute-done.10 = bf16[176,512]{1,0:T(8,128)(2,1)S(1)} collective-permute-done((bf16[176,512]{1,0:T(8,128)(2,1)S(1)}, bf16[176,512]{1,0:T(8,128)(2,1)S(1)}, u32[]{:S(2)}, u32[]{:S(2)}) %collective-permute-start.10) | collective-permute-done | bytes 180256 | tf_op jit(solution)/shard_map/ppermute | solution.py:34
  28.1 3.3 %collective-permute-start.3 = (bf16[520,336]{1,0:T(8,128)(2,1)S(1)}, bf16[520,336]{1,0:T(8,128)(2,1)S(1)}, u32[]{:S(2)}, u32[]{:S(2)}) collective-permute-start(bf16[520,336]{1,0:T(8,128)(2,1)S(1)} %concatenate.49), channel_id=1, source_target_pairs={{0,2},{2,4},{4,6},{6,8},{8,10},{10,12},{12,14},{14,0},{1,3},{3,5},... | collective-permute-start | bytes 1048328 | tf_op jit(solution)/shard_map/ppermute | solution.py:34
  31.4 3.8 %collective-permute-start = (bf16[520,336]{1,0:T(8,128)(2,1)S(1)}, bf16[520,336]{1,0:T(8,128)(2,1)S(1)}, u32[]{:S(2)}, u32[]{:S(2)}) collective-permute-start(bf16[520,336]{1,0:T(8,128)(2,1)S(1)} %concatenate.49), channel_id=1, source_target_pairs={{0,14},{2,0},{4,2},{6,4},{8,6},{10,8},{12,10},{14,12},{1,15},{3,1}... | collective-permute-start | bytes 1048328 | tf_op jit(solution)/shard_map/ppermute | solution.py:37
  35.2 3.3 %collective-permute-done.3 = bf16[520,336]{1,0:T(8,128)(2,1)S(1)} collective-permute-done((bf16[520,336]{1,0:T(8,128)(2,1)S(1)}, bf16[520,336]{1,0:T(8,128)(2,1)S(1)}, u32[]{:S(2)}, u32[]{:S(2)}) %collective-permute-start.3) | collective-permute-done | bytes 349472 | tf_op jit(solution)/shard_map/ppermute | solution.py:34
  40.4 4.7 %collective-permute-start.1 = (bf16[520,336]{1,0:T(8,128)(2,1)S(1)}, bf16[520,336]{1,0:T(8,128)(2,1)S(1)}, u32[]{:S(2)}, u32[]{:S(2)}) collective-permute-start(bf16[520,336]{1,0:T(8,128)(2,1)S(1)} %collective-permute-done), channel_id=1, source_target_pairs={{0,14},{2,0},{4,2},{6,4},{8,6},{10,8},{12,10},{14,12},{1,15},{3,1}... | collective-permute-start | bytes 1048328 | tf_op jit(solution)/shard_map/ppermute | solution.py:37
  45.1 6.5 %collective-permute-done.4 = bf16[520,336]{1,0:T(8,128)(2,1)S(1)} collective-permute-done((bf16[520,336]{1,0:T(8,128)(2,1)S(1)}, bf16[520,336]{1,0:T(8,128)(2,1)S(1)}, u32[]{:S(2)}, u32[]{:S(2)}) %collective-permute-start.4) | collective-permute-done | bytes 349472 | tf_op jit(solution)/shard_map/ppermute | solution.py:34
  53.5 4.8 %collective-permute-start.2 = (bf16[520,336]{1,0:T(8,128)(2,1)S(1)}, bf16[520,336]{1,0:T(8,128)(2,1)S(1)}, u32[]{:S(2)}, u32[]{:S(2)}) collective-permute-start(bf16[520,336]{1,0:T(8,128)(2,1)S(1)} %collective-permute-done.1), channel_id=1, source_target_pairs={{0,14},{2,0},{4,2},{6,4},{8,6},{10,8},{12,10},{14,12},{1,15},{3,1}... | collective-permute-start | bytes 1048328 | tf_op jit(solution)/shard_map/ppermute | solution.py:37
  58.4 6.9 %collective-permute-done.5 = bf16[520,336]{1,0:T(8,128)(2,1)S(1)} collective-permute-done((bf16[520,336]{1,0:T(8,128)(2,1)S(1)}, bf16[520,336]{1,0:T(8,128)(2,1)S(1)}, u32[]{:S(2)}, u32[]{:S(2)}) %collective-permute-start.5) | collective-permute-done | bytes 349472 | tf_op jit(solution)/shard_map/ppermute | solution.py:34
  67.2 12.5 %collective-permute-done.6 = bf16[520,336]{1,0:T(8,128)(2,1)S(1)} collective-permute-done((bf16[520,336]{1,0:T(8,128)(2,1)S(1)}, bf16[520,336]{1,0:T(8,128)(2,1)S(1)}, u32[]{:S(2)}, u32[]{:S(2)}) %collective-permute-start.6) | collective-permute-done | bytes 349472 | tf_op jit(solution)/shard_map/ppermute | solution.py:34
  79.7 7.7 %concatenate.50 = bf16[520,5376]{1,0:T(8,128)(2,1)} concatenate(bf16[520,336]{1,0:T(8,128)(2,1)S(1)} %concatenate.49, bf16[520,336]{1,0:T(8,128)(2,1)S(1)} %collective-permute-done, bf16[520,336]{1,0:T(8,128)(2,1)S(1)} %collective-permute-done.1, bf16[520,336]{1,0:T(8,128)(2,1)S(1)} %collective-permute-done.2, bf16[520,336]{1,0:T(8,128)(2,1)S(1)} %collective-permute-done.6, ...), dimensions={1} | concatenate | bytes 11182080 | tf_op jit(solution)/shard_map/concatenate | solution.py:43
  87.3 3.3 %constant_dynamic-slice_fusion.1 = bf16[520,2688]{1,0:T(8,128)(2,1)S(1)} fusion(bf16[520,5376]{1,0:T(8,128)(2,1)} %concatenate.50, s32[]{:T(128)S(6)} %select_n.29), kind=kLoop, calls=%fused_computation.78 | loop fusion | bytes 5591044 | tf_op jit(solution)/shard_map/dynamic_slice | solution.py:45
  90.7 13.3 %collective-permute-start.7 = (bf16[520,2688]{1,0:T(8,128)(2,1)S(1)}, bf16[520,2688]{1,0:T(8,128)(2,1)}, u32[]{:S(2)}, u32[]{:S(2)}) collective-permute-start(bf16[520,2688]{1,0:T(8,128)(2,1)S(1)} %constant_dynamic-slice_fusion.1), channel_id=1, source_target_pairs={{0,1},{1,0},{2,3},{3,2},{4,5},{5,4},{6,7},{7,6},{8,9},{9,8},{10,11... | collective-permute-start | bytes 8386568 | tf_op jit(solution)/shard_map/ppermute | solution.py:34
  106.2 2.0 %fusion.13 = pred[512,1536]{0,1:T(8,128)(4,1)} fusion(s32[1536]{0:T(1024)S(1)} %iota_add_fusion, s32[512]{0:T(512)S(1)} %iota_add_fusion.1, pred[1536]{0:T(1024)(128)(4,1)S(1)} %broadcast_compare_fusion), kind=kLoop, calls=%fused_computation.24 | loop fusion | flops 3932160 | bytes 796160 | tf_op jit(solution)/shard_map/and | solution.py:146
  108.6 5.2 %fusion.7 = bf16[520,5376]{1,0:T(8,128)(2,1)S(1)} fusion(s32[]{:T(128)S(6)} %select_n.31, bf16[520,2688]{1,0:T(8,128)(2,1)S(1)} %constant_dynamic-slice_fusion.1, bf16[520,2688]{1,0:T(8,128)(2,1)} %collective-permute-done.7), kind=kLoop, calls=%fused_computation.16 | loop fusion | flops 22364160 | bytes 11182084 | tf_op jit(solution)/shard_map/concatenate | solution.py:43
  113.9 2.3 %copy-done = bf16[520,5376]{1,0:T(8,128)(2,1)} copy-done((bf16[520,5376]{1,0:T(8,128)(2,1)}, bf16[520,5376]{1,0:T(8,128)(2,1)S(1)}, u32[]{:S(2)}) %copy-start) | copy-done | bytes 5591064
  117.4 3.1 %slice.79 = bf16[32,168,512]{2,1,0:T(8,128)(2,1)S(1)} slice(bf16[32,176,512]{2,1,0:T(8,128)(2,1)} %bitcast.52), slice={[0:32], [0:168], [0:512]} | slice | bytes 11010048 | tf_op jit(solution)/shard_map/slice | solution.py:94
  123.6 2.0 %fusion.16 = f32[512,256]{0,1:T(8,128)S(1)} fusion(bf16[5376,512]{1,0:T(8,128)(2,1)S(1)} %bitcast.50, f32[5376]{0:T(1024)S(1)} %fusion.37, f32[512]{0:T(512)S(1)} %add_rsqrt_fusion.2, bf16[520,5376]{1,0:T(8,128)(2,1)S(1)} %bitcast.48), kind=kOutput, calls=%fused_computation.27 | convolution fusion | flops 1420296192 | bytes 8808448 | tf_op jit(solution)/shard_map/dot_general | solution.py:117
  127.7 2.0 %collective-permute-start.12 = (bf16[512,2,128]{0,2,1:T(8,128)(2,1)S(1)}, bf16[512,2,128]{0,2,1:T(8,128)(2,1)}, u32[]{:S(2)}, u32[]{:S(2)}) collective-permute-start(bf16[512,2,128]{0,2,1:T(8,128)(2,1)S(1)} %pad_maximum_fusion), channel_id=1, source_target_pairs={{0,16},{16,32},{32,48},{48,64},{64,80},{80,96},{96,112},{112,128},... | collective-permute-start | bytes 786440 | tf_op jit(solution)/shard_map/ppermute | solution.py:23
  129.7 2.0 %multiply_reduce_fusion = (f32[512,2]{0,1:T(2,128)S(1)}, f32[512,256]{0,1:T(8,128)S(1)}) fusion(bf16[5376,512]{1,0:T(8,128)(2,1)S(1)} %bitcast.51, f32[5376]{0:T(1024)S(1)} %fusion.37, f32[512]{0:T(512)S(1)} %add_rsqrt_fusion.2, bf16[520,5376]{1,0:T(8,128)(2,1)S(1)} %bitcast.48), kind=kOutput, calls=%fused_computation.34 | convolution fusion | flops 1420557312 | bytes 8812544 | tf_op jit(solution)/shard_map/dot_general | solution.py:120
  133.3 5.6 %collective-permute-done.12 = bf16[512,2,128]{0,2,1:T(8,128)(2,1)} collective-permute-done((bf16[512,2,128]{0,2,1:T(8,128)(2,1)S(1)}, bf16[512,2,128]{0,2,1:T(8,128)(2,1)}, u32[]{:S(2)}, u32[]{:S(2)}) %collective-permute-start.12) | collective-permute-done | bytes 262176 | tf_op jit(solution)/shard_map/ppermute | solution.py:23
  141.9 2.0 %fusion.18 = bf16[128,2,512]{2,0,1:T(8,128)(2,1)S(1)} fusion(f32[2,512]{1,0:T(2,128)S(1)} %get-tuple-element.18, f32[1536,512,2]{1,0,2:T(8,128)S(1)} %get-tuple-element.19, pred[512,1536]{0,1:T(8,128)(4,1)S(1)} %copy-done.1, bf16[1536,2,128]{0,2,1:T(8,128)(2,1)S(1)} %maximum_maximum_fusion), kind=kOutput, calls=%fused_computation.29 | convolution fusion | flops 409075712 | bytes 7737344 | tf_op jit(solution)/shard_map/kgts,skd->tkgd/dot_general | solution.py:150
  (74 shorter events, 25.1 us)
Async XLA Ops:
  6.5 21.0 %copy-start.3 = (f32[336]{0:T(512)S(1)}, f32[336]{0:T(512)}, u32[]{:S(2)}) copy-start(f32[336]{0:T(512)} %param.8) | copy-start | bytes 4036
  6.5 21.1 %copy-start.2 = (bf16[512,336]{0,1:T(8,128)(2,1)S(1)}, bf16[512,336]{0,1:T(8,128)(2,1)}, u32[]{:S(2)}) copy-start(bf16[512,336]{0,1:T(8,128)(2,1)} %param.7) | copy-start | bytes 1032196
  6.5 110.9 %all-gather.2.cloned.1.call-start = ((), (), s32[]{:S(2)}) async-start(), calls=%async_computation | async-start | bytes 6488064 | tf_op jit(solution)/shard_map/all_gather | solution.py:92
  9.2 8.1 %collective-permute-start.9 = (bf16[176,512]{1,0:T(8,128)(2,1)S(1)}, bf16[176,512]{1,0:T(8,128)(2,1)S(1)}, u32[]{:S(2)}, u32[]{:S(2)}) collective-permute-start(bf16[176,512]{1,0:T(8,128)(2,1)S(1)} %pad_maximum_fusion.1), channel_id=1, source_target_pairs={{0,16},{16,32},{32,48},{48,0},{1,17},{17,33},{33,49},{49,1},{2,18}... | collective-permute-start | bytes 540680 | tf_op jit(solution)/shard_map/ppermute | solution.py:34
  13.1 6.3 %collective-permute-start.8 = (bf16[176,512]{1,0:T(8,128)(2,1)S(1)}, bf16[176,512]{1,0:T(8,128)(2,1)S(1)}, u32[]{:S(2)}, u32[]{:S(2)}) collective-permute-start(bf16[176,512]{1,0:T(8,128)(2,1)S(1)} %pad_maximum_fusion.1), channel_id=1, source_target_pairs={{0,48},{16,0},{32,16},{48,32},{1,49},{17,1},{33,17},{49,33},{2,50}... | collective-permute-start | bytes 540680 | tf_op jit(solution)/shard_map/ppermute | solution.py:37
  17.3 8.6 %collective-permute-start.10 = (bf16[176,512]{1,0:T(8,128)(2,1)S(1)}, bf16[176,512]{1,0:T(8,128)(2,1)S(1)}, u32[]{:S(2)}, u32[]{:S(2)}) collective-permute-start(bf16[176,512]{1,0:T(8,128)(2,1)S(1)} %collective-permute-done.9), channel_id=1, source_target_pairs={{0,16},{16,32},{32,48},{48,0},{1,17},{17,33},{33,49},{49,1},{2,18}... | collective-permute-start | bytes 540680 | tf_op jit(solution)/shard_map/ppermute | solution.py:34
  28.1 10.4 %collective-permute-start.3 = (bf16[520,336]{1,0:T(8,128)(2,1)S(1)}, bf16[520,336]{1,0:T(8,128)(2,1)S(1)}, u32[]{:S(2)}, u32[]{:S(2)}) collective-permute-start(bf16[520,336]{1,0:T(8,128)(2,1)S(1)} %concatenate.49), channel_id=1, source_target_pairs={{0,2},{2,4},{4,6},{6,8},{8,10},{10,12},{12,14},{14,0},{1,3},{3,5},... | collective-permute-start | bytes 1048328 | tf_op jit(solution)/shard_map/ppermute | solution.py:34
  31.4 9.0 %collective-permute-start = (bf16[520,336]{1,0:T(8,128)(2,1)S(1)}, bf16[520,336]{1,0:T(8,128)(2,1)S(1)}, u32[]{:S(2)}, u32[]{:S(2)}) collective-permute-start(bf16[520,336]{1,0:T(8,128)(2,1)S(1)} %concatenate.49), channel_id=1, source_target_pairs={{0,14},{2,0},{4,2},{6,4},{8,6},{10,8},{12,10},{14,12},{1,15},{3,1}... | collective-permute-start | bytes 1048328 | tf_op jit(solution)/shard_map/ppermute | solution.py:37
  38.5 13.1 %collective-permute-start.4 = (bf16[520,336]{1,0:T(8,128)(2,1)S(1)}, bf16[520,336]{1,0:T(8,128)(2,1)S(1)}, u32[]{:S(2)}, u32[]{:S(2)}) collective-permute-start(bf16[520,336]{1,0:T(8,128)(2,1)S(1)} %collective-permute-done.3), channel_id=1, source_target_pairs={{0,2},{2,4},{4,6},{6,8},{8,10},{10,12},{12,14},{14,0},{1,3},{3,5},... | collective-permute-start | bytes 1048328 | tf_op jit(solution)/shard_map/ppermute | solution.py:34
  40.4 13.1 %collective-permute-start.1 = (bf16[520,336]{1,0:T(8,128)(2,1)S(1)}, bf16[520,336]{1,0:T(8,128)(2,1)S(1)}, u32[]{:S(2)}, u32[]{:S(2)}) collective-permute-start(bf16[520,336]{1,0:T(8,128)(2,1)S(1)} %collective-permute-done), channel_id=1, source_target_pairs={{0,14},{2,0},{4,2},{6,4},{8,6},{10,8},{12,10},{14,12},{1,15},{3,1}... | collective-permute-start | bytes 1048328 | tf_op jit(solution)/shard_map/ppermute | solution.py:37
  51.6 13.7 %collective-permute-start.5 = (bf16[520,336]{1,0:T(8,128)(2,1)S(1)}, bf16[520,336]{1,0:T(8,128)(2,1)S(1)}, u32[]{:S(2)}, u32[]{:S(2)}) collective-permute-start(bf16[520,336]{1,0:T(8,128)(2,1)S(1)} %collective-permute-done.4), channel_id=1, source_target_pairs={{0,2},{2,4},{4,6},{6,8},{8,10},{10,12},{12,14},{14,0},{1,3},{3,5},... | collective-permute-start | bytes 1048328 | tf_op jit(solution)/shard_map/ppermute | solution.py:34
  53.5 13.7 %collective-permute-start.2 = (bf16[520,336]{1,0:T(8,128)(2,1)S(1)}, bf16[520,336]{1,0:T(8,128)(2,1)S(1)}, u32[]{:S(2)}, u32[]{:S(2)}) collective-permute-start(bf16[520,336]{1,0:T(8,128)(2,1)S(1)} %collective-permute-done.1), channel_id=1, source_target_pairs={{0,14},{2,0},{4,2},{6,4},{8,6},{10,8},{12,10},{14,12},{1,15},{3,1}... | collective-permute-start | bytes 1048328 | tf_op jit(solution)/shard_map/ppermute | solution.py:37
  65.2 14.4 %collective-permute-start.6 = (bf16[520,336]{1,0:T(8,128)(2,1)S(1)}, bf16[520,336]{1,0:T(8,128)(2,1)S(1)}, u32[]{:S(2)}, u32[]{:S(2)}) collective-permute-start(bf16[520,336]{1,0:T(8,128)(2,1)S(1)} %collective-permute-done.5), channel_id=1, source_target_pairs={{0,2},{2,4},{4,6},{6,8},{8,10},{10,12},{12,14},{14,0},{1,3},{3,5},... | collective-permute-start | bytes 1048328 | tf_op jit(solution)/shard_map/ppermute | solution.py:34
  90.7 18.0 %collective-permute-start.7 = (bf16[520,2688]{1,0:T(8,128)(2,1)S(1)}, bf16[520,2688]{1,0:T(8,128)(2,1)}, u32[]{:S(2)}, u32[]{:S(2)}) collective-permute-start(bf16[520,2688]{1,0:T(8,128)(2,1)S(1)} %constant_dynamic-slice_fusion.1), channel_id=1, source_target_pairs={{0,1},{1,0},{2,3},{3,2},{4,5},{5,4},{6,7},{7,6},{8,9},{9,8},{10,11... | collective-permute-start | bytes 8386568 | tf_op jit(solution)/shard_map/ppermute | solution.py:34
  113.8 2.4 %copy-start = (bf16[520,5376]{1,0:T(8,128)(2,1)}, bf16[520,5376]{1,0:T(8,128)(2,1)S(1)}, u32[]{:S(2)}) copy-start(bf16[520,5376]{1,0:T(8,128)(2,1)S(1)} %fusion.7) | copy-start | bytes 16773124
  117.4 6.1 %slice-start = ((s8[5591040]{0:T(1024)(128)(4,1)}), s8[4194304]{0:T(1024)(128)(4,1)S(1)}, s32[]{:S(2)}) async-start(s8[5591040]{0:T(1024)(128)(4,1)} %bitcast.47), calls=%async_computation.1 | async-start | bytes 8388608
  121.6 1.9 %slice-start.1 = ((s8[5591040]{0:T(1024)(128)(4,1)}), s8[1396736]{0:T(1024)(128)(4,1)S(1)}, s32[]{:S(2)}) async-start(s8[5591040]{0:T(1024)(128)(4,1)} %bitcast.47), calls=%async_computation.2 | async-start | bytes 2793472
  123.6 2.1 %copy-start.4 = (f32[128]{0:T(128)S(1)}, f32[128]{0:T(128)}, u32[]{:S(2)}) copy-start(f32[128]{0:T(128)} %param.10) | copy-start | bytes 1540
  126.4 5.6 %copy-start.5 = (f32[128]{0:T(128)S(1)}, f32[128]{0:T(128)}, u32[]{:S(2)}) copy-start(f32[128]{0:T(128)} %param.9) | copy-start | bytes 1540
  126.4 7.0 %collective-permute-start.11 = (bf16[512,2,128]{0,2,1:T(8,128)(2,1)S(1)}, bf16[512,2,128]{0,2,1:T(8,128)(2,1)S(1)}, u32[]{:S(2)}, u32[]{:S(2)}) collective-permute-start(bf16[512,2,128]{0,2,1:T(8,128)(2,1)S(1)} %pad_maximum_fusion), channel_id=1, source_target_pairs={{0,32},{16,48},{32,64},{48,80},{64,96},{80,112},{96,128},{112,144}... | collective-permute-start | bytes 786440 | tf_op jit(solution)/shard_map/ppermute | solution.py:23
  127.7 11.3 %collective-permute-start.12 = (bf16[512,2,128]{0,2,1:T(8,128)(2,1)S(1)}, bf16[512,2,128]{0,2,1:T(8,128)(2,1)}, u32[]{:S(2)}, u32[]{:S(2)}) collective-permute-start(bf16[512,2,128]{0,2,1:T(8,128)(2,1)S(1)} %pad_maximum_fusion), channel_id=1, source_target_pairs={{0,16},{16,32},{32,48},{48,64},{64,80},{80,96},{96,112},{112,128},... | collective-permute-start | bytes 786440 | tf_op jit(solution)/shard_map/ppermute | solution.py:23
  131.7 8.3 %copy-start.1 = (pred[512,1536]{0,1:T(8,128)(4,1)S(1)}, pred[512,1536]{0,1:T(8,128)(4,1)}, u32[]{:S(2)}) copy-start(pred[512,1536]{0,1:T(8,128)(4,1)} %fusion.13) | copy-start | bytes 2359300
Sparse Core Ops, SparseCore 0:
  27.6 77.3 all-gather.1

commit v9 on v5

--- a/solution.py
+++ b/solution.py
@@ -90,7 +90,11 @@
     )
     slabs = lax.all_gather(padded, ROW, axis=0, tiled=True).reshape(-1, aligned, weight_cols)
     largest = jnp.max(slabs[:, weight_rows].astype(jnp.float32), axis=0)
-    clipped = clip_with(slabs[:, :weight_rows].reshape(-1, weight_cols), largest)
+
+    def clipped_columns(first, last):
+        part = slabs[:, :weight_rows, first:last].reshape(-1, last - first)
+        return clip_with(part, largest[first:last])
+
     rows_tokens, piece = tokens.shape
     cores = lax.axis_size("cc")
     high = gain.astype(jnp.bfloat16)
@@ -108,15 +112,20 @@
     squares = jnp.sum(widened * widened, axis=1)
     inverse = lax.rsqrt(squares / D + EPS)[:, None]
     whole = (widened * inverse * full_gain[None, :]).astype(jnp.bfloat16)
-    ordered = (
-        clipped.reshape(blocks, cores, piece, clipped.shape[1])
-        .transpose(1, 0, 2, 3)
-        .reshape(clipped.shape)
+    def ordered(first, last):
+        part = clipped_columns(first, last)
+        return (
+            part.reshape(blocks, cores, piece, last - first)
+            .transpose(1, 0, 2, 3)
+            .reshape(part.shape)
+        )
+
+    kv_part = jnp.dot(
+        whole, ordered(query_cols, weight_cols), preferred_element_type=jnp.float32
     )
-    kv_part = jnp.dot(whole, ordered[:, query_cols:], preferred_element_type=jnp.float32)
     keys = kv_part[:, :key_cols]
     values = kv_part[:, key_cols:]
-    query = jnp.dot(whole, ordered[:, :query_cols], preferred_element_type=jnp.float32)
+    query = jnp.dot(whole, ordered(0, query_cols), preferred_element_type=jnp.float32)
     heads_local = query_cols // HD
     kv_local = key_cols // HD
     group = heads_local // kv_local

time: 145 us -> 145 us (level)
  the two profiles are of different devices: /device:TPU:64 before, /device:TPU:1 now
where the time goes in v9:
time: 145 us; the launch traced here: 143 us
  starting transfers between devices  40.8 us (28%)
  waiting for transfers between devices  37.1 us (26%)
  local copies, waits for them, and re-layouts  25.3 us (17%)
  other arithmetic  14.8 us (10%)
  between operations  14.5 us (10%)
  matrix products  10.9 us (8%)
    ppermute x5, starting transfers between devices, ring_gather(): forward = lax.ppermute(forward, axis, right)  21.1 us
    all_gather x1, waiting for transfers between devices, local(): lax.all_gather(padded, ROW, axis=0, tiled=True)  18 us
    ppermute x5, waiting for transfers between devices, ring_gather(): forward = lax.ppermute(forward, axis, right)  17.4 us
    ppermute x3, starting transfers between devices, ring_gather(): backward = lax.ppermute(backward, axis, left)  13.4 us
    concatenate x1, local copies, waits for them, and re-layouts, ring_gather(): doubled = jnp.concatenate([stacked, stacked], axis=dim)  7.61 us
    ppermute x2, starting transfers between devices, shifted(): return lax.ppermute(array, axis, pairs)  6.34 us
    unnamed x17, local copies, waits for them, and re-layouts  5.32 us
    dot_general x1, matrix products, local(): jnp.dot(whole, ordered(0, query_cols), preferred_element_type=jnp.float32)  5.19 us
  transfers between devices with their start and end apart: 11, of which 7 were waited for; matrix products, arithmetic and copies ran while one was open for 22% of the time, Pallas kernels for 0%

profile of v9, /device:TPU:1, one launch (start us, length us, event | category | flops | bytes accessed | tf_op | source)
XLA Modules:
  0.0 143.5 jit_solution(14223948098695784840)
XLA Ops:
  12.2 4.0 %collective-permute-start.3 = (bf16[520,336]{1,0:T(8,128)(2,1)S(1)}, bf16[520,336]{1,0:T(8,128)(2,1)S(1)}, u32[]{:S(2)}, u32[]{:S(2)}) collective-permute-start(bf16[520,336]{1,0:T(8,128)(2,1)S(1)} %concatenate.43), channel_id=1, source_target_pairs={{0,2},{2,4},{4,6},{6,8},{8,10},{10,12},{12,14},{14,0},{1,3},{3,5},... | collective-permute-start | bytes 1048328 | tf_op jit(solution)/shard_map/ppermute | solution.py:34
  16.3 3.8 %collective-permute-start = (bf16[520,336]{1,0:T(8,128)(2,1)S(1)}, bf16[520,336]{1,0:T(8,128)(2,1)S(1)}, u32[]{:S(2)}, u32[]{:S(2)}) collective-permute-start(bf16[520,336]{1,0:T(8,128)(2,1)S(1)} %concatenate.43), channel_id=1, source_target_pairs={{0,14},{2,0},{4,2},{6,4},{8,6},{10,8},{12,10},{14,12},{1,15},{3,1}... | collective-permute-start | bytes 1048328 | tf_op jit(solution)/shard_map/ppermute | solution.py:37
  20.1 3.3 %collective-permute-done.3 = bf16[520,336]{1,0:T(8,128)(2,1)S(1)} collective-permute-done((bf16[520,336]{1,0:T(8,128)(2,1)S(1)}, bf16[520,336]{1,0:T(8,128)(2,1)S(1)}, u32[]{:S(2)}, u32[]{:S(2)}) %collective-permute-start.3) | collective-permute-done | bytes 349472 | tf_op jit(solution)/shard_map/ppermute | solution.py:34
  23.4 4.0 %collective-permute-start.4 = (bf16[520,336]{1,0:T(8,128)(2,1)S(1)}, bf16[520,336]{1,0:T(8,128)(2,1)S(1)}, u32[]{:S(2)}, u32[]{:S(2)}) collective-permute-start(bf16[520,336]{1,0:T(8,128)(2,1)S(1)} %collective-permute-done.3), channel_id=1, source_target_pairs={{0,2},{2,4},{4,6},{6,8},{8,10},{10,12},{12,14},{14,0},{1,3},{3,5},... | collective-permute-start | bytes 1048328 | tf_op jit(solution)/shard_map/ppermute | solution.py:34
  27.4 4.7 %collective-permute-start.1 = (bf16[520,336]{1,0:T(8,128)(2,1)S(1)}, bf16[520,336]{1,0:T(8,128)(2,1)S(1)}, u32[]{:S(2)}, u32[]{:S(2)}) collective-permute-start(bf16[520,336]{1,0:T(8,128)(2,1)S(1)} %collective-permute-done), channel_id=1, source_target_pairs={{0,14},{2,0},{4,2},{6,4},{8,6},{10,8},{12,10},{14,12},{1,15},{3,1}... | collective-permute-start | bytes 1048328 | tf_op jit(solution)/shard_map/ppermute | solution.py:37
  32.1 3.3 %collective-permute-done.4 = bf16[520,336]{1,0:T(8,128)(2,1)S(1)} collective-permute-done((bf16[520,336]{1,0:T(8,128)(2,1)S(1)}, bf16[520,336]{1,0:T(8,128)(2,1)S(1)}, u32[]{:S(2)}, u32[]{:S(2)}) %collective-permute-start.4) | collective-permute-done | bytes 349472 | tf_op jit(solution)/shard_map/ppermute | solution.py:34
  35.4 3.1 %collective-permute-start.5 = (bf16[520,336]{1,0:T(8,128)(2,1)S(1)}, bf16[520,336]{1,0:T(8,128)(2,1)S(1)}, u32[]{:S(2)}, u32[]{:S(2)}) collective-permute-start(bf16[520,336]{1,0:T(8,128)(2,1)S(1)} %collective-permute-done.4), channel_id=1, source_target_pairs={{0,2},{2,4},{4,6},{6,8},{8,10},{10,12},{12,14},{14,0},{1,3},{3,5},... | collective-permute-start | bytes 1048328 | tf_op jit(solution)/shard_map/ppermute | solution.py:34
  38.4 4.8 %collective-permute-start.2 = (bf16[520,336]{1,0:T(8,128)(2,1)S(1)}, bf16[520,336]{1,0:T(8,128)(2,1)S(1)}, u32[]{:S(2)}, u32[]{:S(2)}) collective-permute-start(bf16[520,336]{1,0:T(8,128)(2,1)S(1)} %collective-permute-done.1), channel_id=1, source_target_pairs={{0,14},{2,0},{4,2},{6,4},{8,6},{10,8},{12,10},{14,12},{1,15},{3,1}... | collective-permute-start | bytes 1048328 | tf_op jit(solution)/shard_map/ppermute | solution.py:37
  43.3 3.3 %collective-permute-done.5 = bf16[520,336]{1,0:T(8,128)(2,1)S(1)} collective-permute-done((bf16[520,336]{1,0:T(8,128)(2,1)S(1)}, bf16[520,336]{1,0:T(8,128)(2,1)S(1)}, u32[]{:S(2)}, u32[]{:S(2)}) %collective-permute-start.5) | collective-permute-done | bytes 349472 | tf_op jit(solution)/shard_map/ppermute | solution.py:34
  46.5 2.2 %collective-permute-start.6 = (bf16[520,336]{1,0:T(8,128)(2,1)S(1)}, bf16[520,336]{1,0:T(8,128)(2,1)S(1)}, u32[]{:S(2)}, u32[]{:S(2)}) collective-permute-start(bf16[520,336]{1,0:T(8,128)(2,1)S(1)} %collective-permute-done.5), channel_id=1, source_target_pairs={{0,2},{2,4},{4,6},{6,8},{8,10},{10,12},{12,14},{14,0},{1,3},{3,5},... | collective-permute-start | bytes 1048328 | tf_op jit(solution)/shard_map/ppermute | solution.py:34
  50.4 6.7 %collective-permute-done.6 = bf16[520,336]{1,0:T(8,128)(2,1)S(1)} collective-permute-done((bf16[520,336]{1,0:T(8,128)(2,1)S(1)}, bf16[520,336]{1,0:T(8,128)(2,1)S(1)}, u32[]{:S(2)}, u32[]{:S(2)}) %collective-permute-start.6) | collective-permute-done | bytes 349472 | tf_op jit(solution)/shard_map/ppermute | solution.py:34
  57.2 7.6 %concatenate.44 = bf16[520,5376]{1,0:T(8,128)(2,1)} concatenate(bf16[520,336]{1,0:T(8,128)(2,1)S(1)} %concatenate.43, bf16[520,336]{1,0:T(8,128)(2,1)S(1)} %collective-permute-done, bf16[520,336]{1,0:T(8,128)(2,1)S(1)} %collective-permute-done.1, bf16[520,336]{1,0:T(8,128)(2,1)S(1)} %collective-permute-done.2, bf16[520,336]{1,0:T(8,128)(2,1)S(1)} %collective-permute-done.6, ...), dimensions={1} | concatenate | bytes 11182080 | tf_op jit(solution)/shard_map/concatenate | solution.py:43
  64.8 3.3 %constant_dynamic-slice_fusion = bf16[520,2688]{1,0:T(8,128)(2,1)S(1)} fusion(bf16[520,5376]{1,0:T(8,128)(2,1)} %concatenate.44, s32[]{:T(128)S(6)} %select_n.22), kind=kLoop, calls=%fused_computation.80 | loop fusion | bytes 5591044 | tf_op jit(solution)/shard_map/dynamic_slice | solution.py:45
  68.1 7.8 %collective-permute-start.7 = (bf16[520,2688]{1,0:T(8,128)(2,1)S(1)}, bf16[520,2688]{1,0:T(8,128)(2,1)}, u32[]{:S(2)}, u32[]{:S(2)}) collective-permute-start(bf16[520,2688]{1,0:T(8,128)(2,1)S(1)} %constant_dynamic-slice_fusion), channel_id=1, source_target_pairs={{0,1},{1,0},{2,3},{3,2},{4,5},{5,4},{6,7},{7,6},{8,9},{9,8},{10,11... | collective-permute-start | bytes 8386568 | tf_op jit(solution)/shard_map/ppermute | solution.py:34
  80.6 5.2 %fusion.5 = bf16[520,5376]{1,0:T(8,128)(2,1)S(1)} fusion(s32[]{:T(128)S(6)} %select_n.24, bf16[520,2688]{1,0:T(8,128)(2,1)S(1)} %constant_dynamic-slice_fusion, bf16[520,2688]{1,0:T(8,128)(2,1)} %collective-permute-done.7), kind=kLoop, calls=%fused_computation.13 | loop fusion | flops 22364160 | bytes 11182084 | tf_op jit(solution)/shard_map/concatenate | solution.py:43
  85.8 2.4 %copy-done = bf16[520,5376]{1,0:T(8,128)(2,1)} copy-done((bf16[520,5376]{1,0:T(8,128)(2,1)}, bf16[520,5376]{1,0:T(8,128)(2,1)S(1)}, u32[]{:S(2)}) %copy-start) | copy-done | bytes 5591064
  89.4 18.0 %all-gather.2.cloned.1.call-done = bf16[5632,512]{1,0:T(8,128)(2,1)} async-done(((bf16[176,512]{1,0:T(8,128)(2,1)}), bf16[5632,512]{1,0:T(8,128)(2,1)}) %all-gather.2.cloned.1.call-update) | async-done | bytes 5767184 | tf_op jit(solution)/shard_map/all_gather | solution.py:91
  108.5 3.2 %fusion.47 = (bf16[32,168,256]{2,1,0:T(8,128)(2,1)S(1)}, bf16[32,168,256]{2,1,0:T(8,128)(2,1)S(1)}) fusion(bf16[32,176,512]{2,1,0:T(8,128)(2,1)} %bitcast.66), kind=kLoop, calls=%fused_computation.90 | loop fusion | bytes 11010048 | tf_op jit(solution)/shard_map/slice | solution.py:95
  113.2 2.0 %fusion.23 = f32[512,256]{0,1:T(8,128)S(1)} fusion(bf16[5376,256]{1,0:T(8,128)(2,1)S(1)} %bitcast.68, f32[5376]{0:T(1024)S(1)} %fusion.39, f32[512]{0:T(512)S(1)} %add_rsqrt_fusion.2, bf16[520,5376]{1,0:T(8,128)(2,1)S(1)} %bitcast.61), kind=kOutput, calls=%fused_computation.32 | convolution fusion | flops 1420296192 | bytes 8808448 | tf_op jit(solution)/shard_map/dot_general | solution.py:123
  116.0 3.7 %collective-permute-start.8 = (bf16[512,2,128]{0,2,1:T(8,128)(2,1)S(1)}, bf16[512,2,128]{0,2,1:T(8,128)(2,1)}, u32[]{:S(2)}, u32[]{:S(2)}) collective-permute-start(bf16[512,2,128]{0,2,1:T(8,128)(2,1)S(1)} %pad_maximum_fusion), channel_id=1, source_target_pairs={{0,32},{16,48},{32,64},{48,80},{64,96},{80,112},{96,128},{112,144}... | collective-permute-start | bytes 786440 | tf_op jit(solution)/shard_map/ppermute | solution.py:23
  119.7 2.6 %collective-permute-start.9 = (bf16[512,2,128]{0,2,1:T(8,128)(2,1)S(1)}, bf16[512,2,128]{0,2,1:T(8,128)(2,1)}, u32[]{:S(2)}, u32[]{:S(2)}) collective-permute-start(bf16[512,2,128]{0,2,1:T(8,128)(2,1)S(1)} %pad_maximum_fusion), channel_id=1, source_target_pairs={{0,16},{16,32},{32,48},{48,64},{64,80},{80,96},{96,112},{112,128},... | collective-permute-start | bytes 786440 | tf_op jit(solution)/shard_map/ppermute | solution.py:23
  122.5 3.0 %copy.46 = bf16[256,5376]{1,0:T(8,128)(2,1)} copy(bf16[256,5376]{0,1:T(8,128)(2,1)S(1)} %bitcast.64) | data formatting | bytes 5505024 | tf_op jit(solution)/shard_map/dot_general | solution.py:128
  125.5 5.2 %multiply_reduce_fusion = (f32[512,2]{0,1:T(2,128)S(1)}, f32[512,2,128]{0,2,1:T(8,128)S(1)}) fusion(bf16[2,128,5376]{2,1,0:T(8,128)(2,1)} %bitcast.67, f32[5376]{0:T(1024)} %copy-done.2, f32[512]{0:T(512)S(1)} %add_rsqrt_fusion.2, bf16[520,5376]{1,0:T(8,128)(2,1)} %copy-done), kind=kOutput, calls=%fused_computation.35 | convolution fusion | flops 1420557312 | bytes 8812544 | tf_op jit(solution)/shard_map/dot_general | solution.py:128
  133.8 2.0 %fusion.19 = bf16[128,2,512]{2,0,1:T(8,128)(2,1)S(1)} fusion(f32[2,512]{1,0:T(2,128)S(1)} %get-tuple-element.22, f32[1536,512,2]{1,0,2:T(8,128)S(1)} %get-tuple-element.23, pred[512,1536]{0,1:T(8,128)(4,1)S(1)} %copy-done.1, bf16[1536,2,128]{0,2,1:T(8,128)(2,1)S(1)} %maximum_maximum_fusion), kind=kOutput, calls=%fused_computation.31 | convolution fusion | flops 409075712 | bytes 7737344 | tf_op jit(solution)/shard_map/kgts,skd->tkgd/dot_general | solution.py:158
  (67 shorter events, 19.8 us)
Async XLA Ops:
  6.5 100.9 %all-gather.2.cloned.1.call-start = ((), (), s32[]{:S(2)}) async-start(), calls=%async_computation | async-start | bytes 5947392 | tf_op jit(solution)/shard_map/all_gather | solution.py:91
  12.2 11.1 %collective-permute-start.3 = (bf16[520,336]{1,0:T(8,128)(2,1)S(1)}, bf16[520,336]{1,0:T(8,128)(2,1)S(1)}, u32[]{:S(2)}, u32[]{:S(2)}) collective-permute-start(bf16[520,336]{1,0:T(8,128)(2,1)S(1)} %concatenate.43), channel_id=1, source_target_pairs={{0,2},{2,4},{4,6},{6,8},{8,10},{10,12},{12,14},{14,0},{1,3},{3,5},... | collective-permute-start | bytes 1048328 | tf_op jit(solution)/shard_map/ppermute | solution.py:34
  16.3 11.1 %collective-permute-start = (bf16[520,336]{1,0:T(8,128)(2,1)S(1)}, bf16[520,336]{1,0:T(8,128)(2,1)S(1)}, u32[]{:S(2)}, u32[]{:S(2)}) collective-permute-start(bf16[520,336]{1,0:T(8,128)(2,1)S(1)} %concatenate.43), channel_id=1, source_target_pairs={{0,14},{2,0},{4,2},{6,4},{8,6},{10,8},{12,10},{14,12},{1,15},{3,1}... | collective-permute-start | bytes 1048328 | tf_op jit(solution)/shard_map/ppermute | solution.py:37
  23.4 12.0 %collective-permute-start.4 = (bf16[520,336]{1,0:T(8,128)(2,1)S(1)}, bf16[520,336]{1,0:T(8,128)(2,1)S(1)}, u32[]{:S(2)}, u32[]{:S(2)}) collective-permute-start(bf16[520,336]{1,0:T(8,128)(2,1)S(1)} %collective-permute-done.3), channel_id=1, source_target_pairs={{0,2},{2,4},{4,6},{6,8},{8,10},{10,12},{12,14},{14,0},{1,3},{3,5},... | collective-permute-start | bytes 1048328 | tf_op jit(solution)/shard_map/ppermute | solution.py:34
  27.4 11.1 %collective-permute-start.1 = (bf16[520,336]{1,0:T(8,128)(2,1)S(1)}, bf16[520,336]{1,0:T(8,128)(2,1)S(1)}, u32[]{:S(2)}, u32[]{:S(2)}) collective-permute-start(bf16[520,336]{1,0:T(8,128)(2,1)S(1)} %collective-permute-done), channel_id=1, source_target_pairs={{0,14},{2,0},{4,2},{6,4},{8,6},{10,8},{12,10},{14,12},{1,15},{3,1}... | collective-permute-start | bytes 1048328 | tf_op jit(solution)/shard_map/ppermute | solution.py:37
  35.4 11.2 %collective-permute-start.5 = (bf16[520,336]{1,0:T(8,128)(2,1)S(1)}, bf16[520,336]{1,0:T(8,128)(2,1)S(1)}, u32[]{:S(2)}, u32[]{:S(2)}) collective-permute-start(bf16[520,336]{1,0:T(8,128)(2,1)S(1)} %collective-permute-done.4), channel_id=1, source_target_pairs={{0,2},{2,4},{4,6},{6,8},{8,10},{10,12},{12,14},{14,0},{1,3},{3,5},... | collective-permute-start | bytes 1048328 | tf_op jit(solution)/shard_map/ppermute | solution.py:34
  38.4 12.0 %collective-permute-start.2 = (bf16[520,336]{1,0:T(8,128)(2,1)S(1)}, bf16[520,336]{1,0:T(8,128)(2,1)S(1)}, u32[]{:S(2)}, u32[]{:S(2)}) collective-permute-start(bf16[520,336]{1,0:T(8,128)(2,1)S(1)} %collective-permute-done.1), channel_id=1, source_target_pairs={{0,14},{2,0},{4,2},{6,4},{8,6},{10,8},{12,10},{14,12},{1,15},{3,1}... | collective-permute-start | bytes 1048328 | tf_op jit(solution)/shard_map/ppermute | solution.py:37
  46.5 10.6 %collective-permute-start.6 = (bf16[520,336]{1,0:T(8,128)(2,1)S(1)}, bf16[520,336]{1,0:T(8,128)(2,1)S(1)}, u32[]{:S(2)}, u32[]{:S(2)}) collective-permute-start(bf16[520,336]{1,0:T(8,128)(2,1)S(1)} %collective-permute-done.5), channel_id=1, source_target_pairs={{0,2},{2,4},{4,6},{6,8},{8,10},{10,12},{12,14},{14,0},{1,3},{3,5},... | collective-permute-start | bytes 1048328 | tf_op jit(solution)/shard_map/ppermute | solution.py:34
  68.1 12.5 %collective-permute-start.7 = (bf16[520,2688]{1,0:T(8,128)(2,1)S(1)}, bf16[520,2688]{1,0:T(8,128)(2,1)}, u32[]{:S(2)}, u32[]{:S(2)}) collective-permute-start(bf16[520,2688]{1,0:T(8,128)(2,1)S(1)} %constant_dynamic-slice_fusion), channel_id=1, source_target_pairs={{0,1},{1,0},{2,3},{3,2},{4,5},{5,4},{6,7},{7,6},{8,9},{9,8},{10,11... | collective-permute-start | bytes 8386568 | tf_op jit(solution)/shard_map/ppermute | solution.py:34
  85.7 2.5 %copy-start = (bf16[520,5376]{1,0:T(8,128)(2,1)}, bf16[520,5376]{1,0:T(8,128)(2,1)S(1)}, u32[]{:S(2)}) copy-start(bf16[520,5376]{1,0:T(8,128)(2,1)S(1)} %fusion.5) | copy-start | bytes 16773124
  88.2 24.9 %copy-start.2 = (f32[5376]{0:T(1024)}, f32[5376]{0:T(1024)S(1)}, u32[]{:S(2)}) copy-start(f32[5376]{0:T(1024)S(1)} %fusion.39) | copy-start | bytes 64516
  108.5 4.7 %slice-start = ((s8[5591040]{0:T(1024)(128)(4,1)}), s8[4194304]{0:T(1024)(128)(4,1)S(1)}, s32[]{:S(2)}) async-start(s8[5591040]{0:T(1024)(128)(4,1)} %bitcast.60), calls=%async_computation.1 | async-start | bytes 8388608
  111.7 1.5 %slice-start.1 = ((s8[5591040]{0:T(1024)(128)(4,1)}), s8[1396736]{0:T(1024)(128)(4,1)S(1)}, s32[]{:S(2)}) async-start(s8[5591040]{0:T(1024)(128)(4,1)} %bitcast.60), calls=%async_computation.2 | async-start | bytes 2793472
  113.2 2.1 %copy-start.3 = (f32[128]{0:T(128)S(1)}, f32[128]{0:T(128)}, u32[]{:S(2)}) copy-start(f32[128]{0:T(128)} %param.10) | copy-start | bytes 1540
  116.0 15.0 %collective-permute-start.8 = (bf16[512,2,128]{0,2,1:T(8,128)(2,1)S(1)}, bf16[512,2,128]{0,2,1:T(8,128)(2,1)}, u32[]{:S(2)}, u32[]{:S(2)}) collective-permute-start(bf16[512,2,128]{0,2,1:T(8,128)(2,1)S(1)} %pad_maximum_fusion), channel_id=1, source_target_pairs={{0,32},{16,48},{32,64},{48,80},{64,96},{80,112},{96,128},{112,144}... | collective-permute-start | bytes 786440 | tf_op jit(solution)/shard_map/ppermute | solution.py:23
  119.7 11.2 %collective-permute-start.9 = (bf16[512,2,128]{0,2,1:T(8,128)(2,1)S(1)}, bf16[512,2,128]{0,2,1:T(8,128)(2,1)}, u32[]{:S(2)}, u32[]{:S(2)}) collective-permute-start(bf16[512,2,128]{0,2,1:T(8,128)(2,1)S(1)} %pad_maximum_fusion), channel_id=1, source_target_pairs={{0,16},{16,32},{32,48},{48,64},{64,80},{80,96},{96,112},{112,128},... | collective-permute-start | bytes 786440 | tf_op jit(solution)/shard_map/ppermute | solution.py:23
  125.5 5.2 %copy-start.4 = (f32[128]{0:T(128)S(1)}, f32[128]{0:T(128)}, u32[]{:S(2)}) copy-start(f32[128]{0:T(128)} %param.9) | copy-start | bytes 1540
  125.5 6.5 %copy-start.1 = (pred[512,1536]{0,1:T(8,128)(4,1)S(1)}, pred[512,1536]{0,1:T(8,128)(4,1)}, u32[]{:S(2)}) copy-start(pred[512,1536]{0,1:T(8,128)(4,1)} %fusion.16) | copy-start | bytes 2359300
Sparse Core Ops, SparseCore 0:
  10.5 96.8 all-gather.1

commit v10 on v9

--- a/solution.py
+++ b/solution.py
@@ -14,7 +14,7 @@
 ROPE_BASE = 10000.0
 
 
-ROW = ("rz", "rx")
+ROW = ("rz", "rxh", "rxl")
 
 
 def shifted(array, axis, by):
@@ -88,7 +88,8 @@
         ],
         axis=0,
     )
-    slabs = lax.all_gather(padded, ROW, axis=0, tiled=True).reshape(-1, aligned, weight_cols)
+    (paired,) = ring_gather((padded,), "rxl", (0,))
+    slabs = lax.all_gather(paired, ("rz", "rxh"), axis=0, tiled=True).reshape(-1, aligned, weight_cols)
     largest = jnp.max(slabs[:, weight_rows].astype(jnp.float32), axis=0)
 
     def clipped_columns(first, last):
@@ -169,9 +170,12 @@
     minor = len({tuple(getattr(d, "coords", (0,)))[0] for d in mesh.devices[:, 0].flat})
     if rows % minor:
         minor = 1
+    pair = 2 if minor % 2 == 0 else 1
     split = Mesh(
-        mesh.devices.reshape(rows // minor, minor, cols // CORES_PER_CHIP, CORES_PER_CHIP),
-        ("rz", "rx", "cy", "cc"),
+        mesh.devices.reshape(
+            rows // minor, minor // pair, pair, cols // CORES_PER_CHIP, CORES_PER_CHIP
+        ),
+        ("rz", "rxh", "rxl", "cy", "cc"),
     )
     col = ("cy", "cc")
     placed = (

time: 145 us -> 179 us (1.23)
  waiting for transfers between devices: 37.1 us -> 65 us
  starting transfers between devices: 40.8 us -> 45.3 us
    all_gather x1, waiting for transfers between devices: 18 us -> 41.9 us  [local(): lax.all_gather(paired, ('rz', 'rxh'), axis=0, tiled=True)]
    ppermute x5 -> x6, waiting for transfers between devices: 17.4 us -> 22.3 us  [ring_gather(): forward = lax.ppermute(forward, axis, right)]
    ppermute x5 -> x6, starting transfers between devices: 21.1 us -> 25.4 us  [ring_gather(): forward = lax.ppermute(forward, axis, right)]
    dynamic_slice x1 -> x2, local copies, waits for them, and re-layouts: 3.28 us -> 4.07 us  [ring_gather(): lax.dynamic_slice_in_dim(doubled, start * size, peers * size, dim)]
    concatenate x1 -> x2, local copies, waits for them, and re-layouts: 7.61 us -> 8.03 us  [ring_gather(): doubled = jnp.concatenate([stacked, stacked], axis=dim)]
  transfers between devices with their start and end apart: 11 -> 12, of which waited for: 7 -> 8; matrix products, arithmetic and copies ran while one was open for 22% -> 18% of each run, Pallas kernels for 0% -> 0%
where the time goes in v10:
time: 179 us; the launch traced here: 176 us
  waiting for transfers between devices  65 us (36%)
  starting transfers between devices  45.3 us (25%)
  local copies, waits for them, and re-layouts  26.2 us (15%)
  between operations  14.5 us (8%)
  other arithmetic  14.2 us (8%)
  matrix products  10.9 us (6%)
    all_gather x1, waiting for transfers between devices, local(): lax.all_gather(paired, ('rz', 'rxh'), axis=0, tiled=True)  41.9 us
    ppermute x6, starting transfers between devices, ring_gather(): forward = lax.ppermute(forward, axis, right)  25.4 us
    ppermute x6, waiting for transfers between devices, ring_gather(): forward = lax.ppermute(forward, axis, right)  22.3 us
    ppermute x3, starting transfers between devices, ring_gather(): backward = lax.ppermute(backward, axis, left)  13.3 us
    concatenate x2, local copies, waits for them, and re-layouts, ring_gather(): doubled = jnp.concatenate([stacked, stacked], axis=dim)  8.03 us
    ppermute x2, starting transfers between devices, shifted(): return lax.ppermute(array, axis, pairs)  6.6 us
    dot_general x1, matrix products, local(): jnp.dot(whole, ordered(0, query_cols), preferred_element_type=jnp.float32)  5.2 us
    unnamed x17, local copies, waits for them, and re-layouts  5.17 us
  transfers between devices with their start and end apart: 12, of which 8 were waited for; matrix products, arithmetic and copies ran while one was open for 18% of the time, Pallas kernels for 0%

profile of v10, /device:TPU:1, one launch (start us, length us, event | category | flops | bytes accessed | tf_op | source)
XLA Modules:
  0.0 176.2 jit_solution(12630162587578303962)
XLA Ops:
  9.1 3.9 %collective-permute-start.8 = (bf16[176,512]{1,0:T(8,128)(2,1)S(1)}, bf16[176,512]{1,0:T(8,128)(2,1)S(1)}, u32[]{:S(2)}, u32[]{:S(2)}) collective-permute-start(bf16[176,512]{1,0:T(8,128)(2,1)S(1)} %pad_maximum_fusion.1), channel_id=1, source_target_pairs={{0,16},{16,0},{1,17},{17,1},{2,18},{18,2},{3,19},{19,3},{4,20},{20... | collective-permute-start | bytes 540680 | tf_op jit(solution)/shard_map/ppermute | solution.py:34
  13.1 2.9 %collective-permute-done.8 = bf16[176,512]{1,0:T(8,128)(2,1)S(1)} collective-permute-done((bf16[176,512]{1,0:T(8,128)(2,1)S(1)}, bf16[176,512]{1,0:T(8,128)(2,1)S(1)}, u32[]{:S(2)}, u32[]{:S(2)}) %collective-permute-start.8) | collective-permute-done | bytes 180256 | tf_op jit(solution)/shard_map/ppermute | solution.py:34
  19.4 4.5 %collective-permute-start.3 = (bf16[520,336]{1,0:T(8,128)(2,1)S(1)}, bf16[520,336]{1,0:T(8,128)(2,1)S(1)}, u32[]{:S(2)}, u32[]{:S(2)}) collective-permute-start(bf16[520,336]{1,0:T(8,128)(2,1)S(1)} %concatenate.49), channel_id=1, source_target_pairs={{0,2},{2,4},{4,6},{6,8},{8,10},{10,12},{12,14},{14,0},{1,3},{3,5},... | collective-permute-start | bytes 1048328 | tf_op jit(solution)/shard_map/ppermute | solution.py:34
  23.9 3.8 %collective-permute-start = (bf16[520,336]{1,0:T(8,128)(2,1)S(1)}, bf16[520,336]{1,0:T(8,128)(2,1)S(1)}, u32[]{:S(2)}, u32[]{:S(2)}) collective-permute-start(bf16[520,336]{1,0:T(8,128)(2,1)S(1)} %concatenate.49), channel_id=1, source_target_pairs={{0,14},{2,0},{4,2},{6,4},{8,6},{10,8},{12,10},{14,12},{1,15},{3,1}... | collective-permute-start | bytes 1048328 | tf_op jit(solution)/shard_map/ppermute | solution.py:37
  27.7 3.3 %collective-permute-done.3 = bf16[520,336]{1,0:T(8,128)(2,1)S(1)} collective-permute-done((bf16[520,336]{1,0:T(8,128)(2,1)S(1)}, bf16[520,336]{1,0:T(8,128)(2,1)S(1)}, u32[]{:S(2)}, u32[]{:S(2)}) %collective-permute-start.3) | collective-permute-done | bytes 349472 | tf_op jit(solution)/shard_map/ppermute | solution.py:34
  31.0 3.1 %collective-permute-start.4 = (bf16[520,336]{1,0:T(8,128)(2,1)S(1)}, bf16[520,336]{1,0:T(8,128)(2,1)S(1)}, u32[]{:S(2)}, u32[]{:S(2)}) collective-permute-start(bf16[520,336]{1,0:T(8,128)(2,1)S(1)} %collective-permute-done.3), channel_id=1, source_target_pairs={{0,2},{2,4},{4,6},{6,8},{8,10},{10,12},{12,14},{14,0},{1,3},{3,5},... | collective-permute-start | bytes 1048328 | tf_op jit(solution)/shard_map/ppermute | solution.py:34
  34.1 4.7 %collective-permute-start.1 = (bf16[520,336]{1,0:T(8,128)(2,1)S(1)}, bf16[520,336]{1,0:T(8,128)(2,1)S(1)}, u32[]{:S(2)}, u32[]{:S(2)}) collective-permute-start(bf16[520,336]{1,0:T(8,128)(2,1)S(1)} %collective-permute-done), channel_id=1, source_target_pairs={{0,14},{2,0},{4,2},{6,4},{8,6},{10,8},{12,10},{14,12},{1,15},{3,1}... | collective-permute-start | bytes 1048328 | tf_op jit(solution)/shard_map/ppermute | solution.py:37
  38.8 3.3 %collective-permute-done.4 = bf16[520,336]{1,0:T(8,128)(2,1)S(1)} collective-permute-done((bf16[520,336]{1,0:T(8,128)(2,1)S(1)}, bf16[520,336]{1,0:T(8,128)(2,1)S(1)}, u32[]{:S(2)}, u32[]{:S(2)}) %collective-permute-start.4) | collective-permute-done | bytes 349472 | tf_op jit(solution)/shard_map/ppermute | solution.py:34
  42.1 2.1 %collective-permute-start.5 = (bf16[520,336]{1,0:T(8,128)(2,1)S(1)}, bf16[520,336]{1,0:T(8,128)(2,1)S(1)}, u32[]{:S(2)}, u32[]{:S(2)}) collective-permute-start(bf16[520,336]{1,0:T(8,128)(2,1)S(1)} %collective-permute-done.4), channel_id=1, source_target_pairs={{0,2},{2,4},{4,6},{6,8},{8,10},{10,12},{12,14},{14,0},{1,3},{3,5},... | collective-permute-start | bytes 1048328 | tf_op jit(solution)/shard_map/ppermute | solution.py:34
  44.2 4.7 %collective-permute-start.2 = (bf16[520,336]{1,0:T(8,128)(2,1)S(1)}, bf16[520,336]{1,0:T(8,128)(2,1)S(1)}, u32[]{:S(2)}, u32[]{:S(2)}) collective-permute-start(bf16[520,336]{1,0:T(8,128)(2,1)S(1)} %collective-permute-done.1), channel_id=1, source_target_pairs={{0,14},{2,0},{4,2},{6,4},{8,6},{10,8},{12,10},{14,12},{1,15},{3,1}... | collective-permute-start | bytes 1048328 | tf_op jit(solution)/shard_map/ppermute | solution.py:37
  49.0 3.6 %collective-permute-done.5 = bf16[520,336]{1,0:T(8,128)(2,1)S(1)} collective-permute-done((bf16[520,336]{1,0:T(8,128)(2,1)S(1)}, bf16[520,336]{1,0:T(8,128)(2,1)S(1)}, u32[]{:S(2)}, u32[]{:S(2)}) %collective-permute-start.5) | collective-permute-done | bytes 349472 | tf_op jit(solution)/shard_map/ppermute | solution.py:34
  55.2 8.4 %collective-permute-done.6 = bf16[520,336]{1,0:T(8,128)(2,1)S(1)} collective-permute-done((bf16[520,336]{1,0:T(8,128)(2,1)S(1)}, bf16[520,336]{1,0:T(8,128)(2,1)S(1)}, u32[]{:S(2)}, u32[]{:S(2)}) %collective-permute-start.6) | collective-permute-done | bytes 349472 | tf_op jit(solution)/shard_map/ppermute | solution.py:34
  63.6 7.7 %concatenate.50 = bf16[520,5376]{1,0:T(8,128)(2,1)} concatenate(bf16[520,336]{1,0:T(8,128)(2,1)S(1)} %concatenate.49, bf16[520,336]{1,0:T(8,128)(2,1)S(1)} %collective-permute-done, bf16[520,336]{1,0:T(8,128)(2,1)S(1)} %collective-permute-done.1, bf16[520,336]{1,0:T(8,128)(2,1)S(1)} %collective-permute-done.2, bf16[520,336]{1,0:T(8,128)(2,1)S(1)} %collective-permute-done.6, ...), dimensions={1} | concatenate | bytes 11182080 | tf_op jit(solution)/shard_map/concatenate | solution.py:43
  71.3 3.3 %constant_dynamic-slice_fusion.1 = bf16[520,2688]{1,0:T(8,128)(2,1)S(1)} fusion(bf16[520,5376]{1,0:T(8,128)(2,1)} %concatenate.50, s32[]{:T(128)S(6)} %select_n.29), kind=kLoop, calls=%fused_computation.80 | loop fusion | bytes 5591044 | tf_op jit(solution)/shard_map/dynamic_slice | solution.py:45
  74.6 9.8 %collective-permute-start.7 = (bf16[520,2688]{1,0:T(8,128)(2,1)S(1)}, bf16[520,2688]{1,0:T(8,128)(2,1)}, u32[]{:S(2)}, u32[]{:S(2)}) collective-permute-start(bf16[520,2688]{1,0:T(8,128)(2,1)S(1)} %constant_dynamic-slice_fusion.1), channel_id=1, source_target_pairs={{0,1},{1,0},{2,3},{3,2},{4,5},{5,4},{6,7},{7,6},{8,9},{9,8},{10,11... | collective-permute-start | bytes 8386568 | tf_op jit(solution)/shard_map/ppermute | solution.py:34
  89.1 5.2 %fusion.5 = bf16[520,5376]{1,0:T(8,128)(2,1)S(1)} fusion(s32[]{:T(128)S(6)} %select_n.31, bf16[520,2688]{1,0:T(8,128)(2,1)S(1)} %constant_dynamic-slice_fusion.1, bf16[520,2688]{1,0:T(8,128)(2,1)} %collective-permute-done.7), kind=kLoop, calls=%fused_computation.13 | loop fusion | flops 22364160 | bytes 11182084 | tf_op jit(solution)/shard_map/concatenate | solution.py:43
  94.4 2.3 %copy-done = bf16[520,5376]{1,0:T(8,128)(2,1)} copy-done((bf16[520,5376]{1,0:T(8,128)(2,1)}, bf16[520,5376]{1,0:T(8,128)(2,1)S(1)}, u32[]{:S(2)}) %copy-start) | copy-done | bytes 5591064
  97.8 41.9 %all-gather.2.cloned.1.call-done = bf16[5632,512]{1,0:T(8,128)(2,1)} async-done(((bf16[352,512]{1,0:T(8,128)(2,1)}), bf16[5632,512]{1,0:T(8,128)(2,1)}) %all-gather.2.cloned.1.call-update) | async-done | bytes 5767184 | tf_op jit(solution)/shard_map/all_gather | solution.py:92
  139.8 3.2 %fusion.47 = (bf16[32,168,256]{2,1,0:T(8,128)(2,1)S(1)}, bf16[32,168,256]{2,1,0:T(8,128)(2,1)S(1)}) fusion(bf16[32,176,512]{2,1,0:T(8,128)(2,1)} %bitcast.65), kind=kLoop, calls=%fused_computation.91 | loop fusion | bytes 11010048 | tf_op jit(solution)/shard_map/slice | solution.py:96
  145.6 2.0 %fusion.23 = f32[512,256]{0,1:T(8,128)S(1)} fusion(bf16[5376,256]{1,0:T(8,128)(2,1)S(1)} %bitcast.68, f32[5376]{0:T(1024)S(1)} %fusion.39, f32[512]{0:T(512)S(1)} %add_rsqrt_fusion.2, bf16[520,5376]{1,0:T(8,128)(2,1)S(1)} %bitcast.61), kind=kOutput, calls=%fused_computation.32 | convolution fusion | flops 1420296192 | bytes 8808448 | tf_op jit(solution)/shard_map/dot_general | solution.py:124
  148.4 2.9 %collective-permute-start.10 = (bf16[512,2,128]{0,2,1:T(8,128)(2,1)S(1)}, bf16[512,2,128]{0,2,1:T(8,128)(2,1)}, u32[]{:S(2)}, u32[]{:S(2)}) collective-permute-start(bf16[512,2,128]{0,2,1:T(8,128)(2,1)S(1)} %pad_maximum_fusion), channel_id=1, source_target_pairs={{0,16},{16,32},{32,48},{48,64},{64,80},{80,96},{96,112},{112,128},... | collective-permute-start | bytes 786440 | tf_op jit(solution)/shard_map/ppermute | solution.py:23
  151.3 3.7 %collective-permute-start.9 = (bf16[512,2,128]{0,2,1:T(8,128)(2,1)S(1)}, bf16[512,2,128]{0,2,1:T(8,128)(2,1)}, u32[]{:S(2)}, u32[]{:S(2)}) collective-permute-start(bf16[512,2,128]{0,2,1:T(8,128)(2,1)S(1)} %pad_maximum_fusion), channel_id=1, source_target_pairs={{0,32},{16,48},{32,64},{48,80},{64,96},{80,112},{96,128},{112,144}... | collective-permute-start | bytes 786440 | tf_op jit(solution)/shard_map/ppermute | solution.py:23
  155.2 3.0 %copy.46 = bf16[256,5376]{1,0:T(8,128)(2,1)} copy(bf16[256,5376]{0,1:T(8,128)(2,1)S(1)} %bitcast.64) | data formatting | bytes 5505024 | tf_op jit(solution)/shard_map/dot_general | solution.py:129
  158.2 5.2 %multiply_reduce_fusion = (f32[512,2]{0,1:T(2,128)S(1)}, f32[512,2,128]{0,2,1:T(8,128)S(1)}) fusion(bf16[2,128,5376]{2,1,0:T(8,128)(2,1)} %bitcast.67, f32[5376]{0:T(1024)} %copy-done.2, f32[512]{0:T(512)S(1)} %add_rsqrt_fusion.2, bf16[520,5376]{1,0:T(8,128)(2,1)} %copy-done), kind=kOutput, calls=%fused_computation.35 | convolution fusion | flops 1420557312 | bytes 8812544 | tf_op jit(solution)/shard_map/dot_general | solution.py:129
  (70 shorter events, 23.2 us)
Async XLA Ops:
  6.5 133.2 %all-gather.2.cloned.1.call-start = ((), (), s32[]{:S(2)}) async-start(), calls=%async_computation | async-start | bytes 6127616 | tf_op jit(solution)/shard_map/all_gather | solution.py:92
  9.1 6.8 %collective-permute-start.8 = (bf16[176,512]{1,0:T(8,128)(2,1)S(1)}, bf16[176,512]{1,0:T(8,128)(2,1)S(1)}, u32[]{:S(2)}, u32[]{:S(2)}) collective-permute-start(bf16[176,512]{1,0:T(8,128)(2,1)S(1)} %pad_maximum_fusion.1), channel_id=1, source_target_pairs={{0,16},{16,0},{1,17},{17,1},{2,18},{18,2},{3,19},{19,3},{4,20},{20... | collective-permute-start | bytes 540680 | tf_op jit(solution)/shard_map/ppermute | solution.py:34
  19.4 11.6 %collective-permute-start.3 = (bf16[520,336]{1,0:T(8,128)(2,1)S(1)}, bf16[520,336]{1,0:T(8,128)(2,1)S(1)}, u32[]{:S(2)}, u32[]{:S(2)}) collective-permute-start(bf16[520,336]{1,0:T(8,128)(2,1)S(1)} %concatenate.49), channel_id=1, source_target_pairs={{0,2},{2,4},{4,6},{6,8},{8,10},{10,12},{12,14},{14,0},{1,3},{3,5},... | collective-permute-start | bytes 1048328 | tf_op jit(solution)/shard_map/ppermute | solution.py:34
  23.9 10.2 %collective-permute-start = (bf16[520,336]{1,0:T(8,128)(2,1)S(1)}, bf16[520,336]{1,0:T(8,128)(2,1)S(1)}, u32[]{:S(2)}, u32[]{:S(2)}) collective-permute-start(bf16[520,336]{1,0:T(8,128)(2,1)S(1)} %concatenate.49), channel_id=1, source_target_pairs={{0,14},{2,0},{4,2},{6,4},{8,6},{10,8},{12,10},{14,12},{1,15},{3,1}... | collective-permute-start | bytes 1048328 | tf_op jit(solution)/shard_map/ppermute | solution.py:37
  31.0 11.1 %collective-permute-start.4 = (bf16[520,336]{1,0:T(8,128)(2,1)S(1)}, bf16[520,336]{1,0:T(8,128)(2,1)S(1)}, u32[]{:S(2)}, u32[]{:S(2)}) collective-permute-start(bf16[520,336]{1,0:T(8,128)(2,1)S(1)} %collective-permute-done.3), channel_id=1, source_target_pairs={{0,2},{2,4},{4,6},{6,8},{8,10},{10,12},{12,14},{14,0},{1,3},{3,5},... | collective-permute-start | bytes 1048328 | tf_op jit(solution)/shard_map/ppermute | solution.py:34
  34.1 10.1 %collective-permute-start.1 = (bf16[520,336]{1,0:T(8,128)(2,1)S(1)}, bf16[520,336]{1,0:T(8,128)(2,1)S(1)}, u32[]{:S(2)}, u32[]{:S(2)}) collective-permute-start(bf16[520,336]{1,0:T(8,128)(2,1)S(1)} %collective-permute-done), channel_id=1, source_target_pairs={{0,14},{2,0},{4,2},{6,4},{8,6},{10,8},{12,10},{14,12},{1,15},{3,1}... | collective-permute-start | bytes 1048328 | tf_op jit(solution)/shard_map/ppermute | solution.py:37
  42.1 10.5 %collective-permute-start.5 = (bf16[520,336]{1,0:T(8,128)(2,1)S(1)}, bf16[520,336]{1,0:T(8,128)(2,1)S(1)}, u32[]{:S(2)}, u32[]{:S(2)}) collective-permute-start(bf16[520,336]{1,0:T(8,128)(2,1)S(1)} %collective-permute-done.4), channel_id=1, source_target_pairs={{0,2},{2,4},{4,6},{6,8},{8,10},{10,12},{12,14},{14,0},{1,3},{3,5},... | collective-permute-start | bytes 1048328 | tf_op jit(solution)/shard_map/ppermute | solution.py:34
  44.2 11.0 %collective-permute-start.2 = (bf16[520,336]{1,0:T(8,128)(2,1)S(1)}, bf16[520,336]{1,0:T(8,128)(2,1)S(1)}, u32[]{:S(2)}, u32[]{:S(2)}) collective-permute-start(bf16[520,336]{1,0:T(8,128)(2,1)S(1)} %collective-permute-done.1), channel_id=1, source_target_pairs={{0,14},{2,0},{4,2},{6,4},{8,6},{10,8},{12,10},{14,12},{1,15},{3,1}... | collective-permute-start | bytes 1048328 | tf_op jit(solution)/shard_map/ppermute | solution.py:37
  52.6 11.0 %collective-permute-start.6 = (bf16[520,336]{1,0:T(8,128)(2,1)S(1)}, bf16[520,336]{1,0:T(8,128)(2,1)S(1)}, u32[]{:S(2)}, u32[]{:S(2)}) collective-permute-start(bf16[520,336]{1,0:T(8,128)(2,1)S(1)} %collective-permute-done.5), channel_id=1, source_target_pairs={{0,2},{2,4},{4,6},{6,8},{8,10},{10,12},{12,14},{14,0},{1,3},{3,5},... | collective-permute-start | bytes 1048328 | tf_op jit(solution)/shard_map/ppermute | solution.py:34
  74.6 14.5 %collective-permute-start.7 = (bf16[520,2688]{1,0:T(8,128)(2,1)S(1)}, bf16[520,2688]{1,0:T(8,128)(2,1)}, u32[]{:S(2)}, u32[]{:S(2)}) collective-permute-start(bf16[520,2688]{1,0:T(8,128)(2,1)S(1)} %constant_dynamic-slice_fusion.1), channel_id=1, source_target_pairs={{0,1},{1,0},{2,3},{3,2},{4,5},{5,4},{6,7},{7,6},{8,9},{9,8},{10,11... | collective-permute-start | bytes 8386568 | tf_op jit(solution)/shard_map/ppermute | solution.py:34
  94.3 2.4 %copy-start = (bf16[520,5376]{1,0:T(8,128)(2,1)}, bf16[520,5376]{1,0:T(8,128)(2,1)S(1)}, u32[]{:S(2)}) copy-start(bf16[520,5376]{1,0:T(8,128)(2,1)S(1)} %fusion.5) | copy-start | bytes 16773124
  96.7 48.9 %copy-start.2 = (f32[5376]{0:T(1024)}, f32[5376]{0:T(1024)S(1)}, u32[]{:S(2)}) copy-start(f32[5376]{0:T(1024)S(1)} %fusion.39) | copy-start | bytes 64516
  139.8 5.8 %slice-start = ((s8[5591040]{0:T(1024)(128)(4,1)}), s8[4194304]{0:T(1024)(128)(4,1)S(1)}, s32[]{:S(2)}) async-start(s8[5591040]{0:T(1024)(128)(4,1)} %bitcast.60), calls=%async_computation.1 | async-start | bytes 8388608
  144.0 1.6 slice-start.1
  145.6 2.1 %copy-start.3 = (f32[128]{0:T(128)S(1)}, f32[128]{0:T(128)}, u32[]{:S(2)}) copy-start(f32[128]{0:T(128)} %param.10) | copy-start | bytes 1540
  148.4 15.2 %collective-permute-start.10 = (bf16[512,2,128]{0,2,1:T(8,128)(2,1)S(1)}, bf16[512,2,128]{0,2,1:T(8,128)(2,1)}, u32[]{:S(2)}, u32[]{:S(2)}) collective-permute-start(bf16[512,2,128]{0,2,1:T(8,128)(2,1)S(1)} %pad_maximum_fusion), channel_id=1, source_target_pairs={{0,16},{16,32},{32,48},{48,64},{64,80},{80,96},{96,112},{112,128},... | collective-permute-start | bytes 786440 | tf_op jit(solution)/shard_map/ppermute | solution.py:23
  151.3 12.3 %collective-permute-start.9 = (bf16[512,2,128]{0,2,1:T(8,128)(2,1)S(1)}, bf16[512,2,128]{0,2,1:T(8,128)(2,1)}, u32[]{:S(2)}, u32[]{:S(2)}) collective-permute-start(bf16[512,2,128]{0,2,1:T(8,128)(2,1)S(1)} %pad_maximum_fusion), channel_id=1, source_target_pairs={{0,32},{16,48},{32,64},{48,80},{64,96},{80,112},{96,128},{112,144}... | collective-permute-start | bytes 786440 | tf_op jit(solution)/shard_map/ppermute | solution.py:23
  158.2 5.2 %copy-start.4 = (f32[128]{0:T(128)S(1)}, f32[128]{0:T(128)}, u32[]{:S(2)}) copy-start(f32[128]{0:T(128)} %param.9) | copy-start | bytes 1540
  158.2 6.5 %copy-start.1 = (pred[512,1536]{0,1:T(8,128)(4,1)S(1)}, pred[512,1536]{0,1:T(8,128)(4,1)}, u32[]{:S(2)}) copy-start(pred[512,1536]{0,1:T(8,128)(4,1)} %fusion.16) | copy-start | bytes 2359300
Sparse Core Ops, SparseCore 0:
  17.2 122.5 all-gather.1

commit v11 on v7

--- a/solution.py
+++ b/solution.py
@@ -1,6 +1,7 @@
 import jax
 import jax.numpy as jnp
 from jax import lax
+from jax.experimental import pallas as pl
 from jax.sharding import Mesh, PartitionSpec as P
 
 D = 5376
@@ -46,6 +47,37 @@
     return tuple(out)
 
 
+def project_kernel(bound_ref, token_ref, slab_ref, out_ref):
+    @pl.when(pl.program_id(0) == 0)
+    def _():
+        out_ref[...] = jnp.zeros_like(out_ref)
+
+    bound = bound_ref[...]
+    total = out_ref[...]
+    for i in range(token_ref.shape[0]):
+        weight = slab_ref[i].astype(jnp.float32)
+        clipped = jnp.clip(weight, -bound, bound).astype(jnp.bfloat16)
+        total = total + jnp.dot(token_ref[i], clipped, preferred_element_type=jnp.float32)
+    out_ref[...] = total
+
+
+def project(bound, token_slabs, slabs):
+    count, rows, depth = token_slabs.shape
+    cols = slabs.shape[2]
+    group = SLABS_PER_STEP
+    return pl.pallas_call(
+        project_kernel,
+        grid=(count // group,),
+        in_specs=[
+            pl.BlockSpec((1, cols), lambda g: (0, 0)),
+            pl.BlockSpec((group, rows, depth), lambda g: (g, 0, 0)),
+            pl.BlockSpec((group, depth, cols), lambda g: (g, 0, 0)),
+        ],
+        out_specs=pl.BlockSpec((rows, cols), lambda g: (0, 0)),
+        out_shape=jax.ShapeDtypeStruct((rows, cols), jnp.float32),
+    )(bound, token_slabs, slabs)
+
+
 def clip_with(weight, largest):
     bound = CLIP_FRACTION * largest
     return jnp.clip(weight.astype(jnp.float32), -bound, bound).astype(jnp.bfloat16)
@@ -90,7 +122,7 @@
     )
     slabs = lax.all_gather(padded, ROW, axis=0, tiled=True).reshape(-1, aligned, weight_cols)
     largest = jnp.max(slabs[:, weight_rows].astype(jnp.float32), axis=0)
-    clipped = clip_with(slabs.reshape(-1, weight_cols), largest)
+
     rows_tokens, piece = tokens.shape
     cores = lax.axis_size("cc")
     high = gain.astype(jnp.bfloat16)
@@ -109,17 +141,17 @@
     inverse = lax.rsqrt(squares / D + EPS)[:, None]
     normed = (widened * inverse * full_gain[None, :]).astype(jnp.bfloat16)
     halves = piece // weight_rows
-    whole = jnp.pad(
+    token_slabs = jnp.pad(
         normed.reshape(rows_tokens, cores, blocks, halves, weight_rows)
-        .transpose(0, 2, 1, 3, 4)
-        .reshape(rows_tokens, -1, weight_rows),
+        .transpose(2, 1, 3, 0, 4)
+        .reshape(-1, rows_tokens, weight_rows),
         ((0, 0), (0, 0), (0, aligned - weight_rows)),
-    ).reshape(rows_tokens, -1)
-    ordered = clipped
-    kv_part = jnp.dot(whole, ordered[:, query_cols:], preferred_element_type=jnp.float32)
-    keys = kv_part[:, :key_cols]
-    values = kv_part[:, key_cols:]
-    query = jnp.dot(whole, ordered[:, :query_cols], preferred_element_type=jnp.float32)
+    )
+    bound = (CLIP_FRACTION * largest)[None, :]
+    projected = project(bound, token_slabs, slabs)
+    query = projected[:, :query_cols]
+    keys = projected[:, query_cols : query_cols + key_cols]
+    values = projected[:, query_cols + key_cols :]
     heads_local = query_cols // HD
     kv_local = key_cols // HD
     group = heads_local // kv_local
@@ -156,6 +188,7 @@
 CORES_PER_CHIP = 2
 GAIN_ROWS = 8
 TILE_ROWS = 16
+SLABS_PER_STEP = 4
 
 
 def solution(mesh):

time: 150 us -> 177 us (1.18)
  the two profiles are of different devices: /device:TPU:1 before, /device:TPU:257 now
where the time goes in v11:
time: 177 us; the launch traced here: 176 us
  local copies, waits for them, and re-layouts  38 us (21%)
  other arithmetic  37.8 us (21%)
  starting transfers between devices  36.3 us (21%)
  waiting for transfers between devices  34.3 us (19%)
  between operations  14.6 us (8%)
  Pallas kernels  11 us (6%)
  matrix products  3.89 us (2%)
    ppermute x5, waiting for transfers between devices, ring_gather(): forward = lax.ppermute(forward, axis, right)  18.9 us
    concatenate x1, other arithmetic, ring_gather(): doubled = jnp.concatenate([stacked, stacked], axis=dim)  17.3 us
    ppermute x5, starting transfers between devices, ring_gather(): forward = lax.ppermute(forward, axis, right)  15 us
    ppermute x3, starting transfers between devices, ring_gather(): backward = lax.ppermute(backward, axis, left)  14.4 us
    pallas_call x1, Pallas kernels, project(): pl.pallas_call(project_kernel, grid=(count // group,), in_specs=[pl.Block...  11 us
    transpose x1, local copies, waits for them, and re-layouts, local(): token_slabs = jnp.pad(normed.reshape(rows_tokens, cores, blocks, halves,...  10.8 us
    ppermute x2, waiting for transfers between devices, shifted(): return lax.ppermute(array, axis, pairs)  9.52 us
    pad x1, local copies, waits for them, and re-layouts, local(): jnp.pad(normed.reshape(rows_tokens, cores, blocks, halves, weight_rows).t...  8.57 us
  transfers between devices with their start and end apart: 11, of which 9 were waited for; matrix products, arithmetic and copies ran while one was open for 37% of the time, Pallas kernels for 0%

profile of v11, /device:TPU:257, one launch (start us, length us, event | category | flops | bytes accessed | tf_op | source)
XLA Modules:
  0.0 175.7 jit_solution(4462644251313334022)
XLA Ops:
  8.9 3.2 %collective-permute-start.3 = (bf16[520,336]{0,1:T(8,128)(2,1)S(1)}, bf16[520,336]{0,1:T(8,128)(2,1)S(1)}, u32[]{:S(2)}, u32[]{:S(2)}) collective-permute-start(bf16[520,336]{0,1:T(8,128)(2,1)S(1)} %concatenate.45), channel_id=1, source_target_pairs={{0,2},{2,4},{4,6},{6,8},{8,10},{10,12},{12,14},{14,0},{1,3},{3,5},... | collective-permute-start | bytes 1048328 | tf_op jit(solution)/shard_map/ppermute | solution.py:35
  15.5 3.8 %collective-permute-start = (bf16[520,336]{0,1:T(8,128)(2,1)S(1)}, bf16[520,336]{0,1:T(8,128)(2,1)S(1)}, u32[]{:S(2)}, u32[]{:S(2)}) collective-permute-start(bf16[520,336]{0,1:T(8,128)(2,1)S(1)} %concatenate.45), channel_id=1, source_target_pairs={{0,14},{2,0},{4,2},{6,4},{8,6},{10,8},{12,10},{14,12},{1,15},{3,1}... | collective-permute-start | bytes 1048328 | tf_op jit(solution)/shard_map/ppermute | solution.py:38
  19.3 4.3 %collective-permute-done.3 = bf16[520,336]{0,1:T(8,128)(2,1)S(1)} collective-permute-done((bf16[520,336]{0,1:T(8,128)(2,1)S(1)}, bf16[520,336]{0,1:T(8,128)(2,1)S(1)}, u32[]{:S(2)}, u32[]{:S(2)}) %collective-permute-start.3) | collective-permute-done | bytes 349472 | tf_op jit(solution)/shard_map/ppermute | solution.py:35
  25.5 2.4 %collective-permute-done = bf16[520,336]{0,1:T(8,128)(2,1)S(1)} collective-permute-done((bf16[520,336]{0,1:T(8,128)(2,1)S(1)}, bf16[520,336]{0,1:T(8,128)(2,1)S(1)}, u32[]{:S(2)}, u32[]{:S(2)}) %collective-permute-start) | collective-permute-done | bytes 349472 | tf_op jit(solution)/shard_map/ppermute | solution.py:38
  27.9 5.3 %collective-permute-start.1 = (bf16[520,336]{0,1:T(8,128)(2,1)S(1)}, bf16[520,336]{0,1:T(8,128)(2,1)S(1)}, u32[]{:S(2)}, u32[]{:S(2)}) collective-permute-start(bf16[520,336]{0,1:T(8,128)(2,1)S(1)} %collective-permute-done), channel_id=1, source_target_pairs={{0,14},{2,0},{4,2},{6,4},{8,6},{10,8},{12,10},{14,12},{1,15},{3,1}... | collective-permute-start | bytes 1048328 | tf_op jit(solution)/shard_map/ppermute | solution.py:38
  33.2 3.7 %collective-permute-done.4 = bf16[520,336]{0,1:T(8,128)(2,1)S(1)} collective-permute-done((bf16[520,336]{0,1:T(8,128)(2,1)S(1)}, bf16[520,336]{0,1:T(8,128)(2,1)S(1)}, u32[]{:S(2)}, u32[]{:S(2)}) %collective-permute-start.4) | collective-permute-done | bytes 349472 | tf_op jit(solution)/shard_map/ppermute | solution.py:35
  38.8 2.0 %collective-permute-done.1 = bf16[520,336]{0,1:T(8,128)(2,1)S(1)} collective-permute-done((bf16[520,336]{0,1:T(8,128)(2,1)S(1)}, bf16[520,336]{0,1:T(8,128)(2,1)S(1)}, u32[]{:S(2)}, u32[]{:S(2)}) %collective-permute-start.1) | collective-permute-done | bytes 349472 | tf_op jit(solution)/shard_map/ppermute | solution.py:38
  40.8 5.3 %collective-permute-start.2 = (bf16[520,336]{0,1:T(8,128)(2,1)S(1)}, bf16[520,336]{0,1:T(8,128)(2,1)S(1)}, u32[]{:S(2)}, u32[]{:S(2)}) collective-permute-start(bf16[520,336]{0,1:T(8,128)(2,1)S(1)} %collective-permute-done.1), channel_id=1, source_target_pairs={{0,14},{2,0},{4,2},{6,4},{8,6},{10,8},{12,10},{14,12},{1,15},{3,1}... | collective-permute-start | bytes 1048328 | tf_op jit(solution)/shard_map/ppermute | solution.py:38
  46.2 3.1 %collective-permute-done.5 = bf16[520,336]{0,1:T(8,128)(2,1)S(1)} collective-permute-done((bf16[520,336]{0,1:T(8,128)(2,1)S(1)}, bf16[520,336]{0,1:T(8,128)(2,1)S(1)}, u32[]{:S(2)}, u32[]{:S(2)}) %collective-permute-start.5) | collective-permute-done | bytes 349472 | tf_op jit(solution)/shard_map/ppermute | solution.py:35
  52.9 7.8 %collective-permute-done.6 = bf16[520,336]{0,1:T(8,128)(2,1)S(1)} collective-permute-done((bf16[520,336]{0,1:T(8,128)(2,1)S(1)}, bf16[520,336]{0,1:T(8,128)(2,1)S(1)}, u32[]{:S(2)}, u32[]{:S(2)}) %collective-permute-start.6) | collective-permute-done | bytes 349472 | tf_op jit(solution)/shard_map/ppermute | solution.py:35
  61.8 4.1 %copy.43 = bf16[520,2688]{1,0:T(8,128)(2,1)} copy(bf16[520,2688]{0,1:T(8,128)(2,1)S(1)} %constant_dynamic-slice_fusion) | data formatting | bytes 5591040 | tf_op jit(solution)/shard_map/dynamic_slice | solution.py:46
  65.9 6.0 %collective-permute-start.7 = (bf16[520,2688]{1,0:T(8,128)(2,1)}, bf16[520,2688]{1,0:T(8,128)(2,1)}, u32[]{:S(2)}, u32[]{:S(2)}) collective-permute-start(bf16[520,2688]{1,0:T(8,128)(2,1)} %copy.43), channel_id=1, source_target_pairs={{0,1},{1,0},{2,3},{3,2},{4,5},{5,4},{6,7},{7,6},{8,9},{9,8},{10,11... | collective-permute-start | bytes 8386568 | tf_op jit(solution)/shard_map/ppermute | solution.py:35
  77.0 5.4 %copy.44 = bf16[520,2688]{0,1:T(8,128)(2,1)} copy(bf16[520,2688]{1,0:T(8,128)(2,1)} %collective-permute-done.7) | data formatting | bytes 5591040 | tf_op jit(solution)/shard_map/ppermute | solution.py:35
  82.3 17.3 %fusion.5 = bf16[520,5376]{0,1:T(8,128)(2,1)S(1)} fusion(s32[]{:T(128)S(6)} %select_n.24, bf16[520,2688]{0,1:T(8,128)(2,1)S(1)} %constant_dynamic-slice_fusion, bf16[520,2688]{0,1:T(8,128)(2,1)} %copy.44), kind=kLoop, calls=%fused_computation.11 | loop fusion | flops 22364160 | bytes 11182084 | tf_op jit(solution)/shard_map/concatenate | solution.py:44
  101.0 2.3 %fusion.12 = f32[5376]{0:T(1024)S(1)} fusion(f32[3,5376]{0,1:T(8,128)S(1)} %slice_convert_fusion), kind=kLoop, calls=%fused_computation.23 | loop fusion | flops 10752 | bytes 86016 | tf_op jit(solution)/shard_map/add | solution.py:138
  103.3 4.1 %fusion.2 = bf16[512,5376]{0,1:T(8,128)(2,1)} fusion(f32[5376]{0:T(1024)S(1)} %fusion.12, f32[512]{0:T(512)S(1)} %add_rsqrt_fusion.2, bf16[520,5376]{0,1:T(8,128)(2,1)S(1)} %fusion.5), kind=kLoop, calls=%fused_computation.8 | loop fusion | flops 11010048 | bytes 11033600 | tf_op jit(solution)/shard_map/convert_element_type | solution.py:142
  107.3 10.8 %copy.46 = bf16[8,2,2,512,168]{4,3,2,1,0:T(8,128)(2,1)} copy(bf16[8,2,2,512,168]{3,4,2,0,1:T(8,128)(2,1)} %bitcast.52) | data formatting | bytes 11010048 | tf_op jit(solution)/shard_map/transpose | solution.py:146
  118.2 8.6 %pad.4.token_ref = bf16[32,512,176]{2,1,0:T(8,128)(2,1)} pad(bf16[32,512,168]{2,1,0:T(8,128)(2,1)} %bitcast.51, bf16[]{:T(256)} %constant.31.clone.1), padding=0_0x0_0x0_8 | pad | bytes 11272194 | tf_op jit(solution)/shard_map/jit(_pad)/pad | solution.py:144
  128.4 11.0 %shard_map.73 = f32[512,512]{1,0:T(8,128)} custom-call(f32[1,512]{1,0:T(1,128)} %bitcast.56, bf16[32,512,176]{2,1,0:T(8,128)(2,1)} %pad.4.token_ref, bf16[32,176,512]{2,1,0:T(8,128)(2,1)} %bitcast.54), custom_call_target="tpu_custom_call" | custom-call | tf_op jit(solution)/shard_map/pallas_call | solution.py:68
  144.0 4.7 %collective-permute-start.8 = (bf16[512,2,128]{2,0,1:T(8,128)(2,1)S(1)}, bf16[512,2,128]{2,0,1:T(8,128)(2,1)}, u32[]{:S(2)}, u32[]{:S(2)}) collective-permute-start(bf16[512,2,128]{2,0,1:T(8,128)(2,1)S(1)} %pad_maximum_fusion), channel_id=1, source_target_pairs={{0,32},{16,48},{32,64},{48,80},{64,96},{80,112},{96,128},{112,144}... | collective-permute-start | bytes 786440 | tf_op jit(solution)/shard_map/ppermute | solution.py:24
  148.6 2.2 %collective-permute-start.9 = (bf16[512,2,128]{2,0,1:T(8,128)(2,1)S(1)}, bf16[512,2,128]{2,0,1:T(8,128)(2,1)}, u32[]{:S(2)}, u32[]{:S(2)}) collective-permute-start(bf16[512,2,128]{2,0,1:T(8,128)(2,1)S(1)} %pad_maximum_fusion), channel_id=1, source_target_pairs={{0,16},{16,32},{32,48},{48,64},{64,80},{80,96},{96,112},{112,128},... | collective-permute-start | bytes 786440 | tf_op jit(solution)/shard_map/ppermute | solution.py:24
  153.5 3.6 %collective-permute-done.8 = bf16[512,2,128]{2,0,1:T(8,128)(2,1)} collective-permute-done((bf16[512,2,128]{2,0,1:T(8,128)(2,1)S(1)}, bf16[512,2,128]{2,0,1:T(8,128)(2,1)}, u32[]{:S(2)}, u32[]{:S(2)}) %collective-permute-start.8) | collective-permute-done | bytes 262176 | tf_op jit(solution)/shard_map/ppermute | solution.py:24
  157.0 6.0 %collective-permute-done.9 = bf16[512,2,128]{2,0,1:T(8,128)(2,1)} collective-permute-done((bf16[512,2,128]{2,0,1:T(8,128)(2,1)S(1)}, bf16[512,2,128]{2,0,1:T(8,128)(2,1)}, u32[]{:S(2)}, u32[]{:S(2)}) %collective-permute-start.9) | collective-permute-done | bytes 262176 | tf_op jit(solution)/shard_map/ppermute | solution.py:24
  166.0 2.0 %fusion.13 = bf16[128,2,512]{2,0,1:T(8,128)(2,1)S(1)} fusion(f32[2,512]{1,0:T(2,128)S(1)} %get-tuple-element.16, f32[1536,512,2]{1,0,2:T(8,128)S(1)} %get-tuple-element.17, pred[512,1536]{0,1:T(8,128)(4,1)S(1)} %copy-done.2, bf16[1536,2,128]{2,0,1:T(8,128)(2,1)S(1)} %maximum_maximum_fusion), kind=kOutput, calls=%fused_computation.25 | convolution fusion | flops 409075712 | bytes 7737344 | tf_op jit(solution)/shard_map/kgts,skd->tkgd/dot_general | solution.py:184
  (78 shorter events, 32.5 us)
Async XLA Ops:
  6.5 120.2 %all-gather.2.cloned.1.call-start = ((), (), s32[]{:S(2)}) async-start(), calls=%async_computation | async-start | bytes 5947392 | tf_op jit(solution)/shard_map/all_gather | solution.py:123
  8.9 14.7 %collective-permute-start.3 = (bf16[520,336]{0,1:T(8,128)(2,1)S(1)}, bf16[520,336]{0,1:T(8,128)(2,1)S(1)}, u32[]{:S(2)}, u32[]{:S(2)}) collective-permute-start(bf16[520,336]{0,1:T(8,128)(2,1)S(1)} %concatenate.45), channel_id=1, source_target_pairs={{0,2},{2,4},{4,6},{6,8},{8,10},{10,12},{12,14},{14,0},{1,3},{3,5},... | collective-permute-start | bytes 1048328 | tf_op jit(solution)/shard_map/ppermute | solution.py:35
  15.5 12.4 %collective-permute-start = (bf16[520,336]{0,1:T(8,128)(2,1)S(1)}, bf16[520,336]{0,1:T(8,128)(2,1)S(1)}, u32[]{:S(2)}, u32[]{:S(2)}) collective-permute-start(bf16[520,336]{0,1:T(8,128)(2,1)S(1)} %concatenate.45), channel_id=1, source_target_pairs={{0,14},{2,0},{4,2},{6,4},{8,6},{10,8},{12,10},{14,12},{1,15},{3,1}... | collective-permute-start | bytes 1048328 | tf_op jit(solution)/shard_map/ppermute | solution.py:38
  23.6 13.3 %collective-permute-start.4 = (bf16[520,336]{0,1:T(8,128)(2,1)S(1)}, bf16[520,336]{0,1:T(8,128)(2,1)S(1)}, u32[]{:S(2)}, u32[]{:S(2)}) collective-permute-start(bf16[520,336]{0,1:T(8,128)(2,1)S(1)} %collective-permute-done.3), channel_id=1, source_target_pairs={{0,2},{2,4},{4,6},{6,8},{8,10},{10,12},{12,14},{14,0},{1,3},{3,5},... | collective-permute-start | bytes 1048328 | tf_op jit(solution)/shard_map/ppermute | solution.py:35
  27.9 12.9 %collective-permute-start.1 = (bf16[520,336]{0,1:T(8,128)(2,1)S(1)}, bf16[520,336]{0,1:T(8,128)(2,1)S(1)}, u32[]{:S(2)}, u32[]{:S(2)}) collective-permute-start(bf16[520,336]{0,1:T(8,128)(2,1)S(1)} %collective-permute-done), channel_id=1, source_target_pairs={{0,14},{2,0},{4,2},{6,4},{8,6},{10,8},{12,10},{14,12},{1,15},{3,1}... | collective-permute-start | bytes 1048328 | tf_op jit(solution)/shard_map/ppermute | solution.py:38
  36.9 12.4 %collective-permute-start.5 = (bf16[520,336]{0,1:T(8,128)(2,1)S(1)}, bf16[520,336]{0,1:T(8,128)(2,1)S(1)}, u32[]{:S(2)}, u32[]{:S(2)}) collective-permute-start(bf16[520,336]{0,1:T(8,128)(2,1)S(1)} %collective-permute-done.4), channel_id=1, source_target_pairs={{0,2},{2,4},{4,6},{6,8},{8,10},{10,12},{12,14},{14,0},{1,3},{3,5},... | collective-permute-start | bytes 1048328 | tf_op jit(solution)/shard_map/ppermute | solution.py:35
  40.8 12.0 %collective-permute-start.2 = (bf16[520,336]{0,1:T(8,128)(2,1)S(1)}, bf16[520,336]{0,1:T(8,128)(2,1)S(1)}, u32[]{:S(2)}, u32[]{:S(2)}) collective-permute-start(bf16[520,336]{0,1:T(8,128)(2,1)S(1)} %collective-permute-done.1), channel_id=1, source_target_pairs={{0,14},{2,0},{4,2},{6,4},{8,6},{10,8},{12,10},{14,12},{1,15},{3,1}... | collective-permute-start | bytes 1048328 | tf_op jit(solution)/shard_map/ppermute | solution.py:38
  49.3 11.5 %collective-permute-start.6 = (bf16[520,336]{0,1:T(8,128)(2,1)S(1)}, bf16[520,336]{0,1:T(8,128)(2,1)S(1)}, u32[]{:S(2)}, u32[]{:S(2)}) collective-permute-start(bf16[520,336]{0,1:T(8,128)(2,1)S(1)} %collective-permute-done.5), channel_id=1, source_target_pairs={{0,2},{2,4},{4,6},{6,8},{8,10},{10,12},{12,14},{14,0},{1,3},{3,5},... | collective-permute-start | bytes 1048328 | tf_op jit(solution)/shard_map/ppermute | solution.py:35
  65.9 11.1 %collective-permute-start.7 = (bf16[520,2688]{1,0:T(8,128)(2,1)}, bf16[520,2688]{1,0:T(8,128)(2,1)}, u32[]{:S(2)}, u32[]{:S(2)}) collective-permute-start(bf16[520,2688]{1,0:T(8,128)(2,1)} %copy.43), channel_id=1, source_target_pairs={{0,1},{1,0},{2,3},{3,2},{4,5},{5,4},{6,7},{7,6},{8,9},{9,8},{10,11... | collective-permute-start | bytes 8386568 | tf_op jit(solution)/shard_map/ppermute | solution.py:35
  128.4 13.1 %copy-start.3 = (f32[128]{0:T(128)S(1)}, f32[128]{0:T(128)}, u32[]{:S(2)}) copy-start(f32[128]{0:T(128)} %param.10) | copy-start | bytes 1540
  128.4 24.6 %copy-start.4 = (f32[128]{0:T(128)S(1)}, f32[128]{0:T(128)}, u32[]{:S(2)}) copy-start(f32[128]{0:T(128)} %param.9) | copy-start | bytes 1540
  139.3 13.9 %copy-start = (f32[512,64]{1,0:T(8,128)S(1)}, f32[512,64]{1,0:T(8,128)}, u32[]{:S(2)}) copy-start(f32[512,64]{1,0:T(8,128)} %get-tuple-element.11) | copy-start | bytes 393220
  139.3 13.9 %copy-start.1 = (f32[512,64]{1,0:T(8,128)S(1)}, f32[512,64]{1,0:T(8,128)}, u32[]{:S(2)}) copy-start(f32[512,64]{1,0:T(8,128)} %get-tuple-element.12) | copy-start | bytes 393220
  139.3 24.8 %copy-start.2 = (pred[512,1536]{0,1:T(8,128)(4,1)S(1)}, pred[512,1536]{0,1:T(8,128)(4,1)}, u32[]{:S(2)}) copy-start(pred[512,1536]{0,1:T(8,128)(4,1)} %fusion.10) | copy-start | bytes 2359300
  144.0 13.1 %collective-permute-start.8 = (bf16[512,2,128]{2,0,1:T(8,128)(2,1)S(1)}, bf16[512,2,128]{2,0,1:T(8,128)(2,1)}, u32[]{:S(2)}, u32[]{:S(2)}) collective-permute-start(bf16[512,2,128]{2,0,1:T(8,128)(2,1)S(1)} %pad_maximum_fusion), channel_id=1, source_target_pairs={{0,32},{16,48},{32,64},{48,80},{64,96},{80,112},{96,128},{112,144}... | collective-permute-start | bytes 786440 | tf_op jit(solution)/shard_map/ppermute | solution.py:24
  148.6 14.4 %collective-permute-start.9 = (bf16[512,2,128]{2,0,1:T(8,128)(2,1)S(1)}, bf16[512,2,128]{2,0,1:T(8,128)(2,1)}, u32[]{:S(2)}, u32[]{:S(2)}) collective-permute-start(bf16[512,2,128]{2,0,1:T(8,128)(2,1)S(1)} %pad_maximum_fusion), channel_id=1, source_target_pairs={{0,16},{16,32},{32,48},{48,64},{64,80},{80,96},{96,112},{112,128},... | collective-permute-start | bytes 786440 | tf_op jit(solution)/shard_map/ppermute | solution.py:24
Sparse Core Ops, SparseCore 0:
  15.6 89.5 all-gather.1

commit v12 on v9

--- a/solution.py
+++ b/solution.py
@@ -88,7 +88,9 @@
         ],
         axis=0,
     )
-    slabs = lax.all_gather(padded, ROW, axis=0, tiled=True).reshape(-1, aligned, weight_cols)
+    placed = jnp.zeros((lax.axis_size(ROW), aligned, weight_cols), padded.dtype)
+    placed = lax.dynamic_update_slice_in_dim(placed, padded[None], lax.axis_index(ROW), 0)
+    slabs = lax.psum(placed, ROW)
     largest = jnp.max(slabs[:, weight_rows].astype(jnp.float32), axis=0)
 
     def clipped_columns(first, last):

time: 145 us -> 310 us (2.14)
  waiting for transfers between devices: 37.1 us -> 198 us
    psum x0 -> x1, waiting for transfers between devices: none -> 183 us  [local(): slabs = lax.psum(placed, ROW)]
    all_gather x1 -> x0, waiting for transfers between devices: 18 us -> none  [local(): lax.all_gather(padded, ROW, axis=0, tiled=True)]
    broadcast_in_dim x0 -> x1, local copies, waits for them, and re-layouts: none -> 3.21 us  [local(): placed = jnp.zeros((lax.axis_size(ROW), aligned, weight_cols), padded.dtype)]
  transfers between devices with their start and end apart: 11 -> 11, of which waited for: 7 -> 5; matrix products, arithmetic and copies ran while one was open for 22% -> 8% of each run, Pallas kernels for 0% -> 0%
where the time goes in v12:
time: 310 us
  waiting for transfers between devices  198 us (64%)
  starting transfers between devices  43.1 us (14%)
  local copies, waits for them, and re-layouts  28.3 us (9%)
  other arithmetic  14.8 us (5%)
  between operations  14.5 us (5%)
  matrix products  10.9 us (4%)
    psum x1, waiting for transfers between devices, local(): slabs = lax.psum(placed, ROW)  183 us
    ppermute x5, starting transfers between devices, ring_gather(): forward = lax.ppermute(forward, axis, right)  21.5 us
    ppermute x5, waiting for transfers between devices, ring_gather(): forward = lax.ppermute(forward, axis, right)  15.2 us
    ppermute x3, starting transfers between devices, ring_gather(): backward = lax.ppermute(backward, axis, left)  13.2 us
    ppermute x2, starting transfers between devices, shifted(): return lax.ppermute(array, axis, pairs)  8.27 us
    concatenate x1, local copies, waits for them, and re-layouts, ring_gather(): doubled = jnp.concatenate([stacked, stacked], axis=dim)  7.58 us
  transfers between devices with their start and end apart: 11, of which 5 were waited for; matrix products, arithmetic and copies ran while one was open for 8% of the time, Pallas kernels for 0%

profile of v12, /device:TPU:1, one launch (start us, length us, event | category | flops | bytes accessed | tf_op | source)
XLA Modules:
  0.0 309.8 jit_solution(7325285267483653972)
XLA Ops:
  8.8 4.0 %collective-permute-start.3 = (bf16[520,336]{1,0:T(8,128)(2,1)S(1)}, bf16[520,336]{1,0:T(8,128)(2,1)S(1)}, u32[]{:S(2)}, u32[]{:S(2)}) collective-permute-start(bf16[520,336]{1,0:T(8,128)(2,1)S(1)} %concatenate.43), channel_id=1, source_target_pairs={{0,2},{2,4},{4,6},{6,8},{8,10},{10,12},{12,14},{14,0},{1,3},{3,5},... | collective-permute-start | bytes 1048328 | tf_op jit(solution)/shard_map/ppermute | solution.py:34
  12.8 3.8 %collective-permute-start = (bf16[520,336]{1,0:T(8,128)(2,1)S(1)}, bf16[520,336]{1,0:T(8,128)(2,1)S(1)}, u32[]{:S(2)}, u32[]{:S(2)}) collective-permute-start(bf16[520,336]{1,0:T(8,128)(2,1)S(1)} %concatenate.43), channel_id=1, source_target_pairs={{0,14},{2,0},{4,2},{6,4},{8,6},{10,8},{12,10},{14,12},{1,15},{3,1}... | collective-permute-start | bytes 1048328 | tf_op jit(solution)/shard_map/ppermute | solution.py:37
  16.6 3.3 %collective-permute-done.3 = bf16[520,336]{1,0:T(8,128)(2,1)S(1)} collective-permute-done((bf16[520,336]{1,0:T(8,128)(2,1)S(1)}, bf16[520,336]{1,0:T(8,128)(2,1)S(1)}, u32[]{:S(2)}, u32[]{:S(2)}) %collective-permute-start.3) | collective-permute-done | bytes 349472 | tf_op jit(solution)/shard_map/ppermute | solution.py:34
  19.9 4.0 %collective-permute-start.4 = (bf16[520,336]{1,0:T(8,128)(2,1)S(1)}, bf16[520,336]{1,0:T(8,128)(2,1)S(1)}, u32[]{:S(2)}, u32[]{:S(2)}) collective-permute-start(bf16[520,336]{1,0:T(8,128)(2,1)S(1)} %collective-permute-done.3), channel_id=1, source_target_pairs={{0,2},{2,4},{4,6},{6,8},{8,10},{10,12},{12,14},{14,0},{1,3},{3,5},... | collective-permute-start | bytes 1048328 | tf_op jit(solution)/shard_map/ppermute | solution.py:34
  23.9 4.7 %collective-permute-start.1 = (bf16[520,336]{1,0:T(8,128)(2,1)S(1)}, bf16[520,336]{1,0:T(8,128)(2,1)S(1)}, u32[]{:S(2)}, u32[]{:S(2)}) collective-permute-start(bf16[520,336]{1,0:T(8,128)(2,1)S(1)} %collective-permute-done), channel_id=1, source_target_pairs={{0,14},{2,0},{4,2},{6,4},{8,6},{10,8},{12,10},{14,12},{1,15},{3,1}... | collective-permute-start | bytes 1048328 | tf_op jit(solution)/shard_map/ppermute | solution.py:37
  28.7 3.3 %collective-permute-done.4 = bf16[520,336]{1,0:T(8,128)(2,1)S(1)} collective-permute-done((bf16[520,336]{1,0:T(8,128)(2,1)S(1)}, bf16[520,336]{1,0:T(8,128)(2,1)S(1)}, u32[]{:S(2)}, u32[]{:S(2)}) %collective-permute-start.4) | collective-permute-done | bytes 349472 | tf_op jit(solution)/shard_map/ppermute | solution.py:34
  31.9 3.1 collective-permute-start.5
  35.9 4.7 %collective-permute-start.2 = (bf16[520,336]{1,0:T(8,128)(2,1)S(1)}, bf16[520,336]{1,0:T(8,128)(2,1)S(1)}, u32[]{:S(2)}, u32[]{:S(2)}) collective-permute-start(bf16[520,336]{1,0:T(8,128)(2,1)S(1)} %collective-permute-done.1), channel_id=1, source_target_pairs={{0,14},{2,0},{4,2},{6,4},{8,6},{10,8},{12,10},{14,12},{1,15},{3,1}... | collective-permute-start | bytes 1048328 | tf_op jit(solution)/shard_map/ppermute | solution.py:37
  40.6 2.4 collective-permute-done.5
  43.0 2.1 collective-permute-start.6
  46.9 6.3 %collective-permute-done.6 = bf16[520,336]{1,0:T(8,128)(2,1)S(1)} collective-permute-done((bf16[520,336]{1,0:T(8,128)(2,1)S(1)}, bf16[520,336]{1,0:T(8,128)(2,1)S(1)}, u32[]{:S(2)}, u32[]{:S(2)}) %collective-permute-start.6) | collective-permute-done | bytes 349472 | tf_op jit(solution)/shard_map/ppermute | solution.py:34
  53.2 7.6 %concatenate.44 = bf16[520,5376]{1,0:T(8,128)(2,1)} concatenate(bf16[520,336]{1,0:T(8,128)(2,1)S(1)} %concatenate.43, bf16[520,336]{1,0:T(8,128)(2,1)S(1)} %collective-permute-done, bf16[520,336]{1,0:T(8,128)(2,1)S(1)} %collective-permute-done.1, bf16[520,336]{1,0:T(8,128)(2,1)S(1)} %collective-permute-done.2, bf16[520,336]{1,0:T(8,128)(2,1)S(1)} %collective-permute-done.6, ...), dimensions={1} | concatenate | bytes 11182080 | tf_op jit(solution)/shard_map/concatenate | solution.py:43
  60.7 3.3 %constant_dynamic-slice_fusion = bf16[520,2688]{1,0:T(8,128)(2,1)S(1)} fusion(bf16[520,5376]{1,0:T(8,128)(2,1)} %concatenate.44, s32[]{:T(128)S(6)} %select_n.25), kind=kLoop, calls=%fused_computation.80 | loop fusion | bytes 5591044 | tf_op jit(solution)/shard_map/dynamic_slice | solution.py:45
  64.0 8.3 %collective-permute-start.7 = (bf16[520,2688]{1,0:T(8,128)(2,1)S(1)}, bf16[520,2688]{1,0:T(8,128)(2,1)}, u32[]{:S(2)}, u32[]{:S(2)}) collective-permute-start(bf16[520,2688]{1,0:T(8,128)(2,1)S(1)} %constant_dynamic-slice_fusion), channel_id=1, source_target_pairs={{0,1},{1,0},{2,3},{3,2},{4,5},{5,4},{6,7},{7,6},{8,9},{9,8},{10,11... | collective-permute-start | bytes 8386568 | tf_op jit(solution)/shard_map/ppermute | solution.py:34
  72.4 3.2 %broadcast_in_dim.60 = bf16[32,176,512]{2,1,0:T(8,128)(2,1)} broadcast(bf16[]{:T(256)} %constant.29.clone.1), dimensions={} | broadcast | bytes 5767170 | tf_op jit(solution)/shard_map/broadcast_in_dim | solution.py:91
  80.2 5.2 %fusion.5 = bf16[520,5376]{1,0:T(8,128)(2,1)S(1)} fusion(s32[]{:T(128)S(6)} %select_n.27, bf16[520,2688]{1,0:T(8,128)(2,1)S(1)} %constant_dynamic-slice_fusion, bf16[520,2688]{1,0:T(8,128)(2,1)} %collective-permute-done.7), kind=kLoop, calls=%fused_computation.13 | loop fusion | flops 22364160 | bytes 11182084 | tf_op jit(solution)/shard_map/concatenate | solution.py:43
  85.4 2.3 copy-done
  88.9 182.9 %all-reduce.2.cloned.1.call-done = bf16[32,176,512]{2,1,0:T(8,128)(2,1)} async-done(((bf16[32,176,512]{2,1,0:T(8,128)(2,1)}), bf16[32,176,512]{2,1,0:T(8,128)(2,1)}) %all-reduce.2.cloned.1.call-update) | async-done | bytes 5767184 | tf_op jit(solution)/shard_map/psum | solution.py:93
  272.9 3.2 %fusion.48 = (bf16[32,168,256]{2,1,0:T(8,128)(2,1)S(1)}, bf16[32,168,256]{2,1,0:T(8,128)(2,1)S(1)}) fusion(bf16[32,176,512]{2,1,0:T(8,128)(2,1)} %all-reduce.2.cloned.1.call-done), kind=kLoop, calls=%fused_computation.91 | loop fusion | bytes 11010048 | tf_op jit(solution)/shard_map/slice | solution.py:97
  277.6 2.0 fusion.23
  280.4 5.4 %collective-permute-start.8 = (bf16[512,2,128]{0,2,1:T(8,128)(2,1)S(1)}, bf16[512,2,128]{0,2,1:T(8,128)(2,1)}, u32[]{:S(2)}, u32[]{:S(2)}) collective-permute-start(bf16[512,2,128]{0,2,1:T(8,128)(2,1)S(1)} %pad_maximum_fusion), channel_id=1, source_target_pairs={{0,32},{16,48},{32,64},{48,80},{64,96},{80,112},{96,128},{112,144}... | collective-permute-start | bytes 786440 | tf_op jit(solution)/shard_map/ppermute | solution.py:23
  285.7 2.9 collective-permute-start.9
  288.8 3.0 copy.46
  291.8 5.2 %multiply_reduce_fusion = (f32[512,2]{0,1:T(2,128)S(1)}, f32[512,2,128]{0,2,1:T(8,128)S(1)}) fusion(bf16[2,128,5376]{2,1,0:T(8,128)(2,1)} %bitcast.68, f32[5376]{0:T(1024)} %copy-done.2, f32[512]{0:T(512)S(1)} %add_rsqrt_fusion.2, bf16[520,5376]{1,0:T(8,128)(2,1)} %copy-done), kind=kOutput, calls=%fused_computation.35 | convolution fusion | flops 1420557312 | bytes 8812544 | tf_op jit(solution)/shard_map/dot_general | solution.py:130
  (68 shorter events, 19.3 us)
Async XLA Ops:
  6.5 265.3 %all-reduce.2.cloned.1.call-start = ((), (), s32[]{:S(2)}) async-start(), calls=%async_computation | async-start | bytes 11534336 | tf_op jit(solution)/shard_map/psum | solution.py:93
  8.8 11.1 %collective-permute-start.3 = (bf16[520,336]{1,0:T(8,128)(2,1)S(1)}, bf16[520,336]{1,0:T(8,128)(2,1)S(1)}, u32[]{:S(2)}, u32[]{:S(2)}) collective-permute-start(bf16[520,336]{1,0:T(8,128)(2,1)S(1)} %concatenate.43), channel_id=1, source_target_pairs={{0,2},{2,4},{4,6},{6,8},{8,10},{10,12},{12,14},{14,0},{1,3},{3,5},... | collective-permute-start | bytes 1048328 | tf_op jit(solution)/shard_map/ppermute | solution.py:34
  12.8 11.1 %collective-permute-start = (bf16[520,336]{1,0:T(8,128)(2,1)S(1)}, bf16[520,336]{1,0:T(8,128)(2,1)S(1)}, u32[]{:S(2)}, u32[]{:S(2)}) collective-permute-start(bf16[520,336]{1,0:T(8,128)(2,1)S(1)} %concatenate.43), channel_id=1, source_target_pairs={{0,14},{2,0},{4,2},{6,4},{8,6},{10,8},{12,10},{14,12},{1,15},{3,1}... | collective-permute-start | bytes 1048328 | tf_op jit(solution)/shard_map/ppermute | solution.py:37
  19.9 12.0 %collective-permute-start.4 = (bf16[520,336]{1,0:T(8,128)(2,1)S(1)}, bf16[520,336]{1,0:T(8,128)(2,1)S(1)}, u32[]{:S(2)}, u32[]{:S(2)}) collective-permute-start(bf16[520,336]{1,0:T(8,128)(2,1)S(1)} %collective-permute-done.3), channel_id=1, source_target_pairs={{0,2},{2,4},{4,6},{6,8},{8,10},{10,12},{12,14},{14,0},{1,3},{3,5},... | collective-permute-start | bytes 1048328 | tf_op jit(solution)/shard_map/ppermute | solution.py:34
  23.9 12.0 %collective-permute-start.1 = (bf16[520,336]{1,0:T(8,128)(2,1)S(1)}, bf16[520,336]{1,0:T(8,128)(2,1)S(1)}, u32[]{:S(2)}, u32[]{:S(2)}) collective-permute-start(bf16[520,336]{1,0:T(8,128)(2,1)S(1)} %collective-permute-done), channel_id=1, source_target_pairs={{0,14},{2,0},{4,2},{6,4},{8,6},{10,8},{12,10},{14,12},{1,15},{3,1}... | collective-permute-start | bytes 1048328 | tf_op jit(solution)/shard_map/ppermute | solution.py:37
  31.9 11.1 %collective-permute-start.5 = (bf16[520,336]{1,0:T(8,128)(2,1)S(1)}, bf16[520,336]{1,0:T(8,128)(2,1)S(1)}, u32[]{:S(2)}, u32[]{:S(2)}) collective-permute-start(bf16[520,336]{1,0:T(8,128)(2,1)S(1)} %collective-permute-done.4), channel_id=1, source_target_pairs={{0,2},{2,4},{4,6},{6,8},{8,10},{10,12},{12,14},{14,0},{1,3},{3,5},... | collective-permute-start | bytes 1048328 | tf_op jit(solution)/shard_map/ppermute | solution.py:34
  35.9 11.0 %collective-permute-start.2 = (bf16[520,336]{1,0:T(8,128)(2,1)S(1)}, bf16[520,336]{1,0:T(8,128)(2,1)S(1)}, u32[]{:S(2)}, u32[]{:S(2)}) collective-permute-start(bf16[520,336]{1,0:T(8,128)(2,1)S(1)} %collective-permute-done.1), channel_id=1, source_target_pairs={{0,14},{2,0},{4,2},{6,4},{8,6},{10,8},{12,10},{14,12},{1,15},{3,1}... | collective-permute-start | bytes 1048328 | tf_op jit(solution)/shard_map/ppermute | solution.py:37
  43.0 10.2 %collective-permute-start.6 = (bf16[520,336]{1,0:T(8,128)(2,1)S(1)}, bf16[520,336]{1,0:T(8,128)(2,1)S(1)}, u32[]{:S(2)}, u32[]{:S(2)}) collective-permute-start(bf16[520,336]{1,0:T(8,128)(2,1)S(1)} %collective-permute-done.5), channel_id=1, source_target_pairs={{0,2},{2,4},{4,6},{6,8},{8,10},{10,12},{12,14},{14,0},{1,3},{3,5},... | collective-permute-start | bytes 1048328 | tf_op jit(solution)/shard_map/ppermute | solution.py:34
  64.0 16.1 %collective-permute-start.7 = (bf16[520,2688]{1,0:T(8,128)(2,1)S(1)}, bf16[520,2688]{1,0:T(8,128)(2,1)}, u32[]{:S(2)}, u32[]{:S(2)}) collective-permute-start(bf16[520,2688]{1,0:T(8,128)(2,1)S(1)} %constant_dynamic-slice_fusion), channel_id=1, source_target_pairs={{0,1},{1,0},{2,3},{3,2},{4,5},{5,4},{6,7},{7,6},{8,9},{9,8},{10,11... | collective-permute-start | bytes 8386568 | tf_op jit(solution)/shard_map/ppermute | solution.py:34
  85.3 2.4 copy-start
  87.7 189.8 %copy-start.2 = (f32[5376]{0:T(1024)}, f32[5376]{0:T(1024)S(1)}, u32[]{:S(2)}) copy-start(f32[5376]{0:T(1024)S(1)} %fusion.40) | copy-start | bytes 64516
  272.9 4.6 %slice-start = ((s8[5591040]{0:T(1024)(128)(4,1)}), s8[4194304]{0:T(1024)(128)(4,1)S(1)}, s32[]{:S(2)}) async-start(s8[5591040]{0:T(1024)(128)(4,1)} %bitcast.63), calls=%async_computation.1 | async-start | bytes 8388608
  276.0 1.5 slice-start.1
  277.5 2.1 copy-start.3
  280.4 16.9 %collective-permute-start.8 = (bf16[512,2,128]{0,2,1:T(8,128)(2,1)S(1)}, bf16[512,2,128]{0,2,1:T(8,128)(2,1)}, u32[]{:S(2)}, u32[]{:S(2)}) collective-permute-start(bf16[512,2,128]{0,2,1:T(8,128)(2,1)S(1)} %pad_maximum_fusion), channel_id=1, source_target_pairs={{0,32},{16,48},{32,64},{48,80},{64,96},{80,112},{96,128},{112,144}... | collective-permute-start | bytes 786440 | tf_op jit(solution)/shard_map/ppermute | solution.py:23
  285.7 11.5 %collective-permute-start.9 = (bf16[512,2,128]{0,2,1:T(8,128)(2,1)S(1)}, bf16[512,2,128]{0,2,1:T(8,128)(2,1)}, u32[]{:S(2)}, u32[]{:S(2)}) collective-permute-start(bf16[512,2,128]{0,2,1:T(8,128)(2,1)S(1)} %pad_maximum_fusion), channel_id=1, source_target_pairs={{0,16},{16,32},{32,48},{48,64},{64,80},{80,96},{96,112},{112,128},... | collective-permute-start | bytes 786440 | tf_op jit(solution)/shard_map/ppermute | solution.py:23
  291.8 5.2 %copy-start.4 = (f32[128]{0:T(128)S(1)}, f32[128]{0:T(128)}, u32[]{:S(2)}) copy-start(f32[128]{0:T(128)} %param.9) | copy-start | bytes 1540
  291.8 6.5 %copy-start.1 = (pred[512,1536]{0,1:T(8,128)(4,1)S(1)}, pred[512,1536]{0,1:T(8,128)(4,1)}, u32[]{:S(2)}) copy-start(pred[512,1536]{0,1:T(8,128)(4,1)} %fusion.16) | copy-start | bytes 2359300
Sparse Core Ops, SparseCore 0:
  76.5 195.2 all-reduce.1

commit v13 on v5

--- a/solution.py
+++ b/solution.py
@@ -90,7 +90,7 @@
     )
     slabs = lax.all_gather(padded, ROW, axis=0, tiled=True).reshape(-1, aligned, weight_cols)
     largest = jnp.max(slabs[:, weight_rows].astype(jnp.float32), axis=0)
-    clipped = clip_with(slabs[:, :weight_rows].reshape(-1, weight_cols), largest)
+    bound = (CLIP_FRACTION * largest).astype(jnp.bfloat16)
     rows_tokens, piece = tokens.shape
     cores = lax.axis_size("cc")
     high = gain.astype(jnp.bfloat16)
@@ -109,9 +109,10 @@
     inverse = lax.rsqrt(squares / D + EPS)[:, None]
     whole = (widened * inverse * full_gain[None, :]).astype(jnp.bfloat16)
     ordered = (
-        clipped.reshape(blocks, cores, piece, clipped.shape[1])
-        .transpose(1, 0, 2, 3)
-        .reshape(clipped.shape)
+        jnp.clip(slabs[:, :weight_rows], -bound, bound)
+        .reshape(blocks, cores, piece // weight_rows, weight_rows, weight_cols)
+        .transpose(1, 0, 2, 3, 4)
+        .reshape(-1, weight_cols)
     )
     kv_part = jnp.dot(whole, ordered[:, query_cols:], preferred_element_type=jnp.float32)
     keys = kv_part[:, :key_cols]

time: 145 us -> 146 us (level)
  other arithmetic: 15.7 us -> 17.2 us
    slice x1 -> x0, local copies, waits for them, and re-layouts: 3.11 us -> none  [local(): slabs[:, :weight_rows].reshape(-1, weight_cols)]
    min x0 -> x1, other arithmetic: none -> 3 us  [local(): jnp.clip(slabs[:, :weight_rows], -bound, bound)]
    unnamed x15, local copies, waits for them, and re-layouts: 5.2 us -> 7.33 us
    transpose x1 -> x0, other arithmetic: 1.46 us -> none  [local(): ordered = clipped.reshape(blocks, cores, piece, clipped.shape[1]).transpo...]
where the time goes in v13:
time: 146 us; the launch traced here: 145 us
  waiting for transfers between devices  53.3 us (37%)
  starting transfers between devices  30.9 us (21%)
  local copies, waits for them, and re-layouts  21.4 us (15%)
  other arithmetic  17.2 us (12%)
  between operations  14.4 us (10%)
  matrix products  7.99 us (5%)
    ppermute x5, waiting for transfers between devices, ring_gather(): forward = lax.ppermute(forward, axis, right)  30.2 us
    all_gather x1, waiting for transfers between devices, local(): lax.all_gather(padded, ROW, axis=0, tiled=True)  15.3 us
    ppermute x3, starting transfers between devices, ring_gather(): backward = lax.ppermute(backward, axis, left)  14.1 us
    ppermute x5, starting transfers between devices, ring_gather(): forward = lax.ppermute(forward, axis, right)  11.1 us
    ppermute x2, waiting for transfers between devices, shifted(): return lax.ppermute(array, axis, pairs)  7.79 us
    concatenate x1, local copies, waits for them, and re-layouts, ring_gather(): doubled = jnp.concatenate([stacked, stacked], axis=dim)  7.63 us
    unnamed x15, local copies, waits for them, and re-layouts  7.33 us
    ppermute x2, starting transfers between devices, shifted(): return lax.ppermute(array, axis, pairs)  5.7 us
  transfers between devices with their start and end apart: 11, of which 8 were waited for; matrix products, arithmetic and copies ran while one was open for 18% of the time, Pallas kernels for 0%

profile of v13, /device:TPU:64, one launch (start us, length us, event | category | flops | bytes accessed | tf_op | source)
XLA Modules:
  0.0 145.2 jit_solution(2015530005181042260)
XLA Ops:
  12.2 3.5 %collective-permute-start.3 = (bf16[520,336]{1,0:T(8,128)(2,1)S(1)}, bf16[520,336]{1,0:T(8,128)(2,1)S(1)}, u32[]{:S(2)}, u32[]{:S(2)}) collective-permute-start(bf16[520,336]{1,0:T(8,128)(2,1)S(1)} %concatenate.43), channel_id=1, source_target_pairs={{0,2},{2,4},{4,6},{6,8},{8,10},{10,12},{12,14},{14,0},{1,3},{3,5},... | collective-permute-start | bytes 1048328 | tf_op jit(solution)/shard_map/ppermute | solution.py:34
  15.7 3.8 %collective-permute-start = (bf16[520,336]{1,0:T(8,128)(2,1)S(1)}, bf16[520,336]{1,0:T(8,128)(2,1)S(1)}, u32[]{:S(2)}, u32[]{:S(2)}) collective-permute-start(bf16[520,336]{1,0:T(8,128)(2,1)S(1)} %concatenate.43), channel_id=1, source_target_pairs={{0,14},{2,0},{4,2},{6,4},{8,6},{10,8},{12,10},{14,12},{1,15},{3,1}... | collective-permute-start | bytes 1048328 | tf_op jit(solution)/shard_map/ppermute | solution.py:37
  19.5 7.3 %collective-permute-done.3 = bf16[520,336]{1,0:T(8,128)(2,1)S(1)} collective-permute-done((bf16[520,336]{1,0:T(8,128)(2,1)S(1)}, bf16[520,336]{1,0:T(8,128)(2,1)S(1)}, u32[]{:S(2)}, u32[]{:S(2)}) %collective-permute-start.3) | collective-permute-done | bytes 349472 | tf_op jit(solution)/shard_map/ppermute | solution.py:34
  28.8 5.1 %collective-permute-start.1 = (bf16[520,336]{1,0:T(8,128)(2,1)S(1)}, bf16[520,336]{1,0:T(8,128)(2,1)S(1)}, u32[]{:S(2)}, u32[]{:S(2)}) collective-permute-start(bf16[520,336]{1,0:T(8,128)(2,1)S(1)} %collective-permute-done), channel_id=1, source_target_pairs={{0,14},{2,0},{4,2},{6,4},{8,6},{10,8},{12,10},{14,12},{1,15},{3,1}... | collective-permute-start | bytes 1048328 | tf_op jit(solution)/shard_map/ppermute | solution.py:37
  33.9 6.5 %collective-permute-done.4 = bf16[520,336]{1,0:T(8,128)(2,1)S(1)} collective-permute-done((bf16[520,336]{1,0:T(8,128)(2,1)S(1)}, bf16[520,336]{1,0:T(8,128)(2,1)S(1)}, u32[]{:S(2)}, u32[]{:S(2)}) %collective-permute-start.4) | collective-permute-done | bytes 349472 | tf_op jit(solution)/shard_map/ppermute | solution.py:34
  42.3 5.1 %collective-permute-start.2 = (bf16[520,336]{1,0:T(8,128)(2,1)S(1)}, bf16[520,336]{1,0:T(8,128)(2,1)S(1)}, u32[]{:S(2)}, u32[]{:S(2)}) collective-permute-start(bf16[520,336]{1,0:T(8,128)(2,1)S(1)} %collective-permute-done.1), channel_id=1, source_target_pairs={{0,14},{2,0},{4,2},{6,4},{8,6},{10,8},{12,10},{14,12},{1,15},{3,1}... | collective-permute-start | bytes 1048328 | tf_op jit(solution)/shard_map/ppermute | solution.py:37
  47.4 5.5 %collective-permute-done.5 = bf16[520,336]{1,0:T(8,128)(2,1)S(1)} collective-permute-done((bf16[520,336]{1,0:T(8,128)(2,1)S(1)}, bf16[520,336]{1,0:T(8,128)(2,1)S(1)}, u32[]{:S(2)}, u32[]{:S(2)}) %collective-permute-start.5) | collective-permute-done | bytes 349472 | tf_op jit(solution)/shard_map/ppermute | solution.py:34
  54.9 9.7 %collective-permute-done.6 = bf16[520,336]{1,0:T(8,128)(2,1)S(1)} collective-permute-done((bf16[520,336]{1,0:T(8,128)(2,1)S(1)}, bf16[520,336]{1,0:T(8,128)(2,1)S(1)}, u32[]{:S(2)}, u32[]{:S(2)}) %collective-permute-start.6) | collective-permute-done | bytes 349472 | tf_op jit(solution)/shard_map/ppermute | solution.py:34
  64.6 7.6 %concatenate.44 = bf16[520,5376]{1,0:T(8,128)(2,1)} concatenate(bf16[520,336]{1,0:T(8,128)(2,1)S(1)} %concatenate.43, bf16[520,336]{1,0:T(8,128)(2,1)S(1)} %collective-permute-done, bf16[520,336]{1,0:T(8,128)(2,1)S(1)} %collective-permute-done.1, bf16[520,336]{1,0:T(8,128)(2,1)S(1)} %collective-permute-done.2, bf16[520,336]{1,0:T(8,128)(2,1)S(1)} %collective-permute-done.6, ...), dimensions={1} | concatenate | bytes 11182080 | tf_op jit(solution)/shard_map/concatenate | solution.py:43
  72.3 3.3 %constant_dynamic-slice_fusion = bf16[520,2688]{1,0:T(8,128)(2,1)S(1)} fusion(bf16[520,5376]{1,0:T(8,128)(2,1)} %concatenate.44, s32[]{:T(128)S(6)} %select_n.22), kind=kLoop, calls=%fused_computation.76 | loop fusion | bytes 5591044 | tf_op jit(solution)/shard_map/dynamic_slice | solution.py:45
  75.6 1.9 %collective-permute-start.7 = (bf16[520,2688]{1,0:T(8,128)(2,1)S(1)}, bf16[520,2688]{1,0:T(8,128)(2,1)}, u32[]{:S(2)}, u32[]{:S(2)}) collective-permute-start(bf16[520,2688]{1,0:T(8,128)(2,1)S(1)} %constant_dynamic-slice_fusion), channel_id=1, source_target_pairs={{0,1},{1,0},{2,3},{3,2},{4,5},{5,4},{6,7},{7,6},{8,9},{9,8},{10,11... | collective-permute-start | bytes 8386568 | tf_op jit(solution)/shard_map/ppermute | solution.py:34
  79.7 2.0 %fusion.11 = pred[512,1536]{0,1:T(8,128)(4,1)} fusion(s32[1536]{0:T(1024)S(1)} %iota_add_fusion, s32[512]{0:T(512)S(1)} %iota_add_fusion.1, pred[1536]{0:T(1024)(128)(4,1)S(1)} %broadcast_compare_fusion), kind=kLoop, calls=%fused_computation.22 | loop fusion | flops 3932160 | bytes 796160 | tf_op jit(solution)/shard_map/and | solution.py:146
  82.8 5.2 %fusion.5 = bf16[520,5376]{1,0:T(8,128)(2,1)S(1)} fusion(s32[]{:T(128)S(6)} %select_n.24, bf16[520,2688]{1,0:T(8,128)(2,1)S(1)} %constant_dynamic-slice_fusion, bf16[520,2688]{1,0:T(8,128)(2,1)} %collective-permute-done.7), kind=kLoop, calls=%fused_computation.13 | loop fusion | flops 22364160 | bytes 11182084 | tf_op jit(solution)/shard_map/concatenate | solution.py:43
  88.0 2.3 %copy-done = bf16[520,5376]{1,0:T(8,128)(2,1)} copy-done((bf16[520,5376]{1,0:T(8,128)(2,1)}, bf16[520,5376]{1,0:T(8,128)(2,1)S(1)}, u32[]{:S(2)}) %copy-start) | copy-done | bytes 5591064
  91.5 15.3 %all-gather.2.cloned.1.call-done = bf16[5632,512]{1,0:T(8,128)(2,1)} async-done(((bf16[176,512]{1,0:T(8,128)(2,1)}), bf16[5632,512]{1,0:T(8,128)(2,1)}) %all-gather.2.cloned.1.call-update) | async-done | bytes 5767184 | tf_op jit(solution)/shard_map/all_gather | solution.py:91
  107.9 3.0 %fusion.6 = bf16[32,168,512]{2,1,0:T(8,128)(2,1)S(1)} fusion(bf16[32,176,512]{2,1,0:T(8,128)(2,1)} %bitcast.52, bf16[512]{0:T(512)(128)(2,1)S(1)} %fusion.41, bf16[512]{0:T(512)(128)(2,1)S(1)} %multiply_convert_fusion), kind=kLoop, calls=%fused_computation.15 | loop fusion | flops 5505024 | bytes 11012096 | tf_op jit(solution)/shard_map/jit(clip)/min | solution.py:112
  113.5 2.0 %fusion.14 = f32[512,256]{0,1:T(8,128)S(1)} fusion(bf16[5376,512]{1,0:T(8,128)(2,1)S(1)} %bitcast.49, f32[5376]{0:T(1024)S(1)} %fusion.35, f32[512]{0:T(512)S(1)} %add_rsqrt_fusion.2, bf16[520,5376]{1,0:T(8,128)(2,1)S(1)} %bitcast.47), kind=kOutput, calls=%fused_computation.25 | convolution fusion | flops 1420296192 | bytes 8808448 | tf_op jit(solution)/shard_map/dot_general | solution.py:117
  116.3 3.4 %collective-permute-start.8 = (bf16[512,2,128]{0,2,1:T(8,128)(2,1)S(1)}, bf16[512,2,128]{0,2,1:T(8,128)(2,1)S(1)}, u32[]{:S(2)}, u32[]{:S(2)}) collective-permute-start(bf16[512,2,128]{0,2,1:T(8,128)(2,1)S(1)} %pad_maximum_fusion), channel_id=1, source_target_pairs={{0,32},{16,48},{32,64},{48,80},{64,96},{80,112},{96,128},{112,144}... | collective-permute-start | bytes 786440 | tf_op jit(solution)/shard_map/ppermute | solution.py:23
  119.6 2.3 %collective-permute-start.9 = (bf16[512,2,128]{0,2,1:T(8,128)(2,1)S(1)}, bf16[512,2,128]{0,2,1:T(8,128)(2,1)}, u32[]{:S(2)}, u32[]{:S(2)}) collective-permute-start(bf16[512,2,128]{0,2,1:T(8,128)(2,1)S(1)} %pad_maximum_fusion), channel_id=1, source_target_pairs={{0,16},{16,32},{32,48},{48,64},{64,80},{80,96},{96,112},{112,128},... | collective-permute-start | bytes 786440 | tf_op jit(solution)/shard_map/ppermute | solution.py:23
  122.0 2.0 %multiply_reduce_fusion = (f32[512,2]{0,1:T(2,128)S(1)}, f32[512,256]{0,1:T(8,128)S(1)}) fusion(bf16[5376,512]{1,0:T(8,128)(2,1)S(1)} %bitcast.50, f32[5376]{0:T(1024)S(1)} %fusion.35, f32[512]{0:T(512)S(1)} %add_rsqrt_fusion.2, bf16[520,5376]{1,0:T(8,128)(2,1)S(1)} %bitcast.47), kind=kOutput, calls=%fused_computation.32 | convolution fusion | flops 1420557312 | bytes 8812544 | tf_op jit(solution)/shard_map/dot_general | solution.py:120
  124.7 4.0 %collective-permute-done.8 = bf16[512,2,128]{0,2,1:T(8,128)(2,1)S(1)} collective-permute-done((bf16[512,2,128]{0,2,1:T(8,128)(2,1)S(1)}, bf16[512,2,128]{0,2,1:T(8,128)(2,1)S(1)}, u32[]{:S(2)}, u32[]{:S(2)}) %collective-permute-start.8) | collective-permute-done | bytes 262176 | tf_op jit(solution)/shard_map/ppermute | solution.py:23
  128.8 3.8 %collective-permute-done.9 = bf16[512,2,128]{0,2,1:T(8,128)(2,1)} collective-permute-done((bf16[512,2,128]{0,2,1:T(8,128)(2,1)S(1)}, bf16[512,2,128]{0,2,1:T(8,128)(2,1)}, u32[]{:S(2)}, u32[]{:S(2)}) %collective-permute-start.9) | collective-permute-done | bytes 262176 | tf_op jit(solution)/shard_map/ppermute | solution.py:23
  133.5 1.9 %fusion.7 = (f32[2,512]{1,0:T(2,128)S(1)}, f32[1536,512,2]{1,0,2:T(8,128)S(1)}) fusion(pred[512,1536]{0,1:T(8,128)(4,1)S(1)} %copy-done.1, bf16[512,2,64]{2,0,1:T(8,128)(2,1)S(1)} %get-tuple-element.6, bf16[512,2,64]{2,0,1:T(8,128)(2,1)S(1)} %get-tuple-element.5, bf16[1536,2,128]{0,2,1:T(8,128)(2,1)S(1)} %maximum_maximum_fusion), kind=kOutput, calls=%fused_computation.16 | convolution fusion | flops 407895040 | bytes 7999488 | tf_op jit(solution)/shard_map/tkgd,skd->kgts/dot_general | solution.py:142
  135.5 2.0 %fusion.16 = bf16[128,2,512]{2,0,1:T(8,128)(2,1)S(1)} fusion(f32[2,512]{1,0:T(2,128)S(1)} %get-tuple-element.16, f32[1536,512,2]{1,0,2:T(8,128)S(1)} %get-tuple-element.17, pred[512,1536]{0,1:T(8,128)(4,1)S(1)} %copy-done.1, bf16[1536,2,128]{0,2,1:T(8,128)(2,1)S(1)} %maximum_maximum_fusion), kind=kOutput, calls=%fused_computation.27 | convolution fusion | flops 409075712 | bytes 7737344 | tf_op jit(solution)/shard_map/kgts,skd->tkgd/dot_general | solution.py:150
  (63 shorter events, 22.2 us)
Async XLA Ops:
  6.5 100.3 %all-gather.2.cloned.1.call-start = ((), (), s32[]{:S(2)}) async-start(), calls=%async_computation | async-start | bytes 5947392 | tf_op jit(solution)/shard_map/all_gather | solution.py:91
  12.2 14.6 %collective-permute-start.3 = (bf16[520,336]{1,0:T(8,128)(2,1)S(1)}, bf16[520,336]{1,0:T(8,128)(2,1)S(1)}, u32[]{:S(2)}, u32[]{:S(2)}) collective-permute-start(bf16[520,336]{1,0:T(8,128)(2,1)S(1)} %concatenate.43), channel_id=1, source_target_pairs={{0,2},{2,4},{4,6},{6,8},{8,10},{10,12},{12,14},{14,0},{1,3},{3,5},... | collective-permute-start | bytes 1048328 | tf_op jit(solution)/shard_map/ppermute | solution.py:34
  15.7 13.0 %collective-permute-start = (bf16[520,336]{1,0:T(8,128)(2,1)S(1)}, bf16[520,336]{1,0:T(8,128)(2,1)S(1)}, u32[]{:S(2)}, u32[]{:S(2)}) collective-permute-start(bf16[520,336]{1,0:T(8,128)(2,1)S(1)} %concatenate.43), channel_id=1, source_target_pairs={{0,14},{2,0},{4,2},{6,4},{8,6},{10,8},{12,10},{14,12},{1,15},{3,1}... | collective-permute-start | bytes 1048328 | tf_op jit(solution)/shard_map/ppermute | solution.py:37
  26.8 13.5 %collective-permute-start.4 = (bf16[520,336]{1,0:T(8,128)(2,1)S(1)}, bf16[520,336]{1,0:T(8,128)(2,1)S(1)}, u32[]{:S(2)}, u32[]{:S(2)}) collective-permute-start(bf16[520,336]{1,0:T(8,128)(2,1)S(1)} %collective-permute-done.3), channel_id=1, source_target_pairs={{0,2},{2,4},{4,6},{6,8},{8,10},{10,12},{12,14},{14,0},{1,3},{3,5},... | collective-permute-start | bytes 1048328 | tf_op jit(solution)/shard_map/ppermute | solution.py:34
  28.8 13.5 %collective-permute-start.1 = (bf16[520,336]{1,0:T(8,128)(2,1)S(1)}, bf16[520,336]{1,0:T(8,128)(2,1)S(1)}, u32[]{:S(2)}, u32[]{:S(2)}) collective-permute-start(bf16[520,336]{1,0:T(8,128)(2,1)S(1)} %collective-permute-done), channel_id=1, source_target_pairs={{0,14},{2,0},{4,2},{6,4},{8,6},{10,8},{12,10},{14,12},{1,15},{3,1}... | collective-permute-start | bytes 1048328 | tf_op jit(solution)/shard_map/ppermute | solution.py:37
  40.4 12.6 %collective-permute-start.5 = (bf16[520,336]{1,0:T(8,128)(2,1)S(1)}, bf16[520,336]{1,0:T(8,128)(2,1)S(1)}, u32[]{:S(2)}, u32[]{:S(2)}) collective-permute-start(bf16[520,336]{1,0:T(8,128)(2,1)S(1)} %collective-permute-done.4), channel_id=1, source_target_pairs={{0,2},{2,4},{4,6},{6,8},{8,10},{10,12},{12,14},{14,0},{1,3},{3,5},... | collective-permute-start | bytes 1048328 | tf_op jit(solution)/shard_map/ppermute | solution.py:34
  42.3 12.6 %collective-permute-start.2 = (bf16[520,336]{1,0:T(8,128)(2,1)S(1)}, bf16[520,336]{1,0:T(8,128)(2,1)S(1)}, u32[]{:S(2)}, u32[]{:S(2)}) collective-permute-start(bf16[520,336]{1,0:T(8,128)(2,1)S(1)} %collective-permute-done.1), channel_id=1, source_target_pairs={{0,14},{2,0},{4,2},{6,4},{8,6},{10,8},{12,10},{14,12},{1,15},{3,1}... | collective-permute-start | bytes 1048328 | tf_op jit(solution)/shard_map/ppermute | solution.py:37
  53.0 11.7 %collective-permute-start.6 = (bf16[520,336]{1,0:T(8,128)(2,1)S(1)}, bf16[520,336]{1,0:T(8,128)(2,1)S(1)}, u32[]{:S(2)}, u32[]{:S(2)}) collective-permute-start(bf16[520,336]{1,0:T(8,128)(2,1)S(1)} %collective-permute-done.5), channel_id=1, source_target_pairs={{0,2},{2,4},{4,6},{6,8},{8,10},{10,12},{12,14},{14,0},{1,3},{3,5},... | collective-permute-start | bytes 1048328 | tf_op jit(solution)/shard_map/ppermute | solution.py:34
  75.6 7.2 %collective-permute-start.7 = (bf16[520,2688]{1,0:T(8,128)(2,1)S(1)}, bf16[520,2688]{1,0:T(8,128)(2,1)}, u32[]{:S(2)}, u32[]{:S(2)}) collective-permute-start(bf16[520,2688]{1,0:T(8,128)(2,1)S(1)} %constant_dynamic-slice_fusion), channel_id=1, source_target_pairs={{0,1},{1,0},{2,3},{3,2},{4,5},{5,4},{6,7},{7,6},{8,9},{9,8},{10,11... | collective-permute-start | bytes 8386568 | tf_op jit(solution)/shard_map/ppermute | solution.py:34
  87.9 2.4 %copy-start = (bf16[520,5376]{1,0:T(8,128)(2,1)}, bf16[520,5376]{1,0:T(8,128)(2,1)S(1)}, u32[]{:S(2)}) copy-start(bf16[520,5376]{1,0:T(8,128)(2,1)S(1)} %fusion.5) | copy-start | bytes 16773124
  110.9 2.2 %slice-start = ((s8[5591040]{0:T(1024)(128)(4,1)}), s8[4194304]{0:T(1024)(128)(4,1)S(1)}, s32[]{:S(2)}) async-start(s8[5591040]{0:T(1024)(128)(4,1)} %bitcast.46), calls=%async_computation.1 | async-start | bytes 8388608
  110.9 2.6 %slice-start.1 = ((s8[5591040]{0:T(1024)(128)(4,1)}), s8[1396736]{0:T(1024)(128)(4,1)S(1)}, s32[]{:S(2)}) async-start(s8[5591040]{0:T(1024)(128)(4,1)} %bitcast.46), calls=%async_computation.2 | async-start | bytes 2793472
  113.5 2.1 %copy-start.2 = (f32[128]{0:T(128)S(1)}, f32[128]{0:T(128)}, u32[]{:S(2)}) copy-start(f32[128]{0:T(128)} %param.10) | copy-start | bytes 1540
  116.3 8.0 %copy-start.3 = (f32[128]{0:T(128)S(1)}, f32[128]{0:T(128)}, u32[]{:S(2)}) copy-start(f32[128]{0:T(128)} %param.9) | copy-start | bytes 1540
  116.3 12.5 %collective-permute-start.8 = (bf16[512,2,128]{0,2,1:T(8,128)(2,1)S(1)}, bf16[512,2,128]{0,2,1:T(8,128)(2,1)S(1)}, u32[]{:S(2)}, u32[]{:S(2)}) collective-permute-start(bf16[512,2,128]{0,2,1:T(8,128)(2,1)S(1)} %pad_maximum_fusion), channel_id=1, source_target_pairs={{0,32},{16,48},{32,64},{48,80},{64,96},{80,112},{96,128},{112,144}... | collective-permute-start | bytes 786440 | tf_op jit(solution)/shard_map/ppermute | solution.py:23
  119.6 12.9 %collective-permute-start.9 = (bf16[512,2,128]{0,2,1:T(8,128)(2,1)S(1)}, bf16[512,2,128]{0,2,1:T(8,128)(2,1)}, u32[]{:S(2)}, u32[]{:S(2)}) collective-permute-start(bf16[512,2,128]{0,2,1:T(8,128)(2,1)S(1)} %pad_maximum_fusion), channel_id=1, source_target_pairs={{0,16},{16,32},{32,48},{48,64},{64,80},{80,96},{96,112},{112,128},... | collective-permute-start | bytes 786440 | tf_op jit(solution)/shard_map/ppermute | solution.py:23
  124.0 9.5 %copy-start.1 = (pred[512,1536]{0,1:T(8,128)(4,1)S(1)}, pred[512,1536]{0,1:T(8,128)(4,1)}, u32[]{:S(2)}) copy-start(pred[512,1536]{0,1:T(8,128)(4,1)} %fusion.11) | copy-start | bytes 2359300
Sparse Core Ops, SparseCore 0:
  10.5 96.2 all-gather.1

commit v14 on v9

--- a/solution.py
+++ b/solution.py
@@ -138,9 +138,9 @@
     )
     values = values.reshape(rows, kv_local, HD).astype(jnp.bfloat16)
     blocks_back = WINDOW // rows
-    both = jnp.concatenate([keys, values], axis=1)
+    both = jnp.concatenate([keys, values], axis=1).reshape(rows, -1)
     earlier = [shifted(both, ROW, offset) for offset in range(blocks_back, 0, -1)]
-    joined = jnp.concatenate(earlier + [both], axis=0)
+    joined = jnp.concatenate(earlier + [both], axis=0).reshape(-1, 2 * kv_local, HD)
     all_keys = joined[:, :kv_local]
     all_values = joined[:, kv_local:]
     key_pos = (

time: 145 us -> 145 us (level)
  no operation moved by 1% of the time
where the time goes in v14:
time: 145 us; the launch traced here: 143 us
  starting transfers between devices  40.8 us (28%)
  waiting for transfers between devices  37.1 us (26%)
  local copies, waits for them, and re-layouts  25.3 us (17%)
  other arithmetic  14.8 us (10%)
  between operations  14.5 us (10%)
  matrix products  10.9 us (8%)
    ppermute x5, starting transfers between devices, ring_gather(): forward = lax.ppermute(forward, axis, right)  21.1 us
    all_gather x1, waiting for transfers between devices, local(): lax.all_gather(padded, ROW, axis=0, tiled=True)  18 us
    ppermute x5, waiting for transfers between devices, ring_gather(): forward = lax.ppermute(forward, axis, right)  17.4 us
    ppermute x3, starting transfers between devices, ring_gather(): backward = lax.ppermute(backward, axis, left)  13.4 us
    concatenate x1, local copies, waits for them, and re-layouts, ring_gather(): doubled = jnp.concatenate([stacked, stacked], axis=dim)  7.61 us
    ppermute x2, starting transfers between devices, shifted(): return lax.ppermute(array, axis, pairs)  6.34 us
    unnamed x17, local copies, waits for them, and re-layouts  5.32 us
    dot_general x1, matrix products, local(): jnp.dot(whole, ordered(0, query_cols), preferred_element_type=jnp.float32)  5.19 us
  transfers between devices with their start and end apart: 11, of which 7 were waited for; matrix products, arithmetic and copies ran while one was open for 22% of the time, Pallas kernels for 0%

profile of v14, /device:TPU:1, one launch (start us, length us, event | category | flops | bytes accessed | tf_op | source)
XLA Modules:
  0.0 143.5 jit_solution(1509192366166824707)
XLA Ops:
  12.2 4.0 %collective-permute-start.3 = (bf16[520,336]{1,0:T(8,128)(2,1)S(1)}, bf16[520,336]{1,0:T(8,128)(2,1)S(1)}, u32[]{:S(2)}, u32[]{:S(2)}) collective-permute-start(bf16[520,336]{1,0:T(8,128)(2,1)S(1)} %concatenate.48), channel_id=1, source_target_pairs={{0,2},{2,4},{4,6},{6,8},{8,10},{10,12},{12,14},{14,0},{1,3},{3,5},... | collective-permute-start | bytes 1048328 | tf_op jit(solution)/shard_map/ppermute | solution.py:34
  16.3 3.8 %collective-permute-start = (bf16[520,336]{1,0:T(8,128)(2,1)S(1)}, bf16[520,336]{1,0:T(8,128)(2,1)S(1)}, u32[]{:S(2)}, u32[]{:S(2)}) collective-permute-start(bf16[520,336]{1,0:T(8,128)(2,1)S(1)} %concatenate.48), channel_id=1, source_target_pairs={{0,14},{2,0},{4,2},{6,4},{8,6},{10,8},{12,10},{14,12},{1,15},{3,1}... | collective-permute-start | bytes 1048328 | tf_op jit(solution)/shard_map/ppermute | solution.py:37
  20.1 3.3 %collective-permute-done.3 = bf16[520,336]{1,0:T(8,128)(2,1)S(1)} collective-permute-done((bf16[520,336]{1,0:T(8,128)(2,1)S(1)}, bf16[520,336]{1,0:T(8,128)(2,1)S(1)}, u32[]{:S(2)}, u32[]{:S(2)}) %collective-permute-start.3) | collective-permute-done | bytes 349472 | tf_op jit(solution)/shard_map/ppermute | solution.py:34
  23.4 4.0 %collective-permute-start.4 = (bf16[520,336]{1,0:T(8,128)(2,1)S(1)}, bf16[520,336]{1,0:T(8,128)(2,1)S(1)}, u32[]{:S(2)}, u32[]{:S(2)}) collective-permute-start(bf16[520,336]{1,0:T(8,128)(2,1)S(1)} %collective-permute-done.3), channel_id=1, source_target_pairs={{0,2},{2,4},{4,6},{6,8},{8,10},{10,12},{12,14},{14,0},{1,3},{3,5},... | collective-permute-start | bytes 1048328 | tf_op jit(solution)/shard_map/ppermute | solution.py:34
  27.4 4.7 %collective-permute-start.1 = (bf16[520,336]{1,0:T(8,128)(2,1)S(1)}, bf16[520,336]{1,0:T(8,128)(2,1)S(1)}, u32[]{:S(2)}, u32[]{:S(2)}) collective-permute-start(bf16[520,336]{1,0:T(8,128)(2,1)S(1)} %collective-permute-done), channel_id=1, source_target_pairs={{0,14},{2,0},{4,2},{6,4},{8,6},{10,8},{12,10},{14,12},{1,15},{3,1}... | collective-permute-start | bytes 1048328 | tf_op jit(solution)/shard_map/ppermute | solution.py:37
  32.1 3.3 %collective-permute-done.4 = bf16[520,336]{1,0:T(8,128)(2,1)S(1)} collective-permute-done((bf16[520,336]{1,0:T(8,128)(2,1)S(1)}, bf16[520,336]{1,0:T(8,128)(2,1)S(1)}, u32[]{:S(2)}, u32[]{:S(2)}) %collective-permute-start.4) | collective-permute-done | bytes 349472 | tf_op jit(solution)/shard_map/ppermute | solution.py:34
  35.4 3.1 %collective-permute-start.5 = (bf16[520,336]{1,0:T(8,128)(2,1)S(1)}, bf16[520,336]{1,0:T(8,128)(2,1)S(1)}, u32[]{:S(2)}, u32[]{:S(2)}) collective-permute-start(bf16[520,336]{1,0:T(8,128)(2,1)S(1)} %collective-permute-done.4), channel_id=1, source_target_pairs={{0,2},{2,4},{4,6},{6,8},{8,10},{10,12},{12,14},{14,0},{1,3},{3,5},... | collective-permute-start | bytes 1048328 | tf_op jit(solution)/shard_map/ppermute | solution.py:34
  38.4 4.8 %collective-permute-start.2 = (bf16[520,336]{1,0:T(8,128)(2,1)S(1)}, bf16[520,336]{1,0:T(8,128)(2,1)S(1)}, u32[]{:S(2)}, u32[]{:S(2)}) collective-permute-start(bf16[520,336]{1,0:T(8,128)(2,1)S(1)} %collective-permute-done.1), channel_id=1, source_target_pairs={{0,14},{2,0},{4,2},{6,4},{8,6},{10,8},{12,10},{14,12},{1,15},{3,1}... | collective-permute-start | bytes 1048328 | tf_op jit(solution)/shard_map/ppermute | solution.py:37
  43.3 3.3 %collective-permute-done.5 = bf16[520,336]{1,0:T(8,128)(2,1)S(1)} collective-permute-done((bf16[520,336]{1,0:T(8,128)(2,1)S(1)}, bf16[520,336]{1,0:T(8,128)(2,1)S(1)}, u32[]{:S(2)}, u32[]{:S(2)}) %collective-permute-start.5) | collective-permute-done | bytes 349472 | tf_op jit(solution)/shard_map/ppermute | solution.py:34
  46.5 2.2 %collective-permute-start.6 = (bf16[520,336]{1,0:T(8,128)(2,1)S(1)}, bf16[520,336]{1,0:T(8,128)(2,1)S(1)}, u32[]{:S(2)}, u32[]{:S(2)}) collective-permute-start(bf16[520,336]{1,0:T(8,128)(2,1)S(1)} %collective-permute-done.5), channel_id=1, source_target_pairs={{0,2},{2,4},{4,6},{6,8},{8,10},{10,12},{12,14},{14,0},{1,3},{3,5},... | collective-permute-start | bytes 1048328 | tf_op jit(solution)/shard_map/ppermute | solution.py:34
  50.4 6.7 %collective-permute-done.6 = bf16[520,336]{1,0:T(8,128)(2,1)S(1)} collective-permute-done((bf16[520,336]{1,0:T(8,128)(2,1)S(1)}, bf16[520,336]{1,0:T(8,128)(2,1)S(1)}, u32[]{:S(2)}, u32[]{:S(2)}) %collective-permute-start.6) | collective-permute-done | bytes 349472 | tf_op jit(solution)/shard_map/ppermute | solution.py:34
  57.2 7.6 %concatenate.49 = bf16[520,5376]{1,0:T(8,128)(2,1)} concatenate(bf16[520,336]{1,0:T(8,128)(2,1)S(1)} %concatenate.48, bf16[520,336]{1,0:T(8,128)(2,1)S(1)} %collective-permute-done, bf16[520,336]{1,0:T(8,128)(2,1)S(1)} %collective-permute-done.1, bf16[520,336]{1,0:T(8,128)(2,1)S(1)} %collective-permute-done.2, bf16[520,336]{1,0:T(8,128)(2,1)S(1)} %collective-permute-done.6, ...), dimensions={1} | concatenate | bytes 11182080 | tf_op jit(solution)/shard_map/concatenate | solution.py:43
  64.8 3.3 %constant_dynamic-slice_fusion = bf16[520,2688]{1,0:T(8,128)(2,1)S(1)} fusion(bf16[520,5376]{1,0:T(8,128)(2,1)} %concatenate.49, s32[]{:T(128)S(6)} %select_n.22), kind=kLoop, calls=%fused_computation.80 | loop fusion | bytes 5591044 | tf_op jit(solution)/shard_map/dynamic_slice | solution.py:45
  68.1 7.8 %collective-permute-start.7 = (bf16[520,2688]{1,0:T(8,128)(2,1)S(1)}, bf16[520,2688]{1,0:T(8,128)(2,1)}, u32[]{:S(2)}, u32[]{:S(2)}) collective-permute-start(bf16[520,2688]{1,0:T(8,128)(2,1)S(1)} %constant_dynamic-slice_fusion), channel_id=1, source_target_pairs={{0,1},{1,0},{2,3},{3,2},{4,5},{5,4},{6,7},{7,6},{8,9},{9,8},{10,11... | collective-permute-start | bytes 8386568 | tf_op jit(solution)/shard_map/ppermute | solution.py:34
  80.6 5.2 %fusion.5 = bf16[520,5376]{1,0:T(8,128)(2,1)S(1)} fusion(s32[]{:T(128)S(6)} %select_n.24, bf16[520,2688]{1,0:T(8,128)(2,1)S(1)} %constant_dynamic-slice_fusion, bf16[520,2688]{1,0:T(8,128)(2,1)} %collective-permute-done.7), kind=kLoop, calls=%fused_computation.13 | loop fusion | flops 22364160 | bytes 11182084 | tf_op jit(solution)/shard_map/concatenate | solution.py:43
  85.8 2.4 %copy-done = bf16[520,5376]{1,0:T(8,128)(2,1)} copy-done((bf16[520,5376]{1,0:T(8,128)(2,1)}, bf16[520,5376]{1,0:T(8,128)(2,1)S(1)}, u32[]{:S(2)}) %copy-start) | copy-done | bytes 5591064
  89.4 18.0 %all-gather.2.cloned.1.call-done = bf16[5632,512]{1,0:T(8,128)(2,1)} async-done(((bf16[176,512]{1,0:T(8,128)(2,1)}), bf16[5632,512]{1,0:T(8,128)(2,1)}) %all-gather.2.cloned.1.call-update) | async-done | bytes 5767184 | tf_op jit(solution)/shard_map/all_gather | solution.py:91
  108.5 3.2 %fusion.47 = (bf16[32,168,256]{2,1,0:T(8,128)(2,1)S(1)}, bf16[32,168,256]{2,1,0:T(8,128)(2,1)S(1)}) fusion(bf16[32,176,512]{2,1,0:T(8,128)(2,1)} %bitcast.69), kind=kLoop, calls=%fused_computation.90 | loop fusion | bytes 11010048 | tf_op jit(solution)/shard_map/slice | solution.py:95
  113.2 2.0 %fusion.23 = f32[512,256]{0,1:T(8,128)S(1)} fusion(bf16[5376,256]{1,0:T(8,128)(2,1)S(1)} %bitcast.71, f32[5376]{0:T(1024)S(1)} %fusion.39, f32[512]{0:T(512)S(1)} %add_rsqrt_fusion.2, bf16[520,5376]{1,0:T(8,128)(2,1)S(1)} %bitcast.64), kind=kOutput, calls=%fused_computation.32 | convolution fusion | flops 1420296192 | bytes 8808448 | tf_op jit(solution)/shard_map/dot_general | solution.py:123
  116.0 3.7 %collective-permute-start.8 = (bf16[512,256]{0,1:T(8,128)(2,1)S(1)}, bf16[512,256]{0,1:T(8,128)(2,1)}, u32[]{:S(2)}, u32[]{:S(2)}) collective-permute-start(bf16[512,256]{0,1:T(8,128)(2,1)S(1)} %bitcast.72), channel_id=1, source_target_pairs={{0,32},{16,48},{32,64},{48,80},{64,96},{80,112},{96,128},{112,144}... | collective-permute-start | bytes 786440 | tf_op jit(solution)/shard_map/ppermute | solution.py:23
  119.7 2.6 %collective-permute-start.9 = (bf16[512,256]{0,1:T(8,128)(2,1)S(1)}, bf16[512,256]{0,1:T(8,128)(2,1)}, u32[]{:S(2)}, u32[]{:S(2)}) collective-permute-start(bf16[512,256]{0,1:T(8,128)(2,1)S(1)} %bitcast.73), channel_id=1, source_target_pairs={{0,16},{16,32},{32,48},{48,64},{64,80},{80,96},{96,112},{112,128},... | collective-permute-start | bytes 786440 | tf_op jit(solution)/shard_map/ppermute | solution.py:23
  122.5 3.0 %copy.46 = bf16[256,5376]{1,0:T(8,128)(2,1)} copy(bf16[256,5376]{0,1:T(8,128)(2,1)S(1)} %bitcast.67) | data formatting | bytes 5505024 | tf_op jit(solution)/shard_map/dot_general | solution.py:128
  125.5 5.2 %multiply_reduce_fusion = (f32[512,2]{0,1:T(2,128)S(1)}, f32[512,2,128]{0,2,1:T(8,128)S(1)}) fusion(bf16[2,128,5376]{2,1,0:T(8,128)(2,1)} %bitcast.70, f32[5376]{0:T(1024)} %copy-done.2, f32[512]{0:T(512)S(1)} %add_rsqrt_fusion.2, bf16[520,5376]{1,0:T(8,128)(2,1)} %copy-done), kind=kOutput, calls=%fused_computation.35 | convolution fusion | flops 1420557312 | bytes 8812544 | tf_op jit(solution)/shard_map/dot_general | solution.py:128
  133.8 2.0 %fusion.19 = bf16[128,2,512]{2,0,1:T(8,128)(2,1)S(1)} fusion(f32[2,512]{1,0:T(2,128)S(1)} %get-tuple-element.22, f32[1536,512,2]{1,0,2:T(8,128)S(1)} %get-tuple-element.23, pred[512,1536]{0,1:T(8,128)(4,1)S(1)} %copy-done.1, bf16[1536,2,128]{0,2,1:T(8,128)(2,1)S(1)} %maximum_maximum_fusion), kind=kOutput, calls=%fused_computation.31 | convolution fusion | flops 409075712 | bytes 7737344 | tf_op jit(solution)/shard_map/kgts,skd->tkgd/dot_general | solution.py:158
  (67 shorter events, 19.8 us)
Async XLA Ops:
  6.5 100.9 %all-gather.2.cloned.1.call-start = ((), (), s32[]{:S(2)}) async-start(), calls=%async_computation | async-start | bytes 5947392 | tf_op jit(solution)/shard_map/all_gather | solution.py:91
  12.2 11.1 %collective-permute-start.3 = (bf16[520,336]{1,0:T(8,128)(2,1)S(1)}, bf16[520,336]{1,0:T(8,128)(2,1)S(1)}, u32[]{:S(2)}, u32[]{:S(2)}) collective-permute-start(bf16[520,336]{1,0:T(8,128)(2,1)S(1)} %concatenate.48), channel_id=1, source_target_pairs={{0,2},{2,4},{4,6},{6,8},{8,10},{10,12},{12,14},{14,0},{1,3},{3,5},... | collective-permute-start | bytes 1048328 | tf_op jit(solution)/shard_map/ppermute | solution.py:34
  16.3 11.1 %collective-permute-start = (bf16[520,336]{1,0:T(8,128)(2,1)S(1)}, bf16[520,336]{1,0:T(8,128)(2,1)S(1)}, u32[]{:S(2)}, u32[]{:S(2)}) collective-permute-start(bf16[520,336]{1,0:T(8,128)(2,1)S(1)} %concatenate.48), channel_id=1, source_target_pairs={{0,14},{2,0},{4,2},{6,4},{8,6},{10,8},{12,10},{14,12},{1,15},{3,1}... | collective-permute-start | bytes 1048328 | tf_op jit(solution)/shard_map/ppermute | solution.py:37
  23.4 12.0 %collective-permute-start.4 = (bf16[520,336]{1,0:T(8,128)(2,1)S(1)}, bf16[520,336]{1,0:T(8,128)(2,1)S(1)}, u32[]{:S(2)}, u32[]{:S(2)}) collective-permute-start(bf16[520,336]{1,0:T(8,128)(2,1)S(1)} %collective-permute-done.3), channel_id=1, source_target_pairs={{0,2},{2,4},{4,6},{6,8},{8,10},{10,12},{12,14},{14,0},{1,3},{3,5},... | collective-permute-start | bytes 1048328 | tf_op jit(solution)/shard_map/ppermute | solution.py:34
  27.4 11.1 %collective-permute-start.1 = (bf16[520,336]{1,0:T(8,128)(2,1)S(1)}, bf16[520,336]{1,0:T(8,128)(2,1)S(1)}, u32[]{:S(2)}, u32[]{:S(2)}) collective-permute-start(bf16[520,336]{1,0:T(8,128)(2,1)S(1)} %collective-permute-done), channel_id=1, source_target_pairs={{0,14},{2,0},{4,2},{6,4},{8,6},{10,8},{12,10},{14,12},{1,15},{3,1}... | collective-permute-start | bytes 1048328 | tf_op jit(solution)/shard_map/ppermute | solution.py:37
  35.4 11.2 %collective-permute-start.5 = (bf16[520,336]{1,0:T(8,128)(2,1)S(1)}, bf16[520,336]{1,0:T(8,128)(2,1)S(1)}, u32[]{:S(2)}, u32[]{:S(2)}) collective-permute-start(bf16[520,336]{1,0:T(8,128)(2,1)S(1)} %collective-permute-done.4), channel_id=1, source_target_pairs={{0,2},{2,4},{4,6},{6,8},{8,10},{10,12},{12,14},{14,0},{1,3},{3,5},... | collective-permute-start | bytes 1048328 | tf_op jit(solution)/shard_map/ppermute | solution.py:34
  38.4 12.0 %collective-permute-start.2 = (bf16[520,336]{1,0:T(8,128)(2,1)S(1)}, bf16[520,336]{1,0:T(8,128)(2,1)S(1)}, u32[]{:S(2)}, u32[]{:S(2)}) collective-permute-start(bf16[520,336]{1,0:T(8,128)(2,1)S(1)} %collective-permute-done.1), channel_id=1, source_target_pairs={{0,14},{2,0},{4,2},{6,4},{8,6},{10,8},{12,10},{14,12},{1,15},{3,1}... | collective-permute-start | bytes 1048328 | tf_op jit(solution)/shard_map/ppermute | solution.py:37
  46.5 10.6 %collective-permute-start.6 = (bf16[520,336]{1,0:T(8,128)(2,1)S(1)}, bf16[520,336]{1,0:T(8,128)(2,1)S(1)}, u32[]{:S(2)}, u32[]{:S(2)}) collective-permute-start(bf16[520,336]{1,0:T(8,128)(2,1)S(1)} %collective-permute-done.5), channel_id=1, source_target_pairs={{0,2},{2,4},{4,6},{6,8},{8,10},{10,12},{12,14},{14,0},{1,3},{3,5},... | collective-permute-start | bytes 1048328 | tf_op jit(solution)/shard_map/ppermute | solution.py:34
  68.1 12.5 %collective-permute-start.7 = (bf16[520,2688]{1,0:T(8,128)(2,1)S(1)}, bf16[520,2688]{1,0:T(8,128)(2,1)}, u32[]{:S(2)}, u32[]{:S(2)}) collective-permute-start(bf16[520,2688]{1,0:T(8,128)(2,1)S(1)} %constant_dynamic-slice_fusion), channel_id=1, source_target_pairs={{0,1},{1,0},{2,3},{3,2},{4,5},{5,4},{6,7},{7,6},{8,9},{9,8},{10,11... | collective-permute-start | bytes 8386568 | tf_op jit(solution)/shard_map/ppermute | solution.py:34
  85.7 2.5 %copy-start = (bf16[520,5376]{1,0:T(8,128)(2,1)}, bf16[520,5376]{1,0:T(8,128)(2,1)S(1)}, u32[]{:S(2)}) copy-start(bf16[520,5376]{1,0:T(8,128)(2,1)S(1)} %fusion.5) | copy-start | bytes 16773124
  88.2 24.9 %copy-start.2 = (f32[5376]{0:T(1024)}, f32[5376]{0:T(1024)S(1)}, u32[]{:S(2)}) copy-start(f32[5376]{0:T(1024)S(1)} %fusion.39) | copy-start | bytes 64516
  108.5 4.7 %slice-start = ((s8[5591040]{0:T(1024)(128)(4,1)}), s8[4194304]{0:T(1024)(128)(4,1)S(1)}, s32[]{:S(2)}) async-start(s8[5591040]{0:T(1024)(128)(4,1)} %bitcast.63), calls=%async_computation.1 | async-start | bytes 8388608
  111.7 1.5 %slice-start.1 = ((s8[5591040]{0:T(1024)(128)(4,1)}), s8[1396736]{0:T(1024)(128)(4,1)S(1)}, s32[]{:S(2)}) async-start(s8[5591040]{0:T(1024)(128)(4,1)} %bitcast.63), calls=%async_computation.2 | async-start | bytes 2793472
  113.2 2.1 %copy-start.3 = (f32[128]{0:T(128)S(1)}, f32[128]{0:T(128)}, u32[]{:S(2)}) copy-start(f32[128]{0:T(128)} %param.10) | copy-start | bytes 1540
  116.0 15.0 %collective-permute-start.8 = (bf16[512,256]{0,1:T(8,128)(2,1)S(1)}, bf16[512,256]{0,1:T(8,128)(2,1)}, u32[]{:S(2)}, u32[]{:S(2)}) collective-permute-start(bf16[512,256]{0,1:T(8,128)(2,1)S(1)} %bitcast.72), channel_id=1, source_target_pairs={{0,32},{16,48},{32,64},{48,80},{64,96},{80,112},{96,128},{112,144}... | collective-permute-start | bytes 786440 | tf_op jit(solution)/shard_map/ppermute | solution.py:23
  119.7 11.2 %collective-permute-start.9 = (bf16[512,256]{0,1:T(8,128)(2,1)S(1)}, bf16[512,256]{0,1:T(8,128)(2,1)}, u32[]{:S(2)}, u32[]{:S(2)}) collective-permute-start(bf16[512,256]{0,1:T(8,128)(2,1)S(1)} %bitcast.73), channel_id=1, source_target_pairs={{0,16},{16,32},{32,48},{48,64},{64,80},{80,96},{96,112},{112,128},... | collective-permute-start | bytes 786440 | tf_op jit(solution)/shard_map/ppermute | solution.py:23
  125.5 5.2 %copy-start.4 = (f32[128]{0:T(128)S(1)}, f32[128]{0:T(128)}, u32[]{:S(2)}) copy-start(f32[128]{0:T(128)} %param.9) | copy-start | bytes 1540
  125.5 6.5 %copy-start.1 = (pred[512,1536]{0,1:T(8,128)(4,1)S(1)}, pred[512,1536]{0,1:T(8,128)(4,1)}, u32[]{:S(2)}) copy-start(pred[512,1536]{0,1:T(8,128)(4,1)} %fusion.16) | copy-start | bytes 2359300
Sparse Core Ops, SparseCore 0:
  10.5 96.8 all-gather.1

commit v15 on v14

--- a/solution.py
+++ b/solution.py
@@ -140,22 +140,28 @@
     blocks_back = WINDOW // rows
     both = jnp.concatenate([keys, values], axis=1).reshape(rows, -1)
     earlier = [shifted(both, ROW, offset) for offset in range(blocks_back, 0, -1)]
-    joined = jnp.concatenate(earlier + [both], axis=0).reshape(-1, 2 * kv_local, HD)
-    all_keys = joined[:, :kv_local]
-    all_values = joined[:, kv_local:]
-    key_pos = (
-        positions[0] - blocks_back * rows + jnp.arange((blocks_back + 1) * rows, dtype=jnp.int32)
+    grouped = query.reshape(rows, kv_local, group, HD)
+    parts = []
+    for index, block in enumerate(earlier + [both]):
+        pair = block.reshape(rows, 2 * kv_local, HD)
+        block_keys = pair[:, :kv_local]
+        scores = jnp.einsum(
+            "tkgd,skd->kgts", grouped, block_keys, preferred_element_type=jnp.float32
+        ) * QUERY_SCALAR ** (-0.5)
+        key_pos = positions[0] + (index - blocks_back) * rows + jnp.arange(rows, dtype=jnp.int32)
+        distance = positions[:, None] - key_pos[None, :]
+        allowed = (distance >= 0) & (distance < WINDOW) & (key_pos[None, :] >= 0)
+        parts.append((jnp.where(allowed, jnp.exp(scores), 0.0), pair[:, kv_local:]))
+    total = sum(jnp.sum(expo, axis=-1, keepdims=True) for expo, _ in parts)
+    output = sum(
+        jnp.einsum(
+            "kgts,skd->tkgd",
+            (expo / total).astype(jnp.bfloat16),
+            block_values,
+            preferred_element_type=jnp.float32,
+        )
+        for expo, block_values in parts
     )
-    grouped = query.reshape(rows, kv_local, group, HD)
-    scores = jnp.einsum(
-        "tkgd,skd->kgts", grouped, all_keys, preferred_element_type=jnp.float32
-    ) * QUERY_SCALAR ** (-0.5)
-    distance = positions[:, None] - key_pos[None, :]
-    allowed = (distance >= 0) & (distance < WINDOW) & (key_pos[None, :] >= 0)
-    expo = jnp.where(allowed, jnp.exp(scores), 0.0)
-    total = jnp.sum(expo, axis=-1, keepdims=True)
-    probs = (expo / total).astype(jnp.bfloat16)
-    output = jnp.einsum("kgts,skd->tkgd", probs, all_values, preferred_element_type=jnp.float32)
     return output.reshape(rows, query_cols).astype(jnp.bfloat16)
 
 

time: 145 us -> 151 us (1.041); the launches traced: 143 us -> 148 us
  matrix products: 10.9 us -> 15.3 us
    dot_general x2 -> x6, matrix products: 3.71 us -> 8.15 us  [the longest x3 4.1 us: local(): jnp.einsum('kgts,skd->tkgd', (expo / total).astype(jnp.bfloat16), block_v...]
    unnamed x17 -> x29, local copies, waits for them, and re-layouts: 5.32 us -> 4.18 us
  transfers between devices with their start and end apart: 11 -> 11, of which waited for: 7 -> 6; matrix products, arithmetic and copies ran while one was open for 22% -> 23% of each run, Pallas kernels for 0% -> 0%
where the time goes in v15:
time: 151 us; the launch traced here: 148 us
  starting transfers between devices  40.7 us (27%)
  waiting for transfers between devices  36.7 us (24%)
  local copies, waits for them, and re-layouts  24 us (16%)
  other arithmetic  15.7 us (10%)
  matrix products  15.3 us (10%)
  between operations  15.2 us (10%)
    ppermute x5, starting transfers between devices, ring_gather(): forward = lax.ppermute(forward, axis, right)  20.9 us
    all_gather x1, waiting for transfers between devices, local(): lax.all_gather(padded, ROW, axis=0, tiled=True)  18.5 us
    ppermute x5, waiting for transfers between devices, ring_gather(): forward = lax.ppermute(forward, axis, right)  16.6 us
    ppermute x3, starting transfers between devices, ring_gather(): backward = lax.ppermute(backward, axis, left)  13.4 us
    concatenate x1, local copies, waits for them, and re-layouts, ring_gather(): doubled = jnp.concatenate([stacked, stacked], axis=dim)  7.56 us
    ppermute x2, starting transfers between devices, shifted(): return lax.ppermute(array, axis, pairs)  6.43 us
    concatenate x1, other arithmetic, ring_gather(): doubled = jnp.concatenate([stacked, stacked], axis=dim)  5.2 us
    dot_general x1, matrix products, local(): jnp.dot(whole, ordered(0, query_cols), preferred_element_type=jnp.float32)  5.18 us
  transfers between devices with their start and end apart: 11, of which 6 were waited for; matrix products, arithmetic and copies ran while one was open for 23% of the time, Pallas kernels for 0%

profile of v15, /device:TPU:1, one launch (start us, length us, event | category | flops | bytes accessed | tf_op | source)
XLA Modules:
  0.0 147.7 jit_solution(17656587258627975650)
XLA Ops:
  12.2 4.0 %collective-permute-start.3 = (bf16[520,336]{1,0:T(8,128)(2,1)S(1)}, bf16[520,336]{1,0:T(8,128)(2,1)S(1)}, u32[]{:S(2)}, u32[]{:S(2)}) collective-permute-start(bf16[520,336]{1,0:T(8,128)(2,1)S(1)} %concatenate.50), channel_id=1, source_target_pairs={{0,2},{2,4},{4,6},{6,8},{8,10},{10,12},{12,14},{14,0},{1,3},{3,5},... | collective-permute-start | bytes 1048328 | tf_op jit(solution)/shard_map/ppermute | solution.py:34
  16.3 3.8 %collective-permute-start = (bf16[520,336]{1,0:T(8,128)(2,1)S(1)}, bf16[520,336]{1,0:T(8,128)(2,1)S(1)}, u32[]{:S(2)}, u32[]{:S(2)}) collective-permute-start(bf16[520,336]{1,0:T(8,128)(2,1)S(1)} %concatenate.50), channel_id=1, source_target_pairs={{0,14},{2,0},{4,2},{6,4},{8,6},{10,8},{12,10},{14,12},{1,15},{3,1}... | collective-permute-start | bytes 1048328 | tf_op jit(solution)/shard_map/ppermute | solution.py:37
  20.1 3.3 %collective-permute-done.3 = bf16[520,336]{1,0:T(8,128)(2,1)S(1)} collective-permute-done((bf16[520,336]{1,0:T(8,128)(2,1)S(1)}, bf16[520,336]{1,0:T(8,128)(2,1)S(1)}, u32[]{:S(2)}, u32[]{:S(2)}) %collective-permute-start.3) | collective-permute-done | bytes 349472 | tf_op jit(solution)/shard_map/ppermute | solution.py:34
  23.4 4.0 %collective-permute-start.4 = (bf16[520,336]{1,0:T(8,128)(2,1)S(1)}, bf16[520,336]{1,0:T(8,128)(2,1)S(1)}, u32[]{:S(2)}, u32[]{:S(2)}) collective-permute-start(bf16[520,336]{1,0:T(8,128)(2,1)S(1)} %collective-permute-done.3), channel_id=1, source_target_pairs={{0,2},{2,4},{4,6},{6,8},{8,10},{10,12},{12,14},{14,0},{1,3},{3,5},... | collective-permute-start | bytes 1048328 | tf_op jit(solution)/shard_map/ppermute | solution.py:34
  27.4 4.7 %collective-permute-start.1 = (bf16[520,336]{1,0:T(8,128)(2,1)S(1)}, bf16[520,336]{1,0:T(8,128)(2,1)S(1)}, u32[]{:S(2)}, u32[]{:S(2)}) collective-permute-start(bf16[520,336]{1,0:T(8,128)(2,1)S(1)} %collective-permute-done), channel_id=1, source_target_pairs={{0,14},{2,0},{4,2},{6,4},{8,6},{10,8},{12,10},{14,12},{1,15},{3,1}... | collective-permute-start | bytes 1048328 | tf_op jit(solution)/shard_map/ppermute | solution.py:37
  32.1 3.3 %collective-permute-done.4 = bf16[520,336]{1,0:T(8,128)(2,1)S(1)} collective-permute-done((bf16[520,336]{1,0:T(8,128)(2,1)S(1)}, bf16[520,336]{1,0:T(8,128)(2,1)S(1)}, u32[]{:S(2)}, u32[]{:S(2)}) %collective-permute-start.4) | collective-permute-done | bytes 349472 | tf_op jit(solution)/shard_map/ppermute | solution.py:34
  35.4 3.1 %collective-permute-start.5 = (bf16[520,336]{1,0:T(8,128)(2,1)S(1)}, bf16[520,336]{1,0:T(8,128)(2,1)S(1)}, u32[]{:S(2)}, u32[]{:S(2)}) collective-permute-start(bf16[520,336]{1,0:T(8,128)(2,1)S(1)} %collective-permute-done.4), channel_id=1, source_target_pairs={{0,2},{2,4},{4,6},{6,8},{8,10},{10,12},{12,14},{14,0},{1,3},{3,5},... | collective-permute-start | bytes 1048328 | tf_op jit(solution)/shard_map/ppermute | solution.py:34
  38.4 4.8 %collective-permute-start.2 = (bf16[520,336]{1,0:T(8,128)(2,1)S(1)}, bf16[520,336]{1,0:T(8,128)(2,1)S(1)}, u32[]{:S(2)}, u32[]{:S(2)}) collective-permute-start(bf16[520,336]{1,0:T(8,128)(2,1)S(1)} %collective-permute-done.1), channel_id=1, source_target_pairs={{0,14},{2,0},{4,2},{6,4},{8,6},{10,8},{12,10},{14,12},{1,15},{3,1}... | collective-permute-start | bytes 1048328 | tf_op jit(solution)/shard_map/ppermute | solution.py:37
  43.3 3.3 %collective-permute-done.5 = bf16[520,336]{1,0:T(8,128)(2,1)S(1)} collective-permute-done((bf16[520,336]{1,0:T(8,128)(2,1)S(1)}, bf16[520,336]{1,0:T(8,128)(2,1)S(1)}, u32[]{:S(2)}, u32[]{:S(2)}) %collective-permute-start.5) | collective-permute-done | bytes 349472 | tf_op jit(solution)/shard_map/ppermute | solution.py:34
  46.5 2.2 %collective-permute-start.6 = (bf16[520,336]{1,0:T(8,128)(2,1)S(1)}, bf16[520,336]{1,0:T(8,128)(2,1)S(1)}, u32[]{:S(2)}, u32[]{:S(2)}) collective-permute-start(bf16[520,336]{1,0:T(8,128)(2,1)S(1)} %collective-permute-done.5), channel_id=1, source_target_pairs={{0,2},{2,4},{4,6},{6,8},{8,10},{10,12},{12,14},{14,0},{1,3},{3,5},... | collective-permute-start | bytes 1048328 | tf_op jit(solution)/shard_map/ppermute | solution.py:34
  50.4 6.7 %collective-permute-done.6 = bf16[520,336]{1,0:T(8,128)(2,1)S(1)} collective-permute-done((bf16[520,336]{1,0:T(8,128)(2,1)S(1)}, bf16[520,336]{1,0:T(8,128)(2,1)S(1)}, u32[]{:S(2)}, u32[]{:S(2)}) %collective-permute-start.6) | collective-permute-done | bytes 349472 | tf_op jit(solution)/shard_map/ppermute | solution.py:34
  57.2 7.6 %concatenate.51 = bf16[520,5376]{1,0:T(8,128)(2,1)} concatenate(bf16[520,336]{1,0:T(8,128)(2,1)S(1)} %concatenate.50, bf16[520,336]{1,0:T(8,128)(2,1)S(1)} %collective-permute-done, bf16[520,336]{1,0:T(8,128)(2,1)S(1)} %collective-permute-done.1, bf16[520,336]{1,0:T(8,128)(2,1)S(1)} %collective-permute-done.2, bf16[520,336]{1,0:T(8,128)(2,1)S(1)} %collective-permute-done.6, ...), dimensions={1} | concatenate | bytes 11182080 | tf_op jit(solution)/shard_map/concatenate | solution.py:43
  64.7 3.3 %constant_dynamic-slice_fusion = bf16[520,2688]{1,0:T(8,128)(2,1)S(1)} fusion(bf16[520,5376]{1,0:T(8,128)(2,1)} %concatenate.51, s32[]{:T(128)S(6)} %select_n.28), kind=kLoop, calls=%fused_computation.109 | loop fusion | bytes 5591044 | tf_op jit(solution)/shard_map/dynamic_slice | solution.py:45
  68.0 7.6 %collective-permute-start.7 = (bf16[520,2688]{1,0:T(8,128)(2,1)S(1)}, bf16[520,2688]{1,0:T(8,128)(2,1)}, u32[]{:S(2)}, u32[]{:S(2)}) collective-permute-start(bf16[520,2688]{1,0:T(8,128)(2,1)S(1)} %constant_dynamic-slice_fusion), channel_id=1, source_target_pairs={{0,1},{1,0},{2,3},{3,2},{4,5},{5,4},{6,7},{7,6},{8,9},{9,8},{10,11... | collective-permute-start | bytes 8386568 | tf_op jit(solution)/shard_map/ppermute | solution.py:34
  79.4 1.8 %fusion.27 = (pred[512,512]{0,1:T(8,128)(4,1)}, pred[512,512]{0,1:T(8,128)(4,1)}, pred[512,512]{0,1:T(8,128)(4,1)}) fusion(s32[512]{0:T(512)S(1)} %iota_add_fusion.1, s32[512]{0:T(512)S(1)} %get-tuple-element.31, pred[512]{0:T(512)(128)(4,1)S(1)} %broadcast_compare_fusion.1, pred[512]{0:T(512)(128)(4,1)S(1)} %broadcast_compare_fusion, ...), kind=kLoop, calls=%fused_computation.48 | loop fusion | flops 3932160 | bytes 796160 | tf_op jit(solution)/shard_map/and | solution.py:153
  81.2 5.2 %fusion.5 = bf16[520,5376]{1,0:T(8,128)(2,1)S(1)} fusion(s32[]{:T(128)S(6)} %select_n.30, bf16[520,2688]{1,0:T(8,128)(2,1)S(1)} %constant_dynamic-slice_fusion, bf16[520,2688]{1,0:T(8,128)(2,1)} %collective-permute-done.7), kind=kLoop, calls=%fused_computation.11 | loop fusion | flops 22364160 | bytes 11182084 | tf_op jit(solution)/shard_map/concatenate | solution.py:43
  88.9 18.5 %all-gather.2.cloned.1.call-done = bf16[5632,512]{1,0:T(8,128)(2,1)} async-done(((bf16[176,512]{1,0:T(8,128)(2,1)}), bf16[5632,512]{1,0:T(8,128)(2,1)}) %all-gather.2.cloned.1.call-update) | async-done | bytes 5767184 | tf_op jit(solution)/shard_map/all_gather | solution.py:91
  108.5 3.2 %fusion.66 = (bf16[32,168,256]{2,1,0:T(8,128)(2,1)S(1)}, bf16[32,168,256]{2,1,0:T(8,128)(2,1)S(1)}) fusion(bf16[32,176,512]{2,1,0:T(8,128)(2,1)} %bitcast.114), kind=kLoop, calls=%fused_computation.128 | loop fusion | bytes 11010048 | tf_op jit(solution)/shard_map/slice | solution.py:95
  113.2 2.0 %fusion.34 = f32[512,256]{0,1:T(8,128)S(1)} fusion(bf16[5376,256]{1,0:T(8,128)(2,1)S(1)} %bitcast.116, f32[5376]{0:T(1024)S(1)} %fusion.52, f32[512]{0:T(512)S(1)} %add_rsqrt_fusion.2, bf16[520,5376]{1,0:T(8,128)(2,1)S(1)} %bitcast.109), kind=kOutput, calls=%fused_computation.54 | convolution fusion | flops 1420296192 | bytes 8808448 | tf_op jit(solution)/shard_map/dot_general | solution.py:123
  116.7 2.7 %collective-permute-start.9 = (bf16[512,256]{0,1:T(8,128)(2,1)}, bf16[512,256]{0,1:T(8,128)(2,1)}, u32[]{:S(2)}, u32[]{:S(2)}) collective-permute-start(bf16[512,256]{0,1:T(8,128)(2,1)} %bitcast.6), channel_id=1, source_target_pairs={{0,16},{16,32},{32,48},{48,64},{64,80},{80,96},{96,112},{112,128},... | collective-permute-start | bytes 786440 | tf_op jit(solution)/shard_map/ppermute | solution.py:23
  119.4 3.7 %collective-permute-start.8 = (bf16[512,256]{0,1:T(8,128)(2,1)}, bf16[512,256]{0,1:T(8,128)(2,1)}, u32[]{:S(2)}, u32[]{:S(2)}) collective-permute-start(bf16[512,256]{0,1:T(8,128)(2,1)} %bitcast.6), channel_id=1, source_target_pairs={{0,32},{16,48},{32,64},{48,80},{64,96},{80,112},{96,128},{112,144}... | collective-permute-start | bytes 786440 | tf_op jit(solution)/shard_map/ppermute | solution.py:23
  123.4 3.0 %copy.73 = bf16[256,5376]{1,0:T(8,128)(2,1)} copy(bf16[256,5376]{0,1:T(8,128)(2,1)S(1)} %bitcast.112) | data formatting | bytes 5505024 | tf_op jit(solution)/shard_map/dot_general | solution.py:128
  126.3 5.2 %multiply_reduce_fusion = (f32[512,2]{0,1:T(2,128)S(1)}, f32[512,2,128]{0,2,1:T(8,128)S(1)}) fusion(bf16[2,128,5376]{2,1,0:T(8,128)(2,1)} %bitcast.115, f32[5376]{0:T(1024)} %copy-done.8, f32[512]{0:T(512)S(1)} %add_rsqrt_fusion.2, bf16[520,5376]{1,0:T(8,128)(2,1)} %copy-done), kind=kOutput, calls=%fused_computation.56 | convolution fusion | flops 1420557312 | bytes 8812544 | tf_op jit(solution)/shard_map/dot_general | solution.py:128
  138.3 1.7 %fusion.18 = bf16[128,2,512]{2,0,1:T(8,128)(2,1)S(1)} fusion(f32[128,2,512]{2,0,1:T(8,128)S(1)} %fusion.19, f32[128,2,512]{2,0,1:T(8,128)S(1)} %fusion.21, f32[512,512,2]{1,0,2:T(8,128)S(1)} %get-tuple-element.28, f32[2,512]{1,0:T(2,128)S(1)} %add_add_fusion, pred[512,512]{0,1:T(8,128)(4,1)S(1)} %copy-done.1, bf16[512,2,128]{0,2,1:T(8,128)(2,1)} %bitcast.7), kind=kOutput, calls=%fused_computation.39 | convolution fusion | flops 136708096 | bytes 3805184 | tf_op jit(solution)/shard_map/kgts,skd->tkgd/dot_general | solution.py:157
  (86 shorter events, 23.9 us)
Async XLA Ops:
  6.5 100.9 %all-gather.2.cloned.1.call-start = ((), (), s32[]{:S(2)}) async-start(), calls=%async_computation | async-start | bytes 5947392 | tf_op jit(solution)/shard_map/all_gather | solution.py:91
  12.2 11.1 %collective-permute-start.3 = (bf16[520,336]{1,0:T(8,128)(2,1)S(1)}, bf16[520,336]{1,0:T(8,128)(2,1)S(1)}, u32[]{:S(2)}, u32[]{:S(2)}) collective-permute-start(bf16[520,336]{1,0:T(8,128)(2,1)S(1)} %concatenate.50), channel_id=1, source_target_pairs={{0,2},{2,4},{4,6},{6,8},{8,10},{10,12},{12,14},{14,0},{1,3},{3,5},... | collective-permute-start | bytes 1048328 | tf_op jit(solution)/shard_map/ppermute | solution.py:34
  16.3 11.1 %collective-permute-start = (bf16[520,336]{1,0:T(8,128)(2,1)S(1)}, bf16[520,336]{1,0:T(8,128)(2,1)S(1)}, u32[]{:S(2)}, u32[]{:S(2)}) collective-permute-start(bf16[520,336]{1,0:T(8,128)(2,1)S(1)} %concatenate.50), channel_id=1, source_target_pairs={{0,14},{2,0},{4,2},{6,4},{8,6},{10,8},{12,10},{14,12},{1,15},{3,1}... | collective-permute-start | bytes 1048328 | tf_op jit(solution)/shard_map/ppermute | solution.py:37
  23.4 12.0 %collective-permute-start.4 = (bf16[520,336]{1,0:T(8,128)(2,1)S(1)}, bf16[520,336]{1,0:T(8,128)(2,1)S(1)}, u32[]{:S(2)}, u32[]{:S(2)}) collective-permute-start(bf16[520,336]{1,0:T(8,128)(2,1)S(1)} %collective-permute-done.3), channel_id=1, source_target_pairs={{0,2},{2,4},{4,6},{6,8},{8,10},{10,12},{12,14},{14,0},{1,3},{3,5},... | collective-permute-start | bytes 1048328 | tf_op jit(solution)/shard_map/ppermute | solution.py:34
  27.4 11.1 %collective-permute-start.1 = (bf16[520,336]{1,0:T(8,128)(2,1)S(1)}, bf16[520,336]{1,0:T(8,128)(2,1)S(1)}, u32[]{:S(2)}, u32[]{:S(2)}) collective-permute-start(bf16[520,336]{1,0:T(8,128)(2,1)S(1)} %collective-permute-done), channel_id=1, source_target_pairs={{0,14},{2,0},{4,2},{6,4},{8,6},{10,8},{12,10},{14,12},{1,15},{3,1}... | collective-permute-start | bytes 1048328 | tf_op jit(solution)/shard_map/ppermute | solution.py:37
  35.4 11.2 %collective-permute-start.5 = (bf16[520,336]{1,0:T(8,128)(2,1)S(1)}, bf16[520,336]{1,0:T(8,128)(2,1)S(1)}, u32[]{:S(2)}, u32[]{:S(2)}) collective-permute-start(bf16[520,336]{1,0:T(8,128)(2,1)S(1)} %collective-permute-done.4), channel_id=1, source_target_pairs={{0,2},{2,4},{4,6},{6,8},{8,10},{10,12},{12,14},{14,0},{1,3},{3,5},... | collective-permute-start | bytes 1048328 | tf_op jit(solution)/shard_map/ppermute | solution.py:34
  38.4 12.0 %collective-permute-start.2 = (bf16[520,336]{1,0:T(8,128)(2,1)S(1)}, bf16[520,336]{1,0:T(8,128)(2,1)S(1)}, u32[]{:S(2)}, u32[]{:S(2)}) collective-permute-start(bf16[520,336]{1,0:T(8,128)(2,1)S(1)} %collective-permute-done.1), channel_id=1, source_target_pairs={{0,14},{2,0},{4,2},{6,4},{8,6},{10,8},{12,10},{14,12},{1,15},{3,1}... | collective-permute-start | bytes 1048328 | tf_op jit(solution)/shard_map/ppermute | solution.py:37
  46.5 10.6 %collective-permute-start.6 = (bf16[520,336]{1,0:T(8,128)(2,1)S(1)}, bf16[520,336]{1,0:T(8,128)(2,1)S(1)}, u32[]{:S(2)}, u32[]{:S(2)}) collective-permute-start(bf16[520,336]{1,0:T(8,128)(2,1)S(1)} %collective-permute-done.5), channel_id=1, source_target_pairs={{0,2},{2,4},{4,6},{6,8},{8,10},{10,12},{12,14},{14,0},{1,3},{3,5},... | collective-permute-start | bytes 1048328 | tf_op jit(solution)/shard_map/ppermute | solution.py:34
  68.0 13.2 %collective-permute-start.7 = (bf16[520,2688]{1,0:T(8,128)(2,1)S(1)}, bf16[520,2688]{1,0:T(8,128)(2,1)}, u32[]{:S(2)}, u32[]{:S(2)}) collective-permute-start(bf16[520,2688]{1,0:T(8,128)(2,1)S(1)} %constant_dynamic-slice_fusion), channel_id=1, source_target_pairs={{0,1},{1,0},{2,3},{3,2},{4,5},{5,4},{6,7},{7,6},{8,9},{9,8},{10,11... | collective-permute-start | bytes 8386568 | tf_op jit(solution)/shard_map/ppermute | solution.py:34
  86.4 2.5 %copy-start = (bf16[520,5376]{1,0:T(8,128)(2,1)}, bf16[520,5376]{1,0:T(8,128)(2,1)S(1)}, u32[]{:S(2)}) copy-start(bf16[520,5376]{1,0:T(8,128)(2,1)S(1)} %fusion.5) | copy-start | bytes 16773124
  86.5 26.6 %copy-start.8 = (f32[5376]{0:T(1024)}, f32[5376]{0:T(1024)S(1)}, u32[]{:S(2)}) copy-start(f32[5376]{0:T(1024)S(1)} %fusion.52) | copy-start | bytes 64516
  108.5 4.7 %slice-start = ((s8[5591040]{0:T(1024)(128)(4,1)}), s8[4194304]{0:T(1024)(128)(4,1)S(1)}, s32[]{:S(2)}) async-start(s8[5591040]{0:T(1024)(128)(4,1)} %bitcast.108), calls=%async_computation.1 | async-start | bytes 8388608
  111.7 1.5 %slice-start.1 = ((s8[5591040]{0:T(1024)(128)(4,1)}), s8[1396736]{0:T(1024)(128)(4,1)S(1)}, s32[]{:S(2)}) async-start(s8[5591040]{0:T(1024)(128)(4,1)} %bitcast.108), calls=%async_computation.2 | async-start | bytes 2793472
  113.2 2.1 %copy-start.9 = (f32[128]{0:T(128)S(1)}, f32[128]{0:T(128)}, u32[]{:S(2)}) copy-start(f32[128]{0:T(128)} %param.10) | copy-start | bytes 1540
  116.0 7.4 %copy-start.4 = (bf16[512,1,64]{0,2,1:T(8,128)(2,1)}, bf16[512,1,64]{0,2,1:T(8,128)(2,1)S(1)}, u32[]{:S(2)}) copy-start(bf16[512,1,64]{0,2,1:T(8,128)(2,1)S(1)} %get-tuple-element.9) | copy-start | bytes 196612
  116.0 7.4 %copy-start.6 = (bf16[512,1,64]{0,2,1:T(8,128)(2,1)}, bf16[512,1,64]{0,2,1:T(8,128)(2,1)S(1)}, u32[]{:S(2)}) copy-start(bf16[512,1,64]{0,2,1:T(8,128)(2,1)S(1)} %get-tuple-element.10) | copy-start | bytes 196612
  116.7 15.8 %collective-permute-start.9 = (bf16[512,256]{0,1:T(8,128)(2,1)}, bf16[512,256]{0,1:T(8,128)(2,1)}, u32[]{:S(2)}, u32[]{:S(2)}) collective-permute-start(bf16[512,256]{0,1:T(8,128)(2,1)} %bitcast.6), channel_id=1, source_target_pairs={{0,16},{16,32},{32,48},{48,64},{64,80},{80,96},{96,112},{112,128},... | collective-permute-start | bytes 786440 | tf_op jit(solution)/shard_map/ppermute | solution.py:23
  119.4 14.8 %collective-permute-start.8 = (bf16[512,256]{0,1:T(8,128)(2,1)}, bf16[512,256]{0,1:T(8,128)(2,1)}, u32[]{:S(2)}, u32[]{:S(2)}) collective-permute-start(bf16[512,256]{0,1:T(8,128)(2,1)} %bitcast.6), channel_id=1, source_target_pairs={{0,32},{16,48},{32,64},{48,80},{64,96},{80,112},{96,128},{112,144}... | collective-permute-start | bytes 786440 | tf_op jit(solution)/shard_map/ppermute | solution.py:23
  126.3 5.2 %copy-start.10 = (f32[128]{0:T(128)S(1)}, f32[128]{0:T(128)}, u32[]{:S(2)}) copy-start(f32[128]{0:T(128)} %param.9) | copy-start | bytes 1540
  126.3 5.4 %copy-start.2 = (pred[512,512]{0,1:T(8,128)(4,1)S(1)}, pred[512,512]{0,1:T(8,128)(4,1)}, u32[]{:S(2)}) copy-start(pred[512,512]{0,1:T(8,128)(4,1)} %get-tuple-element.14) | copy-start | bytes 786436
  126.3 5.4 %copy-start.5 = (bf16[512,1,64]{0,2,1:T(8,128)(2,1)S(1)}, bf16[512,1,64]{0,2,1:T(8,128)(2,1)}, u32[]{:S(2)}) copy-start(bf16[512,1,64]{0,2,1:T(8,128)(2,1)} %copy-done.4) | copy-start | bytes 196612
  126.3 5.5 %copy-start.7 = (bf16[512,1,64]{0,2,1:T(8,128)(2,1)S(1)}, bf16[512,1,64]{0,2,1:T(8,128)(2,1)}, u32[]{:S(2)}) copy-start(bf16[512,1,64]{0,2,1:T(8,128)(2,1)} %copy-done.6) | copy-start | bytes 196612
  131.5 1.0 copy-start.3
  131.8 2.4 %copy-start.1 = (pred[512,512]{0,1:T(8,128)(4,1)S(1)}, pred[512,512]{0,1:T(8,128)(4,1)}, u32[]{:S(2)}) copy-start(pred[512,512]{0,1:T(8,128)(4,1)} %get-tuple-element.15) | copy-start | bytes 786436
Sparse Core Ops, SparseCore 0:
  10.5 96.8 all-gather.1

commit v16 on v14

--- a/solution.py
+++ b/solution.py
@@ -154,7 +154,7 @@
     allowed = (distance >= 0) & (distance < WINDOW) & (key_pos[None, :] >= 0)
     expo = jnp.where(allowed, jnp.exp(scores), 0.0)
     total = jnp.sum(expo, axis=-1, keepdims=True)
-    probs = (expo / total).astype(jnp.bfloat16)
+    probs = (expo * (1.0 / total)).astype(jnp.bfloat16)
     output = jnp.einsum("kgts,skd->tkgd", probs, all_values, preferred_element_type=jnp.float32)
     return output.reshape(rows, query_cols).astype(jnp.bfloat16)
 

time: 145 us -> 145 us (level)
  no operation moved by 1% of the time
where the time goes in v16:
time: 145 us; the launch traced here: 143 us
  starting transfers between devices  40.8 us (28%)
  waiting for transfers between devices  37.1 us (26%)
  local copies, waits for them, and re-layouts  25.3 us (17%)
  other arithmetic  14.8 us (10%)
  between operations  14.5 us (10%)
  matrix products  10.9 us (8%)
    ppermute x5, starting transfers between devices, ring_gather(): forward = lax.ppermute(forward, axis, right)  21.1 us
    all_gather x1, waiting for transfers between devices, local(): lax.all_gather(padded, ROW, axis=0, tiled=True)  18 us
    ppermute x5, waiting for transfers between devices, ring_gather(): forward = lax.ppermute(forward, axis, right)  17.4 us
    ppermute x3, starting transfers between devices, ring_gather(): backward = lax.ppermute(backward, axis, left)  13.4 us
    concatenate x1, local copies, waits for them, and re-layouts, ring_gather(): doubled = jnp.concatenate([stacked, stacked], axis=dim)  7.61 us
    ppermute x2, starting transfers between devices, shifted(): return lax.ppermute(array, axis, pairs)  6.34 us
    unnamed x17, local copies, waits for them, and re-layouts  5.32 us
    dot_general x1, matrix products, local(): jnp.dot(whole, ordered(0, query_cols), preferred_element_type=jnp.float32)  5.19 us
  transfers between devices with their start and end apart: 11, of which 7 were waited for; matrix products, arithmetic and copies ran while one was open for 22% of the time, Pallas kernels for 0%

profile of v16, /device:TPU:1, one launch (start us, length us, event | category | flops | bytes accessed | tf_op | source)
XLA Modules:
  0.0 143.5 jit_solution(2620232435003202262)
XLA Ops:
  12.2 4.0 %collective-permute-start.3 = (bf16[520,336]{1,0:T(8,128)(2,1)S(1)}, bf16[520,336]{1,0:T(8,128)(2,1)S(1)}, u32[]{:S(2)}, u32[]{:S(2)}) collective-permute-start(bf16[520,336]{1,0:T(8,128)(2,1)S(1)} %concatenate.48), channel_id=1, source_target_pairs={{0,2},{2,4},{4,6},{6,8},{8,10},{10,12},{12,14},{14,0},{1,3},{3,5},... | collective-permute-start | bytes 1048328 | tf_op jit(solution)/shard_map/ppermute | solution.py:34
  16.3 3.8 %collective-permute-start = (bf16[520,336]{1,0:T(8,128)(2,1)S(1)}, bf16[520,336]{1,0:T(8,128)(2,1)S(1)}, u32[]{:S(2)}, u32[]{:S(2)}) collective-permute-start(bf16[520,336]{1,0:T(8,128)(2,1)S(1)} %concatenate.48), channel_id=1, source_target_pairs={{0,14},{2,0},{4,2},{6,4},{8,6},{10,8},{12,10},{14,12},{1,15},{3,1}... | collective-permute-start | bytes 1048328 | tf_op jit(solution)/shard_map/ppermute | solution.py:37
  20.1 3.3 %collective-permute-done.3 = bf16[520,336]{1,0:T(8,128)(2,1)S(1)} collective-permute-done((bf16[520,336]{1,0:T(8,128)(2,1)S(1)}, bf16[520,336]{1,0:T(8,128)(2,1)S(1)}, u32[]{:S(2)}, u32[]{:S(2)}) %collective-permute-start.3) | collective-permute-done | bytes 349472 | tf_op jit(solution)/shard_map/ppermute | solution.py:34
  23.4 4.0 %collective-permute-start.4 = (bf16[520,336]{1,0:T(8,128)(2,1)S(1)}, bf16[520,336]{1,0:T(8,128)(2,1)S(1)}, u32[]{:S(2)}, u32[]{:S(2)}) collective-permute-start(bf16[520,336]{1,0:T(8,128)(2,1)S(1)} %collective-permute-done.3), channel_id=1, source_target_pairs={{0,2},{2,4},{4,6},{6,8},{8,10},{10,12},{12,14},{14,0},{1,3},{3,5},... | collective-permute-start | bytes 1048328 | tf_op jit(solution)/shard_map/ppermute | solution.py:34
  27.4 4.7 %collective-permute-start.1 = (bf16[520,336]{1,0:T(8,128)(2,1)S(1)}, bf16[520,336]{1,0:T(8,128)(2,1)S(1)}, u32[]{:S(2)}, u32[]{:S(2)}) collective-permute-start(bf16[520,336]{1,0:T(8,128)(2,1)S(1)} %collective-permute-done), channel_id=1, source_target_pairs={{0,14},{2,0},{4,2},{6,4},{8,6},{10,8},{12,10},{14,12},{1,15},{3,1}... | collective-permute-start | bytes 1048328 | tf_op jit(solution)/shard_map/ppermute | solution.py:37
  32.1 3.3 %collective-permute-done.4 = bf16[520,336]{1,0:T(8,128)(2,1)S(1)} collective-permute-done((bf16[520,336]{1,0:T(8,128)(2,1)S(1)}, bf16[520,336]{1,0:T(8,128)(2,1)S(1)}, u32[]{:S(2)}, u32[]{:S(2)}) %collective-permute-start.4) | collective-permute-done | bytes 349472 | tf_op jit(solution)/shard_map/ppermute | solution.py:34
  35.4 3.1 %collective-permute-start.5 = (bf16[520,336]{1,0:T(8,128)(2,1)S(1)}, bf16[520,336]{1,0:T(8,128)(2,1)S(1)}, u32[]{:S(2)}, u32[]{:S(2)}) collective-permute-start(bf16[520,336]{1,0:T(8,128)(2,1)S(1)} %collective-permute-done.4), channel_id=1, source_target_pairs={{0,2},{2,4},{4,6},{6,8},{8,10},{10,12},{12,14},{14,0},{1,3},{3,5},... | collective-permute-start | bytes 1048328 | tf_op jit(solution)/shard_map/ppermute | solution.py:34
  38.4 4.8 %collective-permute-start.2 = (bf16[520,336]{1,0:T(8,128)(2,1)S(1)}, bf16[520,336]{1,0:T(8,128)(2,1)S(1)}, u32[]{:S(2)}, u32[]{:S(2)}) collective-permute-start(bf16[520,336]{1,0:T(8,128)(2,1)S(1)} %collective-permute-done.1), channel_id=1, source_target_pairs={{0,14},{2,0},{4,2},{6,4},{8,6},{10,8},{12,10},{14,12},{1,15},{3,1}... | collective-permute-start | bytes 1048328 | tf_op jit(solution)/shard_map/ppermute | solution.py:37
  43.3 3.3 %collective-permute-done.5 = bf16[520,336]{1,0:T(8,128)(2,1)S(1)} collective-permute-done((bf16[520,336]{1,0:T(8,128)(2,1)S(1)}, bf16[520,336]{1,0:T(8,128)(2,1)S(1)}, u32[]{:S(2)}, u32[]{:S(2)}) %collective-permute-start.5) | collective-permute-done | bytes 349472 | tf_op jit(solution)/shard_map/ppermute | solution.py:34
  46.5 2.2 %collective-permute-start.6 = (bf16[520,336]{1,0:T(8,128)(2,1)S(1)}, bf16[520,336]{1,0:T(8,128)(2,1)S(1)}, u32[]{:S(2)}, u32[]{:S(2)}) collective-permute-start(bf16[520,336]{1,0:T(8,128)(2,1)S(1)} %collective-permute-done.5), channel_id=1, source_target_pairs={{0,2},{2,4},{4,6},{6,8},{8,10},{10,12},{12,14},{14,0},{1,3},{3,5},... | collective-permute-start | bytes 1048328 | tf_op jit(solution)/shard_map/ppermute | solution.py:34
  50.4 6.7 %collective-permute-done.6 = bf16[520,336]{1,0:T(8,128)(2,1)S(1)} collective-permute-done((bf16[520,336]{1,0:T(8,128)(2,1)S(1)}, bf16[520,336]{1,0:T(8,128)(2,1)S(1)}, u32[]{:S(2)}, u32[]{:S(2)}) %collective-permute-start.6) | collective-permute-done | bytes 349472 | tf_op jit(solution)/shard_map/ppermute | solution.py:34
  57.2 7.6 %concatenate.49 = bf16[520,5376]{1,0:T(8,128)(2,1)} concatenate(bf16[520,336]{1,0:T(8,128)(2,1)S(1)} %concatenate.48, bf16[520,336]{1,0:T(8,128)(2,1)S(1)} %collective-permute-done, bf16[520,336]{1,0:T(8,128)(2,1)S(1)} %collective-permute-done.1, bf16[520,336]{1,0:T(8,128)(2,1)S(1)} %collective-permute-done.2, bf16[520,336]{1,0:T(8,128)(2,1)S(1)} %collective-permute-done.6, ...), dimensions={1} | concatenate | bytes 11182080 | tf_op jit(solution)/shard_map/concatenate | solution.py:43
  64.8 3.3 %constant_dynamic-slice_fusion = bf16[520,2688]{1,0:T(8,128)(2,1)S(1)} fusion(bf16[520,5376]{1,0:T(8,128)(2,1)} %concatenate.49, s32[]{:T(128)S(6)} %select_n.22), kind=kLoop, calls=%fused_computation.82 | loop fusion | bytes 5591044 | tf_op jit(solution)/shard_map/dynamic_slice | solution.py:45
  68.1 7.8 %collective-permute-start.7 = (bf16[520,2688]{1,0:T(8,128)(2,1)S(1)}, bf16[520,2688]{1,0:T(8,128)(2,1)}, u32[]{:S(2)}, u32[]{:S(2)}) collective-permute-start(bf16[520,2688]{1,0:T(8,128)(2,1)S(1)} %constant_dynamic-slice_fusion), channel_id=1, source_target_pairs={{0,1},{1,0},{2,3},{3,2},{4,5},{5,4},{6,7},{7,6},{8,9},{9,8},{10,11... | collective-permute-start | bytes 8386568 | tf_op jit(solution)/shard_map/ppermute | solution.py:34
  80.6 5.2 %fusion.5 = bf16[520,5376]{1,0:T(8,128)(2,1)S(1)} fusion(s32[]{:T(128)S(6)} %select_n.24, bf16[520,2688]{1,0:T(8,128)(2,1)S(1)} %constant_dynamic-slice_fusion, bf16[520,2688]{1,0:T(8,128)(2,1)} %collective-permute-done.7), kind=kLoop, calls=%fused_computation.13 | loop fusion | flops 22364160 | bytes 11182084 | tf_op jit(solution)/shard_map/concatenate | solution.py:43
  85.8 2.4 %copy-done = bf16[520,5376]{1,0:T(8,128)(2,1)} copy-done((bf16[520,5376]{1,0:T(8,128)(2,1)}, bf16[520,5376]{1,0:T(8,128)(2,1)S(1)}, u32[]{:S(2)}) %copy-start) | copy-done | bytes 5591064
  89.4 18.0 %all-gather.2.cloned.1.call-done = bf16[5632,512]{1,0:T(8,128)(2,1)} async-done(((bf16[176,512]{1,0:T(8,128)(2,1)}), bf16[5632,512]{1,0:T(8,128)(2,1)}) %all-gather.2.cloned.1.call-update) | async-done | bytes 5767184 | tf_op jit(solution)/shard_map/all_gather | solution.py:91
  108.5 3.2 %fusion.49 = (bf16[32,168,256]{2,1,0:T(8,128)(2,1)S(1)}, bf16[32,168,256]{2,1,0:T(8,128)(2,1)S(1)}) fusion(bf16[32,176,512]{2,1,0:T(8,128)(2,1)} %bitcast.69), kind=kLoop, calls=%fused_computation.92 | loop fusion | bytes 11010048 | tf_op jit(solution)/shard_map/slice | solution.py:95
  113.2 2.0 %fusion.25 = f32[512,256]{0,1:T(8,128)S(1)} fusion(bf16[5376,256]{1,0:T(8,128)(2,1)S(1)} %bitcast.71, f32[5376]{0:T(1024)S(1)} %fusion.41, f32[512]{0:T(512)S(1)} %add_rsqrt_fusion.2, bf16[520,5376]{1,0:T(8,128)(2,1)S(1)} %bitcast.64), kind=kOutput, calls=%fused_computation.33 | convolution fusion | flops 1420296192 | bytes 8808448 | tf_op jit(solution)/shard_map/dot_general | solution.py:123
  116.0 3.7 %collective-permute-start.8 = (bf16[512,256]{0,1:T(8,128)(2,1)S(1)}, bf16[512,256]{0,1:T(8,128)(2,1)}, u32[]{:S(2)}, u32[]{:S(2)}) collective-permute-start(bf16[512,256]{0,1:T(8,128)(2,1)S(1)} %bitcast.72), channel_id=1, source_target_pairs={{0,32},{16,48},{32,64},{48,80},{64,96},{80,112},{96,128},{112,144}... | collective-permute-start | bytes 786440 | tf_op jit(solution)/shard_map/ppermute | solution.py:23
  119.7 2.6 %collective-permute-start.9 = (bf16[512,256]{0,1:T(8,128)(2,1)S(1)}, bf16[512,256]{0,1:T(8,128)(2,1)}, u32[]{:S(2)}, u32[]{:S(2)}) collective-permute-start(bf16[512,256]{0,1:T(8,128)(2,1)S(1)} %bitcast.73), channel_id=1, source_target_pairs={{0,16},{16,32},{32,48},{48,64},{64,80},{80,96},{96,112},{112,128},... | collective-permute-start | bytes 786440 | tf_op jit(solution)/shard_map/ppermute | solution.py:23
  122.5 3.0 %copy.46 = bf16[256,5376]{1,0:T(8,128)(2,1)} copy(bf16[256,5376]{0,1:T(8,128)(2,1)S(1)} %bitcast.67) | data formatting | bytes 5505024 | tf_op jit(solution)/shard_map/dot_general | solution.py:128
  125.5 5.2 %multiply_reduce_fusion = (f32[512,2]{0,1:T(2,128)S(1)}, f32[512,2,128]{0,2,1:T(8,128)S(1)}) fusion(bf16[2,128,5376]{2,1,0:T(8,128)(2,1)} %bitcast.70, f32[5376]{0:T(1024)} %copy-done.2, f32[512]{0:T(512)S(1)} %add_rsqrt_fusion.2, bf16[520,5376]{1,0:T(8,128)(2,1)} %copy-done), kind=kOutput, calls=%fused_computation.36 | convolution fusion | flops 1420557312 | bytes 8812544 | tf_op jit(solution)/shard_map/dot_general | solution.py:128
  133.8 2.0 %fusion.21 = bf16[128,2,512]{2,0,1:T(8,128)(2,1)S(1)} fusion(f32[1536,512,2]{1,0,2:T(8,128)S(1)} %get-tuple-element.23, f32[2,512]{1,0:T(2,128)S(1)} %broadcast_divide_fusion, pred[512,1536]{0,1:T(8,128)(4,1)S(1)} %copy-done.1, bf16[1536,2,128]{0,2,1:T(8,128)(2,1)S(1)} %maximum_maximum_fusion), kind=kOutput, calls=%fused_computation.32 | convolution fusion | flops 409075712 | bytes 7737344 | tf_op jit(solution)/shard_map/kgts,skd->tkgd/dot_general | solution.py:158
  (68 shorter events, 19.8 us)
Async XLA Ops:
  6.5 100.9 %all-gather.2.cloned.1.call-start = ((), (), s32[]{:S(2)}) async-start(), calls=%async_computation | async-start | bytes 5947392 | tf_op jit(solution)/shard_map/all_gather | solution.py:91
  12.2 11.1 %collective-permute-start.3 = (bf16[520,336]{1,0:T(8,128)(2,1)S(1)}, bf16[520,336]{1,0:T(8,128)(2,1)S(1)}, u32[]{:S(2)}, u32[]{:S(2)}) collective-permute-start(bf16[520,336]{1,0:T(8,128)(2,1)S(1)} %concatenate.48), channel_id=1, source_target_pairs={{0,2},{2,4},{4,6},{6,8},{8,10},{10,12},{12,14},{14,0},{1,3},{3,5},... | collective-permute-start | bytes 1048328 | tf_op jit(solution)/shard_map/ppermute | solution.py:34
  16.3 11.1 %collective-permute-start = (bf16[520,336]{1,0:T(8,128)(2,1)S(1)}, bf16[520,336]{1,0:T(8,128)(2,1)S(1)}, u32[]{:S(2)}, u32[]{:S(2)}) collective-permute-start(bf16[520,336]{1,0:T(8,128)(2,1)S(1)} %concatenate.48), channel_id=1, source_target_pairs={{0,14},{2,0},{4,2},{6,4},{8,6},{10,8},{12,10},{14,12},{1,15},{3,1}... | collective-permute-start | bytes 1048328 | tf_op jit(solution)/shard_map/ppermute | solution.py:37
  23.4 12.0 %collective-permute-start.4 = (bf16[520,336]{1,0:T(8,128)(2,1)S(1)}, bf16[520,336]{1,0:T(8,128)(2,1)S(1)}, u32[]{:S(2)}, u32[]{:S(2)}) collective-permute-start(bf16[520,336]{1,0:T(8,128)(2,1)S(1)} %collective-permute-done.3), channel_id=1, source_target_pairs={{0,2},{2,4},{4,6},{6,8},{8,10},{10,12},{12,14},{14,0},{1,3},{3,5},... | collective-permute-start | bytes 1048328 | tf_op jit(solution)/shard_map/ppermute | solution.py:34
  27.4 11.1 %collective-permute-start.1 = (bf16[520,336]{1,0:T(8,128)(2,1)S(1)}, bf16[520,336]{1,0:T(8,128)(2,1)S(1)}, u32[]{:S(2)}, u32[]{:S(2)}) collective-permute-start(bf16[520,336]{1,0:T(8,128)(2,1)S(1)} %collective-permute-done), channel_id=1, source_target_pairs={{0,14},{2,0},{4,2},{6,4},{8,6},{10,8},{12,10},{14,12},{1,15},{3,1}... | collective-permute-start | bytes 1048328 | tf_op jit(solution)/shard_map/ppermute | solution.py:37
  35.4 11.2 %collective-permute-start.5 = (bf16[520,336]{1,0:T(8,128)(2,1)S(1)}, bf16[520,336]{1,0:T(8,128)(2,1)S(1)}, u32[]{:S(2)}, u32[]{:S(2)}) collective-permute-start(bf16[520,336]{1,0:T(8,128)(2,1)S(1)} %collective-permute-done.4), channel_id=1, source_target_pairs={{0,2},{2,4},{4,6},{6,8},{8,10},{10,12},{12,14},{14,0},{1,3},{3,5},... | collective-permute-start | bytes 1048328 | tf_op jit(solution)/shard_map/ppermute | solution.py:34
  38.4 12.0 %collective-permute-start.2 = (bf16[520,336]{1,0:T(8,128)(2,1)S(1)}, bf16[520,336]{1,0:T(8,128)(2,1)S(1)}, u32[]{:S(2)}, u32[]{:S(2)}) collective-permute-start(bf16[520,336]{1,0:T(8,128)(2,1)S(1)} %collective-permute-done.1), channel_id=1, source_target_pairs={{0,14},{2,0},{4,2},{6,4},{8,6},{10,8},{12,10},{14,12},{1,15},{3,1}... | collective-permute-start | bytes 1048328 | tf_op jit(solution)/shard_map/ppermute | solution.py:37
  46.5 10.6 %collective-permute-start.6 = (bf16[520,336]{1,0:T(8,128)(2,1)S(1)}, bf16[520,336]{1,0:T(8,128)(2,1)S(1)}, u32[]{:S(2)}, u32[]{:S(2)}) collective-permute-start(bf16[520,336]{1,0:T(8,128)(2,1)S(1)} %collective-permute-done.5), channel_id=1, source_target_pairs={{0,2},{2,4},{4,6},{6,8},{8,10},{10,12},{12,14},{14,0},{1,3},{3,5},... | collective-permute-start | bytes 1048328 | tf_op jit(solution)/shard_map/ppermute | solution.py:34
  68.1 12.5 %collective-permute-start.7 = (bf16[520,2688]{1,0:T(8,128)(2,1)S(1)}, bf16[520,2688]{1,0:T(8,128)(2,1)}, u32[]{:S(2)}, u32[]{:S(2)}) collective-permute-start(bf16[520,2688]{1,0:T(8,128)(2,1)S(1)} %constant_dynamic-slice_fusion), channel_id=1, source_target_pairs={{0,1},{1,0},{2,3},{3,2},{4,5},{5,4},{6,7},{7,6},{8,9},{9,8},{10,11... | collective-permute-start | bytes 8386568 | tf_op jit(solution)/shard_map/ppermute | solution.py:34
  85.7 2.5 %copy-start = (bf16[520,5376]{1,0:T(8,128)(2,1)}, bf16[520,5376]{1,0:T(8,128)(2,1)S(1)}, u32[]{:S(2)}) copy-start(bf16[520,5376]{1,0:T(8,128)(2,1)S(1)} %fusion.5) | copy-start | bytes 16773124
  88.2 24.9 %copy-start.2 = (f32[5376]{0:T(1024)}, f32[5376]{0:T(1024)S(1)}, u32[]{:S(2)}) copy-start(f32[5376]{0:T(1024)S(1)} %fusion.41) | copy-start | bytes 64516
  108.5 4.7 %slice-start = ((s8[5591040]{0:T(1024)(128)(4,1)}), s8[4194304]{0:T(1024)(128)(4,1)S(1)}, s32[]{:S(2)}) async-start(s8[5591040]{0:T(1024)(128)(4,1)} %bitcast.63), calls=%async_computation.1 | async-start | bytes 8388608
  111.7 1.5 %slice-start.1 = ((s8[5591040]{0:T(1024)(128)(4,1)}), s8[1396736]{0:T(1024)(128)(4,1)S(1)}, s32[]{:S(2)}) async-start(s8[5591040]{0:T(1024)(128)(4,1)} %bitcast.63), calls=%async_computation.2 | async-start | bytes 2793472
  113.2 2.1 %copy-start.3 = (f32[128]{0:T(128)S(1)}, f32[128]{0:T(128)}, u32[]{:S(2)}) copy-start(f32[128]{0:T(128)} %param.10) | copy-start | bytes 1540
  116.0 15.0 %collective-permute-start.8 = (bf16[512,256]{0,1:T(8,128)(2,1)S(1)}, bf16[512,256]{0,1:T(8,128)(2,1)}, u32[]{:S(2)}, u32[]{:S(2)}) collective-permute-start(bf16[512,256]{0,1:T(8,128)(2,1)S(1)} %bitcast.72), channel_id=1, source_target_pairs={{0,32},{16,48},{32,64},{48,80},{64,96},{80,112},{96,128},{112,144}... | collective-permute-start | bytes 786440 | tf_op jit(solution)/shard_map/ppermute | solution.py:23
  119.7 11.2 %collective-permute-start.9 = (bf16[512,256]{0,1:T(8,128)(2,1)S(1)}, bf16[512,256]{0,1:T(8,128)(2,1)}, u32[]{:S(2)}, u32[]{:S(2)}) collective-permute-start(bf16[512,256]{0,1:T(8,128)(2,1)S(1)} %bitcast.73), channel_id=1, source_target_pairs={{0,16},{16,32},{32,48},{48,64},{64,80},{80,96},{96,112},{112,128},... | collective-permute-start | bytes 786440 | tf_op jit(solution)/shard_map/ppermute | solution.py:23
  125.5 5.2 %copy-start.4 = (f32[128]{0:T(128)S(1)}, f32[128]{0:T(128)}, u32[]{:S(2)}) copy-start(f32[128]{0:T(128)} %param.9) | copy-start | bytes 1540
  125.5 6.5 %copy-start.1 = (pred[512,1536]{0,1:T(8,128)(4,1)S(1)}, pred[512,1536]{0,1:T(8,128)(4,1)}, u32[]{:S(2)}) copy-start(pred[512,1536]{0,1:T(8,128)(4,1)} %fusion.17) | copy-start | bytes 2359300
Sparse Core Ops, SparseCore 0:
  10.5 96.8 all-gather.1
